TPU v7x, 512 devices: a whole 4x8x8 slice. The times are simulated.
512 devices in a mesh: rep: 8 (over y), tp: 64 (over z, x, core).
Axes of the slice: x: 4, y: 8, z: 8, core: 2. Of those that a mesh axis runs over, the one named last changes fastest.
Arguments:
- hidden: float32 [256, 2304], P('rep', 'tp'), parts along dimension 0
- attn_gain: float32 [2304], P('tp'), may hold values from 0.5 to 1.5
- w_qkv: bfloat16 [2304, 6912], P('tp'), may hold values from -0.125 to 0.125
- w_out: bfloat16 [2304, 2304], P(None, 'tp'), may hold values from -0.125 to 0.125
- prefix_keys: bfloat16 [24, 2048, 2304], P('rep', 'tp'), parts along dimension 0
- prefix_values: bfloat16 [24, 2048, 2304], P('rep', 'tp'), parts along dimension 0, may hold values from -6 to 6
- private_keys: bfloat16 [64, 512, 2304], P('rep', 'tp'), parts along dimension 0, may hold values from -15 to 15
- private_values: bfloat16 [64, 512, 2304], P('rep', 'tp'), parts along dimension 0, may hold values from -6 to 6
- group_ids: int32 [64], P('rep'), parts along dimension 0, may hold values from 0 to 2
- private_lengths: int32 [64], P('rep'), parts along dimension 0, may hold values from 1 to 512, as said below
- moe_gain: float32 [2304], replicated, may hold values from 0.5 to 1.5
- router: bfloat16 [2304, 4], replicated, may hold values from -0.25 to 0.25
- w_gate: bfloat16 [2304, 11520], P(None, 'tp'), may hold values from -0.125 to 0.125
- w_up: bfloat16 [2304, 11520], P(None, 'tp'), may hold values from -0.125 to 0.125
- w_down: bfloat16 [11520, 2304], P('tp'), may hold values from -0.3125 to 0.3125
- routes: int32 [256, 2], P('rep'), parts along dimension 0, may hold values from 0 to 3, all different within a row
Outputs:
- mixed: float32 [256, 2304], P('rep', 'tp'), parts along dimension 0
There are 8 independent parts, one for each index of `rep`. A program takes and returns all parts, laid end to end along the dimension named above; an argument that names none is the same for every part. Nothing has to cross between parts.
Inputs may be any that keep to these rules, and one draw needn't show every extreme that they name: `private_lengths`: some request of every draw has all 512 positions live. `routes`: the two experts of a token differ.
All inputs are finite; a program needn't handle non-finite values.
Results may differ from a plain program's by a relative error of at most 0.0083.
Values may be sent and summed in bfloat16 or wider, within the bound.
No kernel may reach another device: no remote copies, remote signals or barrier semaphores. Data moves between devices by JAX's collectives and lax.ppermute only.
A program may use at most 128 MiB of HBM per device.

v0:
```python
import jax
import jax.numpy as jnp
from jax import lax
from jax.sharding import PartitionSpec as P

HEADS = 36
HDIM = 64
FF = 2880
NEW = 4


EPSILON = 1e-05
BLOCKED = -1e30


def rotate_heads(vectors, places):
    half_dim = HDIM // 2
    frequencies = 10000.0 ** (-jnp.arange(half_dim, dtype=jnp.float32) / half_dim)
    angles = places.astype(jnp.float32)[:, None] * frequencies[None, :]
    cosine = jnp.cos(angles)[:, None, :]
    sine_part = jnp.sin(angles)[:, None, :]
    first = vectors[..., :half_dim]
    second = vectors[..., half_dim:]
    return jnp.concatenate(
        [first * cosine - second * sine_part, second * cosine + first * sine_part], axis=-1
    )


def scale_rows(values, factor):
    row_count, head_count = factor.shape
    return (values.reshape(row_count, head_count, -1) * factor[..., None]).reshape(row_count, -1)


def merge_parts(first, second):
    joint_peak = jnp.maximum(first[0], second[0])
    first_factor = jnp.exp(first[0] - joint_peak)
    second_factor = jnp.exp(second[0] - joint_peak)
    totals = first[1] * first_factor + second[1] * second_factor
    weighted = scale_rows(first[2], first_factor) + scale_rows(second[2], second_factor)
    return (joint_peak, totals, weighted)


def on_device(
    hidden,
    attn_gain,
    w_qkv,
    w_out,
    prefix_keys,
    prefix_values,
    private_keys,
    private_values,
    group_ids,
    private_lengths,
    moe_gain,
    router,
    w_gate,
    w_up,
    w_down,
    routes,
):
    model_width = w_out.shape[0]
    all_tokens = hidden.shape[0]
    requests = group_ids.shape[0]
    group_count = prefix_keys.shape[0]
    prefix_block = prefix_keys.shape[1]
    private_block = private_keys.shape[1]
    own_rank = lax.axis_index("tp")
    score_scale = HDIM ** (-0.5)
    scaled = (hidden * attn_gain[None, :]).astype(jnp.bfloat16)
    partial_qkv = jnp.dot(scaled, w_qkv, preferred_element_type=jnp.float32)
    own_squares = jnp.sum(hidden * hidden, axis=1)
    summed, squares = lax.psum((partial_qkv, own_squares), "tp")
    inv_attn = lax.rsqrt(squares / model_width + EPSILON)
    qkv = (inv_attn[:, None] * summed).astype(jnp.bfloat16)
    own_lengths = jnp.broadcast_to(private_lengths[:, None], (requests, NEW)).reshape(all_tokens)
    places = (
        prefix_block * lax.axis_size("tp")
        + own_lengths
        + jnp.arange(all_tokens, dtype=jnp.int32) % NEW
    )
    queries = rotate_heads(
        qkv[:, :model_width].astype(jnp.float32).reshape(all_tokens, HEADS, HDIM), places
    ).astype(jnp.bfloat16)
    fresh_keys = rotate_heads(
        qkv[:, model_width : 2 * model_width].astype(jnp.float32).reshape(all_tokens, HEADS, HDIM),
        places,
    ).astype(jnp.bfloat16)
    fresh_values = qkv[:, 2 * model_width :].astype(jnp.float32).reshape(requests, NEW, HEADS, HDIM)
    query_f = queries.astype(jnp.float32).reshape(requests, NEW, HEADS, HDIM)
    pre_keys = prefix_keys.astype(jnp.float32).reshape(group_count, prefix_block, HEADS, HDIM)
    pre_scores = jnp.einsum("rjhd,gphd->rjhgp", query_f, pre_keys) * score_scale
    member = group_ids[:, None] == jnp.arange(group_count, dtype=jnp.int32)[None, :]
    pre_scores = jnp.where(member[:, None, None, :, None], pre_scores, BLOCKED)
    priv_keys = private_keys.astype(jnp.float32).reshape(requests, private_block, HEADS, HDIM)
    priv_scores = jnp.einsum("rjhd,rphd->rjhp", query_f, priv_keys) * score_scale
    slots = own_rank * private_block + jnp.arange(private_block, dtype=jnp.int32)
    live = slots[None, :] < private_lengths[:, None]
    priv_scores = jnp.where(live[:, None, None, :], priv_scores, BLOCKED)
    local_peak = jnp.maximum(jnp.max(pre_scores, axis=(3, 4)), jnp.max(priv_scores, axis=3))
    pre_weights = jnp.exp(pre_scores - local_peak[..., None, None])
    priv_weights = jnp.exp(priv_scores - local_peak[..., None])
    local_total = jnp.sum(pre_weights, axis=(3, 4)) + jnp.sum(priv_weights, axis=3)
    pre_vals = prefix_values.astype(jnp.float32).reshape(group_count, prefix_block, HEADS, HDIM)
    priv_vals = private_values.astype(jnp.float32).reshape(requests, private_block, HEADS, HDIM)
    local_weighted = jnp.einsum("rjhgp,gphd->rjhd", pre_weights, pre_vals) + jnp.einsum(
        "rjhp,rphd->rjhd", priv_weights, priv_vals
    )
    local_peak = local_peak.reshape(all_tokens, HEADS)
    local_total = local_total.reshape(all_tokens, HEADS)
    local_weighted = local_weighted.reshape(all_tokens, model_width)
    cache_peak = lax.pmax(local_peak, "tp")
    factor = jnp.exp(local_peak - cache_peak)
    cache_total, cache_weighted = lax.psum(
        (local_total * factor, scale_rows(local_weighted, factor)), "tp"
    )
    key_f = fresh_keys.astype(jnp.float32).reshape(requests, NEW, HEADS, HDIM)
    new_scores = jnp.einsum("rjhd,rihd->rjhi", query_f, key_f) * score_scale
    causal = jnp.arange(NEW)[:, None] >= jnp.arange(NEW)[None, :]
    new_scores = jnp.where(causal[None, :, None, :], new_scores, BLOCKED)
    new_peak = jnp.max(new_scores, axis=3)
    new_weights = jnp.exp(new_scores - new_peak[..., None])
    new_total = jnp.sum(new_weights, axis=3).reshape(all_tokens, HEADS)
    new_weighted = jnp.einsum("rjhi,rihd->rjhd", new_weights, fresh_values).reshape(
        all_tokens, model_width
    )
    new_peak = new_peak.reshape(all_tokens, HEADS)
    final_state = merge_parts(
        (cache_peak, cache_total, cache_weighted), (new_peak, new_total, new_weighted)
    )
    attended = scale_rows(final_state[2], 1.0 / final_state[1]).astype(jnp.bfloat16)
    residual_cols = hidden + jnp.dot(attended, w_out, preferred_element_type=jnp.float32)
    full_rows = lax.all_gather(residual_cols, "tp", axis=1, tiled=True)
    inv_norm = lax.rsqrt(jnp.mean(full_rows * full_rows, axis=1) + EPSILON)
    normed = (full_rows * inv_norm[:, None] * moe_gain[None, :]).astype(jnp.bfloat16)
    logits = jnp.dot(normed, router, preferred_element_type=jnp.float32)
    expert_ids = jnp.arange(logits.shape[1], dtype=jnp.int32)
    first_pick = routes[:, 0:1] == expert_ids[None, :]
    second_pick = routes[:, 1:2] == expert_ids[None, :]
    first_logit = jnp.sum(jnp.where(first_pick, logits, 0.0), axis=1)
    second_logit = jnp.sum(jnp.where(second_pick, logits, 0.0), axis=1)
    first_weight = jax.nn.sigmoid(first_logit - second_logit)
    unit_count = w_gate.shape[1]
    own_expert = own_rank * unit_count // FF
    mix_coef = first_weight * (routes[:, 0] == own_expert).astype(jnp.float32) + (
        1.0 - first_weight
    ) * (routes[:, 1] == own_expert).astype(jnp.float32)
    gate_out = jnp.dot(normed, w_gate, preferred_element_type=jnp.float32)
    up_out = jnp.dot(normed, w_up, preferred_element_type=jnp.float32)
    inner_act = (jax.nn.silu(gate_out) * up_out * mix_coef[:, None]).astype(jnp.bfloat16)
    expert_term = jnp.dot(inner_act, w_down, preferred_element_type=jnp.float32)
    return residual_cols + lax.psum_scatter(expert_term, "tp", scatter_dimension=1, tiled=True)


def solution(mesh):
    placed = (
        P("rep", "tp"),
        P("tp"),
        P("tp", None),
        P(None, "tp"),
        P("rep", "tp", None),
        P("rep", "tp", None),
        P("rep", "tp", None),
        P("rep", "tp", None),
        P("rep"),
        P("rep"),
        P(),
        P(),
        P(None, "tp"),
        P(None, "tp"),
        P("tp", None),
        P("rep", None),
    )
    return jax.shard_map(
        on_device, mesh=mesh, in_specs=placed, out_specs=P("rep", "tp"), check_vma=False
    )
```

profile of v0, /device:TPU:1, one launch (start us, length us, event | category | flops | bytes accessed | tf_op | source)
XLA Modules:
  0.0 985.5 jit_solution(11834845233673120196)
XLA Ops:
  6.6 2.4 fusion.47
  9.8 131.2 %psum.28 = f32[32]{0:T(128)S(1)} all-reduce(f32[32]{0:T(128)S(1)} %multiply_reduce_fusion.1), channel_id=1, replica_groups=mesh['rep'=8,'tp'=64] {'tp'}, use_global_device_ids=true, to_apply=%region_1.0 | all-reduce | flops 32 | bytes 256 | tf_op jit(solution)/shard_map/psum | solution.py:72
  141.2 1.7 reshape.255
  143.5 1.3 reshape.256
  144.8 1.3 reshape.258
  146.1 1.7 reshape.257
  148.5 63.0 %all-reduce.5.cloned.1.call-done = f32[32,6912]{1,0:T(8,128)} async-done(((f32[32,6912]{1,0:T(8,128)}), f32[32,6912]{1,0:T(8,128)}) %all-reduce.5.cloned.1.call-update) | async-done | bytes 884752 | tf_op jit(solution)/shard_map/psum | solution.py:72
  211.5 1.3 multiply_convert_fusion
  212.8 0.7 fusion.60
  213.9 1.3 subtract_convert_fusion.1
  215.7 0.8 copy-done.1
  216.4 1.2 bitcast_reduce_fusion
  218.4 2.4 fusion.62
  220.7 1.2 copy.110
  222.8 1.7 fusion.1
  225.9 0.7 copy.128
  226.6 0.7 add.126
  227.4 245.1 %pmax.7 = f32[32,36]{1,0:T(8,128)S(1)} all-reduce(f32[32,36]{1,0:T(8,128)} %bitcast.83), channel_id=1, replica_groups=mesh['rep'=8,'tp'=64] {'tp'}, use_global_device_ids=true, to_apply=%region_5.6 | all-reduce | flops 1152 | bytes 9216 | tf_op jit(solution)/shard_map/pmax | solution.py:111
  472.4 1.3 fusion.59
  474.0 0.9 mul.242
  474.9 1.9 fusion.24
  476.9 0.8 fusion.11
  478.7 0.7 mul.243
  479.5 246.4 %psum.31 = f32[32,36]{1,0:T(8,128)S(1)} all-reduce(f32[32,36]{1,0:T(8,128)S(1)} %copy-done.19), channel_id=1, replica_groups=mesh['rep'=8,'tp'=64] {'tp'}, use_global_device_ids=true, to_apply=%region_10.11 | all-reduce | flops 1152 | bytes 9216 | tf_op jit(solution)/shard_map/psum | solution.py:113
  726.1 0.9 fusion.61
  730.3 1.2 convolution_add_fusion
  731.5 53.8 %all-gather = f32[64,36,32]{1,2,0:T(8,128)S(1)} all-gather(f32[1,36,32]{1,2,0:T(8,128)S(1)} %bitcast.82), channel_id=1, replica_groups=mesh['rep'=8,'tp'=64] {'tp'}, dimensions={0}, use_global_device_ids=true | all-gather | bytes 299520 | tf_op jit(solution)/shard_map/all_gather | solution.py:132
  786.9 1.5 fusion.63
  788.6 1.5 fusion.16
  790.2 1.3 dynamic-slice
  792.1 185.5 %all-reduce.9.cloned.1.call-done = f32[32,2304]{1,0:T(8,128)} async-done(((f32[32,2304]{1,0:T(8,128)}), f32[32,2304]{1,0:T(8,128)}) %all-reduce.9.cloned.1.call-update) | async-done | bytes 294928
  977.5 1.4 dynamic-slice_add_fusion
  (120 shorter events, 12.5 us)
Async XLA Ops:
  6.5 782.1 %copy-start = (bf16[180,2304]{1,0:T(8,128)(2,1)S(1)}, bf16[180,2304]{1,0:T(8,128)(2,1)}, u32[]{:S(2)}) copy-start(bf16[180,2304]{1,0:T(8,128)(2,1)} %param.30) | copy-start | bytes 2488324
  6.5 2.5 copy-start.18
  6.5 134.5 %copy-start.25 = (s32[8]{0:T(128)S(1)}, s32[8]{0:T(128)}, u32[]{:S(2)}) copy-start(s32[8]{0:T(128)} %param.25) | copy-start | bytes 100
  6.5 134.6 %copy-start.11 = (bf16[3,32,2304]{2,1,0:T(8,128)(2,1)S(1)}, bf16[3,32,2304]{2,1,0:T(8,128)(2,1)}, u32[]{:S(2)}) copy-start(bf16[3,32,2304]{2,1,0:T(8,128)(2,1)} %param.20) | copy-start | bytes 1327108
  6.5 137.0 %copy-start.15 = (bf16[8,8,2304]{2,1,0:T(8,128)(2,1)S(1)}, bf16[8,8,2304]{2,1,0:T(8,128)(2,1)}, u32[]{:S(2)}) copy-start(bf16[8,8,2304]{2,1,0:T(8,128)(2,1)} %param.22) | copy-start | bytes 884740
  6.5 204.9 %all-reduce.5.cloned.1.call-start = ((), (), s32[]{:S(2)}) async-start(), calls=%async_computation | async-start | bytes 1769472 | tf_op jit(solution)/shard_map/psum | solution.py:72
  9.0 135.8 %copy-start.16 = (bf16[8,8,2304]{2,1,0:T(8,128)(2,1)S(1)}, bf16[8,8,2304]{2,1,0:T(8,128)(2,1)}, u32[]{:S(2)}) copy-start(bf16[8,8,2304]{2,1,0:T(8,128)(2,1)} %param.23) | copy-start | bytes 884740
  9.0 137.1 %copy-start.12 = (bf16[3,32,2304]{2,1,0:T(8,128)(2,1)S(1)}, bf16[3,32,2304]{2,1,0:T(8,128)(2,1)}, u32[]{:S(2)}) copy-start(bf16[3,32,2304]{2,1,0:T(8,128)(2,1)} %param.21) | copy-start | bytes 1327108
  9.0 721.2 %all-reduce.7.cloned.1.call-start = ((), (), s32[]{:S(2)}) async-start(), calls=%async_computation.1 | async-start | bytes 589824 | tf_op jit(solution)/shard_map/psum | solution.py:113
  142.9 4.9 copy-start.22
  142.9 5.5 copy-start.29
  148.4 67.3 %copy-start.23 = (pred[8,3]{0,1:T(4,128)(4,1)}, pred[8,3]{0,1:T(4,128)(4,1)S(1)}, u32[]{:S(2)}) copy-start(pred[8,3]{0,1:T(4,128)(4,1)S(1)} %iota_compare_fusion.3) | copy-start | bytes 76
  215.2 1.2 copy-start.1
  215.6 5.1 copy-start.4
  218.4 3.6 copy-start.20
  220.7 5.9 copy-start.10
  222.0 3.1 copy-start.13
  474.0 2.8 copy-start.14
  474.0 2.8 copy-start.24
  474.9 1.9 copy-start.7
  477.7 1.0 copy-start.6
  477.7 1.8 copy-start.19
  477.7 248.1 %copy-start.3 = (bf16[32,36,32]{2,1,0:T(8,128)(2,1)S(1)}, bf16[32,36,32]{2,1,0:T(8,128)(2,1)}, u32[]{:S(2)}) copy-start(bf16[32,36,32]{2,1,0:T(8,128)(2,1)} %get-tuple-element.20) | copy-start | bytes 221188
  477.7 248.2 %copy-start.2 = (bf16[32,36,32]{2,1,0:T(8,128)(2,1)S(1)}, bf16[32,36,32]{2,1,0:T(8,128)(2,1)}, u32[]{:S(2)}) copy-start(bf16[32,36,32]{2,1,0:T(8,128)(2,1)} %get-tuple-element.19) | copy-start | bytes 221188
  478.1 248.0 %copy-start.5 = (bf16[8,4,36,64]{3,0,1,2:T(8,128)(2,1)S(1)}, bf16[8,4,36,64]{3,0,1,2:T(8,128)(2,1)}, u32[]{:S(2)}) copy-start(bf16[8,4,36,64]{3,0,1,2:T(8,128)(2,1)} %copy-done.4) | copy-start | bytes 442372
  478.1 248.0 %copy-start.30 = (pred[4,4]{0,1:T(4,128)(4,1)S(1)}, pred[4,4]{0,1:T(4,128)(4,1)}, u32[]{:S(2)}) copy-start(pred[4,4]{0,1:T(4,128)(4,1)} %iota_compare_fusion.2) | copy-start | bytes 52
  479.4 498.1 %all-reduce.9.cloned.1.call-start = ((), (), s32[]{:S(2)}) async-start(), calls=%async_computation.2 | async-start | bytes 589824
  785.3 1.4 copy-start.21
  785.9 2.4 copy-start.26
  785.9 2.5 copy-start.27
  786.0 2.5 copy-start.28
  786.0 2.7 copy-start.8
  (2 other events, 1.8 us)
Sparse Core Ops, SparseCore 0:
  10.8 200.6 all-reduce.4
  479.5 191.3 all-reduce.6
  790.3 187.2 all-reduce.8
where the time goes:
time: 986 us
  blocking collectives  676 us (69%)
  waiting for transfers between devices  248 us (25%)
  local copies, waits for them, and re-layouts  19.3 us (2%)
  matrix products  14.4 us (1%)
  between operations  14.3 us (1%)
  other arithmetic  12.4 us (1%)
    psum x1, blocking collectives, on_device(): lax.psum((local_total * factor, scale_rows(local_weighted, factor)), 'tp')  246 us
    pmax x1, blocking collectives, on_device(): cache_peak = lax.pmax(local_peak, 'tp')  245 us
    unnamed x4, waiting for transfers between devices  186 us
    psum x1, blocking collectives, on_device(): summed, squares = lax.psum((partial_qkv, own_squares), 'tp')  131 us
    psum x1, waiting for transfers between devices, on_device(): summed, squares = lax.psum((partial_qkv, own_squares), 'tp')  63 us
    all_gather x1, blocking collectives, on_device(): full_rows = lax.all_gather(residual_cols, 'tp', axis=1, tiled=True)  53.8 us
  transfers between devices with their start and end apart: 3, of which 2 were waited for; matrix products, arithmetic and copies ran while one was open for 1% of the time, Pallas kernels for 0%

commit v1 on v0

--- a/solution.py
+++ b/solution.py
@@ -29,6 +29,64 @@
 def scale_rows(values, factor):
     row_count, head_count = factor.shape
     return (values.reshape(row_count, head_count, -1) * factor[..., None]).reshape(row_count, -1)
+
+
+def partner_pairs(count, bit):
+    return [(i, i ^ bit) for i in range(count)]
+
+
+def tp_bits():
+    count = lax.axis_size("tp")
+    bits = []
+    bit = count // 2
+    while bit >= 1:
+        bits.append(bit)
+        bit //= 2
+    return count, bits
+
+
+def scatter_sum(values):
+    count, bits = tp_bits()
+    own_rank = lax.axis_index("tp")
+    for bit in bits:
+        half = values.shape[1] // 2
+        side = (own_rank // bit) % 2
+        keep = lax.dynamic_slice_in_dim(values, side * half, half, axis=1)
+        send = lax.dynamic_slice_in_dim(values, (1 - side) * half, half, axis=1)
+        values = keep + lax.ppermute(send, "tp", partner_pairs(count, bit))
+    return values
+
+
+def gather_cols(values):
+    count, bits = tp_bits()
+    own_rank = lax.axis_index("tp")
+    for bit in reversed(bits):
+        side = (own_rank // bit) % 2
+        other = lax.ppermute(values, "tp", partner_pairs(count, bit))
+        values = jnp.where(
+            side == 0,
+            jnp.concatenate([values, other], axis=1),
+            jnp.concatenate([other, values], axis=1),
+        )
+    return values
+
+
+def merge_softmax(peak, total, weighted):
+    count, bits = tp_bits()
+    heads = peak.shape[1]
+    for bit in reversed(bits):
+        packed = jnp.concatenate([peak, total, weighted], axis=1)
+        other = lax.ppermute(packed, "tp", partner_pairs(count, bit))
+        other_peak = other[:, :heads]
+        other_total = other[:, heads : 2 * heads]
+        other_weighted = other[:, 2 * heads :]
+        joint = jnp.maximum(peak, other_peak)
+        own_factor = jnp.exp(peak - joint)
+        other_factor = jnp.exp(other_peak - joint)
+        total = total * own_factor + other_total * other_factor
+        weighted = scale_rows(weighted, own_factor) + scale_rows(other_weighted, other_factor)
+        peak = joint
+    return peak, total, weighted
 
 
 def merge_parts(first, second):
@@ -69,7 +127,20 @@
     scaled = (hidden * attn_gain[None, :]).astype(jnp.bfloat16)
     partial_qkv = jnp.dot(scaled, w_qkv, preferred_element_type=jnp.float32)
     own_squares = jnp.sum(hidden * hidden, axis=1)
-    summed, squares = lax.psum((partial_qkv, own_squares), "tp")
+    qkv_width = partial_qkv.shape[1]
+    tp_count = lax.axis_size("tp")
+    padded_width = -(-(qkv_width + 1) // tp_count) * tp_count
+    packed = jnp.concatenate(
+        [
+            partial_qkv,
+            own_squares[:, None],
+            jnp.zeros((all_tokens, padded_width - qkv_width - 1), jnp.float32),
+        ],
+        axis=1,
+    )
+    packed = gather_cols(scatter_sum(packed))
+    summed = packed[:, :qkv_width]
+    squares = packed[:, qkv_width]
     inv_attn = lax.rsqrt(squares / model_width + EPSILON)
     qkv = (inv_attn[:, None] * summed).astype(jnp.bfloat16)
     own_lengths = jnp.broadcast_to(private_lengths[:, None], (requests, NEW)).reshape(all_tokens)
@@ -108,11 +179,7 @@
     local_peak = local_peak.reshape(all_tokens, HEADS)
     local_total = local_total.reshape(all_tokens, HEADS)
     local_weighted = local_weighted.reshape(all_tokens, model_width)
-    cache_peak = lax.pmax(local_peak, "tp")
-    factor = jnp.exp(local_peak - cache_peak)
-    cache_total, cache_weighted = lax.psum(
-        (local_total * factor, scale_rows(local_weighted, factor)), "tp"
-    )
+    cache_peak, cache_total, cache_weighted = merge_softmax(local_peak, local_total, local_weighted)
     key_f = fresh_keys.astype(jnp.float32).reshape(requests, NEW, HEADS, HDIM)
     new_scores = jnp.einsum("rjhd,rihd->rjhi", query_f, key_f) * score_scale
     causal = jnp.arange(NEW)[:, None] >= jnp.arange(NEW)[None, :]
@@ -129,7 +196,7 @@
     )
     attended = scale_rows(final_state[2], 1.0 / final_state[1]).astype(jnp.bfloat16)
     residual_cols = hidden + jnp.dot(attended, w_out, preferred_element_type=jnp.float32)
-    full_rows = lax.all_gather(residual_cols, "tp", axis=1, tiled=True)
+    full_rows = gather_cols(residual_cols)
     inv_norm = lax.rsqrt(jnp.mean(full_rows * full_rows, axis=1) + EPSILON)
     normed = (full_rows * inv_norm[:, None] * moe_gain[None, :]).astype(jnp.bfloat16)
     logits = jnp.dot(normed, router, preferred_element_type=jnp.float32)
@@ -148,7 +215,7 @@
     up_out = jnp.dot(normed, w_up, preferred_element_type=jnp.float32)
     inner_act = (jax.nn.silu(gate_out) * up_out * mix_coef[:, None]).astype(jnp.bfloat16)
     expert_term = jnp.dot(inner_act, w_down, preferred_element_type=jnp.float32)
-    return residual_cols + lax.psum_scatter(expert_term, "tp", scatter_dimension=1, tiled=True)
+    return residual_cols + scatter_sum(expert_term)
 
 
 def solution(mesh):

time: 986 us -> 340 us (0.34)
  blocking collectives: 676 us -> 0 us
  starting transfers between devices: 0.12 us -> 127 us
  waiting for transfers between devices: 248 us -> 158 us
  between operations: 14.3 us -> 1.48 us
    psum x2 -> x0, blocking collectives: 378 us -> none  [the longest x1 246 us: on_device(): lax.psum((local_total * factor, scale_rows(local_weighted, factor)), 'tp')]
    pmax x1 -> x0, blocking collectives: 245 us -> none  [on_device(): cache_peak = lax.pmax(local_peak, 'tp')]
    unnamed x4 -> x0, waiting for transfers between devices: 186 us -> none
    ppermute x0 -> x30, waiting for transfers between devices: none -> 158 us  [the longest x12 55.9 us: gather_cols(): other = lax.ppermute(values, 'tp', partner_pairs(count, bit))]
    ppermute x0 -> x30, starting transfers between devices: none -> 127 us  [the longest x12 70.1 us: scatter_sum(): values = keep + lax.ppermute(send, 'tp', partner_pairs(count, bit))]
    psum x2 -> x0, waiting for transfers between devices: 63 us -> none  [the longest x1 63 us: on_device(): summed, squares = lax.psum((partial_qkv, own_squares), 'tp')]
    all_gather x1 -> x0, blocking collectives: 53.8 us -> none  [on_device(): full_rows = lax.all_gather(residual_cols, 'tp', axis=1, tiled=True)]
  transfers between devices with their start and end apart: 3 -> 30, of which waited for: 2 -> 29; matrix products, arithmetic and copies ran while one was open for 1% -> 3% of each run, Pallas kernels for 0% -> 0%
where the time goes in v1:
time: 340 us; the launch traced here: 339 us
  waiting for transfers between devices  158 us (46%)
  starting transfers between devices  127 us (37%)
  local copies, waits for them, and re-layouts  23 us (7%)
  other arithmetic  15.1 us (4%)
  matrix products  14.3 us (4%)
    ppermute x12, starting transfers between devices, scatter_sum(): values = keep + lax.ppermute(send, 'tp', partner_pairs(count, bit))  70.1 us
    ppermute x12, waiting for transfers between devices, gather_cols(): other = lax.ppermute(values, 'tp', partner_pairs(count, bit))  55.9 us
    ppermute x6, waiting for transfers between devices, merge_softmax(): other = lax.ppermute(packed, 'tp', partner_pairs(count, bit))  54.7 us
    ppermute x12, waiting for transfers between devices, scatter_sum(): values = keep + lax.ppermute(send, 'tp', partner_pairs(count, bit))  47.2 us
    ppermute x12, starting transfers between devices, gather_cols(): other = lax.ppermute(values, 'tp', partner_pairs(count, bit))  38.2 us
    ppermute x6, starting transfers between devices, merge_softmax(): other = lax.ppermute(packed, 'tp', partner_pairs(count, bit))  18.5 us
    mul x30, local copies, waits for them, and re-layouts, scale_rows(): values.reshape(row_count, head_count, -1) * factor[..., None]  7.52 us
  transfers between devices with their start and end apart: 30, of which 29 were waited for; matrix products, arithmetic and copies ran while one was open for 3% of the time, Pallas kernels for 0%

profile of v1, /device:TPU:1, one launch (start us, length us, event | category | flops | bytes accessed | tf_op | source)
XLA Modules:
  0.0 338.5 jit_solution(6720743432899893090)
XLA Ops:
  2.6 11.5 %collective-permute-start = (f32[32,3488]{1,0:T(8,128)S(1)}, f32[32,3488]{1,0:T(8,128)S(1)}, u32[]{:S(2)}, u32[]{:S(2)}) collective-permute-start(f32[32,3488]{1,0:T(8,128)S(1)} %constant_dynamic-slice_fusion.11), channel_id=1, source_target_pairs={{0,32},{1,33},{2,34},{3,35},{4,36},{5,37},{6,38},{7,39},{8,40},{9,... | collective-permute-start | bytes 1339400 | tf_op jit(solution)/shard_map/ppermute | solution.py:56
  14.2 9.3 %collective-permute-done = f32[32,3488]{1,0:T(8,128)S(1)} collective-permute-done((f32[32,3488]{1,0:T(8,128)S(1)}, f32[32,3488]{1,0:T(8,128)S(1)}, u32[]{:S(2)}, u32[]{:S(2)}) %collective-permute-start) | collective-permute-done | bytes 446496 | tf_op jit(solution)/shard_map/ppermute | solution.py:56
  23.8 15.4 %collective-permute-start.1 = (f32[32,1744]{1,0:T(8,128)S(1)}, f32[32,1744]{1,0:T(8,128)S(1)}, u32[]{:S(2)}, u32[]{:S(2)}) collective-permute-start(f32[32,1744]{1,0:T(8,128)S(1)} %constant_dynamic-slice_fusion.10), channel_id=1, source_target_pairs={{0,16},{1,17},{2,18},{3,19},{4,20},{5,21},{6,22},{7,23},{8,24},{9,... | collective-permute-start | bytes 669704 | tf_op jit(solution)/shard_map/ppermute | solution.py:56
  39.3 10.5 %collective-permute-done.1 = f32[32,1744]{1,0:T(8,128)S(1)} collective-permute-done((f32[32,1744]{1,0:T(8,128)S(1)}, f32[32,1744]{1,0:T(8,128)S(1)}, u32[]{:S(2)}, u32[]{:S(2)}) %collective-permute-start.1) | collective-permute-done | bytes 223264 | tf_op jit(solution)/shard_map/ppermute | solution.py:56
  52.2 3.6 %collective-permute-done.2 = f32[32,872]{1,0:T(8,128)S(1)} collective-permute-done((f32[32,872]{1,0:T(8,128)S(1)}, f32[32,872]{1,0:T(8,128)S(1)}, u32[]{:S(2)}, u32[]{:S(2)}) %collective-permute-start.2) | collective-permute-done | bytes 111648 | tf_op jit(solution)/shard_map/ppermute | solution.py:56
  56.0 4.7 %collective-permute-start.3 = (f32[32,436]{1,0:T(8,128)S(1)}, f32[32,436]{1,0:T(8,128)S(1)}, u32[]{:S(2)}, u32[]{:S(2)}) collective-permute-start(f32[32,436]{1,0:T(8,128)S(1)} %constant_dynamic-slice_fusion.8), channel_id=1, source_target_pairs={{0,4},{1,5},{2,6},{3,7},{4,0},{5,1},{6,2},{7,3},{8,12},{9,13},{10,... | collective-permute-start | bytes 167432 | tf_op jit(solution)/shard_map/ppermute | solution.py:56
  62.7 3.1 collective-permute-start.4
  67.5 6.2 %collective-permute-start.5 = (f32[32,109]{1,0:T(8,128)S(1)}, f32[32,109]{1,0:T(8,128)S(1)}, u32[]{:S(2)}, u32[]{:S(2)}) collective-permute-start(f32[32,109]{1,0:T(8,128)S(1)} %constant_dynamic-slice_fusion.6), channel_id=1, source_target_pairs={{0,1},{1,0},{2,3},{3,2},{4,5},{5,4},{6,7},{7,6},{8,9},{9,8},{10,11... | collective-permute-start | bytes 41864 | tf_op jit(solution)/shard_map/ppermute | solution.py:56
  77.8 3.1 collective-permute-start.7
  82.5 4.7 %collective-permute-start.8 = (f32[32,436]{1,0:T(8,128)S(1)}, f32[32,436]{1,0:T(8,128)S(1)}, u32[]{:S(2)}, u32[]{:S(2)}) collective-permute-start(f32[32,436]{1,0:T(8,128)S(1)} %maximum_select_fusion.7), channel_id=1, source_target_pairs={{0,4},{1,5},{2,6},{3,7},{4,0},{5,1},{6,2},{7,3},{8,12},{9,13},{10,... | collective-permute-start | bytes 167432 | tf_op jit(solution)/shard_map/ppermute | solution.py:65
  95.5 3.6 %collective-permute-done.9 = f32[32,872]{1,0:T(8,128)S(1)} collective-permute-done((f32[32,872]{1,0:T(8,128)S(1)}, f32[32,872]{1,0:T(8,128)S(1)}, u32[]{:S(2)}, u32[]{:S(2)}) %collective-permute-start.9) | collective-permute-done | bytes 111648 | tf_op jit(solution)/shard_map/ppermute | solution.py:65
  101.2 12.1 %collective-permute-done.10 = f32[32,1744]{1,0:T(8,128)S(1)} collective-permute-done((f32[32,1744]{1,0:T(8,128)S(1)}, f32[32,1744]{1,0:T(8,128)S(1)}, u32[]{:S(2)}, u32[]{:S(2)}) %collective-permute-start.10) | collective-permute-done | bytes 223264 | tf_op jit(solution)/shard_map/ppermute | solution.py:65
  113.5 7.3 %collective-permute-start.11 = (f32[32,3488]{1,0:T(8,128)S(1)}, f32[32,3488]{1,0:T(8,128)S(1)}, u32[]{:S(2)}, u32[]{:S(2)}) collective-permute-start(f32[32,3488]{1,0:T(8,128)S(1)} %maximum_select_fusion.1), channel_id=1, source_target_pairs={{0,32},{1,33},{2,34},{3,35},{4,36},{5,37},{6,38},{7,39},{8,40},{9,... | collective-permute-start | bytes 1339400 | tf_op jit(solution)/shard_map/ppermute | solution.py:65
  121.0 18.1 %collective-permute-done.11 = f32[32,3488]{1,0:T(8,128)S(1)} collective-permute-done((f32[32,3488]{1,0:T(8,128)S(1)}, f32[32,3488]{1,0:T(8,128)S(1)}, u32[]{:S(2)}, u32[]{:S(2)}) %collective-permute-start.11) | collective-permute-done | bytes 446496 | tf_op jit(solution)/shard_map/ppermute | solution.py:65
  158.7 5.1 %collective-permute-start.12 = (f32[32,2376]{1,0:T(8,128)S(1)}, f32[32,2376]{1,0:T(8,128)S(1)}, u32[]{:S(2)}, u32[]{:S(2)}) collective-permute-start(f32[32,2376]{1,0:T(8,128)S(1)} %concatenate.127), channel_id=1, source_target_pairs={{0,1},{1,0},{2,3},{3,2},{4,5},{5,4},{6,7},{7,6},{8,9},{9,8},{10,11... | collective-permute-start | bytes 912392 | tf_op jit(solution)/shard_map/ppermute | solution.py:79
  170.1 8.2 %collective-permute-done.13 = f32[32,2376]{1,0:T(8,128)S(1)} collective-permute-done((f32[32,2376]{1,0:T(8,128)S(1)}, f32[32,2376]{1,0:T(8,128)S(1)}, u32[]{:S(2)}, u32[]{:S(2)}) %collective-permute-start.13) | collective-permute-done | bytes 304160 | tf_op jit(solution)/shard_map/ppermute | solution.py:79
  182.4 8.2 %collective-permute-done.14 = f32[32,2376]{1,0:T(8,128)S(1)} collective-permute-done((f32[32,2376]{1,0:T(8,128)S(1)}, f32[32,2376]{1,0:T(8,128)S(1)}, u32[]{:S(2)}, u32[]{:S(2)}) %collective-permute-start.14) | collective-permute-done | bytes 304160 | tf_op jit(solution)/shard_map/ppermute | solution.py:79
  193.8 6.7 %collective-permute-done.15 = f32[32,2376]{1,0:T(8,128)S(1)} collective-permute-done((f32[32,2376]{1,0:T(8,128)S(1)}, f32[32,2376]{1,0:T(8,128)S(1)}, u32[]{:S(2)}, u32[]{:S(2)}) %collective-permute-start.15) | collective-permute-done | bytes 304160 | tf_op jit(solution)/shard_map/ppermute | solution.py:79
  206.9 15.4 %collective-permute-done.16 = f32[32,2376]{1,0:T(8,128)S(1)} collective-permute-done((f32[32,2376]{1,0:T(8,128)S(1)}, f32[32,2376]{1,0:T(8,128)S(1)}, u32[]{:S(2)}, u32[]{:S(2)}) %collective-permute-start.16) | collective-permute-done | bytes 304160 | tf_op jit(solution)/shard_map/ppermute | solution.py:79
  225.3 4.3 %collective-permute-start.17 = (f32[32,2376]{1,0:T(8,128)S(1)}, f32[32,2376]{1,0:T(8,128)S(1)}, u32[]{:S(2)}, u32[]{:S(2)}) collective-permute-start(f32[32,2376]{1,0:T(8,128)S(1)} %concatenate.132), channel_id=1, source_target_pairs={{0,32},{1,33},{2,34},{3,35},{4,36},{5,37},{6,38},{7,39},{8,40},{9,... | collective-permute-start | bytes 912392 | tf_op jit(solution)/shard_map/ppermute | solution.py:79
  231.4 14.9 %collective-permute-done.17 = f32[32,2376]{1,0:T(8,128)S(1)} collective-permute-done((f32[32,2376]{1,0:T(8,128)S(1)}, f32[32,2376]{1,0:T(8,128)S(1)}, u32[]{:S(2)}, u32[]{:S(2)}) %collective-permute-start.17) | collective-permute-done | bytes 304160 | tf_op jit(solution)/shard_map/ppermute | solution.py:79
  259.0 3.5 %collective-permute-start.20 = (f32[32,144]{1,0:T(8,128)S(1)}, f32[32,144]{1,0:T(8,128)S(1)}, u32[]{:S(2)}, u32[]{:S(2)}) collective-permute-start(f32[32,144]{1,0:T(8,128)S(1)} %maximum_select_fusion.10), channel_id=1, source_target_pairs={{0,4},{1,5},{2,6},{3,7},{4,0},{5,1},{6,2},{7,3},{8,12},{9,13},{10,... | collective-permute-start | bytes 55304 | tf_op jit(solution)/shard_map/ppermute | solution.py:65
  267.1 2.9 collective-permute-done.21
  272.1 4.7 %collective-permute-done.22 = f32[32,576]{1,0:T(8,128)S(1)} collective-permute-done((f32[32,576]{1,0:T(8,128)S(1)}, f32[32,576]{1,0:T(8,128)S(1)}, u32[]{:S(2)}, u32[]{:S(2)}) %collective-permute-start.22) | collective-permute-done | bytes 73760 | tf_op jit(solution)/shard_map/ppermute | solution.py:65
  276.9 4.9 %collective-permute-start.23 = (f32[32,1152]{1,0:T(8,128)S(1)}, f32[32,1152]{1,0:T(8,128)S(1)}, u32[]{:S(2)}, u32[]{:S(2)}) collective-permute-start(f32[32,1152]{1,0:T(8,128)S(1)} %maximum_select_fusion.4), channel_id=1, source_target_pairs={{0,32},{1,33},{2,34},{3,35},{4,36},{5,37},{6,38},{7,39},{8,40},{9,... | collective-permute-start | bytes 442376 | tf_op jit(solution)/shard_map/ppermute | solution.py:65
  281.9 6.5 %collective-permute-done.23 = f32[32,1152]{1,0:T(8,128)S(1)} collective-permute-done((f32[32,1152]{1,0:T(8,128)S(1)}, f32[32,1152]{1,0:T(8,128)S(1)}, u32[]{:S(2)}, u32[]{:S(2)}) %collective-permute-start.23) | collective-permute-done | bytes 147488 | tf_op jit(solution)/shard_map/ppermute | solution.py:65
  290.1 4.4 %collective-permute-start.24 = (f32[32,1152]{1,0:T(8,128)S(1)}, f32[32,1152]{1,0:T(8,128)S(1)}, u32[]{:S(2)}, u32[]{:S(2)}) collective-permute-start(f32[32,1152]{1,0:T(8,128)S(1)} %constant_dynamic-slice_fusion.5), channel_id=1, source_target_pairs={{0,32},{1,33},{2,34},{3,35},{4,36},{5,37},{6,38},{7,39},{8,40},{9,... | collective-permute-start | bytes 442376 | tf_op jit(solution)/shard_map/ppermute | solution.py:56
  294.5 5.5 %collective-permute-done.24 = f32[32,1152]{1,0:T(8,128)S(1)} collective-permute-done((f32[32,1152]{1,0:T(8,128)S(1)}, f32[32,1152]{1,0:T(8,128)S(1)}, u32[]{:S(2)}, u32[]{:S(2)}) %collective-permute-start.24) | collective-permute-done | bytes 147488 | tf_op jit(solution)/shard_map/ppermute | solution.py:56
  302.1 5.6 %collective-permute-done.25 = f32[32,576]{1,0:T(8,128)S(1)} collective-permute-done((f32[32,576]{1,0:T(8,128)S(1)}, f32[32,576]{1,0:T(8,128)S(1)}, u32[]{:S(2)}, u32[]{:S(2)}) %collective-permute-start.25) | collective-permute-done | bytes 73760 | tf_op jit(solution)/shard_map/ppermute | solution.py:56
  309.8 2.9 collective-permute-done.26
  312.9 3.5 %collective-permute-start.27 = (f32[32,144]{1,0:T(8,128)S(1)}, f32[32,144]{1,0:T(8,128)S(1)}, u32[]{:S(2)}, u32[]{:S(2)}) collective-permute-start(f32[32,144]{1,0:T(8,128)S(1)} %constant_dynamic-slice_fusion.2), channel_id=1, source_target_pairs={{0,4},{1,5},{2,6},{3,7},{4,0},{5,1},{6,2},{7,3},{8,12},{9,13},{10,... | collective-permute-start | bytes 55304 | tf_op jit(solution)/shard_map/ppermute | solution.py:56
  323.8 13.2 %collective-permute-start.29 = (f32[32,36]{1,0:T(8,128)S(1)}, f32[32,36]{1,0:T(8,128)S(1)}, u32[]{:S(2)}, u32[]{:S(2)}) collective-permute-start(f32[32,36]{1,0:T(8,128)S(1)} %constant_dynamic-slice_fusion), channel_id=1, source_target_pairs={{0,1},{1,0},{2,3},{3,2},{4,5},{5,4},{6,7},{7,6},{8,9},{9,8},{10,11... | collective-permute-start | bytes 13832 | tf_op jit(solution)/shard_map/ppermute | solution.py:56
  (213 shorter events, 103.3 us)
Async XLA Ops:
  0.0 289.3 %copy-start = (bf16[180,2304]{1,0:T(8,128)(2,1)S(1)}, bf16[180,2304]{1,0:T(8,128)(2,1)}, u32[]{:S(2)}) copy-start(bf16[180,2304]{1,0:T(8,128)(2,1)} %param.30) | copy-start | bytes 2488324
  2.6 20.8 %collective-permute-start = (f32[32,3488]{1,0:T(8,128)S(1)}, f32[32,3488]{1,0:T(8,128)S(1)}, u32[]{:S(2)}, u32[]{:S(2)}) collective-permute-start(f32[32,3488]{1,0:T(8,128)S(1)} %constant_dynamic-slice_fusion.11), channel_id=1, source_target_pairs={{0,32},{1,33},{2,34},{3,35},{4,36},{5,37},{6,38},{7,39},{8,40},{9,... | collective-permute-start | bytes 1339400 | tf_op jit(solution)/shard_map/ppermute | solution.py:56
  14.2 66.7 %copy-start.16 = (s32[8]{0:T(128)S(1)}, s32[8]{0:T(128)}, u32[]{:S(2)}) copy-start(s32[8]{0:T(128)} %param.25) | copy-start | bytes 100
  23.8 26.0 %collective-permute-start.1 = (f32[32,1744]{1,0:T(8,128)S(1)}, f32[32,1744]{1,0:T(8,128)S(1)}, u32[]{:S(2)}, u32[]{:S(2)}) collective-permute-start(f32[32,1744]{1,0:T(8,128)S(1)} %constant_dynamic-slice_fusion.10), channel_id=1, source_target_pairs={{0,16},{1,17},{2,18},{3,19},{4,20},{5,21},{6,22},{7,23},{8,24},{9,... | collective-permute-start | bytes 669704 | tf_op jit(solution)/shard_map/ppermute | solution.py:56
  50.1 5.7 %collective-permute-start.2 = (f32[32,872]{1,0:T(8,128)S(1)}, f32[32,872]{1,0:T(8,128)S(1)}, u32[]{:S(2)}, u32[]{:S(2)}) collective-permute-start(f32[32,872]{1,0:T(8,128)S(1)} %constant_dynamic-slice_fusion.9), channel_id=1, source_target_pairs={{0,8},{1,9},{2,10},{3,11},{4,12},{5,13},{6,14},{7,15},{8,0},{9,1},... | collective-permute-start | bytes 334856 | tf_op jit(solution)/shard_map/ppermute | solution.py:56
  56.0 6.5 %collective-permute-start.3 = (f32[32,436]{1,0:T(8,128)S(1)}, f32[32,436]{1,0:T(8,128)S(1)}, u32[]{:S(2)}, u32[]{:S(2)}) collective-permute-start(f32[32,436]{1,0:T(8,128)S(1)} %constant_dynamic-slice_fusion.8), channel_id=1, source_target_pairs={{0,4},{1,5},{2,6},{3,7},{4,0},{5,1},{6,2},{7,3},{8,12},{9,13},{10,... | collective-permute-start | bytes 167432 | tf_op jit(solution)/shard_map/ppermute | solution.py:56
  62.7 4.6 %collective-permute-start.4 = (f32[32,218]{1,0:T(8,128)S(1)}, f32[32,218]{1,0:T(8,128)S(1)}, u32[]{:S(2)}, u32[]{:S(2)}) collective-permute-start(f32[32,218]{1,0:T(8,128)S(1)} %constant_dynamic-slice_fusion.7), channel_id=1, source_target_pairs={{0,2},{1,3},{2,0},{3,1},{4,6},{5,7},{6,4},{7,5},{8,10},{9,11},{10,... | collective-permute-start | bytes 83720 | tf_op jit(solution)/shard_map/ppermute | solution.py:56
  67.5 7.1 %collective-permute-start.5 = (f32[32,109]{1,0:T(8,128)S(1)}, f32[32,109]{1,0:T(8,128)S(1)}, u32[]{:S(2)}, u32[]{:S(2)}) collective-permute-start(f32[32,109]{1,0:T(8,128)S(1)} %constant_dynamic-slice_fusion.6), channel_id=1, source_target_pairs={{0,1},{1,0},{2,3},{3,2},{4,5},{5,4},{6,7},{7,6},{8,9},{9,8},{10,11... | collective-permute-start | bytes 41864 | tf_op jit(solution)/shard_map/ppermute | solution.py:56
  74.6 3.1 collective-permute-start.6
  77.8 4.7 %collective-permute-start.7 = (f32[32,218]{1,0:T(8,128)S(1)}, f32[32,218]{1,0:T(8,128)S(1)}, u32[]{:S(2)}, u32[]{:S(2)}) collective-permute-start(f32[32,218]{1,0:T(8,128)S(1)} %maximum_select_fusion.9), channel_id=1, source_target_pairs={{0,2},{1,3},{2,0},{3,1},{4,6},{5,7},{6,4},{7,5},{8,10},{9,11},{10,... | collective-permute-start | bytes 83720 | tf_op jit(solution)/shard_map/ppermute | solution.py:65
  82.5 11.0 %collective-permute-start.8 = (f32[32,436]{1,0:T(8,128)S(1)}, f32[32,436]{1,0:T(8,128)S(1)}, u32[]{:S(2)}, u32[]{:S(2)}) collective-permute-start(f32[32,436]{1,0:T(8,128)S(1)} %maximum_select_fusion.7), channel_id=1, source_target_pairs={{0,4},{1,5},{2,6},{3,7},{4,0},{5,1},{6,2},{7,3},{8,12},{9,13},{10,... | collective-permute-start | bytes 167432 | tf_op jit(solution)/shard_map/ppermute | solution.py:65
  93.6 5.5 %collective-permute-start.9 = (f32[32,872]{1,0:T(8,128)S(1)}, f32[32,872]{1,0:T(8,128)S(1)}, u32[]{:S(2)}, u32[]{:S(2)}) collective-permute-start(f32[32,872]{1,0:T(8,128)S(1)} %maximum_select_fusion.5), channel_id=1, source_target_pairs={{0,8},{1,9},{2,10},{3,11},{4,12},{5,13},{6,14},{7,15},{8,0},{9,1},... | collective-permute-start | bytes 334856 | tf_op jit(solution)/shard_map/ppermute | solution.py:65
  99.2 14.1 %collective-permute-start.10 = (f32[32,1744]{1,0:T(8,128)S(1)}, f32[32,1744]{1,0:T(8,128)S(1)}, u32[]{:S(2)}, u32[]{:S(2)}) collective-permute-start(f32[32,1744]{1,0:T(8,128)S(1)} %maximum_select_fusion.3), channel_id=1, source_target_pairs={{0,16},{1,17},{2,18},{3,19},{4,20},{5,21},{6,22},{7,23},{8,24},{9,... | collective-permute-start | bytes 669704 | tf_op jit(solution)/shard_map/ppermute | solution.py:65
  113.5 25.6 %collective-permute-start.11 = (f32[32,3488]{1,0:T(8,128)S(1)}, f32[32,3488]{1,0:T(8,128)S(1)}, u32[]{:S(2)}, u32[]{:S(2)}) collective-permute-start(f32[32,3488]{1,0:T(8,128)S(1)} %maximum_select_fusion.1), channel_id=1, source_target_pairs={{0,32},{1,33},{2,34},{3,35},{4,36},{5,37},{6,38},{7,39},{8,40},{9,... | collective-permute-start | bytes 1339400 | tf_op jit(solution)/shard_map/ppermute | solution.py:65
  158.7 6.3 %collective-permute-start.12 = (f32[32,2376]{1,0:T(8,128)S(1)}, f32[32,2376]{1,0:T(8,128)S(1)}, u32[]{:S(2)}, u32[]{:S(2)}) collective-permute-start(f32[32,2376]{1,0:T(8,128)S(1)} %concatenate.127), channel_id=1, source_target_pairs={{0,1},{1,0},{2,3},{3,2},{4,5},{5,4},{6,7},{7,6},{8,9},{9,8},{10,11... | collective-permute-start | bytes 912392 | tf_op jit(solution)/shard_map/ppermute | solution.py:79
  167.8 10.5 %collective-permute-start.13 = (f32[32,2376]{1,0:T(8,128)S(1)}, f32[32,2376]{1,0:T(8,128)S(1)}, u32[]{:S(2)}, u32[]{:S(2)}) collective-permute-start(f32[32,2376]{1,0:T(8,128)S(1)} %concatenate.128), channel_id=1, source_target_pairs={{0,2},{1,3},{2,0},{3,1},{4,6},{5,7},{6,4},{7,5},{8,10},{9,11},{10,... | collective-permute-start | bytes 912392 | tf_op jit(solution)/shard_map/ppermute | solution.py:79
  179.6 11.0 %collective-permute-start.14 = (f32[32,2376]{1,0:T(8,128)S(1)}, f32[32,2376]{1,0:T(8,128)S(1)}, u32[]{:S(2)}, u32[]{:S(2)}) collective-permute-start(f32[32,2376]{1,0:T(8,128)S(1)} %concatenate.129), channel_id=1, source_target_pairs={{0,4},{1,5},{2,6},{3,7},{4,0},{5,1},{6,2},{7,3},{8,12},{9,13},{10,... | collective-permute-start | bytes 912392 | tf_op jit(solution)/shard_map/ppermute | solution.py:79
  191.9 8.6 %collective-permute-start.15 = (f32[32,2376]{1,0:T(8,128)S(1)}, f32[32,2376]{1,0:T(8,128)S(1)}, u32[]{:S(2)}, u32[]{:S(2)}) collective-permute-start(f32[32,2376]{1,0:T(8,128)S(1)} %concatenate.130), channel_id=1, source_target_pairs={{0,8},{1,9},{2,10},{3,11},{4,12},{5,13},{6,14},{7,15},{8,0},{9,1},... | collective-permute-start | bytes 912392 | tf_op jit(solution)/shard_map/ppermute | solution.py:79
  203.6 18.7 %collective-permute-start.16 = (f32[32,2376]{1,0:T(8,128)S(1)}, f32[32,2376]{1,0:T(8,128)S(1)}, u32[]{:S(2)}, u32[]{:S(2)}) collective-permute-start(f32[32,2376]{1,0:T(8,128)S(1)} %concatenate.131), channel_id=1, source_target_pairs={{0,16},{1,17},{2,18},{3,19},{4,20},{5,21},{6,22},{7,23},{8,24},{9,... | collective-permute-start | bytes 912392 | tf_op jit(solution)/shard_map/ppermute | solution.py:79
  225.3 21.1 %collective-permute-start.17 = (f32[32,2376]{1,0:T(8,128)S(1)}, f32[32,2376]{1,0:T(8,128)S(1)}, u32[]{:S(2)}, u32[]{:S(2)}) collective-permute-start(f32[32,2376]{1,0:T(8,128)S(1)} %concatenate.132), channel_id=1, source_target_pairs={{0,32},{1,33},{2,34},{3,35},{4,36},{5,37},{6,38},{7,39},{8,40},{9,... | collective-permute-start | bytes 912392 | tf_op jit(solution)/shard_map/ppermute | solution.py:79
  251.0 3.4 collective-permute-start.18
  254.4 4.5 %collective-permute-start.19 = (f32[32,72]{1,0:T(8,128)S(1)}, f32[32,72]{1,0:T(8,128)S(1)}, u32[]{:S(2)}, u32[]{:S(2)}) collective-permute-start(f32[32,72]{1,0:T(8,128)S(1)} %maximum_select_fusion.11), channel_id=1, source_target_pairs={{0,2},{1,3},{2,0},{3,1},{4,6},{5,7},{6,4},{7,5},{8,10},{9,11},{10,... | collective-permute-start | bytes 27656 | tf_op jit(solution)/shard_map/ppermute | solution.py:65
  259.0 6.2 %collective-permute-start.20 = (f32[32,144]{1,0:T(8,128)S(1)}, f32[32,144]{1,0:T(8,128)S(1)}, u32[]{:S(2)}, u32[]{:S(2)}) collective-permute-start(f32[32,144]{1,0:T(8,128)S(1)} %maximum_select_fusion.10), channel_id=1, source_target_pairs={{0,4},{1,5},{2,6},{3,7},{4,0},{5,1},{6,2},{7,3},{8,12},{9,13},{10,... | collective-permute-start | bytes 55304 | tf_op jit(solution)/shard_map/ppermute | solution.py:65
  265.2 4.8 %collective-permute-start.21 = (f32[32,288]{1,0:T(8,128)S(1)}, f32[32,288]{1,0:T(8,128)S(1)}, u32[]{:S(2)}, u32[]{:S(2)}) collective-permute-start(f32[32,288]{1,0:T(8,128)S(1)} %maximum_select_fusion.8), channel_id=1, source_target_pairs={{0,8},{1,9},{2,10},{3,11},{4,12},{5,13},{6,14},{7,15},{8,0},{9,1},... | collective-permute-start | bytes 110600 | tf_op jit(solution)/shard_map/ppermute | solution.py:65
  270.1 6.7 %collective-permute-start.22 = (f32[32,576]{1,0:T(8,128)S(1)}, f32[32,576]{1,0:T(8,128)S(1)}, u32[]{:S(2)}, u32[]{:S(2)}) collective-permute-start(f32[32,576]{1,0:T(8,128)S(1)} %maximum_select_fusion.6), channel_id=1, source_target_pairs={{0,16},{1,17},{2,18},{3,19},{4,20},{5,21},{6,22},{7,23},{8,24},{9,... | collective-permute-start | bytes 221192 | tf_op jit(solution)/shard_map/ppermute | solution.py:65
  276.9 11.4 %collective-permute-start.23 = (f32[32,1152]{1,0:T(8,128)S(1)}, f32[32,1152]{1,0:T(8,128)S(1)}, u32[]{:S(2)}, u32[]{:S(2)}) collective-permute-start(f32[32,1152]{1,0:T(8,128)S(1)} %maximum_select_fusion.4), channel_id=1, source_target_pairs={{0,32},{1,33},{2,34},{3,35},{4,36},{5,37},{6,38},{7,39},{8,40},{9,... | collective-permute-start | bytes 442376 | tf_op jit(solution)/shard_map/ppermute | solution.py:65
  290.1 10.0 %collective-permute-start.24 = (f32[32,1152]{1,0:T(8,128)S(1)}, f32[32,1152]{1,0:T(8,128)S(1)}, u32[]{:S(2)}, u32[]{:S(2)}) collective-permute-start(f32[32,1152]{1,0:T(8,128)S(1)} %constant_dynamic-slice_fusion.5), channel_id=1, source_target_pairs={{0,32},{1,33},{2,34},{3,35},{4,36},{5,37},{6,38},{7,39},{8,40},{9,... | collective-permute-start | bytes 442376 | tf_op jit(solution)/shard_map/ppermute | solution.py:56
  300.2 7.5 %collective-permute-start.25 = (f32[32,576]{1,0:T(8,128)S(1)}, f32[32,576]{1,0:T(8,128)S(1)}, u32[]{:S(2)}, u32[]{:S(2)}) collective-permute-start(f32[32,576]{1,0:T(8,128)S(1)} %constant_dynamic-slice_fusion.4), channel_id=1, source_target_pairs={{0,16},{1,17},{2,18},{3,19},{4,20},{5,21},{6,22},{7,23},{8,24},{9,... | collective-permute-start | bytes 221192 | tf_op jit(solution)/shard_map/ppermute | solution.py:56
  307.9 4.8 %collective-permute-start.26 = (f32[32,288]{1,0:T(8,128)S(1)}, f32[32,288]{1,0:T(8,128)S(1)}, u32[]{:S(2)}, u32[]{:S(2)}) collective-permute-start(f32[32,288]{1,0:T(8,128)S(1)} %constant_dynamic-slice_fusion.3), channel_id=1, source_target_pairs={{0,8},{1,9},{2,10},{3,11},{4,12},{5,13},{6,14},{7,15},{8,0},{9,1},... | collective-permute-start | bytes 110600 | tf_op jit(solution)/shard_map/ppermute | solution.py:56
  312.9 6.2 %collective-permute-start.27 = (f32[32,144]{1,0:T(8,128)S(1)}, f32[32,144]{1,0:T(8,128)S(1)}, u32[]{:S(2)}, u32[]{:S(2)}) collective-permute-start(f32[32,144]{1,0:T(8,128)S(1)} %constant_dynamic-slice_fusion.2), channel_id=1, source_target_pairs={{0,4},{1,5},{2,6},{3,7},{4,0},{5,1},{6,2},{7,3},{8,12},{9,13},{10,... | collective-permute-start | bytes 55304 | tf_op jit(solution)/shard_map/ppermute | solution.py:56
  319.2 4.5 %collective-permute-start.28 = (f32[32,72]{1,0:T(8,128)S(1)}, f32[32,72]{1,0:T(8,128)S(1)}, u32[]{:S(2)}, u32[]{:S(2)}) collective-permute-start(f32[32,72]{1,0:T(8,128)S(1)} %constant_dynamic-slice_fusion.1), channel_id=1, source_target_pairs={{0,2},{1,3},{2,0},{3,1},{4,6},{5,7},{6,4},{7,5},{8,10},{9,11},{10,... | collective-permute-start | bytes 27656 | tf_op jit(solution)/shard_map/ppermute | solution.py:56
  323.8 14.0 %collective-permute-start.29 = (f32[32,36]{1,0:T(8,128)S(1)}, f32[32,36]{1,0:T(8,128)S(1)}, u32[]{:S(2)}, u32[]{:S(2)}) collective-permute-start(f32[32,36]{1,0:T(8,128)S(1)} %constant_dynamic-slice_fusion), channel_id=1, source_target_pairs={{0,1},{1,0},{2,3},{3,2},{4,5},{5,4},{6,7},{7,6},{8,9},{9,8},{10,11... | collective-permute-start | bytes 13832 | tf_op jit(solution)/shard_map/ppermute | solution.py:56
  (17 other events, 333.6 us)

commit v2 on v1

--- a/solution.py
+++ b/solution.py
@@ -38,10 +38,10 @@
 def tp_bits():
     count = lax.axis_size("tp")
     bits = []
-    bit = count // 2
-    while bit >= 1:
+    bit = 1
+    while bit < count:
         bits.append(bit)
-        bit //= 2
+        bit *= 2
     return count, bits
 
 
@@ -69,6 +69,14 @@
             jnp.concatenate([other, values], axis=1),
         )
     return values
+
+
+def reverse_blocks(values, count):
+    rows, width = values.shape
+    levels = count.bit_length() - 1
+    split = values.reshape((rows,) + (2,) * levels + (width // count,))
+    order = (0,) + tuple(range(levels, 0, -1)) + (levels + 1,)
+    return split.transpose(order).reshape(rows, width)
 
 
 def merge_softmax(peak, total, weighted):
@@ -129,20 +137,17 @@
     own_squares = jnp.sum(hidden * hidden, axis=1)
     qkv_width = partial_qkv.shape[1]
     tp_count = lax.axis_size("tp")
-    padded_width = -(-(qkv_width + 1) // tp_count) * tp_count
+    block = qkv_width // tp_count
     packed = jnp.concatenate(
         [
-            partial_qkv,
-            own_squares[:, None],
-            jnp.zeros((all_tokens, padded_width - qkv_width - 1), jnp.float32),
+            partial_qkv.reshape(all_tokens, tp_count, block),
+            jnp.broadcast_to(own_squares[:, None, None], (all_tokens, tp_count, 1)),
         ],
-        axis=1,
-    )
-    packed = gather_cols(scatter_sum(packed))
-    summed = packed[:, :qkv_width]
-    squares = packed[:, qkv_width]
-    inv_attn = lax.rsqrt(squares / model_width + EPSILON)
-    qkv = (inv_attn[:, None] * summed).astype(jnp.bfloat16)
+        axis=2,
+    ).reshape(all_tokens, tp_count * (block + 1))
+    own_block = scatter_sum(packed)
+    inv_attn = lax.rsqrt(own_block[:, block] / model_width + EPSILON)
+    qkv = gather_cols((inv_attn[:, None] * own_block[:, :block]).astype(jnp.bfloat16))
     own_lengths = jnp.broadcast_to(private_lengths[:, None], (requests, NEW)).reshape(all_tokens)
     places = (
         prefix_block * lax.axis_size("tp")
@@ -196,7 +201,7 @@
     )
     attended = scale_rows(final_state[2], 1.0 / final_state[1]).astype(jnp.bfloat16)
     residual_cols = hidden + jnp.dot(attended, w_out, preferred_element_type=jnp.float32)
-    full_rows = gather_cols(residual_cols)
+    full_rows = reverse_blocks(gather_cols(residual_cols), tp_count)
     inv_norm = lax.rsqrt(jnp.mean(full_rows * full_rows, axis=1) + EPSILON)
     normed = (full_rows * inv_norm[:, None] * moe_gain[None, :]).astype(jnp.bfloat16)
     logits = jnp.dot(normed, router, preferred_element_type=jnp.float32)
@@ -215,7 +220,7 @@
     up_out = jnp.dot(normed, w_up, preferred_element_type=jnp.float32)
     inner_act = (jax.nn.silu(gate_out) * up_out * mix_coef[:, None]).astype(jnp.bfloat16)
     expert_term = jnp.dot(inner_act, w_down, preferred_element_type=jnp.float32)
-    return residual_cols + scatter_sum(expert_term)
+    return residual_cols + scatter_sum(reverse_blocks(expert_term, tp_count))
 
 
 def solution(mesh):

time: 340 us -> 305 us (0.90); the launches traced: 339 us -> 299 us
  waiting for transfers between devices: 158 us -> 99.4 us
  local copies, waits for them, and re-layouts: 23 us -> 37.5 us
  other arithmetic: 15.1 us -> 20.2 us
    ppermute x12, waiting for transfers between devices: 55.9 us -> 25.5 us  [gather_cols(): other = lax.ppermute(values, 'tp', partner_pairs(count, bit))]
    ppermute x12, starting transfers between devices: 70.1 us -> 42.7 us  [scatter_sum(): values = keep + lax.ppermute(send, 'tp', partner_pairs(count, bit))]
    ppermute x6, waiting for transfers between devices: 54.7 us -> 38 us  [merge_softmax(): other = lax.ppermute(packed, 'tp', partner_pairs(count, bit))]
    ppermute x12, starting transfers between devices: 38.2 us -> 52.7 us  [gather_cols(): other = lax.ppermute(values, 'tp', partner_pairs(count, bit))]
    ppermute x6, starting transfers between devices: 18.5 us -> 30.9 us  [merge_softmax(): other = lax.ppermute(packed, 'tp', partner_pairs(count, bit))]
    ppermute x12, waiting for transfers between devices: 47.2 us -> 35.9 us  [scatter_sum(): values = keep + lax.ppermute(send, 'tp', partner_pairs(count, bit))]
    reshape x0 -> x6, local copies, waits for them, and re-layouts: none -> 8.06 us  [the longest x2 2.78 us: reverse_blocks(): return split.transpose(order).reshape(rows, width)]
  transfers between devices with their start and end apart: 30 -> 30, of which waited for: 29 -> 27; matrix products, arithmetic and copies ran while one was open for 3% -> 5% of each run, Pallas kernels for 0% -> 0%
where the time goes in v2:
time: 305 us; the launch traced here: 299 us
  starting transfers between devices  126 us (41%)
  waiting for transfers between devices  99.4 us (33%)
  local copies, waits for them, and re-layouts  37.5 us (12%)
  other arithmetic  20.2 us (7%)
  matrix products  14.2 us (5%)
    ppermute x12, starting transfers between devices, gather_cols(): other = lax.ppermute(values, 'tp', partner_pairs(count, bit))  52.7 us
    ppermute x12, starting transfers between devices, scatter_sum(): values = keep + lax.ppermute(send, 'tp', partner_pairs(count, bit))  42.7 us
    ppermute x6, waiting for transfers between devices, merge_softmax(): other = lax.ppermute(packed, 'tp', partner_pairs(count, bit))  38 us
    ppermute x12, waiting for transfers between devices, scatter_sum(): values = keep + lax.ppermute(send, 'tp', partner_pairs(count, bit))  35.9 us
    ppermute x6, starting transfers between devices, merge_softmax(): other = lax.ppermute(packed, 'tp', partner_pairs(count, bit))  30.9 us
    ppermute x12, waiting for transfers between devices, gather_cols(): other = lax.ppermute(values, 'tp', partner_pairs(count, bit))  25.5 us
    mul x30, local copies, waits for them, and re-layouts, scale_rows(): values.reshape(row_count, head_count, -1) * factor[..., None]  7.54 us
  transfers between devices with their start and end apart: 30, of which 27 were waited for; matrix products, arithmetic and copies ran while one was open for 5% of the time, Pallas kernels for 0%

profile of v2, /device:TPU:1, one launch (start us, length us, event | category | flops | bytes accessed | tf_op | source)
XLA Modules:
  0.0 299.2 jit_solution(16318363937006461861)
XLA Ops:
  5.5 8.8 %collective-permute-start = (f32[32,3488]{1,0:T(8,128)S(1)}, f32[32,3488]{1,0:T(8,128)S(1)}, u32[]{:S(2)}, u32[]{:S(2)}) collective-permute-start(f32[32,3488]{1,0:T(8,128)S(1)} %constant_dynamic-slice_fusion.11), channel_id=1, source_target_pairs={{0,1},{1,0},{2,3},{3,2},{4,5},{5,4},{6,7},{7,6},{8,9},{9,8},{10,11... | collective-permute-start | bytes 1339400 | tf_op jit(solution)/shard_map/ppermute | solution.py:56
  18.0 6.7 %collective-permute-done.1 = f32[32,1744]{1,0:T(8,128)S(1)} collective-permute-done((f32[32,1744]{1,0:T(8,128)S(1)}, f32[32,1744]{1,0:T(8,128)S(1)}, u32[]{:S(2)}, u32[]{:S(2)}) %collective-permute-start.1) | collective-permute-done | bytes 223264 | tf_op jit(solution)/shard_map/ppermute | solution.py:56
  27.0 5.1 %collective-permute-done.2 = f32[32,872]{1,0:T(8,128)S(1)} collective-permute-done((f32[32,872]{1,0:T(8,128)S(1)}, f32[32,872]{1,0:T(8,128)S(1)}, u32[]{:S(2)}, u32[]{:S(2)}) %collective-permute-start.2) | collective-permute-done | bytes 111648 | tf_op jit(solution)/shard_map/ppermute | solution.py:56
  34.4 3.0 %collective-permute-done.3 = f32[32,436]{1,0:T(8,128)S(1)} collective-permute-done((f32[32,436]{1,0:T(8,128)S(1)}, f32[32,436]{1,0:T(8,128)S(1)}, u32[]{:S(2)}, u32[]{:S(2)}) %collective-permute-start.3) | collective-permute-done | bytes 55840 | tf_op jit(solution)/shard_map/ppermute | solution.py:56
  39.6 3.7 %collective-permute-done.4 = f32[32,218]{1,0:T(8,128)S(1)} collective-permute-done((f32[32,218]{1,0:T(8,128)S(1)}, f32[32,218]{1,0:T(8,128)S(1)}, u32[]{:S(2)}, u32[]{:S(2)}) %collective-permute-start.4) | collective-permute-done | bytes 27936 | tf_op jit(solution)/shard_map/ppermute | solution.py:56
  43.4 5.2 %collective-permute-start.5 = (f32[32,109]{1,0:T(8,128)S(1)}, f32[32,109]{1,0:T(8,128)S(1)}, u32[]{:S(2)}, u32[]{:S(2)}) collective-permute-start(f32[32,109]{1,0:T(8,128)S(1)} %constant_dynamic-slice_fusion.6), channel_id=1, source_target_pairs={{0,32},{1,33},{2,34},{3,35},{4,36},{5,37},{6,38},{7,39},{8,40},{9,... | collective-permute-start | bytes 41864 | tf_op jit(solution)/shard_map/ppermute | solution.py:56
  48.8 3.0 %collective-permute-done.5 = f32[32,109]{1,0:T(8,128)S(1)} collective-permute-done((f32[32,109]{1,0:T(8,128)S(1)}, f32[32,109]{1,0:T(8,128)S(1)}, u32[]{:S(2)}, u32[]{:S(2)}) %collective-permute-start.5) | collective-permute-done | bytes 13984 | tf_op jit(solution)/shard_map/ppermute | solution.py:56
  52.1 5.2 %collective-permute-start.6 = (bf16[32,108]{1,0:T(8,128)(2,1)S(1)}, bf16[32,108]{1,0:T(8,128)(2,1)S(1)}, u32[]{:S(2)}, u32[]{:S(2)}) collective-permute-start(bf16[32,108]{1,0:T(8,128)(2,1)S(1)} %fusion.66), channel_id=1, source_target_pairs={{0,32},{1,33},{2,34},{3,35},{4,36},{5,37},{6,38},{7,39},{8,40},{9,... | collective-permute-start | bytes 20744 | tf_op jit(solution)/shard_map/ppermute | solution.py:65
  57.3 3.1 %collective-permute-done.6 = bf16[32,108]{1,0:T(8,128)(2,1)S(1)} collective-permute-done((bf16[32,108]{1,0:T(8,128)(2,1)S(1)}, bf16[32,108]{1,0:T(8,128)(2,1)S(1)}, u32[]{:S(2)}, u32[]{:S(2)}) %collective-permute-start.6) | collective-permute-done | bytes 6944 | tf_op jit(solution)/shard_map/ppermute | solution.py:65
  62.6 3.6 %collective-permute-done.7 = bf16[32,216]{1,0:T(8,128)(2,1)S(1)} collective-permute-done((bf16[32,216]{1,0:T(8,128)(2,1)S(1)}, bf16[32,216]{1,0:T(8,128)(2,1)S(1)}, u32[]{:S(2)}, u32[]{:S(2)}) %collective-permute-start.7) | collective-permute-done | bytes 13856 | tf_op jit(solution)/shard_map/ppermute | solution.py:65
  68.3 2.6 collective-permute-done.8
  71.0 2.8 collective-permute-start.9
  73.8 3.6 %collective-permute-done.9 = bf16[32,864]{1,0:T(8,128)(2,1)S(1)} collective-permute-done((bf16[32,864]{1,0:T(8,128)(2,1)S(1)}, bf16[32,864]{1,0:T(8,128)(2,1)S(1)}, u32[]{:S(2)}, u32[]{:S(2)}) %collective-permute-start.9) | collective-permute-done | bytes 55328 | tf_op jit(solution)/shard_map/ppermute | solution.py:65
  85.9 12.1 %collective-permute-start.11 = (bf16[32,3456]{1,0:T(8,128)(2,1)S(1)}, bf16[32,3456]{1,0:T(8,128)(2,1)S(1)}, u32[]{:S(2)}, u32[]{:S(2)}) collective-permute-start(bf16[32,3456]{1,0:T(8,128)(2,1)S(1)} %maximum_select_fusion.2), channel_id=1, source_target_pairs={{0,1},{1,0},{2,3},{3,2},{4,5},{5,4},{6,7},{7,6},{8,9},{9,8},{10,11... | collective-permute-start | bytes 663560 | tf_op jit(solution)/shard_map/ppermute | solution.py:65
  114.4 6.5 %collective-permute-start.12 = (f32[32,2376]{1,0:T(8,128)S(1)}, f32[32,2376]{1,0:T(8,128)S(1)}, u32[]{:S(2)}, u32[]{:S(2)}) collective-permute-start(f32[32,2376]{1,0:T(8,128)S(1)} %concatenate.131), channel_id=1, source_target_pairs={{0,32},{1,33},{2,34},{3,35},{4,36},{5,37},{6,38},{7,39},{8,40},{9,... | collective-permute-start | bytes 912392 | tf_op jit(solution)/shard_map/ppermute | solution.py:87
  120.9 8.4 %collective-permute-done.12 = f32[32,2376]{1,0:T(8,128)S(1)} collective-permute-done((f32[32,2376]{1,0:T(8,128)S(1)}, f32[32,2376]{1,0:T(8,128)S(1)}, u32[]{:S(2)}, u32[]{:S(2)}) %collective-permute-start.12) | collective-permute-done | bytes 304160 | tf_op jit(solution)/shard_map/ppermute | solution.py:87
  132.2 9.8 %collective-permute-start.13 = (f32[32,2376]{1,0:T(8,128)S(1)}, f32[32,2376]{1,0:T(8,128)S(1)}, u32[]{:S(2)}, u32[]{:S(2)}) collective-permute-start(f32[32,2376]{1,0:T(8,128)S(1)} %concatenate.132), channel_id=1, source_target_pairs={{0,16},{1,17},{2,18},{3,19},{4,20},{5,21},{6,22},{7,23},{8,24},{9,... | collective-permute-start | bytes 912392 | tf_op jit(solution)/shard_map/ppermute | solution.py:87
  142.0 14.1 %collective-permute-done.13 = f32[32,2376]{1,0:T(8,128)S(1)} collective-permute-done((f32[32,2376]{1,0:T(8,128)S(1)}, f32[32,2376]{1,0:T(8,128)S(1)}, u32[]{:S(2)}, u32[]{:S(2)}) %collective-permute-start.13) | collective-permute-done | bytes 304160 | tf_op jit(solution)/shard_map/ppermute | solution.py:87
  160.9 8.0 %collective-permute-done.14 = f32[32,2376]{1,0:T(8,128)S(1)} collective-permute-done((f32[32,2376]{1,0:T(8,128)S(1)}, f32[32,2376]{1,0:T(8,128)S(1)}, u32[]{:S(2)}, u32[]{:S(2)}) %collective-permute-start.14) | collective-permute-done | bytes 304160 | tf_op jit(solution)/shard_map/ppermute | solution.py:87
  171.8 5.2 %collective-permute-start.15 = (f32[32,2376]{1,0:T(8,128)S(1)}, f32[32,2376]{1,0:T(8,128)S(1)}, u32[]{:S(2)}, u32[]{:S(2)}) collective-permute-start(f32[32,2376]{1,0:T(8,128)S(1)} %concatenate.134), channel_id=1, source_target_pairs={{0,4},{1,5},{2,6},{3,7},{4,0},{5,1},{6,2},{7,3},{8,12},{9,13},{10,... | collective-permute-start | bytes 912392 | tf_op jit(solution)/shard_map/ppermute | solution.py:87
  177.1 6.0 %collective-permute-done.15 = f32[32,2376]{1,0:T(8,128)S(1)} collective-permute-done((f32[32,2376]{1,0:T(8,128)S(1)}, f32[32,2376]{1,0:T(8,128)S(1)}, u32[]{:S(2)}, u32[]{:S(2)}) %collective-permute-start.15) | collective-permute-done | bytes 304160 | tf_op jit(solution)/shard_map/ppermute | solution.py:87
  198.9 5.1 %collective-permute-start.17 = (f32[32,2376]{1,0:T(8,128)}, f32[32,2376]{1,0:T(8,128)S(1)}, u32[]{:S(2)}, u32[]{:S(2)}) collective-permute-start(f32[32,2376]{1,0:T(8,128)} %concatenate.136), channel_id=1, source_target_pairs={{0,1},{1,0},{2,3},{3,2},{4,5},{5,4},{6,7},{7,6},{8,9},{9,8},{10,11... | collective-permute-start | bytes 912392 | tf_op jit(solution)/shard_map/ppermute | solution.py:87
  210.4 7.6 %collective-permute-start.18 = (f32[32,36]{1,0:T(8,128)S(1)}, f32[32,36]{1,0:T(8,128)S(1)}, u32[]{:S(2)}, u32[]{:S(2)}) collective-permute-start(f32[32,36]{1,0:T(8,128)S(1)} %convolution_add_fusion), channel_id=1, source_target_pairs={{0,32},{1,33},{2,34},{3,35},{4,36},{5,37},{6,38},{7,39},{8,40},{9,... | collective-permute-start | bytes 13832 | tf_op jit(solution)/shard_map/ppermute | solution.py:65
  221.1 3.5 %collective-permute-done.19 = f32[32,72]{1,0:T(8,128)S(1)} collective-permute-done((f32[32,72]{1,0:T(8,128)S(1)}, f32[32,72]{1,0:T(8,128)S(1)}, u32[]{:S(2)}, u32[]{:S(2)}) %collective-permute-start.19) | collective-permute-done | bytes 9248 | tf_op jit(solution)/shard_map/ppermute | solution.py:65
  229.4 4.5 %collective-permute-start.21 = (f32[32,288]{1,0:T(8,128)S(1)}, f32[32,288]{1,0:T(8,128)S(1)}, u32[]{:S(2)}, u32[]{:S(2)}) collective-permute-start(f32[32,288]{1,0:T(8,128)S(1)} %maximum_select_fusion.7), channel_id=1, source_target_pairs={{0,4},{1,5},{2,6},{3,7},{4,0},{5,1},{6,2},{7,3},{8,12},{9,13},{10,... | collective-permute-start | bytes 110600 | tf_op jit(solution)/shard_map/ppermute | solution.py:65
  237.8 3.2 %collective-permute-done.22 = f32[32,576]{1,0:T(8,128)S(1)} collective-permute-done((f32[32,576]{1,0:T(8,128)S(1)}, f32[32,576]{1,0:T(8,128)S(1)}, u32[]{:S(2)}, u32[]{:S(2)}) %collective-permute-start.22) | collective-permute-done | bytes 73760 | tf_op jit(solution)/shard_map/ppermute | solution.py:65
  241.2 8.0 %collective-permute-start.23 = (f32[32,1152]{1,0:T(8,128)S(1)}, f32[32,1152]{1,0:T(8,128)S(1)}, u32[]{:S(2)}, u32[]{:S(2)}) collective-permute-start(f32[32,1152]{1,0:T(8,128)S(1)} %maximum_select_fusion.3), channel_id=1, source_target_pairs={{0,1},{1,0},{2,3},{3,2},{4,5},{5,4},{6,7},{7,6},{8,9},{9,8},{10,11... | collective-permute-start | bytes 442376 | tf_op jit(solution)/shard_map/ppermute | solution.py:65
  252.1 3.3 %multiply_reduce_fusion = (f32[32]{0:T(128)S(1)}, f32[32,2,2,2,2,2,2,36]{7,6,5,4,3,2,1,0:T(2,128)S(1)}) fusion(f32[32,1,2,2,2,2,2,36]{7,1,2,3,4,5,6,0:T(1,128)S(1)} %copy.171, f32[32,1,2,2,2,2,2,36]{7,1,2,3,4,5,6,0:T(1,128)S(1)} %copy.172, pred[]{:T(512)S(6)} %eq.113), kind=kLoop, calls=%fused_computation.24 | loop fusion | flops 368608 | bytes 589953 | tf_op jit(solution)/shard_map/reduce_sum | solution.py:205
  269.2 3.6 %collective-permute-done.25 = f32[32,576]{1,0:T(8,128)S(1)} collective-permute-done((f32[32,576]{1,0:T(8,128)S(1)}, f32[32,576]{1,0:T(8,128)S(1)}, u32[]{:S(2)}, u32[]{:S(2)}) %collective-permute-start.25) | collective-permute-done | bytes 73760 | tf_op jit(solution)/shard_map/ppermute | solution.py:56
  273.0 5.2 %collective-permute-start.26 = (f32[32,288]{1,0:T(8,128)S(1)}, f32[32,288]{1,0:T(8,128)S(1)}, u32[]{:S(2)}, u32[]{:S(2)}) collective-permute-start(f32[32,288]{1,0:T(8,128)S(1)} %constant_dynamic-slice_fusion.3), channel_id=1, source_target_pairs={{0,4},{1,5},{2,6},{3,7},{4,0},{5,1},{6,2},{7,3},{8,12},{9,13},{10,... | collective-permute-start | bytes 110600 | tf_op jit(solution)/shard_map/ppermute | solution.py:56
  286.6 3.4 %collective-permute-done.28 = f32[32,72]{1,0:T(8,128)S(1)} collective-permute-done((f32[32,72]{1,0:T(8,128)S(1)}, f32[32,72]{1,0:T(8,128)S(1)}, u32[]{:S(2)}, u32[]{:S(2)}) %collective-permute-start.28) | collective-permute-done | bytes 9248 | tf_op jit(solution)/shard_map/ppermute | solution.py:56
  290.2 7.2 %collective-permute-start.29 = (f32[32,36]{1,0:T(8,128)S(1)}, f32[32,36]{1,0:T(8,128)S(1)}, u32[]{:S(2)}, u32[]{:S(2)}) collective-permute-start(f32[32,36]{1,0:T(8,128)S(1)} %constant_dynamic-slice_fusion), channel_id=1, source_target_pairs={{0,32},{1,33},{2,34},{3,35},{4,36},{5,37},{6,38},{7,39},{8,40},{9,... | collective-permute-start | bytes 13832 | tf_op jit(solution)/shard_map/ppermute | solution.py:56
  (240 shorter events, 116.6 us)
Async XLA Ops:
  0.0 258.7 %copy-start = (bf16[180,2304]{1,0:T(8,128)(2,1)S(1)}, bf16[180,2304]{1,0:T(8,128)(2,1)}, u32[]{:S(2)}) copy-start(bf16[180,2304]{1,0:T(8,128)(2,1)} %param.30) | copy-start | bytes 2488324
  5.5 10.2 %collective-permute-start = (f32[32,3488]{1,0:T(8,128)S(1)}, f32[32,3488]{1,0:T(8,128)S(1)}, u32[]{:S(2)}, u32[]{:S(2)}) collective-permute-start(f32[32,3488]{1,0:T(8,128)S(1)} %constant_dynamic-slice_fusion.11), channel_id=1, source_target_pairs={{0,1},{1,0},{2,3},{3,2},{4,5},{5,4},{6,7},{7,6},{8,9},{9,8},{10,11... | collective-permute-start | bytes 1339400 | tf_op jit(solution)/shard_map/ppermute | solution.py:56
  15.9 64.0 %copy-start.7 = (bf16[3,32,2304]{2,1,0:T(8,128)(2,1)S(1)}, bf16[3,32,2304]{2,1,0:T(8,128)(2,1)}, u32[]{:S(2)}) copy-start(bf16[3,32,2304]{2,1,0:T(8,128)(2,1)} %param.20) | copy-start | bytes 1327108
  16.1 8.7 %collective-permute-start.1 = (f32[32,1744]{1,0:T(8,128)S(1)}, f32[32,1744]{1,0:T(8,128)S(1)}, u32[]{:S(2)}, u32[]{:S(2)}) collective-permute-start(f32[32,1744]{1,0:T(8,128)S(1)} %constant_dynamic-slice_fusion.10), channel_id=1, source_target_pairs={{0,2},{1,3},{2,0},{3,1},{4,6},{5,7},{6,4},{7,5},{8,10},{9,11},{10,... | collective-permute-start | bytes 669704 | tf_op jit(solution)/shard_map/ppermute | solution.py:56
  25.0 7.0 %collective-permute-start.2 = (f32[32,872]{1,0:T(8,128)S(1)}, f32[32,872]{1,0:T(8,128)S(1)}, u32[]{:S(2)}, u32[]{:S(2)}) collective-permute-start(f32[32,872]{1,0:T(8,128)S(1)} %constant_dynamic-slice_fusion.9), channel_id=1, source_target_pairs={{0,4},{1,5},{2,6},{3,7},{4,0},{5,1},{6,2},{7,3},{8,12},{9,13},{10,... | collective-permute-start | bytes 334856 | tf_op jit(solution)/shard_map/ppermute | solution.py:56
  32.3 5.1 %collective-permute-start.3 = (f32[32,436]{1,0:T(8,128)S(1)}, f32[32,436]{1,0:T(8,128)S(1)}, u32[]{:S(2)}, u32[]{:S(2)}) collective-permute-start(f32[32,436]{1,0:T(8,128)S(1)} %constant_dynamic-slice_fusion.8), channel_id=1, source_target_pairs={{0,8},{1,9},{2,10},{3,11},{4,12},{5,13},{6,14},{7,15},{8,0},{9,1},... | collective-permute-start | bytes 167432 | tf_op jit(solution)/shard_map/ppermute | solution.py:56
  37.6 5.6 %collective-permute-start.4 = (f32[32,218]{1,0:T(8,128)S(1)}, f32[32,218]{1,0:T(8,128)S(1)}, u32[]{:S(2)}, u32[]{:S(2)}) collective-permute-start(f32[32,218]{1,0:T(8,128)S(1)} %constant_dynamic-slice_fusion.7), channel_id=1, source_target_pairs={{0,16},{1,17},{2,18},{3,19},{4,20},{5,21},{6,22},{7,23},{8,24},{9,... | collective-permute-start | bytes 83720 | tf_op jit(solution)/shard_map/ppermute | solution.py:56
  43.4 8.4 %collective-permute-start.5 = (f32[32,109]{1,0:T(8,128)S(1)}, f32[32,109]{1,0:T(8,128)S(1)}, u32[]{:S(2)}, u32[]{:S(2)}) collective-permute-start(f32[32,109]{1,0:T(8,128)S(1)} %constant_dynamic-slice_fusion.6), channel_id=1, source_target_pairs={{0,32},{1,33},{2,34},{3,35},{4,36},{5,37},{6,38},{7,39},{8,40},{9,... | collective-permute-start | bytes 41864 | tf_op jit(solution)/shard_map/ppermute | solution.py:56
  52.1 8.3 %collective-permute-start.6 = (bf16[32,108]{1,0:T(8,128)(2,1)S(1)}, bf16[32,108]{1,0:T(8,128)(2,1)S(1)}, u32[]{:S(2)}, u32[]{:S(2)}) collective-permute-start(bf16[32,108]{1,0:T(8,128)(2,1)S(1)} %fusion.66), channel_id=1, source_target_pairs={{0,32},{1,33},{2,34},{3,35},{4,36},{5,37},{6,38},{7,39},{8,40},{9,... | collective-permute-start | bytes 20744 | tf_op jit(solution)/shard_map/ppermute | solution.py:65
  60.5 5.7 %collective-permute-start.7 = (bf16[32,216]{1,0:T(8,128)(2,1)S(1)}, bf16[32,216]{1,0:T(8,128)(2,1)S(1)}, u32[]{:S(2)}, u32[]{:S(2)}) collective-permute-start(bf16[32,216]{1,0:T(8,128)(2,1)S(1)} %maximum_select_fusion.10), channel_id=1, source_target_pairs={{0,16},{1,17},{2,18},{3,19},{4,20},{5,21},{6,22},{7,23},{8,24},{9,... | collective-permute-start | bytes 41480 | tf_op jit(solution)/shard_map/ppermute | solution.py:65
  66.3 4.7 %collective-permute-start.8 = (bf16[32,432]{1,0:T(8,128)(2,1)S(1)}, bf16[32,432]{1,0:T(8,128)(2,1)S(1)}, u32[]{:S(2)}, u32[]{:S(2)}) collective-permute-start(bf16[32,432]{1,0:T(8,128)(2,1)S(1)} %maximum_select_fusion.8), channel_id=1, source_target_pairs={{0,8},{1,9},{2,10},{3,11},{4,12},{5,13},{6,14},{7,15},{8,0},{9,1},... | collective-permute-start | bytes 82952 | tf_op jit(solution)/shard_map/ppermute | solution.py:65
  71.0 6.4 %collective-permute-start.9 = (bf16[32,864]{1,0:T(8,128)(2,1)S(1)}, bf16[32,864]{1,0:T(8,128)(2,1)S(1)}, u32[]{:S(2)}, u32[]{:S(2)}) collective-permute-start(bf16[32,864]{1,0:T(8,128)(2,1)S(1)} %maximum_select_fusion.6), channel_id=1, source_target_pairs={{0,4},{1,5},{2,6},{3,7},{4,0},{5,1},{6,2},{7,3},{8,12},{9,13},{10,... | collective-permute-start | bytes 165896 | tf_op jit(solution)/shard_map/ppermute | solution.py:65
  77.6 8.2 %collective-permute-start.10 = (bf16[32,1728]{1,0:T(8,128)(2,1)S(1)}, bf16[32,1728]{1,0:T(8,128)(2,1)S(1)}, u32[]{:S(2)}, u32[]{:S(2)}) collective-permute-start(bf16[32,1728]{1,0:T(8,128)(2,1)S(1)} %maximum_select_fusion.4), channel_id=1, source_target_pairs={{0,2},{1,3},{2,0},{3,1},{4,6},{5,7},{6,4},{7,5},{8,10},{9,11},{10,... | collective-permute-start | bytes 331784 | tf_op jit(solution)/shard_map/ppermute | solution.py:65
  85.9 13.0 %collective-permute-start.11 = (bf16[32,3456]{1,0:T(8,128)(2,1)S(1)}, bf16[32,3456]{1,0:T(8,128)(2,1)S(1)}, u32[]{:S(2)}, u32[]{:S(2)}) collective-permute-start(bf16[32,3456]{1,0:T(8,128)(2,1)S(1)} %maximum_select_fusion.2), channel_id=1, source_target_pairs={{0,1},{1,0},{2,3},{3,2},{4,5},{5,4},{6,7},{7,6},{8,9},{9,8},{10,11... | collective-permute-start | bytes 663560 | tf_op jit(solution)/shard_map/ppermute | solution.py:65
  114.4 14.9 %collective-permute-start.12 = (f32[32,2376]{1,0:T(8,128)S(1)}, f32[32,2376]{1,0:T(8,128)S(1)}, u32[]{:S(2)}, u32[]{:S(2)}) collective-permute-start(f32[32,2376]{1,0:T(8,128)S(1)} %concatenate.131), channel_id=1, source_target_pairs={{0,32},{1,33},{2,34},{3,35},{4,36},{5,37},{6,38},{7,39},{8,40},{9,... | collective-permute-start | bytes 912392 | tf_op jit(solution)/shard_map/ppermute | solution.py:87
  132.2 23.9 %collective-permute-start.13 = (f32[32,2376]{1,0:T(8,128)S(1)}, f32[32,2376]{1,0:T(8,128)S(1)}, u32[]{:S(2)}, u32[]{:S(2)}) collective-permute-start(f32[32,2376]{1,0:T(8,128)S(1)} %concatenate.132), channel_id=1, source_target_pairs={{0,16},{1,17},{2,18},{3,19},{4,20},{5,21},{6,22},{7,23},{8,24},{9,... | collective-permute-start | bytes 912392 | tf_op jit(solution)/shard_map/ppermute | solution.py:87
  159.0 9.9 %collective-permute-start.14 = (f32[32,2376]{1,0:T(8,128)S(1)}, f32[32,2376]{1,0:T(8,128)S(1)}, u32[]{:S(2)}, u32[]{:S(2)}) collective-permute-start(f32[32,2376]{1,0:T(8,128)S(1)} %concatenate.133), channel_id=1, source_target_pairs={{0,8},{1,9},{2,10},{3,11},{4,12},{5,13},{6,14},{7,15},{8,0},{9,1},... | collective-permute-start | bytes 912392 | tf_op jit(solution)/shard_map/ppermute | solution.py:87
  171.8 11.2 %collective-permute-start.15 = (f32[32,2376]{1,0:T(8,128)S(1)}, f32[32,2376]{1,0:T(8,128)S(1)}, u32[]{:S(2)}, u32[]{:S(2)}) collective-permute-start(f32[32,2376]{1,0:T(8,128)S(1)} %concatenate.134), channel_id=1, source_target_pairs={{0,4},{1,5},{2,6},{3,7},{4,0},{5,1},{6,2},{7,3},{8,12},{9,13},{10,... | collective-permute-start | bytes 912392 | tf_op jit(solution)/shard_map/ppermute | solution.py:87
  186.0 8.5 %collective-permute-start.16 = (f32[32,2376]{1,0:T(8,128)S(1)}, f32[32,2376]{1,0:T(8,128)S(1)}, u32[]{:S(2)}, u32[]{:S(2)}) collective-permute-start(f32[32,2376]{1,0:T(8,128)S(1)} %concatenate.135), channel_id=1, source_target_pairs={{0,2},{1,3},{2,0},{3,1},{4,6},{5,7},{6,4},{7,5},{8,10},{9,11},{10,... | collective-permute-start | bytes 912392 | tf_op jit(solution)/shard_map/ppermute | solution.py:87
  198.9 6.6 %collective-permute-start.17 = (f32[32,2376]{1,0:T(8,128)}, f32[32,2376]{1,0:T(8,128)S(1)}, u32[]{:S(2)}, u32[]{:S(2)}) collective-permute-start(f32[32,2376]{1,0:T(8,128)} %concatenate.136), channel_id=1, source_target_pairs={{0,1},{1,0},{2,3},{3,2},{4,5},{5,4},{6,7},{7,6},{8,9},{9,8},{10,11... | collective-permute-start | bytes 912392 | tf_op jit(solution)/shard_map/ppermute | solution.py:87
  210.4 8.7 %collective-permute-start.18 = (f32[32,36]{1,0:T(8,128)S(1)}, f32[32,36]{1,0:T(8,128)S(1)}, u32[]{:S(2)}, u32[]{:S(2)}) collective-permute-start(f32[32,36]{1,0:T(8,128)S(1)} %convolution_add_fusion), channel_id=1, source_target_pairs={{0,32},{1,33},{2,34},{3,35},{4,36},{5,37},{6,38},{7,39},{8,40},{9,... | collective-permute-start | bytes 13832 | tf_op jit(solution)/shard_map/ppermute | solution.py:65
  219.2 5.4 %collective-permute-start.19 = (f32[32,72]{1,0:T(8,128)S(1)}, f32[32,72]{1,0:T(8,128)S(1)}, u32[]{:S(2)}, u32[]{:S(2)}) collective-permute-start(f32[32,72]{1,0:T(8,128)S(1)} %maximum_select_fusion.11), channel_id=1, source_target_pairs={{0,16},{1,17},{2,18},{3,19},{4,20},{5,21},{6,22},{7,23},{8,24},{9,... | collective-permute-start | bytes 27656 | tf_op jit(solution)/shard_map/ppermute | solution.py:65
  224.7 4.7 %collective-permute-start.20 = (f32[32,144]{1,0:T(8,128)S(1)}, f32[32,144]{1,0:T(8,128)S(1)}, u32[]{:S(2)}, u32[]{:S(2)}) collective-permute-start(f32[32,144]{1,0:T(8,128)S(1)} %maximum_select_fusion.9), channel_id=1, source_target_pairs={{0,8},{1,9},{2,10},{3,11},{4,12},{5,13},{6,14},{7,15},{8,0},{9,1},... | collective-permute-start | bytes 55304 | tf_op jit(solution)/shard_map/ppermute | solution.py:65
  229.4 6.3 %collective-permute-start.21 = (f32[32,288]{1,0:T(8,128)S(1)}, f32[32,288]{1,0:T(8,128)S(1)}, u32[]{:S(2)}, u32[]{:S(2)}) collective-permute-start(f32[32,288]{1,0:T(8,128)S(1)} %maximum_select_fusion.7), channel_id=1, source_target_pairs={{0,4},{1,5},{2,6},{3,7},{4,0},{5,1},{6,2},{7,3},{8,12},{9,13},{10,... | collective-permute-start | bytes 110600 | tf_op jit(solution)/shard_map/ppermute | solution.py:65
  235.9 5.2 %collective-permute-start.22 = (f32[32,576]{1,0:T(8,128)S(1)}, f32[32,576]{1,0:T(8,128)S(1)}, u32[]{:S(2)}, u32[]{:S(2)}) collective-permute-start(f32[32,576]{1,0:T(8,128)S(1)} %maximum_select_fusion.5), channel_id=1, source_target_pairs={{0,2},{1,3},{2,0},{3,1},{4,6},{5,7},{6,4},{7,5},{8,10},{9,11},{10,... | collective-permute-start | bytes 221192 | tf_op jit(solution)/shard_map/ppermute | solution.py:65
  241.2 9.5 %collective-permute-start.23 = (f32[32,1152]{1,0:T(8,128)S(1)}, f32[32,1152]{1,0:T(8,128)S(1)}, u32[]{:S(2)}, u32[]{:S(2)}) collective-permute-start(f32[32,1152]{1,0:T(8,128)S(1)} %maximum_select_fusion.3), channel_id=1, source_target_pairs={{0,1},{1,0},{2,3},{3,2},{4,5},{5,4},{6,7},{7,6},{8,9},{9,8},{10,11... | collective-permute-start | bytes 442376 | tf_op jit(solution)/shard_map/ppermute | solution.py:65
  263.7 3.3 %collective-permute-start.24 = (f32[32,1152]{1,0:T(8,128)S(1)}, f32[32,1152]{1,0:T(8,128)S(1)}, u32[]{:S(2)}, u32[]{:S(2)}) collective-permute-start(f32[32,1152]{1,0:T(8,128)S(1)} %constant_dynamic-slice_fusion.5), channel_id=1, source_target_pairs={{0,1},{1,0},{2,3},{3,2},{4,5},{5,4},{6,7},{7,6},{8,9},{9,8},{10,11... | collective-permute-start | bytes 442376 | tf_op jit(solution)/shard_map/ppermute | solution.py:56
  267.0 5.8 %collective-permute-start.25 = (f32[32,576]{1,0:T(8,128)S(1)}, f32[32,576]{1,0:T(8,128)S(1)}, u32[]{:S(2)}, u32[]{:S(2)}) collective-permute-start(f32[32,576]{1,0:T(8,128)S(1)} %constant_dynamic-slice_fusion.4), channel_id=1, source_target_pairs={{0,2},{1,3},{2,0},{3,1},{4,6},{5,7},{6,4},{7,5},{8,10},{9,11},{10,... | collective-permute-start | bytes 221192 | tf_op jit(solution)/shard_map/ppermute | solution.py:56
  273.0 6.7 %collective-permute-start.26 = (f32[32,288]{1,0:T(8,128)S(1)}, f32[32,288]{1,0:T(8,128)S(1)}, u32[]{:S(2)}, u32[]{:S(2)}) collective-permute-start(f32[32,288]{1,0:T(8,128)S(1)} %constant_dynamic-slice_fusion.3), channel_id=1, source_target_pairs={{0,4},{1,5},{2,6},{3,7},{4,0},{5,1},{6,2},{7,3},{8,12},{9,13},{10,... | collective-permute-start | bytes 110600 | tf_op jit(solution)/shard_map/ppermute | solution.py:56
  279.9 4.6 %collective-permute-start.27 = (f32[32,144]{1,0:T(8,128)S(1)}, f32[32,144]{1,0:T(8,128)S(1)}, u32[]{:S(2)}, u32[]{:S(2)}) collective-permute-start(f32[32,144]{1,0:T(8,128)S(1)} %constant_dynamic-slice_fusion.2), channel_id=1, source_target_pairs={{0,8},{1,9},{2,10},{3,11},{4,12},{5,13},{6,14},{7,15},{8,0},{9,1},... | collective-permute-start | bytes 55304 | tf_op jit(solution)/shard_map/ppermute | solution.py:56
  284.7 5.4 %collective-permute-start.28 = (f32[32,72]{1,0:T(8,128)S(1)}, f32[32,72]{1,0:T(8,128)S(1)}, u32[]{:S(2)}, u32[]{:S(2)}) collective-permute-start(f32[32,72]{1,0:T(8,128)S(1)} %constant_dynamic-slice_fusion.1), channel_id=1, source_target_pairs={{0,16},{1,17},{2,18},{3,19},{4,20},{5,21},{6,22},{7,23},{8,24},{9,... | collective-permute-start | bytes 27656 | tf_op jit(solution)/shard_map/ppermute | solution.py:56
  290.2 8.4 %collective-permute-start.29 = (f32[32,36]{1,0:T(8,128)S(1)}, f32[32,36]{1,0:T(8,128)S(1)}, u32[]{:S(2)}, u32[]{:S(2)}) collective-permute-start(f32[32,36]{1,0:T(8,128)S(1)} %constant_dynamic-slice_fusion), channel_id=1, source_target_pairs={{0,32},{1,33},{2,34},{3,35},{4,36},{5,37},{6,38},{7,39},{8,40},{9,... | collective-permute-start | bytes 13832 | tf_op jit(solution)/shard_map/ppermute | solution.py:56
  (26 other events, 249.8 us)

commit v3 on v2

--- a/solution.py
+++ b/solution.py
@@ -57,7 +57,7 @@
     return values
 
 
-def gather_cols(values):
+def gather_cols(values, axis=1):
     count, bits = tp_bits()
     own_rank = lax.axis_index("tp")
     for bit in reversed(bits):
@@ -65,10 +65,47 @@
         other = lax.ppermute(values, "tp", partner_pairs(count, bit))
         values = jnp.where(
             side == 0,
-            jnp.concatenate([values, other], axis=1),
-            jnp.concatenate([other, values], axis=1),
+            jnp.concatenate([values, other], axis=axis),
+            jnp.concatenate([other, values], axis=axis),
         )
     return values
+
+
+def reversed_rank(count):
+    own_rank = lax.axis_index("tp")
+    levels = count.bit_length() - 1
+    position = 0
+    for level in range(levels):
+        position = position + ((own_rank // 2**level) % 2) * 2 ** (levels - 1 - level)
+    return position
+
+
+def merge_rows(first, second):
+    joint = jnp.maximum(first[:, -1:], second[:, -1:])
+    first_factor = jnp.exp(first[:, -1:] - joint)
+    second_factor = jnp.exp(second[:, -1:] - joint)
+    body = first[:, :-1] * first_factor + second[:, :-1] * second_factor
+    return jnp.concatenate([body, joint], axis=1)
+
+
+def scatter_merge(rows):
+    count, bits = tp_bits()
+    own_rank = lax.axis_index("tp")
+    for bit in bits:
+        half = rows.shape[0] // 2
+        side = (own_rank // bit) % 2
+        keep = lax.dynamic_slice_in_dim(rows, side * half, half, axis=0)
+        send = lax.dynamic_slice_in_dim(rows, (1 - side) * half, half, axis=0)
+        rows = merge_rows(keep, lax.ppermute(send, "tp", partner_pairs(count, bit)))
+    return rows
+
+
+def state_rows(peak, total, weighted):
+    row_count = peak.shape[0] * peak.shape[1]
+    return jnp.concatenate(
+        [weighted.reshape(row_count, -1), total.reshape(row_count, 1), peak.reshape(row_count, 1)],
+        axis=1,
+    )
 
 
 def reverse_blocks(values, count):
@@ -77,33 +114,6 @@
     split = values.reshape((rows,) + (2,) * levels + (width // count,))
     order = (0,) + tuple(range(levels, 0, -1)) + (levels + 1,)
     return split.transpose(order).reshape(rows, width)
-
-
-def merge_softmax(peak, total, weighted):
-    count, bits = tp_bits()
-    heads = peak.shape[1]
-    for bit in reversed(bits):
-        packed = jnp.concatenate([peak, total, weighted], axis=1)
-        other = lax.ppermute(packed, "tp", partner_pairs(count, bit))
-        other_peak = other[:, :heads]
-        other_total = other[:, heads : 2 * heads]
-        other_weighted = other[:, 2 * heads :]
-        joint = jnp.maximum(peak, other_peak)
-        own_factor = jnp.exp(peak - joint)
-        other_factor = jnp.exp(other_peak - joint)
-        total = total * own_factor + other_total * other_factor
-        weighted = scale_rows(weighted, own_factor) + scale_rows(other_weighted, other_factor)
-        peak = joint
-    return peak, total, weighted
-
-
-def merge_parts(first, second):
-    joint_peak = jnp.maximum(first[0], second[0])
-    first_factor = jnp.exp(first[0] - joint_peak)
-    second_factor = jnp.exp(second[0] - joint_peak)
-    totals = first[1] * first_factor + second[1] * second_factor
-    weighted = scale_rows(first[2], first_factor) + scale_rows(second[2], second_factor)
-    return (joint_peak, totals, weighted)
 
 
 def on_device(
@@ -184,7 +194,7 @@
     local_peak = local_peak.reshape(all_tokens, HEADS)
     local_total = local_total.reshape(all_tokens, HEADS)
     local_weighted = local_weighted.reshape(all_tokens, model_width)
-    cache_peak, cache_total, cache_weighted = merge_softmax(local_peak, local_total, local_weighted)
+    cache_rows = scatter_merge(state_rows(local_peak, local_total, local_weighted))
     key_f = fresh_keys.astype(jnp.float32).reshape(requests, NEW, HEADS, HDIM)
     new_scores = jnp.einsum("rjhd,rihd->rjhi", query_f, key_f) * score_scale
     causal = jnp.arange(NEW)[:, None] >= jnp.arange(NEW)[None, :]
@@ -196,10 +206,12 @@
         all_tokens, model_width
     )
     new_peak = new_peak.reshape(all_tokens, HEADS)
-    final_state = merge_parts(
-        (cache_peak, cache_total, cache_weighted), (new_peak, new_total, new_weighted)
-    )
-    attended = scale_rows(final_state[2], 1.0 / final_state[1]).astype(jnp.bfloat16)
+    new_rows = state_rows(new_peak, new_total, new_weighted)
+    own_count = cache_rows.shape[0]
+    new_rows = lax.dynamic_slice_in_dim(new_rows, reversed_rank(tp_count) * own_count, own_count, axis=0)
+    final_rows = merge_rows(cache_rows, new_rows)
+    attended_rows = (final_rows[:, :HDIM] / final_rows[:, HDIM : HDIM + 1]).astype(jnp.bfloat16)
+    attended = gather_cols(attended_rows, axis=0).reshape(all_tokens, model_width)
     residual_cols = hidden + jnp.dot(attended, w_out, preferred_element_type=jnp.float32)
     full_rows = reverse_blocks(gather_cols(residual_cols), tp_count)
     inv_norm = lax.rsqrt(jnp.mean(full_rows * full_rows, axis=1) + EPSILON)

time: 305 us -> 291 us (0.954)
  starting transfers between devices: 126 us -> 148 us
  local copies, waits for them, and re-layouts: 37.5 us -> 23 us
  waiting for transfers between devices: 99.4 us -> 85 us
  other arithmetic: 20.2 us -> 16.5 us
    ppermute x12 -> x18, starting transfers between devices: 52.7 us -> 85.9 us  [gather_cols(): other = lax.ppermute(values, 'tp', partner_pairs(count, bit))]
    ppermute x6, waiting for transfers between devices: 38 us -> 11.2 us  [scatter_merge(): rows = merge_rows(keep, lax.ppermute(send, 'tp', partner_pairs(count, bit)))]
    ppermute x12 -> x18, waiting for transfers between devices: 25.5 us -> 35.7 us  [gather_cols(): other = lax.ppermute(values, 'tp', partner_pairs(count, bit))]
    ppermute x6, starting transfers between devices: 30.9 us -> 21.2 us  [scatter_merge(): rows = merge_rows(keep, lax.ppermute(send, 'tp', partner_pairs(count, bit)))]
    mul x30 -> x0, local copies, waits for them, and re-layouts: 7.54 us -> none  [scale_rows(): values.reshape(row_count, head_count, -1) * factor[..., None]]
    add x10 -> x6, other arithmetic: 6.08 us -> 0.73 us  [merge_rows(): body = first[:, :-1] * first_factor + second[:, :-1] * second_factor]
    unnamed x56 -> x38, local copies, waits for them, and re-layouts: 4.34 us -> 0.87 us
  transfers between devices with their start and end apart: 30 -> 36, of which waited for: 27 -> 34; matrix products, arithmetic and copies ran while one was open for 5% -> 4% of each run, Pallas kernels for 0% -> 0%
where the time goes in v3:
time: 291 us; the launch traced here: 286 us
  starting transfers between devices  148 us (51%)
  waiting for transfers between devices  85 us (29%)
  local copies, waits for them, and re-layouts  23 us (8%)
  other arithmetic  16.5 us (6%)
  matrix products  11.8 us (4%)
    ppermute x18, starting transfers between devices, gather_cols(): other = lax.ppermute(values, 'tp', partner_pairs(count, bit))  85.9 us
    ppermute x12, starting transfers between devices, scatter_sum(): values = keep + lax.ppermute(send, 'tp', partner_pairs(count, bit))  40.7 us
    ppermute x12, waiting for transfers between devices, scatter_sum(): values = keep + lax.ppermute(send, 'tp', partner_pairs(count, bit))  38 us
    ppermute x18, waiting for transfers between devices, gather_cols(): other = lax.ppermute(values, 'tp', partner_pairs(count, bit))  35.7 us
    ppermute x6, starting transfers between devices, scatter_merge(): rows = merge_rows(keep, lax.ppermute(send, 'tp', partner_pairs(count, bit)))  21.2 us
    ppermute x6, waiting for transfers between devices, scatter_merge(): rows = merge_rows(keep, lax.ppermute(send, 'tp', partner_pairs(count, bit)))  11.2 us
  transfers between devices with their start and end apart: 36, of which 34 were waited for; matrix products, arithmetic and copies ran while one was open for 4% of the time, Pallas kernels for 0%

profile of v3, /device:TPU:1, one launch (start us, length us, event | category | flops | bytes accessed | tf_op | source)
XLA Modules:
  0.0 285.6 jit_solution(18434534006370278728)
XLA Ops:
  5.5 8.8 %collective-permute-start = (f32[32,3488]{1,0:T(8,128)S(1)}, f32[32,3488]{1,0:T(8,128)S(1)}, u32[]{:S(2)}, u32[]{:S(2)}) collective-permute-start(f32[32,3488]{1,0:T(8,128)S(1)} %constant_dynamic-slice_fusion.12), channel_id=1, source_target_pairs={{0,1},{1,0},{2,3},{3,2},{4,5},{5,4},{6,7},{7,6},{8,9},{9,8},{10,11... | collective-permute-start | bytes 1339400 | tf_op jit(solution)/shard_map/ppermute | solution.py:56
  18.0 6.7 %collective-permute-done.1 = f32[32,1744]{1,0:T(8,128)S(1)} collective-permute-done((f32[32,1744]{1,0:T(8,128)S(1)}, f32[32,1744]{1,0:T(8,128)S(1)}, u32[]{:S(2)}, u32[]{:S(2)}) %collective-permute-start.1) | collective-permute-done | bytes 223264 | tf_op jit(solution)/shard_map/ppermute | solution.py:56
  27.0 5.1 %collective-permute-done.2 = f32[32,872]{1,0:T(8,128)S(1)} collective-permute-done((f32[32,872]{1,0:T(8,128)S(1)}, f32[32,872]{1,0:T(8,128)S(1)}, u32[]{:S(2)}, u32[]{:S(2)}) %collective-permute-start.2) | collective-permute-done | bytes 111648 | tf_op jit(solution)/shard_map/ppermute | solution.py:56
  34.4 3.0 %collective-permute-done.3 = f32[32,436]{1,0:T(8,128)S(1)} collective-permute-done((f32[32,436]{1,0:T(8,128)S(1)}, f32[32,436]{1,0:T(8,128)S(1)}, u32[]{:S(2)}, u32[]{:S(2)}) %collective-permute-start.3) | collective-permute-done | bytes 55840 | tf_op jit(solution)/shard_map/ppermute | solution.py:56
  39.6 3.7 %collective-permute-done.4 = f32[32,218]{1,0:T(8,128)S(1)} collective-permute-done((f32[32,218]{1,0:T(8,128)S(1)}, f32[32,218]{1,0:T(8,128)S(1)}, u32[]{:S(2)}, u32[]{:S(2)}) %collective-permute-start.4) | collective-permute-done | bytes 27936 | tf_op jit(solution)/shard_map/ppermute | solution.py:56
  43.4 5.2 %collective-permute-start.5 = (f32[32,109]{1,0:T(8,128)S(1)}, f32[32,109]{1,0:T(8,128)S(1)}, u32[]{:S(2)}, u32[]{:S(2)}) collective-permute-start(f32[32,109]{1,0:T(8,128)S(1)} %constant_dynamic-slice_fusion.7), channel_id=1, source_target_pairs={{0,32},{1,33},{2,34},{3,35},{4,36},{5,37},{6,38},{7,39},{8,40},{9,... | collective-permute-start | bytes 41864 | tf_op jit(solution)/shard_map/ppermute | solution.py:56
  48.8 3.0 %collective-permute-done.5 = f32[32,109]{1,0:T(8,128)S(1)} collective-permute-done((f32[32,109]{1,0:T(8,128)S(1)}, f32[32,109]{1,0:T(8,128)S(1)}, u32[]{:S(2)}, u32[]{:S(2)}) %collective-permute-start.5) | collective-permute-done | bytes 13984 | tf_op jit(solution)/shard_map/ppermute | solution.py:56
  52.1 5.2 %collective-permute-start.6 = (bf16[32,108]{1,0:T(8,128)(2,1)S(1)}, bf16[32,108]{1,0:T(8,128)(2,1)S(1)}, u32[]{:S(2)}, u32[]{:S(2)}) collective-permute-start(bf16[32,108]{1,0:T(8,128)(2,1)S(1)} %fusion.57), channel_id=1, source_target_pairs={{0,32},{1,33},{2,34},{3,35},{4,36},{5,37},{6,38},{7,39},{8,40},{9,... | collective-permute-start | bytes 20744 | tf_op jit(solution)/shard_map/ppermute | solution.py:65
  57.3 3.1 %collective-permute-done.6 = bf16[32,108]{1,0:T(8,128)(2,1)S(1)} collective-permute-done((bf16[32,108]{1,0:T(8,128)(2,1)S(1)}, bf16[32,108]{1,0:T(8,128)(2,1)S(1)}, u32[]{:S(2)}, u32[]{:S(2)}) %collective-permute-start.6) | collective-permute-done | bytes 6944 | tf_op jit(solution)/shard_map/ppermute | solution.py:65
  62.6 3.6 %collective-permute-done.7 = bf16[32,216]{1,0:T(8,128)(2,1)S(1)} collective-permute-done((bf16[32,216]{1,0:T(8,128)(2,1)S(1)}, bf16[32,216]{1,0:T(8,128)(2,1)S(1)}, u32[]{:S(2)}, u32[]{:S(2)}) %collective-permute-start.7) | collective-permute-done | bytes 13856 | tf_op jit(solution)/shard_map/ppermute | solution.py:65
  73.8 3.6 %collective-permute-done.9 = bf16[32,864]{1,0:T(8,128)(2,1)S(1)} collective-permute-done((bf16[32,864]{1,0:T(8,128)(2,1)S(1)}, bf16[32,864]{1,0:T(8,128)(2,1)S(1)}, u32[]{:S(2)}, u32[]{:S(2)}) %collective-permute-start.9) | collective-permute-done | bytes 55328 | tf_op jit(solution)/shard_map/ppermute | solution.py:65
  86.0 12.1 %collective-permute-start.11 = (bf16[32,3456]{1,0:T(8,128)(2,1)S(1)}, bf16[32,3456]{1,0:T(8,128)(2,1)S(1)}, u32[]{:S(2)}, u32[]{:S(2)}) collective-permute-start(bf16[32,3456]{1,0:T(8,128)(2,1)S(1)} %maximum_select_fusion.3), channel_id=1, source_target_pairs={{0,1},{1,0},{2,3},{3,2},{4,5},{5,4},{6,7},{7,6},{8,9},{9,8},{10,11... | collective-permute-start | bytes 663560 | tf_op jit(solution)/shard_map/ppermute | solution.py:65
  117.9 3.4 %collective-permute-start.13 = (f32[288,66]{1,0:T(8,128)S(1)}, f32[288,66]{1,0:T(8,128)S(1)}, u32[]{:S(2)}, u32[]{:S(2)}) collective-permute-start(f32[288,66]{1,0:T(8,128)S(1)} %get-tuple-element.33), channel_id=1, source_target_pairs={{0,2},{1,3},{2,0},{3,1},{4,6},{5,7},{6,4},{7,5},{8,10},{9,11},{10,... | collective-permute-start | bytes 228104 | tf_op jit(solution)/shard_map/ppermute | solution.py:99
  121.5 3.3 %collective-permute-done.13 = f32[288,66]{1,0:T(8,128)S(1)} collective-permute-done((f32[288,66]{1,0:T(8,128)S(1)}, f32[288,66]{1,0:T(8,128)S(1)}, u32[]{:S(2)}, u32[]{:S(2)}) %collective-permute-start.13) | collective-permute-done | bytes 76064 | tf_op jit(solution)/shard_map/ppermute | solution.py:99
  125.4 3.3 %collective-permute-start.14 = (f32[144,66]{1,0:T(8,128)S(1)}, f32[144,66]{1,0:T(8,128)S(1)}, u32[]{:S(2)}, u32[]{:S(2)}) collective-permute-start(f32[144,66]{1,0:T(8,128)S(1)} %get-tuple-element.38), channel_id=1, source_target_pairs={{0,4},{1,5},{2,6},{3,7},{4,0},{5,1},{6,2},{7,3},{8,12},{9,13},{10,... | collective-permute-start | bytes 114056 | tf_op jit(solution)/shard_map/ppermute | solution.py:99
  137.6 3.3 %collective-permute-start.16 = (f32[36,66]{1,0:T(8,128)S(1)}, f32[36,66]{1,0:T(8,128)S(1)}, u32[]{:S(2)}, u32[]{:S(2)}) collective-permute-start(f32[36,66]{1,0:T(8,128)S(1)} %get-tuple-element.42), channel_id=1, source_target_pairs={{0,16},{1,17},{2,18},{3,19},{4,20},{5,21},{6,22},{7,23},{8,24},{9,... | collective-permute-start | bytes 28520 | tf_op jit(solution)/shard_map/ppermute | solution.py:99
  143.5 6.8 %collective-permute-start.17 = (f32[18,66]{1,0:T(8,128)S(1)}, f32[18,66]{1,0:T(8,128)S(1)}, u32[]{:S(2)}, u32[]{:S(2)}) collective-permute-start(f32[18,66]{1,0:T(8,128)S(1)} %get-tuple-element.44), channel_id=1, source_target_pairs={{0,32},{1,33},{2,34},{3,35},{4,36},{5,37},{6,38},{7,39},{8,40},{9,... | collective-permute-start | bytes 14264 | tf_op jit(solution)/shard_map/ppermute | solution.py:99
  152.5 6.7 %collective-permute-start.18 = (bf16[18,64]{1,0:T(8,128)(2,1)S(1)}, bf16[18,64]{1,0:T(8,128)(2,1)S(1)}, u32[]{:S(2)}, u32[]{:S(2)}) collective-permute-start(bf16[18,64]{1,0:T(8,128)(2,1)S(1)} %fusion.71), channel_id=1, source_target_pairs={{0,32},{1,33},{2,34},{3,35},{4,36},{5,37},{6,38},{7,39},{8,40},{9,... | collective-permute-start | bytes 6920 | tf_op jit(solution)/shard_map/ppermute | solution.py:65
  160.8 3.2 %collective-permute-start.19 = (bf16[36,64]{1,0:T(8,128)(2,1)S(1)}, bf16[36,64]{1,0:T(8,128)(2,1)S(1)}, u32[]{:S(2)}, u32[]{:S(2)}) collective-permute-start(bf16[36,64]{1,0:T(8,128)(2,1)S(1)} %maximum_select_fusion.17), channel_id=1, source_target_pairs={{0,16},{1,17},{2,18},{3,19},{4,20},{5,21},{6,22},{7,23},{8,24},{9,... | collective-permute-start | bytes 13832 | tf_op jit(solution)/shard_map/ppermute | solution.py:65
  171.0 3.9 %collective-permute-start.21 = (bf16[144,64]{1,0:T(8,128)(2,1)S(1)}, bf16[144,64]{1,0:T(8,128)(2,1)S(1)}, u32[]{:S(2)}, u32[]{:S(2)}) collective-permute-start(bf16[144,64]{1,0:T(8,128)(2,1)S(1)} %maximum_select_fusion.11), channel_id=1, source_target_pairs={{0,4},{1,5},{2,6},{3,7},{4,0},{5,1},{6,2},{7,3},{8,12},{9,13},{10,... | collective-permute-start | bytes 55304 | tf_op jit(solution)/shard_map/ppermute | solution.py:65
  177.2 3.2 %collective-permute-start.22 = (bf16[288,64]{1,0:T(8,128)(2,1)S(1)}, bf16[288,64]{1,0:T(8,128)(2,1)S(1)}, u32[]{:S(2)}, u32[]{:S(2)}) collective-permute-start(bf16[288,64]{1,0:T(8,128)(2,1)S(1)} %maximum_select_fusion.8), channel_id=1, source_target_pairs={{0,2},{1,3},{2,0},{3,1},{4,6},{5,7},{6,4},{7,5},{8,10},{9,11},{10,... | collective-permute-start | bytes 110600 | tf_op jit(solution)/shard_map/ppermute | solution.py:65
  182.4 13.1 %collective-permute-start.23 = (bf16[576,64]{1,0:T(8,128)(2,1)S(1)}, bf16[576,64]{1,0:T(8,128)(2,1)S(1)}, u32[]{:S(2)}, u32[]{:S(2)}) collective-permute-start(bf16[576,64]{1,0:T(8,128)(2,1)S(1)} %maximum_select_fusion.4), channel_id=1, source_target_pairs={{0,1},{1,0},{2,3},{3,2},{4,5},{5,4},{6,7},{7,6},{8,9},{9,8},{10,11... | collective-permute-start | bytes 221192 | tf_op jit(solution)/shard_map/ppermute | solution.py:65
  197.0 6.4 %collective-permute-start.24 = (f32[32,36]{1,0:T(8,128)S(1)}, f32[32,36]{1,0:T(8,128)S(1)}, u32[]{:S(2)}, u32[]{:S(2)}) collective-permute-start(f32[32,36]{1,0:T(8,128)S(1)} %convolution_add_fusion), channel_id=1, source_target_pairs={{0,32},{1,33},{2,34},{3,35},{4,36},{5,37},{6,38},{7,39},{8,40},{9,... | collective-permute-start | bytes 13832 | tf_op jit(solution)/shard_map/ppermute | solution.py:65
  205.5 3.3 %collective-permute-start.25 = (f32[32,72]{1,0:T(8,128)S(1)}, f32[32,72]{1,0:T(8,128)S(1)}, u32[]{:S(2)}, u32[]{:S(2)}) collective-permute-start(f32[32,72]{1,0:T(8,128)S(1)} %maximum_select_fusion.16), channel_id=1, source_target_pairs={{0,16},{1,17},{2,18},{3,19},{4,20},{5,21},{6,22},{7,23},{8,24},{9,... | collective-permute-start | bytes 27656 | tf_op jit(solution)/shard_map/ppermute | solution.py:65
  215.7 3.6 %collective-permute-start.27 = (f32[32,288]{1,0:T(8,128)S(1)}, f32[32,288]{1,0:T(8,128)S(1)}, u32[]{:S(2)}, u32[]{:S(2)}) collective-permute-start(f32[32,288]{1,0:T(8,128)S(1)} %maximum_select_fusion.10), channel_id=1, source_target_pairs={{0,4},{1,5},{2,6},{3,7},{4,0},{5,1},{6,2},{7,3},{8,12},{9,13},{10,... | collective-permute-start | bytes 110600 | tf_op jit(solution)/shard_map/ppermute | solution.py:65
  222.1 3.3 %collective-permute-start.28 = (f32[32,576]{1,0:T(8,128)S(1)}, f32[32,576]{1,0:T(8,128)S(1)}, u32[]{:S(2)}, u32[]{:S(2)}) collective-permute-start(f32[32,576]{1,0:T(8,128)S(1)} %maximum_select_fusion.7), channel_id=1, source_target_pairs={{0,2},{1,3},{2,0},{3,1},{4,6},{5,7},{6,4},{7,5},{8,10},{9,11},{10,... | collective-permute-start | bytes 221192 | tf_op jit(solution)/shard_map/ppermute | solution.py:65
  227.4 8.0 %collective-permute-start.29 = (f32[32,1152]{1,0:T(8,128)S(1)}, f32[32,1152]{1,0:T(8,128)S(1)}, u32[]{:S(2)}, u32[]{:S(2)}) collective-permute-start(f32[32,1152]{1,0:T(8,128)S(1)} %maximum_select_fusion.5), channel_id=1, source_target_pairs={{0,1},{1,0},{2,3},{3,2},{4,5},{5,4},{6,7},{7,6},{8,9},{9,8},{10,11... | collective-permute-start | bytes 442376 | tf_op jit(solution)/shard_map/ppermute | solution.py:65
  238.4 3.3 %multiply_reduce_fusion = (f32[32]{0:T(128)S(1)}, f32[32,2,2,2,2,2,2,36]{7,6,5,4,3,2,1,0:T(2,128)S(1)}) fusion(f32[32,1,2,2,2,2,2,36]{7,1,2,3,4,5,6,0:T(1,128)S(1)} %copy.156, f32[32,1,2,2,2,2,2,36]{7,1,2,3,4,5,6,0:T(1,128)S(1)} %copy.157, pred[]{:T(512)S(6)} %eq.134), kind=kLoop, calls=%fused_computation.24 | loop fusion | flops 368608 | bytes 589953 | tf_op jit(solution)/shard_map/reduce_sum | solution.py:217
  253.3 3.6 %collective-permute-start.31 = (f32[32,576]{1,0:T(8,128)S(1)}, f32[32,576]{1,0:T(8,128)S(1)}, u32[]{:S(2)}, u32[]{:S(2)}) collective-permute-start(f32[32,576]{1,0:T(8,128)S(1)} %constant_dynamic-slice_fusion.4), channel_id=1, source_target_pairs={{0,2},{1,3},{2,0},{3,1},{4,6},{5,7},{6,4},{7,5},{8,10},{9,11},{10,... | collective-permute-start | bytes 221192 | tf_op jit(solution)/shard_map/ppermute | solution.py:56
  259.7 2.8 collective-permute-start.32
  262.5 3.5 %collective-permute-done.32 = f32[32,288]{1,0:T(8,128)S(1)} collective-permute-done((f32[32,288]{1,0:T(8,128)S(1)}, f32[32,288]{1,0:T(8,128)S(1)}, u32[]{:S(2)}, u32[]{:S(2)}) %collective-permute-start.32) | collective-permute-done | bytes 36896 | tf_op jit(solution)/shard_map/ppermute | solution.py:56
  276.5 6.1 %collective-permute-start.35 = (f32[32,36]{1,0:T(8,128)S(1)}, f32[32,36]{1,0:T(8,128)S(1)}, u32[]{:S(2)}, u32[]{:S(2)}) collective-permute-start(f32[32,36]{1,0:T(8,128)S(1)} %constant_dynamic-slice_fusion), channel_id=1, source_target_pairs={{0,32},{1,33},{2,34},{3,35},{4,36},{5,37},{6,38},{7,39},{8,40},{9,... | collective-permute-start | bytes 13832 | tf_op jit(solution)/shard_map/ppermute | solution.py:56
  (220 shorter events, 127.1 us)
Async XLA Ops:
  5.5 10.2 %collective-permute-start = (f32[32,3488]{1,0:T(8,128)S(1)}, f32[32,3488]{1,0:T(8,128)S(1)}, u32[]{:S(2)}, u32[]{:S(2)}) collective-permute-start(f32[32,3488]{1,0:T(8,128)S(1)} %constant_dynamic-slice_fusion.12), channel_id=1, source_target_pairs={{0,1},{1,0},{2,3},{3,2},{4,5},{5,4},{6,7},{7,6},{8,9},{9,8},{10,11... | collective-permute-start | bytes 1339400 | tf_op jit(solution)/shard_map/ppermute | solution.py:56
  16.1 8.7 %collective-permute-start.1 = (f32[32,1744]{1,0:T(8,128)S(1)}, f32[32,1744]{1,0:T(8,128)S(1)}, u32[]{:S(2)}, u32[]{:S(2)}) collective-permute-start(f32[32,1744]{1,0:T(8,128)S(1)} %constant_dynamic-slice_fusion.11), channel_id=1, source_target_pairs={{0,2},{1,3},{2,0},{3,1},{4,6},{5,7},{6,4},{7,5},{8,10},{9,11},{10,... | collective-permute-start | bytes 669704 | tf_op jit(solution)/shard_map/ppermute | solution.py:56
  25.0 7.0 %collective-permute-start.2 = (f32[32,872]{1,0:T(8,128)S(1)}, f32[32,872]{1,0:T(8,128)S(1)}, u32[]{:S(2)}, u32[]{:S(2)}) collective-permute-start(f32[32,872]{1,0:T(8,128)S(1)} %constant_dynamic-slice_fusion.10), channel_id=1, source_target_pairs={{0,4},{1,5},{2,6},{3,7},{4,0},{5,1},{6,2},{7,3},{8,12},{9,13},{10,... | collective-permute-start | bytes 334856 | tf_op jit(solution)/shard_map/ppermute | solution.py:56
  32.3 5.1 %collective-permute-start.3 = (f32[32,436]{1,0:T(8,128)S(1)}, f32[32,436]{1,0:T(8,128)S(1)}, u32[]{:S(2)}, u32[]{:S(2)}) collective-permute-start(f32[32,436]{1,0:T(8,128)S(1)} %constant_dynamic-slice_fusion.9), channel_id=1, source_target_pairs={{0,8},{1,9},{2,10},{3,11},{4,12},{5,13},{6,14},{7,15},{8,0},{9,1},... | collective-permute-start | bytes 167432 | tf_op jit(solution)/shard_map/ppermute | solution.py:56
  37.6 5.6 %collective-permute-start.4 = (f32[32,218]{1,0:T(8,128)S(1)}, f32[32,218]{1,0:T(8,128)S(1)}, u32[]{:S(2)}, u32[]{:S(2)}) collective-permute-start(f32[32,218]{1,0:T(8,128)S(1)} %constant_dynamic-slice_fusion.8), channel_id=1, source_target_pairs={{0,16},{1,17},{2,18},{3,19},{4,20},{5,21},{6,22},{7,23},{8,24},{9,... | collective-permute-start | bytes 83720 | tf_op jit(solution)/shard_map/ppermute | solution.py:56
  43.4 8.4 %collective-permute-start.5 = (f32[32,109]{1,0:T(8,128)S(1)}, f32[32,109]{1,0:T(8,128)S(1)}, u32[]{:S(2)}, u32[]{:S(2)}) collective-permute-start(f32[32,109]{1,0:T(8,128)S(1)} %constant_dynamic-slice_fusion.7), channel_id=1, source_target_pairs={{0,32},{1,33},{2,34},{3,35},{4,36},{5,37},{6,38},{7,39},{8,40},{9,... | collective-permute-start | bytes 41864 | tf_op jit(solution)/shard_map/ppermute | solution.py:56
  52.1 8.3 %collective-permute-start.6 = (bf16[32,108]{1,0:T(8,128)(2,1)S(1)}, bf16[32,108]{1,0:T(8,128)(2,1)S(1)}, u32[]{:S(2)}, u32[]{:S(2)}) collective-permute-start(bf16[32,108]{1,0:T(8,128)(2,1)S(1)} %fusion.57), channel_id=1, source_target_pairs={{0,32},{1,33},{2,34},{3,35},{4,36},{5,37},{6,38},{7,39},{8,40},{9,... | collective-permute-start | bytes 20744 | tf_op jit(solution)/shard_map/ppermute | solution.py:65
  60.5 5.7 %collective-permute-start.7 = (bf16[32,216]{1,0:T(8,128)(2,1)S(1)}, bf16[32,216]{1,0:T(8,128)(2,1)S(1)}, u32[]{:S(2)}, u32[]{:S(2)}) collective-permute-start(bf16[32,216]{1,0:T(8,128)(2,1)S(1)} %maximum_select_fusion.15), channel_id=1, source_target_pairs={{0,16},{1,17},{2,18},{3,19},{4,20},{5,21},{6,22},{7,23},{8,24},{9,... | collective-permute-start | bytes 41480 | tf_op jit(solution)/shard_map/ppermute | solution.py:65
  66.3 4.7 %collective-permute-start.8 = (bf16[32,432]{1,0:T(8,128)(2,1)S(1)}, bf16[32,432]{1,0:T(8,128)(2,1)S(1)}, u32[]{:S(2)}, u32[]{:S(2)}) collective-permute-start(bf16[32,432]{1,0:T(8,128)(2,1)S(1)} %maximum_select_fusion.12), channel_id=1, source_target_pairs={{0,8},{1,9},{2,10},{3,11},{4,12},{5,13},{6,14},{7,15},{8,0},{9,1},... | collective-permute-start | bytes 82952 | tf_op jit(solution)/shard_map/ppermute | solution.py:65
  71.0 6.4 %collective-permute-start.9 = (bf16[32,864]{1,0:T(8,128)(2,1)S(1)}, bf16[32,864]{1,0:T(8,128)(2,1)S(1)}, u32[]{:S(2)}, u32[]{:S(2)}) collective-permute-start(bf16[32,864]{1,0:T(8,128)(2,1)S(1)} %maximum_select_fusion.9), channel_id=1, source_target_pairs={{0,4},{1,5},{2,6},{3,7},{4,0},{5,1},{6,2},{7,3},{8,12},{9,13},{10,... | collective-permute-start | bytes 165896 | tf_op jit(solution)/shard_map/ppermute | solution.py:65
  77.6 8.3 %collective-permute-start.10 = (bf16[32,1728]{1,0:T(8,128)(2,1)S(1)}, bf16[32,1728]{1,0:T(8,128)(2,1)S(1)}, u32[]{:S(2)}, u32[]{:S(2)}) collective-permute-start(bf16[32,1728]{1,0:T(8,128)(2,1)S(1)} %maximum_select_fusion.6), channel_id=1, source_target_pairs={{0,2},{1,3},{2,0},{3,1},{4,6},{5,7},{6,4},{7,5},{8,10},{9,11},{10,... | collective-permute-start | bytes 331784 | tf_op jit(solution)/shard_map/ppermute | solution.py:65
  86.0 13.0 %collective-permute-start.11 = (bf16[32,3456]{1,0:T(8,128)(2,1)S(1)}, bf16[32,3456]{1,0:T(8,128)(2,1)S(1)}, u32[]{:S(2)}, u32[]{:S(2)}) collective-permute-start(bf16[32,3456]{1,0:T(8,128)(2,1)S(1)} %maximum_select_fusion.3), channel_id=1, source_target_pairs={{0,1},{1,0},{2,3},{3,2},{4,5},{5,4},{6,7},{7,6},{8,9},{9,8},{10,11... | collective-permute-start | bytes 663560 | tf_op jit(solution)/shard_map/ppermute | solution.py:65
  117.9 7.0 %collective-permute-start.13 = (f32[288,66]{1,0:T(8,128)S(1)}, f32[288,66]{1,0:T(8,128)S(1)}, u32[]{:S(2)}, u32[]{:S(2)}) collective-permute-start(f32[288,66]{1,0:T(8,128)S(1)} %get-tuple-element.33), channel_id=1, source_target_pairs={{0,2},{1,3},{2,0},{3,1},{4,6},{5,7},{6,4},{7,5},{8,10},{9,11},{10,... | collective-permute-start | bytes 228104 | tf_op jit(solution)/shard_map/ppermute | solution.py:99
  125.4 6.6 %collective-permute-start.14 = (f32[144,66]{1,0:T(8,128)S(1)}, f32[144,66]{1,0:T(8,128)S(1)}, u32[]{:S(2)}, u32[]{:S(2)}) collective-permute-start(f32[144,66]{1,0:T(8,128)S(1)} %get-tuple-element.38), channel_id=1, source_target_pairs={{0,4},{1,5},{2,6},{3,7},{4,0},{5,1},{6,2},{7,3},{8,12},{9,13},{10,... | collective-permute-start | bytes 114056 | tf_op jit(solution)/shard_map/ppermute | solution.py:99
  132.5 4.7 %collective-permute-start.15 = (f32[72,66]{1,0:T(8,128)S(1)}, f32[72,66]{1,0:T(8,128)S(1)}, u32[]{:S(2)}, u32[]{:S(2)}) collective-permute-start(f32[72,66]{1,0:T(8,128)S(1)} %get-tuple-element.40), channel_id=1, source_target_pairs={{0,8},{1,9},{2,10},{3,11},{4,12},{5,13},{6,14},{7,15},{8,0},{9,1},... | collective-permute-start | bytes 57032 | tf_op jit(solution)/shard_map/ppermute | solution.py:99
  137.6 5.5 %collective-permute-start.16 = (f32[36,66]{1,0:T(8,128)S(1)}, f32[36,66]{1,0:T(8,128)S(1)}, u32[]{:S(2)}, u32[]{:S(2)}) collective-permute-start(f32[36,66]{1,0:T(8,128)S(1)} %get-tuple-element.42), channel_id=1, source_target_pairs={{0,16},{1,17},{2,18},{3,19},{4,20},{5,21},{6,22},{7,23},{8,24},{9,... | collective-permute-start | bytes 28520 | tf_op jit(solution)/shard_map/ppermute | solution.py:99
  143.5 8.5 %collective-permute-start.17 = (f32[18,66]{1,0:T(8,128)S(1)}, f32[18,66]{1,0:T(8,128)S(1)}, u32[]{:S(2)}, u32[]{:S(2)}) collective-permute-start(f32[18,66]{1,0:T(8,128)S(1)} %get-tuple-element.44), channel_id=1, source_target_pairs={{0,32},{1,33},{2,34},{3,35},{4,36},{5,37},{6,38},{7,39},{8,40},{9,... | collective-permute-start | bytes 14264 | tf_op jit(solution)/shard_map/ppermute | solution.py:99
  152.5 8.3 %collective-permute-start.18 = (bf16[18,64]{1,0:T(8,128)(2,1)S(1)}, bf16[18,64]{1,0:T(8,128)(2,1)S(1)}, u32[]{:S(2)}, u32[]{:S(2)}) collective-permute-start(bf16[18,64]{1,0:T(8,128)(2,1)S(1)} %fusion.71), channel_id=1, source_target_pairs={{0,32},{1,33},{2,34},{3,35},{4,36},{5,37},{6,38},{7,39},{8,40},{9,... | collective-permute-start | bytes 6920 | tf_op jit(solution)/shard_map/ppermute | solution.py:65
  160.8 5.6 %collective-permute-start.19 = (bf16[36,64]{1,0:T(8,128)(2,1)S(1)}, bf16[36,64]{1,0:T(8,128)(2,1)S(1)}, u32[]{:S(2)}, u32[]{:S(2)}) collective-permute-start(bf16[36,64]{1,0:T(8,128)(2,1)S(1)} %maximum_select_fusion.17), channel_id=1, source_target_pairs={{0,16},{1,17},{2,18},{3,19},{4,20},{5,21},{6,22},{7,23},{8,24},{9,... | collective-permute-start | bytes 13832 | tf_op jit(solution)/shard_map/ppermute | solution.py:65
  171.0 6.2 %collective-permute-start.21 = (bf16[144,64]{1,0:T(8,128)(2,1)S(1)}, bf16[144,64]{1,0:T(8,128)(2,1)S(1)}, u32[]{:S(2)}, u32[]{:S(2)}) collective-permute-start(bf16[144,64]{1,0:T(8,128)(2,1)S(1)} %maximum_select_fusion.11), channel_id=1, source_target_pairs={{0,4},{1,5},{2,6},{3,7},{4,0},{5,1},{6,2},{7,3},{8,12},{9,13},{10,... | collective-permute-start | bytes 55304 | tf_op jit(solution)/shard_map/ppermute | solution.py:65
  177.2 5.1 %collective-permute-start.22 = (bf16[288,64]{1,0:T(8,128)(2,1)S(1)}, bf16[288,64]{1,0:T(8,128)(2,1)S(1)}, u32[]{:S(2)}, u32[]{:S(2)}) collective-permute-start(bf16[288,64]{1,0:T(8,128)(2,1)S(1)} %maximum_select_fusion.8), channel_id=1, source_target_pairs={{0,2},{1,3},{2,0},{3,1},{4,6},{5,7},{6,4},{7,5},{8,10},{9,11},{10,... | collective-permute-start | bytes 110600 | tf_op jit(solution)/shard_map/ppermute | solution.py:65
  182.4 14.1 %collective-permute-start.23 = (bf16[576,64]{1,0:T(8,128)(2,1)S(1)}, bf16[576,64]{1,0:T(8,128)(2,1)S(1)}, u32[]{:S(2)}, u32[]{:S(2)}) collective-permute-start(bf16[576,64]{1,0:T(8,128)(2,1)S(1)} %maximum_select_fusion.4), channel_id=1, source_target_pairs={{0,1},{1,0},{2,3},{3,2},{4,5},{5,4},{6,7},{7,6},{8,9},{9,8},{10,11... | collective-permute-start | bytes 221192 | tf_op jit(solution)/shard_map/ppermute | solution.py:65
  197.0 8.4 %collective-permute-start.24 = (f32[32,36]{1,0:T(8,128)S(1)}, f32[32,36]{1,0:T(8,128)S(1)}, u32[]{:S(2)}, u32[]{:S(2)}) collective-permute-start(f32[32,36]{1,0:T(8,128)S(1)} %convolution_add_fusion), channel_id=1, source_target_pairs={{0,32},{1,33},{2,34},{3,35},{4,36},{5,37},{6,38},{7,39},{8,40},{9,... | collective-permute-start | bytes 13832 | tf_op jit(solution)/shard_map/ppermute | solution.py:65
  205.5 5.4 %collective-permute-start.25 = (f32[32,72]{1,0:T(8,128)S(1)}, f32[32,72]{1,0:T(8,128)S(1)}, u32[]{:S(2)}, u32[]{:S(2)}) collective-permute-start(f32[32,72]{1,0:T(8,128)S(1)} %maximum_select_fusion.16), channel_id=1, source_target_pairs={{0,16},{1,17},{2,18},{3,19},{4,20},{5,21},{6,22},{7,23},{8,24},{9,... | collective-permute-start | bytes 27656 | tf_op jit(solution)/shard_map/ppermute | solution.py:65
  211.0 4.7 %collective-permute-start.26 = (f32[32,144]{1,0:T(8,128)S(1)}, f32[32,144]{1,0:T(8,128)S(1)}, u32[]{:S(2)}, u32[]{:S(2)}) collective-permute-start(f32[32,144]{1,0:T(8,128)S(1)} %maximum_select_fusion.13), channel_id=1, source_target_pairs={{0,8},{1,9},{2,10},{3,11},{4,12},{5,13},{6,14},{7,15},{8,0},{9,1},... | collective-permute-start | bytes 55304 | tf_op jit(solution)/shard_map/ppermute | solution.py:65
  215.7 6.3 %collective-permute-start.27 = (f32[32,288]{1,0:T(8,128)S(1)}, f32[32,288]{1,0:T(8,128)S(1)}, u32[]{:S(2)}, u32[]{:S(2)}) collective-permute-start(f32[32,288]{1,0:T(8,128)S(1)} %maximum_select_fusion.10), channel_id=1, source_target_pairs={{0,4},{1,5},{2,6},{3,7},{4,0},{5,1},{6,2},{7,3},{8,12},{9,13},{10,... | collective-permute-start | bytes 110600 | tf_op jit(solution)/shard_map/ppermute | solution.py:65
  222.1 5.2 %collective-permute-start.28 = (f32[32,576]{1,0:T(8,128)S(1)}, f32[32,576]{1,0:T(8,128)S(1)}, u32[]{:S(2)}, u32[]{:S(2)}) collective-permute-start(f32[32,576]{1,0:T(8,128)S(1)} %maximum_select_fusion.7), channel_id=1, source_target_pairs={{0,2},{1,3},{2,0},{3,1},{4,6},{5,7},{6,4},{7,5},{8,10},{9,11},{10,... | collective-permute-start | bytes 221192 | tf_op jit(solution)/shard_map/ppermute | solution.py:65
  227.4 9.5 %collective-permute-start.29 = (f32[32,1152]{1,0:T(8,128)S(1)}, f32[32,1152]{1,0:T(8,128)S(1)}, u32[]{:S(2)}, u32[]{:S(2)}) collective-permute-start(f32[32,1152]{1,0:T(8,128)S(1)} %maximum_select_fusion.5), channel_id=1, source_target_pairs={{0,1},{1,0},{2,3},{3,2},{4,5},{5,4},{6,7},{7,6},{8,9},{9,8},{10,11... | collective-permute-start | bytes 442376 | tf_op jit(solution)/shard_map/ppermute | solution.py:65
  253.3 6.2 %collective-permute-start.31 = (f32[32,576]{1,0:T(8,128)S(1)}, f32[32,576]{1,0:T(8,128)S(1)}, u32[]{:S(2)}, u32[]{:S(2)}) collective-permute-start(f32[32,576]{1,0:T(8,128)S(1)} %constant_dynamic-slice_fusion.4), channel_id=1, source_target_pairs={{0,2},{1,3},{2,0},{3,1},{4,6},{5,7},{6,4},{7,5},{8,10},{9,11},{10,... | collective-permute-start | bytes 221192 | tf_op jit(solution)/shard_map/ppermute | solution.py:56
  259.7 6.3 %collective-permute-start.32 = (f32[32,288]{1,0:T(8,128)S(1)}, f32[32,288]{1,0:T(8,128)S(1)}, u32[]{:S(2)}, u32[]{:S(2)}) collective-permute-start(f32[32,288]{1,0:T(8,128)S(1)} %constant_dynamic-slice_fusion.3), channel_id=1, source_target_pairs={{0,4},{1,5},{2,6},{3,7},{4,0},{5,1},{6,2},{7,3},{8,12},{9,13},{10,... | collective-permute-start | bytes 110600 | tf_op jit(solution)/shard_map/ppermute | solution.py:56
  271.0 5.4 %collective-permute-start.34 = (f32[32,72]{1,0:T(8,128)S(1)}, f32[32,72]{1,0:T(8,128)S(1)}, u32[]{:S(2)}, u32[]{:S(2)}) collective-permute-start(f32[32,72]{1,0:T(8,128)S(1)} %constant_dynamic-slice_fusion.1), channel_id=1, source_target_pairs={{0,16},{1,17},{2,18},{3,19},{4,20},{5,21},{6,22},{7,23},{8,24},{9,... | collective-permute-start | bytes 27656 | tf_op jit(solution)/shard_map/ppermute | solution.py:56
  276.5 8.4 %collective-permute-start.35 = (f32[32,36]{1,0:T(8,128)S(1)}, f32[32,36]{1,0:T(8,128)S(1)}, u32[]{:S(2)}, u32[]{:S(2)}) collective-permute-start(f32[32,36]{1,0:T(8,128)S(1)} %constant_dynamic-slice_fusion), channel_id=1, source_target_pairs={{0,32},{1,33},{2,34},{3,35},{4,36},{5,37},{6,38},{7,39},{8,40},{9,... | collective-permute-start | bytes 13832 | tf_op jit(solution)/shard_map/ppermute | solution.py:56
  (23 other events, 731.6 us)

commit v4 on v3

--- a/solution.py
+++ b/solution.py
@@ -45,8 +45,9 @@
     return count, bits
 
 
-def scatter_sum(values):
-    count, bits = tp_bits()
+def scatter_sum(values, bits=None):
+    count, all_bits = tp_bits()
+    bits = all_bits if bits is None else bits
     own_rank = lax.axis_index("tp")
     for bit in bits:
         half = values.shape[1] // 2
@@ -57,8 +58,9 @@
     return values
 
 
-def gather_cols(values, axis=1):
-    count, bits = tp_bits()
+def gather_cols(values, axis=1, bits=None):
+    count, all_bits = tp_bits()
+    bits = all_bits if bits is None else bits
     own_rank = lax.axis_index("tp")
     for bit in reversed(bits):
         side = (own_rank // bit) % 2
@@ -71,13 +73,26 @@
     return values
 
 
-def reversed_rank(count):
-    own_rank = lax.axis_index("tp")
-    levels = count.bit_length() - 1
+def kept_position(bits):
+    own_rank = lax.axis_index("tp")
     position = 0
-    for level in range(levels):
-        position = position + ((own_rank // 2**level) % 2) * 2 ** (levels - 1 - level)
+    for level, bit in enumerate(bits):
+        position = position + ((own_rank // bit) % 2) * 2 ** (len(bits) - 1 - level)
     return position
+
+
+def exchange_sum(values, bits):
+    count, _ = tp_bits()
+    for bit in bits:
+        values = values + lax.ppermute(values, "tp", partner_pairs(count, bit))
+    return values
+
+
+def exchange_merge(rows, bits):
+    count, _ = tp_bits()
+    for bit in bits:
+        rows = merge_rows(rows, lax.ppermute(rows, "tp", partner_pairs(count, bit)))
+    return rows
 
 
 def merge_rows(first, second):
@@ -88,8 +103,8 @@
     return jnp.concatenate([body, joint], axis=1)
 
 
-def scatter_merge(rows):
-    count, bits = tp_bits()
+def scatter_merge(rows, bits):
+    count, _ = tp_bits()
     own_rank = lax.axis_index("tp")
     for bit in bits:
         half = rows.shape[0] // 2
@@ -155,9 +170,14 @@
         ],
         axis=2,
     ).reshape(all_tokens, tp_count * (block + 1))
-    own_block = scatter_sum(packed)
-    inv_attn = lax.rsqrt(own_block[:, block] / model_width + EPSILON)
-    qkv = gather_cols((inv_attn[:, None] * own_block[:, :block]).astype(jnp.bfloat16))
+    _, all_bits = tp_bits()
+    near_bits = all_bits[: len(all_bits) // 2]
+    far_bits = all_bits[len(all_bits) // 2 :]
+    own_block = exchange_sum(scatter_sum(packed, near_bits), far_bits)
+    own_block = own_block.reshape(all_tokens, -1, block + 1)
+    inv_attn = lax.rsqrt(own_block[:, 0, block] / model_width + EPSILON)
+    own_qkv = (inv_attn[:, None, None] * own_block[:, :, :block]).astype(jnp.bfloat16)
+    qkv = gather_cols(own_qkv.reshape(all_tokens, -1), bits=near_bits)
     own_lengths = jnp.broadcast_to(private_lengths[:, None], (requests, NEW)).reshape(all_tokens)
     places = (
         prefix_block * lax.axis_size("tp")
@@ -194,7 +214,8 @@
     local_peak = local_peak.reshape(all_tokens, HEADS)
     local_total = local_total.reshape(all_tokens, HEADS)
     local_weighted = local_weighted.reshape(all_tokens, model_width)
-    cache_rows = scatter_merge(state_rows(local_peak, local_total, local_weighted))
+    cache_rows = scatter_merge(state_rows(local_peak, local_total, local_weighted), near_bits)
+    cache_rows = exchange_merge(cache_rows, far_bits)
     key_f = fresh_keys.astype(jnp.float32).reshape(requests, NEW, HEADS, HDIM)
     new_scores = jnp.einsum("rjhd,rihd->rjhi", query_f, key_f) * score_scale
     causal = jnp.arange(NEW)[:, None] >= jnp.arange(NEW)[None, :]
@@ -208,10 +229,10 @@
     new_peak = new_peak.reshape(all_tokens, HEADS)
     new_rows = state_rows(new_peak, new_total, new_weighted)
     own_count = cache_rows.shape[0]
-    new_rows = lax.dynamic_slice_in_dim(new_rows, reversed_rank(tp_count) * own_count, own_count, axis=0)
+    new_rows = lax.dynamic_slice_in_dim(new_rows, kept_position(near_bits) * own_count, own_count, axis=0)
     final_rows = merge_rows(cache_rows, new_rows)
     attended_rows = (final_rows[:, :HDIM] / final_rows[:, HDIM : HDIM + 1]).astype(jnp.bfloat16)
-    attended = gather_cols(attended_rows, axis=0).reshape(all_tokens, model_width)
+    attended = gather_cols(attended_rows, axis=0, bits=near_bits).reshape(all_tokens, model_width)
     residual_cols = hidden + jnp.dot(attended, w_out, preferred_element_type=jnp.float32)
     full_rows = reverse_blocks(gather_cols(residual_cols), tp_count)
     inv_norm = lax.rsqrt(jnp.mean(full_rows * full_rows, axis=1) + EPSILON)

time: 291 us -> 253 us (0.87)
  starting transfers between devices: 148 us -> 125 us
  waiting for transfers between devices: 85 us -> 70.9 us
    ppermute x18 -> x12, starting transfers between devices: 85.9 us -> 59 us  [gather_cols(): other = lax.ppermute(values, 'tp', partner_pairs(count, bit))]
    ppermute x0 -> x6, starting transfers between devices: none -> 21.5 us  [the longest x3 12.2 us: exchange_merge(): rows = merge_rows(rows, lax.ppermute(rows, 'tp', partner_pairs(count, bit)))]
    ppermute x0 -> x6, waiting for transfers between devices: none -> 19.6 us  [the longest x3 12.8 us: exchange_sum(): values = values + lax.ppermute(values, 'tp', partner_pairs(count, bit))]
    ppermute x18 -> x12, waiting for transfers between devices: 35.7 us -> 20.3 us  [gather_cols(): other = lax.ppermute(values, 'tp', partner_pairs(count, bit))]
    ppermute x12 -> x9, waiting for transfers between devices: 38 us -> 25.1 us  [scatter_sum(): values = keep + lax.ppermute(send, 'tp', partner_pairs(count, bit))]
    ppermute x6 -> x3, starting transfers between devices: 21.2 us -> 9.72 us  [scatter_merge(): rows = merge_rows(keep, lax.ppermute(send, 'tp', partner_pairs(count, bit)))]
    ppermute x12 -> x9, starting transfers between devices: 40.7 us -> 34.3 us  [scatter_sum(): values = keep + lax.ppermute(send, 'tp', partner_pairs(count, bit))]
    ppermute x6 -> x3, waiting for transfers between devices: 11.2 us -> 5.97 us  [scatter_merge(): rows = merge_rows(keep, lax.ppermute(send, 'tp', partner_pairs(count, bit)))]
  transfers between devices with their start and end apart: 36 -> 30, of which waited for: 34 -> 28; matrix products, arithmetic and copies ran while one was open for 4% -> 4% of each run, Pallas kernels for 0% -> 0%
where the time goes in v4:
time: 253 us; the launch traced here: 248 us
  starting transfers between devices  125 us (49%)
  waiting for transfers between devices  70.9 us (28%)
  local copies, waits for them, and re-layouts  23 us (9%)
  other arithmetic  16.6 us (7%)
  matrix products  11.8 us (5%)
    ppermute x12, starting transfers between devices, gather_cols(): other = lax.ppermute(values, 'tp', partner_pairs(count, bit))  59 us
    ppermute x9, starting transfers between devices, scatter_sum(): values = keep + lax.ppermute(send, 'tp', partner_pairs(count, bit))  34.3 us
    ppermute x9, waiting for transfers between devices, scatter_sum(): values = keep + lax.ppermute(send, 'tp', partner_pairs(count, bit))  25.1 us
    ppermute x12, waiting for transfers between devices, gather_cols(): other = lax.ppermute(values, 'tp', partner_pairs(count, bit))  20.3 us
    ppermute x3, waiting for transfers between devices, exchange_sum(): values = values + lax.ppermute(values, 'tp', partner_pairs(count, bit))  12.8 us
    ppermute x3, starting transfers between devices, exchange_merge(): rows = merge_rows(rows, lax.ppermute(rows, 'tp', partner_pairs(count, bit)))  12.2 us
    ppermute x3, starting transfers between devices, scatter_merge(): rows = merge_rows(keep, lax.ppermute(send, 'tp', partner_pairs(count, bit)))  9.72 us
    ppermute x3, starting transfers between devices, exchange_sum(): values = values + lax.ppermute(values, 'tp', partner_pairs(count, bit))  9.37 us
  transfers between devices with their start and end apart: 30, of which 28 were waited for; matrix products, arithmetic and copies ran while one was open for 4% of the time, Pallas kernels for 0%

profile of v4, /device:TPU:1, one launch (start us, length us, event | category | flops | bytes accessed | tf_op | source)
XLA Modules:
  0.0 248.3 jit_solution(17458621762100267974)
XLA Ops:
  5.5 8.8 %collective-permute-start = (f32[32,3488]{1,0:T(8,128)S(1)}, f32[32,3488]{1,0:T(8,128)S(1)}, u32[]{:S(2)}, u32[]{:S(2)}) collective-permute-start(f32[32,3488]{1,0:T(8,128)S(1)} %constant_dynamic-slice_fusion.9), channel_id=1, source_target_pairs={{0,1},{1,0},{2,3},{3,2},{4,5},{5,4},{6,7},{7,6},{8,9},{9,8},{10,11... | collective-permute-start | bytes 1339400 | tf_op jit(solution)/shard_map/ppermute | solution.py:57
  18.1 6.7 %collective-permute-done.1 = f32[32,1744]{1,0:T(8,128)S(1)} collective-permute-done((f32[32,1744]{1,0:T(8,128)S(1)}, f32[32,1744]{1,0:T(8,128)S(1)}, u32[]{:S(2)}, u32[]{:S(2)}) %collective-permute-start.1) | collective-permute-done | bytes 223264 | tf_op jit(solution)/shard_map/ppermute | solution.py:57
  27.1 4.9 %collective-permute-done.2 = f32[32,872]{1,0:T(8,128)S(1)} collective-permute-done((f32[32,872]{1,0:T(8,128)S(1)}, f32[32,872]{1,0:T(8,128)S(1)}, u32[]{:S(2)}, u32[]{:S(2)}) %collective-permute-start.2) | collective-permute-done | bytes 111648 | tf_op jit(solution)/shard_map/ppermute | solution.py:57
  34.1 3.6 %collective-permute-done.3 = f32[32,872]{1,0:T(8,128)S(1)} collective-permute-done((f32[32,872]{1,0:T(8,128)S(1)}, f32[32,872]{1,0:T(8,128)S(1)}, u32[]{:S(2)}, u32[]{:S(2)}) %collective-permute-start.3) | collective-permute-done | bytes 111648 | tf_op jit(solution)/shard_map/ppermute | solution.py:87
  39.7 5.4 %collective-permute-done.4 = f32[32,872]{1,0:T(8,128)S(1)} collective-permute-done((f32[32,872]{1,0:T(8,128)S(1)}, f32[32,872]{1,0:T(8,128)S(1)}, u32[]{:S(2)}, u32[]{:S(2)}) %collective-permute-start.4) | collective-permute-done | bytes 111648 | tf_op jit(solution)/shard_map/ppermute | solution.py:87
  45.1 5.5 %collective-permute-start.5 = (f32[32,872]{1,0:T(8,128)S(1)}, f32[32,872]{1,0:T(8,128)S(1)}, u32[]{:S(2)}, u32[]{:S(2)}) collective-permute-start(f32[32,872]{1,0:T(8,128)S(1)} %add.302), channel_id=1, source_target_pairs={{0,32},{1,33},{2,34},{3,35},{4,36},{5,37},{6,38},{7,39},{8,40},{9,... | collective-permute-start | bytes 334856 | tf_op jit(solution)/shard_map/ppermute | solution.py:87
  50.8 3.7 %collective-permute-done.5 = f32[32,872]{1,0:T(8,128)S(1)} collective-permute-done((f32[32,872]{1,0:T(8,128)S(1)}, f32[32,872]{1,0:T(8,128)S(1)}, u32[]{:S(2)}, u32[]{:S(2)}) %collective-permute-start.5) | collective-permute-done | bytes 111648 | tf_op jit(solution)/shard_map/ppermute | solution.py:87
  55.4 3.0 %collective-permute-start.6 = (bf16[32,864]{1,0:T(8,128)(2,1)S(1)}, bf16[32,864]{1,0:T(8,128)(2,1)S(1)}, u32[]{:S(2)}, u32[]{:S(2)}) collective-permute-start(bf16[32,864]{1,0:T(8,128)(2,1)S(1)} %reshape.309), channel_id=1, source_target_pairs={{0,4},{1,5},{2,6},{3,7},{4,0},{5,1},{6,2},{7,3},{8,12},{9,13},{10,... | collective-permute-start | bytes 165896 | tf_op jit(solution)/shard_map/ppermute | solution.py:67
  58.5 3.4 %collective-permute-done.6 = bf16[32,864]{1,0:T(8,128)(2,1)S(1)} collective-permute-done((bf16[32,864]{1,0:T(8,128)(2,1)S(1)}, bf16[32,864]{1,0:T(8,128)(2,1)S(1)}, u32[]{:S(2)}, u32[]{:S(2)}) %collective-permute-start.6) | collective-permute-done | bytes 55328 | tf_op jit(solution)/shard_map/ppermute | solution.py:67
  70.5 9.2 %collective-permute-start.8 = (bf16[32,3456]{1,0:T(8,128)(2,1)S(1)}, bf16[32,3456]{1,0:T(8,128)(2,1)S(1)}, u32[]{:S(2)}, u32[]{:S(2)}) collective-permute-start(bf16[32,3456]{1,0:T(8,128)(2,1)S(1)} %maximum_select_fusion.3), channel_id=1, source_target_pairs={{0,1},{1,0},{2,3},{3,2},{4,5},{5,4},{6,7},{7,6},{8,9},{9,8},{10,11... | collective-permute-start | bytes 663560 | tf_op jit(solution)/shard_map/ppermute | solution.py:67
  99.5 3.3 %collective-permute-start.10 = (f32[288,66]{1,0:T(8,128)S(1)}, f32[288,66]{1,0:T(8,128)S(1)}, u32[]{:S(2)}, u32[]{:S(2)}) collective-permute-start(f32[288,66]{1,0:T(8,128)S(1)} %get-tuple-element.33), channel_id=1, source_target_pairs={{0,2},{1,3},{2,0},{3,1},{4,6},{5,7},{6,4},{7,5},{8,10},{9,11},{10,... | collective-permute-start | bytes 228104 | tf_op jit(solution)/shard_map/ppermute | solution.py:114
  103.1 3.3 %collective-permute-done.10 = f32[288,66]{1,0:T(8,128)S(1)} collective-permute-done((f32[288,66]{1,0:T(8,128)S(1)}, f32[288,66]{1,0:T(8,128)S(1)}, u32[]{:S(2)}, u32[]{:S(2)}) %collective-permute-start.10) | collective-permute-done | bytes 76064 | tf_op jit(solution)/shard_map/ppermute | solution.py:114
  107.0 4.0 %collective-permute-start.11 = (f32[144,66]{1,0:T(8,128)S(1)}, f32[144,66]{1,0:T(8,128)S(1)}, u32[]{:S(2)}, u32[]{:S(2)}) collective-permute-start(f32[144,66]{1,0:T(8,128)S(1)} %get-tuple-element.37), channel_id=1, source_target_pairs={{0,4},{1,5},{2,6},{3,7},{4,0},{5,1},{6,2},{7,3},{8,12},{9,13},{10,... | collective-permute-start | bytes 114056 | tf_op jit(solution)/shard_map/ppermute | solution.py:114
  116.5 2.6 %collective-permute-done.12 = f32[144,66]{1,0:T(8,128)S(1)} collective-permute-done((f32[144,66]{1,0:T(8,128)S(1)}, f32[144,66]{1,0:T(8,128)S(1)}, u32[]{:S(2)}, u32[]{:S(2)}) %collective-permute-start.12) | collective-permute-done | bytes 38048 | tf_op jit(solution)/shard_map/ppermute | solution.py:94
  119.6 3.7 %collective-permute-start.13 = (f32[144,66]{1,0:T(8,128)S(1)}, f32[144,66]{1,0:T(8,128)S(1)}, u32[]{:S(2)}, u32[]{:S(2)}) collective-permute-start(f32[144,66]{1,0:T(8,128)S(1)} %pad_maximum_fusion.4), channel_id=1, source_target_pairs={{0,16},{1,17},{2,18},{3,19},{4,20},{5,21},{6,22},{7,23},{8,24},{9,... | collective-permute-start | bytes 114056 | tf_op jit(solution)/shard_map/ppermute | solution.py:94
  126.9 6.6 %collective-permute-start.14 = (f32[144,66]{1,0:T(8,128)S(1)}, f32[144,66]{1,0:T(8,128)S(1)}, u32[]{:S(2)}, u32[]{:S(2)}) collective-permute-start(f32[144,66]{1,0:T(8,128)S(1)} %pad_maximum_fusion.5), channel_id=1, source_target_pairs={{0,32},{1,33},{2,34},{3,35},{4,36},{5,37},{6,38},{7,39},{8,40},{9,... | collective-permute-start | bytes 114056 | tf_op jit(solution)/shard_map/ppermute | solution.py:94
  136.8 3.9 %collective-permute-start.15 = (bf16[144,64]{1,0:T(8,128)(2,1)S(1)}, bf16[144,64]{1,0:T(8,128)(2,1)S(1)}, u32[]{:S(2)}, u32[]{:S(2)}) collective-permute-start(bf16[144,64]{1,0:T(8,128)(2,1)S(1)} %fusion.52), channel_id=1, source_target_pairs={{0,4},{1,5},{2,6},{3,7},{4,0},{5,1},{6,2},{7,3},{8,12},{9,13},{10,... | collective-permute-start | bytes 55304 | tf_op jit(solution)/shard_map/ppermute | solution.py:67
  143.0 3.2 %collective-permute-start.16 = (bf16[288,64]{1,0:T(8,128)(2,1)S(1)}, bf16[288,64]{1,0:T(8,128)(2,1)S(1)}, u32[]{:S(2)}, u32[]{:S(2)}) collective-permute-start(bf16[288,64]{1,0:T(8,128)(2,1)S(1)} %maximum_select_fusion.8), channel_id=1, source_target_pairs={{0,2},{1,3},{2,0},{3,1},{4,6},{5,7},{6,4},{7,5},{8,10},{9,11},{10,... | collective-permute-start | bytes 110600 | tf_op jit(solution)/shard_map/ppermute | solution.py:67
  148.6 9.9 %collective-permute-start.17 = (bf16[576,64]{1,0:T(8,128)(2,1)S(1)}, bf16[576,64]{1,0:T(8,128)(2,1)S(1)}, u32[]{:S(2)}, u32[]{:S(2)}) collective-permute-start(bf16[576,64]{1,0:T(8,128)(2,1)S(1)} %maximum_select_fusion.4), channel_id=1, source_target_pairs={{0,1},{1,0},{2,3},{3,2},{4,5},{5,4},{6,7},{7,6},{8,9},{9,8},{10,11... | collective-permute-start | bytes 221192 | tf_op jit(solution)/shard_map/ppermute | solution.py:67
  160.0 7.1 %collective-permute-start.18 = (f32[32,36]{1,0:T(8,128)S(1)}, f32[32,36]{1,0:T(8,128)S(1)}, u32[]{:S(2)}, u32[]{:S(2)}) collective-permute-start(f32[32,36]{1,0:T(8,128)S(1)} %convolution_add_fusion), channel_id=1, source_target_pairs={{0,32},{1,33},{2,34},{3,35},{4,36},{5,37},{6,38},{7,39},{8,40},{9,... | collective-permute-start | bytes 13832 | tf_op jit(solution)/shard_map/ppermute | solution.py:67
  171.1 2.8 %collective-permute-done.19 = f32[32,72]{1,0:T(8,128)S(1)} collective-permute-done((f32[32,72]{1,0:T(8,128)S(1)}, f32[32,72]{1,0:T(8,128)S(1)}, u32[]{:S(2)}, u32[]{:S(2)}) %collective-permute-start.19) | collective-permute-done | bytes 9248 | tf_op jit(solution)/shard_map/ppermute | solution.py:67
  174.0 2.6 %collective-permute-start.20 = (f32[32,144]{1,0:T(8,128)S(1)}, f32[32,144]{1,0:T(8,128)S(1)}, u32[]{:S(2)}, u32[]{:S(2)}) collective-permute-start(f32[32,144]{1,0:T(8,128)S(1)} %maximum_select_fusion.10), channel_id=1, source_target_pairs={{0,8},{1,9},{2,10},{3,11},{4,12},{5,13},{6,14},{7,15},{8,0},{9,1},... | collective-permute-start | bytes 55304 | tf_op jit(solution)/shard_map/ppermute | solution.py:67
  178.7 4.3 %collective-permute-start.21 = (f32[32,288]{1,0:T(8,128)S(1)}, f32[32,288]{1,0:T(8,128)S(1)}, u32[]{:S(2)}, u32[]{:S(2)}) collective-permute-start(f32[32,288]{1,0:T(8,128)S(1)} %maximum_select_fusion.9), channel_id=1, source_target_pairs={{0,4},{1,5},{2,6},{3,7},{4,0},{5,1},{6,2},{7,3},{8,12},{9,13},{10,... | collective-permute-start | bytes 110600 | tf_op jit(solution)/shard_map/ppermute | solution.py:67
  185.1 2.8 %collective-permute-start.22 = (f32[32,576]{1,0:T(8,128)S(1)}, f32[32,576]{1,0:T(8,128)S(1)}, u32[]{:S(2)}, u32[]{:S(2)}) collective-permute-start(f32[32,576]{1,0:T(8,128)S(1)} %maximum_select_fusion.7), channel_id=1, source_target_pairs={{0,2},{1,3},{2,0},{3,1},{4,6},{5,7},{6,4},{7,5},{8,10},{9,11},{10,... | collective-permute-start | bytes 221192 | tf_op jit(solution)/shard_map/ppermute | solution.py:67
  190.4 8.1 %collective-permute-start.23 = (f32[32,1152]{1,0:T(8,128)S(1)}, f32[32,1152]{1,0:T(8,128)S(1)}, u32[]{:S(2)}, u32[]{:S(2)}) collective-permute-start(f32[32,1152]{1,0:T(8,128)S(1)} %maximum_select_fusion.5), channel_id=1, source_target_pairs={{0,1},{1,0},{2,3},{3,2},{4,5},{5,4},{6,7},{7,6},{8,9},{9,8},{10,11... | collective-permute-start | bytes 442376 | tf_op jit(solution)/shard_map/ppermute | solution.py:67
  201.5 3.3 %multiply_reduce_fusion = (f32[32]{0:T(128)S(1)}, f32[32,2,2,2,2,2,2,36]{7,6,5,4,3,2,1,0:T(2,128)S(1)}) fusion(f32[32,1,2,2,2,2,2,36]{7,1,2,3,4,5,6,0:T(1,128)S(1)} %copy.159, f32[32,1,2,2,2,2,2,36]{7,1,2,3,4,5,6,0:T(1,128)S(1)} %copy.160, pred[]{:T(512)S(6)} %eq.113), kind=kLoop, calls=%fused_computation.24 | loop fusion | flops 368608 | bytes 589953 | tf_op jit(solution)/shard_map/reduce_sum | solution.py:238
  219.0 3.2 %collective-permute-done.25 = f32[32,576]{1,0:T(8,128)S(1)} collective-permute-done((f32[32,576]{1,0:T(8,128)S(1)}, f32[32,576]{1,0:T(8,128)S(1)}, u32[]{:S(2)}, u32[]{:S(2)}) %collective-permute-start.25) | collective-permute-done | bytes 73760 | tf_op jit(solution)/shard_map/ppermute | solution.py:57
  222.4 3.6 %collective-permute-start.26 = (f32[32,288]{1,0:T(8,128)S(1)}, f32[32,288]{1,0:T(8,128)S(1)}, u32[]{:S(2)}, u32[]{:S(2)}) collective-permute-start(f32[32,288]{1,0:T(8,128)S(1)} %constant_dynamic-slice_fusion.3), channel_id=1, source_target_pairs={{0,4},{1,5},{2,6},{3,7},{4,0},{5,1},{6,2},{7,3},{8,12},{9,13},{10,... | collective-permute-start | bytes 110600 | tf_op jit(solution)/shard_map/ppermute | solution.py:57
  226.0 2.7 %collective-permute-done.26 = f32[32,288]{1,0:T(8,128)S(1)} collective-permute-done((f32[32,288]{1,0:T(8,128)S(1)}, f32[32,288]{1,0:T(8,128)S(1)}, u32[]{:S(2)}, u32[]{:S(2)}) %collective-permute-start.26) | collective-permute-done | bytes 36896 | tf_op jit(solution)/shard_map/ppermute | solution.py:57
  228.9 2.7 %collective-permute-start.27 = (f32[32,144]{1,0:T(8,128)S(1)}, f32[32,144]{1,0:T(8,128)S(1)}, u32[]{:S(2)}, u32[]{:S(2)}) collective-permute-start(f32[32,144]{1,0:T(8,128)S(1)} %constant_dynamic-slice_fusion.2), channel_id=1, source_target_pairs={{0,8},{1,9},{2,10},{3,11},{4,12},{5,13},{6,14},{7,15},{8,0},{9,1},... | collective-permute-start | bytes 55304 | tf_op jit(solution)/shard_map/ppermute | solution.py:57
  233.7 3.9 %collective-permute-start.28 = (f32[32,72]{1,0:T(8,128)S(1)}, f32[32,72]{1,0:T(8,128)S(1)}, u32[]{:S(2)}, u32[]{:S(2)}) collective-permute-start(f32[32,72]{1,0:T(8,128)S(1)} %constant_dynamic-slice_fusion.1), channel_id=1, source_target_pairs={{0,16},{1,17},{2,18},{3,19},{4,20},{5,21},{6,22},{7,23},{8,24},{9,... | collective-permute-start | bytes 27656 | tf_op jit(solution)/shard_map/ppermute | solution.py:57
  239.2 7.0 %collective-permute-start.29 = (f32[32,36]{1,0:T(8,128)S(1)}, f32[32,36]{1,0:T(8,128)S(1)}, u32[]{:S(2)}, u32[]{:S(2)}) collective-permute-start(f32[32,36]{1,0:T(8,128)S(1)} %constant_dynamic-slice_fusion), channel_id=1, source_target_pairs={{0,32},{1,33},{2,34},{3,35},{4,36},{5,37},{6,38},{7,39},{8,40},{9,... | collective-permute-start | bytes 13832 | tf_op jit(solution)/shard_map/ppermute | solution.py:57
  (201 shorter events, 98.0 us)
Async XLA Ops:
  0.0 208.1 %copy-start = (bf16[180,2304]{1,0:T(8,128)(2,1)S(1)}, bf16[180,2304]{1,0:T(8,128)(2,1)}, u32[]{:S(2)}) copy-start(bf16[180,2304]{1,0:T(8,128)(2,1)} %param.30) | copy-start | bytes 2488324
  5.5 10.2 %collective-permute-start = (f32[32,3488]{1,0:T(8,128)S(1)}, f32[32,3488]{1,0:T(8,128)S(1)}, u32[]{:S(2)}, u32[]{:S(2)}) collective-permute-start(f32[32,3488]{1,0:T(8,128)S(1)} %constant_dynamic-slice_fusion.9), channel_id=1, source_target_pairs={{0,1},{1,0},{2,3},{3,2},{4,5},{5,4},{6,7},{7,6},{8,9},{9,8},{10,11... | collective-permute-start | bytes 1339400 | tf_op jit(solution)/shard_map/ppermute | solution.py:57
  16.1 8.7 %collective-permute-start.1 = (f32[32,1744]{1,0:T(8,128)S(1)}, f32[32,1744]{1,0:T(8,128)S(1)}, u32[]{:S(2)}, u32[]{:S(2)}) collective-permute-start(f32[32,1744]{1,0:T(8,128)S(1)} %constant_dynamic-slice_fusion.8), channel_id=1, source_target_pairs={{0,2},{1,3},{2,0},{3,1},{4,6},{5,7},{6,4},{7,5},{8,10},{9,11},{10,... | collective-permute-start | bytes 669704 | tf_op jit(solution)/shard_map/ppermute | solution.py:57
  25.0 7.0 %collective-permute-start.2 = (f32[32,872]{1,0:T(8,128)S(1)}, f32[32,872]{1,0:T(8,128)S(1)}, u32[]{:S(2)}, u32[]{:S(2)}) collective-permute-start(f32[32,872]{1,0:T(8,128)S(1)} %constant_dynamic-slice_fusion.7), channel_id=1, source_target_pairs={{0,4},{1,5},{2,6},{3,7},{4,0},{5,1},{6,2},{7,3},{8,12},{9,13},{10,... | collective-permute-start | bytes 334856 | tf_op jit(solution)/shard_map/ppermute | solution.py:57
  32.2 5.5 %collective-permute-start.3 = (f32[32,872]{1,0:T(8,128)S(1)}, f32[32,872]{1,0:T(8,128)S(1)}, u32[]{:S(2)}, u32[]{:S(2)}) collective-permute-start(f32[32,872]{1,0:T(8,128)S(1)} %dynamic-slice_add_fusion.3), channel_id=1, source_target_pairs={{0,8},{1,9},{2,10},{3,11},{4,12},{5,13},{6,14},{7,15},{8,0},{9,1},... | collective-permute-start | bytes 334856 | tf_op jit(solution)/shard_map/ppermute | solution.py:87
  37.7 7.4 %collective-permute-start.4 = (f32[32,872]{1,0:T(8,128)S(1)}, f32[32,872]{1,0:T(8,128)S(1)}, u32[]{:S(2)}, u32[]{:S(2)}) collective-permute-start(f32[32,872]{1,0:T(8,128)S(1)} %add.301), channel_id=1, source_target_pairs={{0,16},{1,17},{2,18},{3,19},{4,20},{5,21},{6,22},{7,23},{8,24},{9,... | collective-permute-start | bytes 334856 | tf_op jit(solution)/shard_map/ppermute | solution.py:87
  45.1 9.4 %collective-permute-start.5 = (f32[32,872]{1,0:T(8,128)S(1)}, f32[32,872]{1,0:T(8,128)S(1)}, u32[]{:S(2)}, u32[]{:S(2)}) collective-permute-start(f32[32,872]{1,0:T(8,128)S(1)} %add.302), channel_id=1, source_target_pairs={{0,32},{1,33},{2,34},{3,35},{4,36},{5,37},{6,38},{7,39},{8,40},{9,... | collective-permute-start | bytes 334856 | tf_op jit(solution)/shard_map/ppermute | solution.py:87
  55.4 6.4 %collective-permute-start.6 = (bf16[32,864]{1,0:T(8,128)(2,1)S(1)}, bf16[32,864]{1,0:T(8,128)(2,1)S(1)}, u32[]{:S(2)}, u32[]{:S(2)}) collective-permute-start(bf16[32,864]{1,0:T(8,128)(2,1)S(1)} %reshape.309), channel_id=1, source_target_pairs={{0,4},{1,5},{2,6},{3,7},{4,0},{5,1},{6,2},{7,3},{8,12},{9,13},{10,... | collective-permute-start | bytes 165896 | tf_op jit(solution)/shard_map/ppermute | solution.py:67
  62.0 8.3 %collective-permute-start.7 = (bf16[32,1728]{1,0:T(8,128)(2,1)S(1)}, bf16[32,1728]{1,0:T(8,128)(2,1)S(1)}, u32[]{:S(2)}, u32[]{:S(2)}) collective-permute-start(bf16[32,1728]{1,0:T(8,128)(2,1)S(1)} %maximum_select_fusion.6), channel_id=1, source_target_pairs={{0,2},{1,3},{2,0},{3,1},{4,6},{5,7},{6,4},{7,5},{8,10},{9,11},{10,... | collective-permute-start | bytes 331784 | tf_op jit(solution)/shard_map/ppermute | solution.py:67
  70.5 10.1 %collective-permute-start.8 = (bf16[32,3456]{1,0:T(8,128)(2,1)S(1)}, bf16[32,3456]{1,0:T(8,128)(2,1)S(1)}, u32[]{:S(2)}, u32[]{:S(2)}) collective-permute-start(bf16[32,3456]{1,0:T(8,128)(2,1)S(1)} %maximum_select_fusion.3), channel_id=1, source_target_pairs={{0,1},{1,0},{2,3},{3,2},{4,5},{5,4},{6,7},{7,6},{8,9},{9,8},{10,11... | collective-permute-start | bytes 663560 | tf_op jit(solution)/shard_map/ppermute | solution.py:67
  95.1 3.6 %collective-permute-start.9 = (f32[576,66]{1,0:T(8,128)S(1)}, f32[576,66]{1,0:T(8,128)S(1)}, u32[]{:S(2)}, u32[]{:S(2)}) collective-permute-start(f32[576,66]{1,0:T(8,128)S(1)} %constant_dynamic-slice_fusion.6), channel_id=1, source_target_pairs={{0,1},{1,0},{2,3},{3,2},{4,5},{5,4},{6,7},{7,6},{8,9},{9,8},{10,11... | collective-permute-start | bytes 456200 | tf_op jit(solution)/shard_map/ppermute | solution.py:114
  99.5 7.0 %collective-permute-start.10 = (f32[288,66]{1,0:T(8,128)S(1)}, f32[288,66]{1,0:T(8,128)S(1)}, u32[]{:S(2)}, u32[]{:S(2)}) collective-permute-start(f32[288,66]{1,0:T(8,128)S(1)} %get-tuple-element.33), channel_id=1, source_target_pairs={{0,2},{1,3},{2,0},{3,1},{4,6},{5,7},{6,4},{7,5},{8,10},{9,11},{10,... | collective-permute-start | bytes 228104 | tf_op jit(solution)/shard_map/ppermute | solution.py:114
  107.0 6.6 %collective-permute-start.11 = (f32[144,66]{1,0:T(8,128)S(1)}, f32[144,66]{1,0:T(8,128)S(1)}, u32[]{:S(2)}, u32[]{:S(2)}) collective-permute-start(f32[144,66]{1,0:T(8,128)S(1)} %get-tuple-element.37), channel_id=1, source_target_pairs={{0,4},{1,5},{2,6},{3,7},{4,0},{5,1},{6,2},{7,3},{8,12},{9,13},{10,... | collective-permute-start | bytes 114056 | tf_op jit(solution)/shard_map/ppermute | solution.py:114
  114.1 5.1 %collective-permute-start.12 = (f32[144,66]{1,0:T(8,128)S(1)}, f32[144,66]{1,0:T(8,128)S(1)}, u32[]{:S(2)}, u32[]{:S(2)}) collective-permute-start(f32[144,66]{1,0:T(8,128)S(1)} %pad_maximum_fusion.3), channel_id=1, source_target_pairs={{0,8},{1,9},{2,10},{3,11},{4,12},{5,13},{6,14},{7,15},{8,0},{9,1},... | collective-permute-start | bytes 114056 | tf_op jit(solution)/shard_map/ppermute | solution.py:94
  119.6 6.8 %collective-permute-start.13 = (f32[144,66]{1,0:T(8,128)S(1)}, f32[144,66]{1,0:T(8,128)S(1)}, u32[]{:S(2)}, u32[]{:S(2)}) collective-permute-start(f32[144,66]{1,0:T(8,128)S(1)} %pad_maximum_fusion.4), channel_id=1, source_target_pairs={{0,16},{1,17},{2,18},{3,19},{4,20},{5,21},{6,22},{7,23},{8,24},{9,... | collective-permute-start | bytes 114056 | tf_op jit(solution)/shard_map/ppermute | solution.py:94
  126.9 9.1 %collective-permute-start.14 = (f32[144,66]{1,0:T(8,128)S(1)}, f32[144,66]{1,0:T(8,128)S(1)}, u32[]{:S(2)}, u32[]{:S(2)}) collective-permute-start(f32[144,66]{1,0:T(8,128)S(1)} %pad_maximum_fusion.5), channel_id=1, source_target_pairs={{0,32},{1,33},{2,34},{3,35},{4,36},{5,37},{6,38},{7,39},{8,40},{9,... | collective-permute-start | bytes 114056 | tf_op jit(solution)/shard_map/ppermute | solution.py:94
  133.5 65.0 %copy-start.15 = (s32[32,2]{0,1:T(2,128)S(1)}, s32[32,2]{0,1:T(2,128)}, u32[]{:S(2)}) copy-start(s32[32,2]{0,1:T(2,128)} %param.31) | copy-start | bytes 772
  136.8 6.2 %collective-permute-start.15 = (bf16[144,64]{1,0:T(8,128)(2,1)S(1)}, bf16[144,64]{1,0:T(8,128)(2,1)S(1)}, u32[]{:S(2)}, u32[]{:S(2)}) collective-permute-start(bf16[144,64]{1,0:T(8,128)(2,1)S(1)} %fusion.52), channel_id=1, source_target_pairs={{0,4},{1,5},{2,6},{3,7},{4,0},{5,1},{6,2},{7,3},{8,12},{9,13},{10,... | collective-permute-start | bytes 55304 | tf_op jit(solution)/shard_map/ppermute | solution.py:67
  143.0 5.5 %collective-permute-start.16 = (bf16[288,64]{1,0:T(8,128)(2,1)S(1)}, bf16[288,64]{1,0:T(8,128)(2,1)S(1)}, u32[]{:S(2)}, u32[]{:S(2)}) collective-permute-start(bf16[288,64]{1,0:T(8,128)(2,1)S(1)} %maximum_select_fusion.8), channel_id=1, source_target_pairs={{0,2},{1,3},{2,0},{3,1},{4,6},{5,7},{6,4},{7,5},{8,10},{9,11},{10,... | collective-permute-start | bytes 110600 | tf_op jit(solution)/shard_map/ppermute | solution.py:67
  148.6 10.9 %collective-permute-start.17 = (bf16[576,64]{1,0:T(8,128)(2,1)S(1)}, bf16[576,64]{1,0:T(8,128)(2,1)S(1)}, u32[]{:S(2)}, u32[]{:S(2)}) collective-permute-start(bf16[576,64]{1,0:T(8,128)(2,1)S(1)} %maximum_select_fusion.4), channel_id=1, source_target_pairs={{0,1},{1,0},{2,3},{3,2},{4,5},{5,4},{6,7},{7,6},{8,9},{9,8},{10,11... | collective-permute-start | bytes 221192 | tf_op jit(solution)/shard_map/ppermute | solution.py:67
  160.0 8.4 %collective-permute-start.18 = (f32[32,36]{1,0:T(8,128)S(1)}, f32[32,36]{1,0:T(8,128)S(1)}, u32[]{:S(2)}, u32[]{:S(2)}) collective-permute-start(f32[32,36]{1,0:T(8,128)S(1)} %convolution_add_fusion), channel_id=1, source_target_pairs={{0,32},{1,33},{2,34},{3,35},{4,36},{5,37},{6,38},{7,39},{8,40},{9,... | collective-permute-start | bytes 13832 | tf_op jit(solution)/shard_map/ppermute | solution.py:67
  168.5 5.4 %collective-permute-start.19 = (f32[32,72]{1,0:T(8,128)S(1)}, f32[32,72]{1,0:T(8,128)S(1)}, u32[]{:S(2)}, u32[]{:S(2)}) collective-permute-start(f32[32,72]{1,0:T(8,128)S(1)} %maximum_select_fusion.11), channel_id=1, source_target_pairs={{0,16},{1,17},{2,18},{3,19},{4,20},{5,21},{6,22},{7,23},{8,24},{9,... | collective-permute-start | bytes 27656 | tf_op jit(solution)/shard_map/ppermute | solution.py:67
  174.0 4.7 %collective-permute-start.20 = (f32[32,144]{1,0:T(8,128)S(1)}, f32[32,144]{1,0:T(8,128)S(1)}, u32[]{:S(2)}, u32[]{:S(2)}) collective-permute-start(f32[32,144]{1,0:T(8,128)S(1)} %maximum_select_fusion.10), channel_id=1, source_target_pairs={{0,8},{1,9},{2,10},{3,11},{4,12},{5,13},{6,14},{7,15},{8,0},{9,1},... | collective-permute-start | bytes 55304 | tf_op jit(solution)/shard_map/ppermute | solution.py:67
  178.7 6.3 %collective-permute-start.21 = (f32[32,288]{1,0:T(8,128)S(1)}, f32[32,288]{1,0:T(8,128)S(1)}, u32[]{:S(2)}, u32[]{:S(2)}) collective-permute-start(f32[32,288]{1,0:T(8,128)S(1)} %maximum_select_fusion.9), channel_id=1, source_target_pairs={{0,4},{1,5},{2,6},{3,7},{4,0},{5,1},{6,2},{7,3},{8,12},{9,13},{10,... | collective-permute-start | bytes 110600 | tf_op jit(solution)/shard_map/ppermute | solution.py:67
  185.1 5.2 %collective-permute-start.22 = (f32[32,576]{1,0:T(8,128)S(1)}, f32[32,576]{1,0:T(8,128)S(1)}, u32[]{:S(2)}, u32[]{:S(2)}) collective-permute-start(f32[32,576]{1,0:T(8,128)S(1)} %maximum_select_fusion.7), channel_id=1, source_target_pairs={{0,2},{1,3},{2,0},{3,1},{4,6},{5,7},{6,4},{7,5},{8,10},{9,11},{10,... | collective-permute-start | bytes 221192 | tf_op jit(solution)/shard_map/ppermute | solution.py:67
  190.4 9.6 %collective-permute-start.23 = (f32[32,1152]{1,0:T(8,128)S(1)}, f32[32,1152]{1,0:T(8,128)S(1)}, u32[]{:S(2)}, u32[]{:S(2)}) collective-permute-start(f32[32,1152]{1,0:T(8,128)S(1)} %maximum_select_fusion.5), channel_id=1, source_target_pairs={{0,1},{1,0},{2,3},{3,2},{4,5},{5,4},{6,7},{7,6},{8,9},{9,8},{10,11... | collective-permute-start | bytes 442376 | tf_op jit(solution)/shard_map/ppermute | solution.py:67
  213.0 3.3 %collective-permute-start.24 = (f32[32,1152]{1,0:T(8,128)S(1)}, f32[32,1152]{1,0:T(8,128)S(1)}, u32[]{:S(2)}, u32[]{:S(2)}) collective-permute-start(f32[32,1152]{1,0:T(8,128)S(1)} %constant_dynamic-slice_fusion.5), channel_id=1, source_target_pairs={{0,1},{1,0},{2,3},{3,2},{4,5},{5,4},{6,7},{7,6},{8,9},{9,8},{10,11... | collective-permute-start | bytes 442376 | tf_op jit(solution)/shard_map/ppermute | solution.py:57
  216.4 5.8 %collective-permute-start.25 = (f32[32,576]{1,0:T(8,128)S(1)}, f32[32,576]{1,0:T(8,128)S(1)}, u32[]{:S(2)}, u32[]{:S(2)}) collective-permute-start(f32[32,576]{1,0:T(8,128)S(1)} %constant_dynamic-slice_fusion.4), channel_id=1, source_target_pairs={{0,2},{1,3},{2,0},{3,1},{4,6},{5,7},{6,4},{7,5},{8,10},{9,11},{10,... | collective-permute-start | bytes 221192 | tf_op jit(solution)/shard_map/ppermute | solution.py:57
  222.4 6.3 %collective-permute-start.26 = (f32[32,288]{1,0:T(8,128)S(1)}, f32[32,288]{1,0:T(8,128)S(1)}, u32[]{:S(2)}, u32[]{:S(2)}) collective-permute-start(f32[32,288]{1,0:T(8,128)S(1)} %constant_dynamic-slice_fusion.3), channel_id=1, source_target_pairs={{0,4},{1,5},{2,6},{3,7},{4,0},{5,1},{6,2},{7,3},{8,12},{9,13},{10,... | collective-permute-start | bytes 110600 | tf_op jit(solution)/shard_map/ppermute | solution.py:57
  228.9 4.6 %collective-permute-start.27 = (f32[32,144]{1,0:T(8,128)S(1)}, f32[32,144]{1,0:T(8,128)S(1)}, u32[]{:S(2)}, u32[]{:S(2)}) collective-permute-start(f32[32,144]{1,0:T(8,128)S(1)} %constant_dynamic-slice_fusion.2), channel_id=1, source_target_pairs={{0,8},{1,9},{2,10},{3,11},{4,12},{5,13},{6,14},{7,15},{8,0},{9,1},... | collective-permute-start | bytes 55304 | tf_op jit(solution)/shard_map/ppermute | solution.py:57
  233.7 5.4 %collective-permute-start.28 = (f32[32,72]{1,0:T(8,128)S(1)}, f32[32,72]{1,0:T(8,128)S(1)}, u32[]{:S(2)}, u32[]{:S(2)}) collective-permute-start(f32[32,72]{1,0:T(8,128)S(1)} %constant_dynamic-slice_fusion.1), channel_id=1, source_target_pairs={{0,16},{1,17},{2,18},{3,19},{4,20},{5,21},{6,22},{7,23},{8,24},{9,... | collective-permute-start | bytes 27656 | tf_op jit(solution)/shard_map/ppermute | solution.py:57
  239.2 8.4 %collective-permute-start.29 = (f32[32,36]{1,0:T(8,128)S(1)}, f32[32,36]{1,0:T(8,128)S(1)}, u32[]{:S(2)}, u32[]{:S(2)}) collective-permute-start(f32[32,36]{1,0:T(8,128)S(1)} %constant_dynamic-slice_fusion), channel_id=1, source_target_pairs={{0,32},{1,33},{2,34},{3,35},{4,36},{5,37},{6,38},{7,39},{8,40},{9,... | collective-permute-start | bytes 13832 | tf_op jit(solution)/shard_map/ppermute | solution.py:57
  (17 other events, 262.6 us)

commit v5 on v4

--- a/solution.py
+++ b/solution.py
@@ -160,24 +160,27 @@
     scaled = (hidden * attn_gain[None, :]).astype(jnp.bfloat16)
     partial_qkv = jnp.dot(scaled, w_qkv, preferred_element_type=jnp.float32)
     own_squares = jnp.sum(hidden * hidden, axis=1)
-    qkv_width = partial_qkv.shape[1]
     tp_count = lax.axis_size("tp")
-    block = qkv_width // tp_count
+    _, all_bits = tp_bits()
+    near_bits = all_bits[: len(all_bits) // 2]
+    far_bits = all_bits[len(all_bits) // 2 :]
+    query_block = model_width // tp_count
     packed = jnp.concatenate(
         [
-            partial_qkv.reshape(all_tokens, tp_count, block),
+            partial_qkv[:, :model_width].reshape(all_tokens, tp_count, query_block),
             jnp.broadcast_to(own_squares[:, None, None], (all_tokens, tp_count, 1)),
         ],
         axis=2,
-    ).reshape(all_tokens, tp_count * (block + 1))
-    _, all_bits = tp_bits()
-    near_bits = all_bits[: len(all_bits) // 2]
-    far_bits = all_bits[len(all_bits) // 2 :]
+    ).reshape(all_tokens, tp_count * (query_block + 1))
     own_block = exchange_sum(scatter_sum(packed, near_bits), far_bits)
-    own_block = own_block.reshape(all_tokens, -1, block + 1)
-    inv_attn = lax.rsqrt(own_block[:, 0, block] / model_width + EPSILON)
-    own_qkv = (inv_attn[:, None, None] * own_block[:, :, :block]).astype(jnp.bfloat16)
-    qkv = gather_cols(own_qkv.reshape(all_tokens, -1), bits=near_bits)
+    own_block = own_block.reshape(all_tokens, -1, query_block + 1)
+    inv_attn = lax.rsqrt(own_block[:, 0, query_block] / model_width + EPSILON)
+    own_query = (inv_attn[:, None, None] * own_block[:, :, :query_block]).astype(jnp.bfloat16)
+    query_cols = gather_cols(own_query.reshape(all_tokens, -1), bits=near_bits)
+    own_kv = exchange_sum(scatter_sum(partial_qkv[:, model_width:], near_bits), far_bits)
+    own_kv = (inv_attn[:, None] * own_kv).astype(jnp.bfloat16)
+    kv_cols = gather_cols(own_kv, bits=near_bits)
+    qkv = jnp.concatenate([query_cols, kv_cols], axis=1)
     own_lengths = jnp.broadcast_to(private_lengths[:, None], (requests, NEW)).reshape(all_tokens)
     places = (
         prefix_block * lax.axis_size("tp")

time: 253 us -> 274 us (1.083)
  the two profiles are of different devices: /device:TPU:1 before, /device:TPU:40 now
where the time goes in v5:
time: 274 us; the launch traced here: 273 us
  starting transfers between devices  113 us (41%)
  waiting for transfers between devices  103 us (38%)
  local copies, waits for them, and re-layouts  26 us (9%)
  other arithmetic  17.5 us (6%)
  matrix products  11.6 us (4%)
    ppermute x15, starting transfers between devices, gather_cols(): other = lax.ppermute(values, 'tp', partner_pairs(count, bit))  37 us
    ppermute x15, waiting for transfers between devices, gather_cols(): other = lax.ppermute(values, 'tp', partner_pairs(count, bit))  37 us
    ppermute x12, starting transfers between devices, scatter_sum(): values = keep + lax.ppermute(send, 'tp', partner_pairs(count, bit))  33.4 us
    ppermute x12, waiting for transfers between devices, scatter_sum(): values = keep + lax.ppermute(send, 'tp', partner_pairs(count, bit))  28.8 us
    ppermute x6, starting transfers between devices, exchange_sum(): values = values + lax.ppermute(values, 'tp', partner_pairs(count, bit))  27.5 us
    ppermute x3, waiting for transfers between devices, exchange_merge(): rows = merge_rows(rows, lax.ppermute(rows, 'tp', partner_pairs(count, bit)))  16.3 us
    ppermute x6, waiting for transfers between devices, exchange_sum(): values = values + lax.ppermute(values, 'tp', partner_pairs(count, bit))  11.7 us
    ppermute x3, waiting for transfers between devices, scatter_merge(): rows = merge_rows(keep, lax.ppermute(send, 'tp', partner_pairs(count, bit)))  9.4 us
  transfers between devices with their start and end apart: 39, of which 28 were waited for; matrix products, arithmetic and copies ran while one was open for 7% of the time, Pallas kernels for 0%

profile of v5, /device:TPU:40, one launch (start us, length us, event | category | flops | bytes accessed | tf_op | source)
XLA Modules:
  0.0 272.9 jit_solution(8044692457343404326)
XLA Ops:
  10.4 3.4 %collective-permute-start.1 = (f32[32,592]{1,0:T(8,128)S(1)}, f32[32,592]{1,0:T(8,128)S(1)}, u32[]{:S(2)}, u32[]{:S(2)}) collective-permute-start(f32[32,592]{1,0:T(8,128)S(1)} %constant_dynamic-slice_fusion.11), channel_id=1, source_target_pairs={{0,2},{1,3},{2,0},{3,1},{4,6},{5,7},{6,4},{7,5},{8,10},{9,11},{10,... | collective-permute-start | bytes 227336 | tf_op jit(solution)/shard_map/ppermute | solution.py:57
  17.2 5.1 %collective-permute-start.2 = (f32[32,296]{1,0:T(8,128)S(1)}, f32[32,296]{1,0:T(8,128)S(1)}, u32[]{:S(2)}, u32[]{:S(2)}) collective-permute-start(f32[32,296]{1,0:T(8,128)S(1)} %constant_dynamic-slice_fusion.10), channel_id=1, source_target_pairs={{0,4},{1,5},{2,6},{3,7},{4,0},{5,1},{6,2},{7,3},{8,12},{9,13},{10,... | collective-permute-start | bytes 113672 | tf_op jit(solution)/shard_map/ppermute | solution.py:57
  26.0 4.3 %collective-permute-start.3 = (f32[32,296]{1,0:T(8,128)S(1)}, f32[32,296]{1,0:T(8,128)S(1)}, u32[]{:S(2)}, u32[]{:S(2)}) collective-permute-start(f32[32,296]{1,0:T(8,128)S(1)} %dynamic-slice_add_fusion.8), channel_id=1, source_target_pairs={{0,8},{1,9},{2,10},{3,11},{4,12},{5,13},{6,14},{7,15},{8,0},{9,1},... | collective-permute-start | bytes 113672 | tf_op jit(solution)/shard_map/ppermute | solution.py:87
  32.3 6.1 %collective-permute-start.4 = (f32[32,296]{1,0:T(8,128)S(1)}, f32[32,296]{1,0:T(8,128)S(1)}, u32[]{:S(2)}, u32[]{:S(2)}) collective-permute-start(f32[32,296]{1,0:T(8,128)S(1)} %add.348), channel_id=1, source_target_pairs={{0,16},{1,17},{2,18},{3,19},{4,20},{5,21},{6,22},{7,23},{8,24},{9,... | collective-permute-start | bytes 113672 | tf_op jit(solution)/shard_map/ppermute | solution.py:87
  38.5 3.9 %collective-permute-start.17 = (f32[32,576]{1,0:T(8,128)S(1)}, f32[32,576]{1,0:T(8,128)S(1)}, u32[]{:S(2)}, u32[]{:S(2)}) collective-permute-start(f32[32,576]{1,0:T(8,128)S(1)} %constant_dynamic-slice_fusion.6), channel_id=1, source_target_pairs={{0,4},{1,5},{2,6},{3,7},{4,0},{5,1},{6,2},{7,3},{8,12},{9,13},{10,... | collective-permute-start | bytes 221192 | tf_op jit(solution)/shard_map/ppermute | solution.py:57
  43.2 8.9 %collective-permute-start.5 = (f32[32,296]{1,0:T(8,128)S(1)}, f32[32,296]{1,0:T(8,128)S(1)}, u32[]{:S(2)}, u32[]{:S(2)}) collective-permute-start(f32[32,296]{1,0:T(8,128)S(1)} %add.349), channel_id=1, source_target_pairs={{0,32},{1,33},{2,34},{3,35},{4,36},{5,37},{6,38},{7,39},{8,40},{9,... | collective-permute-start | bytes 113672 | tf_op jit(solution)/shard_map/ppermute | solution.py:87
  52.2 3.4 %collective-permute-start.18 = (f32[32,576]{1,0:T(8,128)S(1)}, f32[32,576]{1,0:T(8,128)S(1)}, u32[]{:S(2)}, u32[]{:S(2)}) collective-permute-start(f32[32,576]{1,0:T(8,128)S(1)} %dynamic-slice_add_fusion.5), channel_id=1, source_target_pairs={{0,8},{1,9},{2,10},{3,11},{4,12},{5,13},{6,14},{7,15},{8,0},{9,1},... | collective-permute-start | bytes 221192 | tf_op jit(solution)/shard_map/ppermute | solution.py:87
  64.9 5.8 %collective-permute-done.19 = f32[32,576]{1,0:T(8,128)S(1)} collective-permute-done((f32[32,576]{1,0:T(8,128)S(1)}, f32[32,576]{1,0:T(8,128)S(1)}, u32[]{:S(2)}, u32[]{:S(2)}) %collective-permute-start.19) | collective-permute-done | bytes 73760 | tf_op jit(solution)/shard_map/ppermute | solution.py:87
  73.1 3.9 %collective-permute-start.6 = (bf16[32,288]{1,0:T(8,128)(2,1)S(1)}, bf16[32,288]{1,0:T(8,128)(2,1)S(1)}, u32[]{:S(2)}, u32[]{:S(2)}) collective-permute-start(bf16[32,288]{1,0:T(8,128)(2,1)S(1)} %reshape.328), channel_id=1, source_target_pairs={{0,4},{1,5},{2,6},{3,7},{4,0},{5,1},{6,2},{7,3},{8,12},{9,13},{10,... | collective-permute-start | bytes 55304 | tf_op jit(solution)/shard_map/ppermute | solution.py:67
  77.0 3.9 %collective-permute-done.20 = f32[32,576]{1,0:T(8,128)S(1)} collective-permute-done((f32[32,576]{1,0:T(8,128)S(1)}, f32[32,576]{1,0:T(8,128)S(1)}, u32[]{:S(2)}, u32[]{:S(2)}) %collective-permute-start.20) | collective-permute-done | bytes 73760 | tf_op jit(solution)/shard_map/ppermute | solution.py:87
  81.0 3.4 %collective-permute-start.21 = (bf16[32,576]{1,0:T(8,128)(2,1)S(1)}, bf16[32,576]{1,0:T(8,128)(2,1)S(1)}, u32[]{:S(2)}, u32[]{:S(2)}) collective-permute-start(bf16[32,576]{1,0:T(8,128)(2,1)S(1)} %multiply_convert_fusion.1), channel_id=1, source_target_pairs={{0,4},{1,5},{2,6},{3,7},{4,0},{5,1},{6,2},{7,3},{8,12},{9,13},{10,... | collective-permute-start | bytes 110600 | tf_op jit(solution)/shard_map/ppermute | solution.py:67
  121.7 4.9 %collective-permute-done.10 = f32[288,66]{1,0:T(8,128)S(1)} collective-permute-done((f32[288,66]{1,0:T(8,128)S(1)}, f32[288,66]{1,0:T(8,128)S(1)}, u32[]{:S(2)}, u32[]{:S(2)}) %collective-permute-start.10) | collective-permute-done | bytes 76064 | tf_op jit(solution)/shard_map/ppermute | solution.py:114
  127.2 3.5 %collective-permute-start.11 = (f32[144,66]{1,0:T(8,128)S(1)}, f32[144,66]{1,0:T(8,128)S(1)}, u32[]{:S(2)}, u32[]{:S(2)}) collective-permute-start(f32[144,66]{1,0:T(8,128)S(1)} %get-tuple-element.34), channel_id=1, source_target_pairs={{0,4},{1,5},{2,6},{3,7},{4,0},{5,1},{6,2},{7,3},{8,12},{9,13},{10,... | collective-permute-start | bytes 114056 | tf_op jit(solution)/shard_map/ppermute | solution.py:114
  131.8 3.1 %collective-permute-done.11 = f32[144,66]{1,0:T(8,128)S(1)} collective-permute-done((f32[144,66]{1,0:T(8,128)S(1)}, f32[144,66]{1,0:T(8,128)S(1)}, u32[]{:S(2)}, u32[]{:S(2)}) %collective-permute-start.11) | collective-permute-done | bytes 38048 | tf_op jit(solution)/shard_map/ppermute | solution.py:114
  137.9 3.7 %collective-permute-done.12 = f32[144,66]{1,0:T(8,128)S(1)} collective-permute-done((f32[144,66]{1,0:T(8,128)S(1)}, f32[144,66]{1,0:T(8,128)S(1)}, u32[]{:S(2)}, u32[]{:S(2)}) %collective-permute-start.12) | collective-permute-done | bytes 38048 | tf_op jit(solution)/shard_map/ppermute | solution.py:94
  145.5 4.8 %collective-permute-done.13 = f32[144,66]{1,0:T(8,128)S(1)} collective-permute-done((f32[144,66]{1,0:T(8,128)S(1)}, f32[144,66]{1,0:T(8,128)S(1)}, u32[]{:S(2)}, u32[]{:S(2)}) %collective-permute-start.13) | collective-permute-done | bytes 38048 | tf_op jit(solution)/shard_map/ppermute | solution.py:94
  153.3 7.8 %collective-permute-done.14 = f32[144,66]{1,0:T(8,128)S(1)} collective-permute-done((f32[144,66]{1,0:T(8,128)S(1)}, f32[144,66]{1,0:T(8,128)S(1)}, u32[]{:S(2)}, u32[]{:S(2)}) %collective-permute-start.14) | collective-permute-done | bytes 38048 | tf_op jit(solution)/shard_map/ppermute | solution.py:94
  164.5 4.7 %collective-permute-done.24 = bf16[144,64]{1,0:T(8,128)(2,1)S(1)} collective-permute-done((bf16[144,64]{1,0:T(8,128)(2,1)S(1)}, bf16[144,64]{1,0:T(8,128)(2,1)S(1)}, u32[]{:S(2)}, u32[]{:S(2)}) %collective-permute-start.24) | collective-permute-done | bytes 18464 | tf_op jit(solution)/shard_map/ppermute | solution.py:67
  171.2 4.3 %collective-permute-done.25 = bf16[288,64]{1,0:T(8,128)(2,1)S(1)} collective-permute-done((bf16[288,64]{1,0:T(8,128)(2,1)S(1)}, bf16[288,64]{1,0:T(8,128)(2,1)S(1)}, u32[]{:S(2)}, u32[]{:S(2)}) %collective-permute-start.25) | collective-permute-done | bytes 36896 | tf_op jit(solution)/shard_map/ppermute | solution.py:67
  182.0 6.9 %collective-permute-done.27 = f32[32,36]{1,0:T(8,128)S(1)} collective-permute-done((f32[32,36]{1,0:T(8,128)S(1)}, f32[32,36]{1,0:T(8,128)S(1)}, u32[]{:S(2)}, u32[]{:S(2)}) %collective-permute-start.27) | collective-permute-done | bytes 4640 | tf_op jit(solution)/shard_map/ppermute | solution.py:67
  190.9 4.6 %collective-permute-done.28 = f32[32,72]{1,0:T(8,128)S(1)} collective-permute-done((f32[32,72]{1,0:T(8,128)S(1)}, f32[32,72]{1,0:T(8,128)S(1)}, u32[]{:S(2)}, u32[]{:S(2)}) %collective-permute-start.28) | collective-permute-done | bytes 9248 | tf_op jit(solution)/shard_map/ppermute | solution.py:67
  197.6 3.8 %collective-permute-done.29 = f32[32,144]{1,0:T(8,128)S(1)} collective-permute-done((f32[32,144]{1,0:T(8,128)S(1)}, f32[32,144]{1,0:T(8,128)S(1)}, u32[]{:S(2)}, u32[]{:S(2)}) %collective-permute-start.29) | collective-permute-done | bytes 18464 | tf_op jit(solution)/shard_map/ppermute | solution.py:67
  201.5 3.2 %collective-permute-start.30 = (f32[32,288]{1,0:T(8,128)S(1)}, f32[32,288]{1,0:T(8,128)S(1)}, u32[]{:S(2)}, u32[]{:S(2)}) collective-permute-start(f32[32,288]{1,0:T(8,128)S(1)} %maximum_select_fusion.12), channel_id=1, source_target_pairs={{0,4},{1,5},{2,6},{3,7},{4,0},{5,1},{6,2},{7,3},{8,12},{9,13},{10,... | collective-permute-start | bytes 110600 | tf_op jit(solution)/shard_map/ppermute | solution.py:67
  204.7 4.3 %collective-permute-done.30 = f32[32,288]{1,0:T(8,128)S(1)} collective-permute-done((f32[32,288]{1,0:T(8,128)S(1)}, f32[32,288]{1,0:T(8,128)S(1)}, u32[]{:S(2)}, u32[]{:S(2)}) %collective-permute-start.30) | collective-permute-done | bytes 36896 | tf_op jit(solution)/shard_map/ppermute | solution.py:67
  211.0 4.4 %collective-permute-done.31 = f32[32,576]{1,0:T(8,128)S(1)} collective-permute-done((f32[32,576]{1,0:T(8,128)S(1)}, f32[32,576]{1,0:T(8,128)S(1)}, u32[]{:S(2)}, u32[]{:S(2)}) %collective-permute-start.31) | collective-permute-done | bytes 73760 | tf_op jit(solution)/shard_map/ppermute | solution.py:67
  220.4 3.3 %multiply_reduce_fusion = (f32[32]{0:T(128)S(1)}, f32[32,2,2,2,2,2,2,36]{7,6,5,4,3,2,1,0:T(2,128)S(1)}) fusion(f32[32,1,2,2,2,2,2,36]{7,1,2,3,4,5,6,0:T(1,128)S(1)} %copy.161, f32[32,1,2,2,2,2,2,36]{7,1,2,3,4,5,6,0:T(1,128)S(1)} %copy.162, pred[]{:T(512)S(6)} %eq.122), kind=kLoop, calls=%fused_computation.24 | loop fusion | flops 368608 | bytes 589953 | tf_op jit(solution)/shard_map/reduce_sum | solution.py:241
  237.5 4.6 %collective-permute-done.34 = f32[32,576]{1,0:T(8,128)S(1)} collective-permute-done((f32[32,576]{1,0:T(8,128)S(1)}, f32[32,576]{1,0:T(8,128)S(1)}, u32[]{:S(2)}, u32[]{:S(2)}) %collective-permute-start.34) | collective-permute-done | bytes 73760 | tf_op jit(solution)/shard_map/ppermute | solution.py:57
  242.3 3.5 %collective-permute-start.35 = (f32[32,288]{1,0:T(8,128)S(1)}, f32[32,288]{1,0:T(8,128)S(1)}, u32[]{:S(2)}, u32[]{:S(2)}) collective-permute-start(f32[32,288]{1,0:T(8,128)S(1)} %constant_dynamic-slice_fusion.3), channel_id=1, source_target_pairs={{0,4},{1,5},{2,6},{3,7},{4,0},{5,1},{6,2},{7,3},{8,12},{9,13},{10,... | collective-permute-start | bytes 110600 | tf_op jit(solution)/shard_map/ppermute | solution.py:57
  245.8 4.0 %collective-permute-done.35 = f32[32,288]{1,0:T(8,128)S(1)} collective-permute-done((f32[32,288]{1,0:T(8,128)S(1)}, f32[32,288]{1,0:T(8,128)S(1)}, u32[]{:S(2)}, u32[]{:S(2)}) %collective-permute-start.35) | collective-permute-done | bytes 36896 | tf_op jit(solution)/shard_map/ppermute | solution.py:57
  251.9 3.9 %collective-permute-done.36 = f32[32,144]{1,0:T(8,128)S(1)} collective-permute-done((f32[32,144]{1,0:T(8,128)S(1)}, f32[32,144]{1,0:T(8,128)S(1)}, u32[]{:S(2)}, u32[]{:S(2)}) %collective-permute-start.36) | collective-permute-done | bytes 18464 | tf_op jit(solution)/shard_map/ppermute | solution.py:57
  257.9 4.7 %collective-permute-done.37 = f32[32,72]{1,0:T(8,128)S(1)} collective-permute-done((f32[32,72]{1,0:T(8,128)S(1)}, f32[32,72]{1,0:T(8,128)S(1)}, u32[]{:S(2)}, u32[]{:S(2)}) %collective-permute-start.37) | collective-permute-done | bytes 9248 | tf_op jit(solution)/shard_map/ppermute | solution.py:57
  265.3 7.0 %collective-permute-done.38 = f32[32,36]{1,0:T(8,128)S(1)} collective-permute-done((f32[32,36]{1,0:T(8,128)S(1)}, f32[32,36]{1,0:T(8,128)S(1)}, u32[]{:S(2)}, u32[]{:S(2)}) %collective-permute-start.38) | collective-permute-done | bytes 4640 | tf_op jit(solution)/shard_map/ppermute | solution.py:57
  (244 shorter events, 124.1 us)
Async XLA Ops:
  2.2 20.1 %collective-permute-start.15 = (f32[32,2304]{1,0:T(8,128)}, f32[32,2304]{1,0:T(8,128)}, u32[]{:S(2)}, u32[]{:S(2)}) collective-permute-start(f32[32,2304]{1,0:T(8,128)} %constant_dynamic-slice_fusion.8), channel_id=1, source_target_pairs={{0,1},{1,0},{2,3},{3,2},{4,5},{5,4},{6,7},{7,6},{8,9},{9,8},{10,11... | collective-permute-start | bytes 884744 | tf_op jit(solution)/shard_map/ppermute | solution.py:57
  10.4 6.6 %collective-permute-start.1 = (f32[32,592]{1,0:T(8,128)S(1)}, f32[32,592]{1,0:T(8,128)S(1)}, u32[]{:S(2)}, u32[]{:S(2)}) collective-permute-start(f32[32,592]{1,0:T(8,128)S(1)} %constant_dynamic-slice_fusion.11), channel_id=1, source_target_pairs={{0,2},{1,3},{2,0},{3,1},{4,6},{5,7},{6,4},{7,5},{8,10},{9,11},{10,... | collective-permute-start | bytes 227336 | tf_op jit(solution)/shard_map/ppermute | solution.py:57
  17.2 8.6 %collective-permute-start.2 = (f32[32,296]{1,0:T(8,128)S(1)}, f32[32,296]{1,0:T(8,128)S(1)}, u32[]{:S(2)}, u32[]{:S(2)}) collective-permute-start(f32[32,296]{1,0:T(8,128)S(1)} %constant_dynamic-slice_fusion.10), channel_id=1, source_target_pairs={{0,4},{1,5},{2,6},{3,7},{4,0},{5,1},{6,2},{7,3},{8,12},{9,13},{10,... | collective-permute-start | bytes 113672 | tf_op jit(solution)/shard_map/ppermute | solution.py:57
  23.4 15.1 %collective-permute-start.16 = (f32[32,1152]{1,0:T(8,128)S(1)}, f32[32,1152]{1,0:T(8,128)S(1)}, u32[]{:S(2)}, u32[]{:S(2)}) collective-permute-start(f32[32,1152]{1,0:T(8,128)S(1)} %constant_dynamic-slice_fusion.7), channel_id=1, source_target_pairs={{0,2},{1,3},{2,0},{3,1},{4,6},{5,7},{6,4},{7,5},{8,10},{9,11},{10,... | collective-permute-start | bytes 442376 | tf_op jit(solution)/shard_map/ppermute | solution.py:57
  26.0 6.3 %collective-permute-start.3 = (f32[32,296]{1,0:T(8,128)S(1)}, f32[32,296]{1,0:T(8,128)S(1)}, u32[]{:S(2)}, u32[]{:S(2)}) collective-permute-start(f32[32,296]{1,0:T(8,128)S(1)} %dynamic-slice_add_fusion.8), channel_id=1, source_target_pairs={{0,8},{1,9},{2,10},{3,11},{4,12},{5,13},{6,14},{7,15},{8,0},{9,1},... | collective-permute-start | bytes 113672 | tf_op jit(solution)/shard_map/ppermute | solution.py:87
  32.3 10.8 %collective-permute-start.4 = (f32[32,296]{1,0:T(8,128)S(1)}, f32[32,296]{1,0:T(8,128)S(1)}, u32[]{:S(2)}, u32[]{:S(2)}) collective-permute-start(f32[32,296]{1,0:T(8,128)S(1)} %add.348), channel_id=1, source_target_pairs={{0,16},{1,17},{2,18},{3,19},{4,20},{5,21},{6,22},{7,23},{8,24},{9,... | collective-permute-start | bytes 113672 | tf_op jit(solution)/shard_map/ppermute | solution.py:87
  38.5 13.5 %collective-permute-start.17 = (f32[32,576]{1,0:T(8,128)S(1)}, f32[32,576]{1,0:T(8,128)S(1)}, u32[]{:S(2)}, u32[]{:S(2)}) collective-permute-start(f32[32,576]{1,0:T(8,128)S(1)} %constant_dynamic-slice_fusion.6), channel_id=1, source_target_pairs={{0,4},{1,5},{2,6},{3,7},{4,0},{5,1},{6,2},{7,3},{8,12},{9,13},{10,... | collective-permute-start | bytes 221192 | tf_op jit(solution)/shard_map/ppermute | solution.py:57
  43.2 18.4 %collective-permute-start.5 = (f32[32,296]{1,0:T(8,128)S(1)}, f32[32,296]{1,0:T(8,128)S(1)}, u32[]{:S(2)}, u32[]{:S(2)}) collective-permute-start(f32[32,296]{1,0:T(8,128)S(1)} %add.349), channel_id=1, source_target_pairs={{0,32},{1,33},{2,34},{3,35},{4,36},{5,37},{6,38},{7,39},{8,40},{9,... | collective-permute-start | bytes 113672 | tf_op jit(solution)/shard_map/ppermute | solution.py:87
  52.2 9.5 %collective-permute-start.18 = (f32[32,576]{1,0:T(8,128)S(1)}, f32[32,576]{1,0:T(8,128)S(1)}, u32[]{:S(2)}, u32[]{:S(2)}) collective-permute-start(f32[32,576]{1,0:T(8,128)S(1)} %dynamic-slice_add_fusion.5), channel_id=1, source_target_pairs={{0,8},{1,9},{2,10},{3,11},{4,12},{5,13},{6,14},{7,15},{8,0},{9,1},... | collective-permute-start | bytes 221192 | tf_op jit(solution)/shard_map/ppermute | solution.py:87
  61.7 9.0 %collective-permute-start.19 = (f32[32,576]{1,0:T(8,128)S(1)}, f32[32,576]{1,0:T(8,128)S(1)}, u32[]{:S(2)}, u32[]{:S(2)}) collective-permute-start(f32[32,576]{1,0:T(8,128)S(1)} %add.384), channel_id=1, source_target_pairs={{0,16},{1,17},{2,18},{3,19},{4,20},{5,21},{6,22},{7,23},{8,24},{9,... | collective-permute-start | bytes 221192 | tf_op jit(solution)/shard_map/ppermute | solution.py:87
  70.7 10.2 %collective-permute-start.20 = (f32[32,576]{1,0:T(8,128)S(1)}, f32[32,576]{1,0:T(8,128)S(1)}, u32[]{:S(2)}, u32[]{:S(2)}) collective-permute-start(f32[32,576]{1,0:T(8,128)S(1)} %add.385), channel_id=1, source_target_pairs={{0,32},{1,33},{2,34},{3,35},{4,36},{5,37},{6,38},{7,39},{8,40},{9,... | collective-permute-start | bytes 221192 | tf_op jit(solution)/shard_map/ppermute | solution.py:87
  73.1 11.3 %collective-permute-start.6 = (bf16[32,288]{1,0:T(8,128)(2,1)S(1)}, bf16[32,288]{1,0:T(8,128)(2,1)S(1)}, u32[]{:S(2)}, u32[]{:S(2)}) collective-permute-start(bf16[32,288]{1,0:T(8,128)(2,1)S(1)} %reshape.328), channel_id=1, source_target_pairs={{0,4},{1,5},{2,6},{3,7},{4,0},{5,1},{6,2},{7,3},{8,12},{9,13},{10,... | collective-permute-start | bytes 55304 | tf_op jit(solution)/shard_map/ppermute | solution.py:67
  81.0 7.4 %collective-permute-start.21 = (bf16[32,576]{1,0:T(8,128)(2,1)S(1)}, bf16[32,576]{1,0:T(8,128)(2,1)S(1)}, u32[]{:S(2)}, u32[]{:S(2)}) collective-permute-start(bf16[32,576]{1,0:T(8,128)(2,1)S(1)} %multiply_convert_fusion.1), channel_id=1, source_target_pairs={{0,4},{1,5},{2,6},{3,7},{4,0},{5,1},{6,2},{7,3},{8,12},{9,13},{10,... | collective-permute-start | bytes 110600 | tf_op jit(solution)/shard_map/ppermute | solution.py:67
  84.6 6.6 %collective-permute-start.7 = (bf16[32,576]{1,0:T(8,128)(2,1)S(1)}, bf16[32,576]{1,0:T(8,128)(2,1)S(1)}, u32[]{:S(2)}, u32[]{:S(2)}) collective-permute-start(bf16[32,576]{1,0:T(8,128)(2,1)S(1)} %maximum_select_fusion.13), channel_id=1, source_target_pairs={{0,2},{1,3},{2,0},{3,1},{4,6},{5,7},{6,4},{7,5},{8,10},{9,11},{10,... | collective-permute-start | bytes 110600 | tf_op jit(solution)/shard_map/ppermute | solution.py:67
  88.5 6.2 %collective-permute-start.22 = (bf16[32,1152]{1,0:T(8,128)(2,1)S(1)}, bf16[32,1152]{1,0:T(8,128)(2,1)S(1)}, u32[]{:S(2)}, u32[]{:S(2)}) collective-permute-start(bf16[32,1152]{1,0:T(8,128)(2,1)S(1)} %maximum_select_fusion.10), channel_id=1, source_target_pairs={{0,2},{1,3},{2,0},{3,1},{4,6},{5,7},{6,4},{7,5},{8,10},{9,11},{10,... | collective-permute-start | bytes 221192 | tf_op jit(solution)/shard_map/ppermute | solution.py:67
  91.2 5.8 %collective-permute-start.8 = (bf16[32,1152]{1,0:T(8,128)(2,1)S(1)}, bf16[32,1152]{1,0:T(8,128)(2,1)S(1)}, u32[]{:S(2)}, u32[]{:S(2)}) collective-permute-start(bf16[32,1152]{1,0:T(8,128)(2,1)S(1)} %maximum_select_fusion.9), channel_id=1, source_target_pairs={{0,1},{1,0},{2,3},{3,2},{4,5},{5,4},{6,7},{7,6},{8,9},{9,8},{10,11... | collective-permute-start | bytes 221192 | tf_op jit(solution)/shard_map/ppermute | solution.py:67
  118.8 7.8 %collective-permute-start.10 = (f32[288,66]{1,0:T(8,128)S(1)}, f32[288,66]{1,0:T(8,128)S(1)}, u32[]{:S(2)}, u32[]{:S(2)}) collective-permute-start(f32[288,66]{1,0:T(8,128)S(1)} %get-tuple-element.33), channel_id=1, source_target_pairs={{0,2},{1,3},{2,0},{3,1},{4,6},{5,7},{6,4},{7,5},{8,10},{9,11},{10,... | collective-permute-start | bytes 228104 | tf_op jit(solution)/shard_map/ppermute | solution.py:114
  127.2 7.8 %collective-permute-start.11 = (f32[144,66]{1,0:T(8,128)S(1)}, f32[144,66]{1,0:T(8,128)S(1)}, u32[]{:S(2)}, u32[]{:S(2)}) collective-permute-start(f32[144,66]{1,0:T(8,128)S(1)} %get-tuple-element.34), channel_id=1, source_target_pairs={{0,4},{1,5},{2,6},{3,7},{4,0},{5,1},{6,2},{7,3},{8,12},{9,13},{10,... | collective-permute-start | bytes 114056 | tf_op jit(solution)/shard_map/ppermute | solution.py:114
  135.4 6.2 %collective-permute-start.12 = (f32[144,66]{1,0:T(8,128)S(1)}, f32[144,66]{1,0:T(8,128)S(1)}, u32[]{:S(2)}, u32[]{:S(2)}) collective-permute-start(f32[144,66]{1,0:T(8,128)S(1)} %pad_maximum_fusion.3), channel_id=1, source_target_pairs={{0,8},{1,9},{2,10},{3,11},{4,12},{5,13},{6,14},{7,15},{8,0},{9,1},... | collective-permute-start | bytes 114056 | tf_op jit(solution)/shard_map/ppermute | solution.py:94
  142.0 8.3 %collective-permute-start.13 = (f32[144,66]{1,0:T(8,128)S(1)}, f32[144,66]{1,0:T(8,128)S(1)}, u32[]{:S(2)}, u32[]{:S(2)}) collective-permute-start(f32[144,66]{1,0:T(8,128)S(1)} %pad_maximum_fusion.4), channel_id=1, source_target_pairs={{0,16},{1,17},{2,18},{3,19},{4,20},{5,21},{6,22},{7,23},{8,24},{9,... | collective-permute-start | bytes 114056 | tf_op jit(solution)/shard_map/ppermute | solution.py:94
  150.8 10.3 %collective-permute-start.14 = (f32[144,66]{1,0:T(8,128)S(1)}, f32[144,66]{1,0:T(8,128)S(1)}, u32[]{:S(2)}, u32[]{:S(2)}) collective-permute-start(f32[144,66]{1,0:T(8,128)S(1)} %pad_maximum_fusion.5), channel_id=1, source_target_pairs={{0,32},{1,33},{2,34},{3,35},{4,36},{5,37},{6,38},{7,39},{8,40},{9,... | collective-permute-start | bytes 114056 | tf_op jit(solution)/shard_map/ppermute | solution.py:94
  161.9 7.4 %collective-permute-start.24 = (bf16[144,64]{1,0:T(8,128)(2,1)S(1)}, bf16[144,64]{1,0:T(8,128)(2,1)S(1)}, u32[]{:S(2)}, u32[]{:S(2)}) collective-permute-start(bf16[144,64]{1,0:T(8,128)(2,1)S(1)} %fusion.53), channel_id=1, source_target_pairs={{0,4},{1,5},{2,6},{3,7},{4,0},{5,1},{6,2},{7,3},{8,12},{9,13},{10,... | collective-permute-start | bytes 55304 | tf_op jit(solution)/shard_map/ppermute | solution.py:67
  169.3 6.2 %collective-permute-start.25 = (bf16[288,64]{1,0:T(8,128)(2,1)S(1)}, bf16[288,64]{1,0:T(8,128)(2,1)S(1)}, u32[]{:S(2)}, u32[]{:S(2)}) collective-permute-start(bf16[288,64]{1,0:T(8,128)(2,1)S(1)} %maximum_select_fusion.11), channel_id=1, source_target_pairs={{0,2},{1,3},{2,0},{3,1},{4,6},{5,7},{6,4},{7,5},{8,10},{9,11},{10,... | collective-permute-start | bytes 110600 | tf_op jit(solution)/shard_map/ppermute | solution.py:67
  179.4 9.5 %collective-permute-start.27 = (f32[32,36]{1,0:T(8,128)S(1)}, f32[32,36]{1,0:T(8,128)S(1)}, u32[]{:S(2)}, u32[]{:S(2)}) collective-permute-start(f32[32,36]{1,0:T(8,128)S(1)} %convolution_add_fusion), channel_id=1, source_target_pairs={{0,32},{1,33},{2,34},{3,35},{4,36},{5,37},{6,38},{7,39},{8,40},{9,... | collective-permute-start | bytes 13832 | tf_op jit(solution)/shard_map/ppermute | solution.py:67
  189.0 6.5 %collective-permute-start.28 = (f32[32,72]{1,0:T(8,128)S(1)}, f32[32,72]{1,0:T(8,128)S(1)}, u32[]{:S(2)}, u32[]{:S(2)}) collective-permute-start(f32[32,72]{1,0:T(8,128)S(1)} %maximum_select_fusion.15), channel_id=1, source_target_pairs={{0,16},{1,17},{2,18},{3,19},{4,20},{5,21},{6,22},{7,23},{8,24},{9,... | collective-permute-start | bytes 27656 | tf_op jit(solution)/shard_map/ppermute | solution.py:67
  195.6 5.8 %collective-permute-start.29 = (f32[32,144]{1,0:T(8,128)S(1)}, f32[32,144]{1,0:T(8,128)S(1)}, u32[]{:S(2)}, u32[]{:S(2)}) collective-permute-start(f32[32,144]{1,0:T(8,128)S(1)} %maximum_select_fusion.14), channel_id=1, source_target_pairs={{0,8},{1,9},{2,10},{3,11},{4,12},{5,13},{6,14},{7,15},{8,0},{9,1},... | collective-permute-start | bytes 55304 | tf_op jit(solution)/shard_map/ppermute | solution.py:67
  201.5 7.5 %collective-permute-start.30 = (f32[32,288]{1,0:T(8,128)S(1)}, f32[32,288]{1,0:T(8,128)S(1)}, u32[]{:S(2)}, u32[]{:S(2)}) collective-permute-start(f32[32,288]{1,0:T(8,128)S(1)} %maximum_select_fusion.12), channel_id=1, source_target_pairs={{0,4},{1,5},{2,6},{3,7},{4,0},{5,1},{6,2},{7,3},{8,12},{9,13},{10,... | collective-permute-start | bytes 110600 | tf_op jit(solution)/shard_map/ppermute | solution.py:67
  209.1 6.3 %collective-permute-start.31 = (f32[32,576]{1,0:T(8,128)S(1)}, f32[32,576]{1,0:T(8,128)S(1)}, u32[]{:S(2)}, u32[]{:S(2)}) collective-permute-start(f32[32,576]{1,0:T(8,128)S(1)} %maximum_select_fusion.8), channel_id=1, source_target_pairs={{0,2},{1,3},{2,0},{3,1},{4,6},{5,7},{6,4},{7,5},{8,10},{9,11},{10,... | collective-permute-start | bytes 221192 | tf_op jit(solution)/shard_map/ppermute | solution.py:67
  235.5 6.6 %collective-permute-start.34 = (f32[32,576]{1,0:T(8,128)S(1)}, f32[32,576]{1,0:T(8,128)S(1)}, u32[]{:S(2)}, u32[]{:S(2)}) collective-permute-start(f32[32,576]{1,0:T(8,128)S(1)} %constant_dynamic-slice_fusion.4), channel_id=1, source_target_pairs={{0,2},{1,3},{2,0},{3,1},{4,6},{5,7},{6,4},{7,5},{8,10},{9,11},{10,... | collective-permute-start | bytes 221192 | tf_op jit(solution)/shard_map/ppermute | solution.py:57
  242.3 7.5 %collective-permute-start.35 = (f32[32,288]{1,0:T(8,128)S(1)}, f32[32,288]{1,0:T(8,128)S(1)}, u32[]{:S(2)}, u32[]{:S(2)}) collective-permute-start(f32[32,288]{1,0:T(8,128)S(1)} %constant_dynamic-slice_fusion.3), channel_id=1, source_target_pairs={{0,4},{1,5},{2,6},{3,7},{4,0},{5,1},{6,2},{7,3},{8,12},{9,13},{10,... | collective-permute-start | bytes 110600 | tf_op jit(solution)/shard_map/ppermute | solution.py:57
  255.9 6.6 %collective-permute-start.37 = (f32[32,72]{1,0:T(8,128)S(1)}, f32[32,72]{1,0:T(8,128)S(1)}, u32[]{:S(2)}, u32[]{:S(2)}) collective-permute-start(f32[32,72]{1,0:T(8,128)S(1)} %constant_dynamic-slice_fusion.1), channel_id=1, source_target_pairs={{0,16},{1,17},{2,18},{3,19},{4,20},{5,21},{6,22},{7,23},{8,24},{9,... | collective-permute-start | bytes 27656 | tf_op jit(solution)/shard_map/ppermute | solution.py:57
  262.7 9.5 %collective-permute-start.38 = (f32[32,36]{1,0:T(8,128)S(1)}, f32[32,36]{1,0:T(8,128)S(1)}, u32[]{:S(2)}, u32[]{:S(2)}) collective-permute-start(f32[32,36]{1,0:T(8,128)S(1)} %constant_dynamic-slice_fusion), channel_id=1, source_target_pairs={{0,32},{1,33},{2,34},{3,35},{4,36},{5,37},{6,38},{7,39},{8,40},{9,... | collective-permute-start | bytes 13832 | tf_op jit(solution)/shard_map/ppermute | solution.py:57
  (30 other events, 589.3 us)

commit v6 on v4

--- a/solution.py
+++ b/solution.py
@@ -121,6 +121,21 @@
         [weighted.reshape(row_count, -1), total.reshape(row_count, 1), peak.reshape(row_count, 1)],
         axis=1,
     )
+
+
+def exchange_gather(values):
+    count = lax.axis_size("tp")
+    copies = jnp.broadcast_to(values[None], (count,) + values.shape)
+    received = lax.all_to_all(copies, "tp", 0, 0, tiled=True)
+    return jnp.transpose(received, (1, 0, 2)).reshape(values.shape[0], -1)
+
+
+def exchange_scatter_sum(values):
+    count = lax.axis_size("tp")
+    rows = values.shape[0]
+    blocks = jnp.transpose(values.reshape(rows, count, -1), (1, 0, 2))
+    received = lax.all_to_all(blocks, "tp", 0, 0, tiled=True)
+    return jnp.sum(received, axis=0)
 
 
 def reverse_blocks(values, count):
@@ -234,7 +249,7 @@
     attended_rows = (final_rows[:, :HDIM] / final_rows[:, HDIM : HDIM + 1]).astype(jnp.bfloat16)
     attended = gather_cols(attended_rows, axis=0, bits=near_bits).reshape(all_tokens, model_width)
     residual_cols = hidden + jnp.dot(attended, w_out, preferred_element_type=jnp.float32)
-    full_rows = reverse_blocks(gather_cols(residual_cols), tp_count)
+    full_rows = exchange_gather(residual_cols)
     inv_norm = lax.rsqrt(jnp.mean(full_rows * full_rows, axis=1) + EPSILON)
     normed = (full_rows * inv_norm[:, None] * moe_gain[None, :]).astype(jnp.bfloat16)
     logits = jnp.dot(normed, router, preferred_element_type=jnp.float32)
@@ -253,7 +268,7 @@
     up_out = jnp.dot(normed, w_up, preferred_element_type=jnp.float32)
     inner_act = (jax.nn.silu(gate_out) * up_out * mix_coef[:, None]).astype(jnp.bfloat16)
     expert_term = jnp.dot(inner_act, w_down, preferred_element_type=jnp.float32)
-    return residual_cols + scatter_sum(reverse_blocks(expert_term, tp_count))
+    return residual_cols + exchange_scatter_sum(expert_term)
 
 
 def solution(mesh):

time: 253 us -> 220 us (0.87); the launches traced: 248 us -> 219 us
  starting transfers between devices: 125 us -> 85.9 us
  blocking collectives: 0 us -> 18.4 us
  waiting for transfers between devices: 70.9 us -> 62.2 us
    ppermute x12 -> x6, starting transfers between devices: 59 us -> 31.5 us  [gather_cols(): other = lax.ppermute(values, 'tp', partner_pairs(count, bit))]
    ppermute x9 -> x3, starting transfers between devices: 34.3 us -> 12.6 us  [scatter_sum(): values = keep + lax.ppermute(send, 'tp', partner_pairs(count, bit))]
    all_to_all x0 -> x1, blocking collectives: none -> 18.4 us  [exchange_scatter_sum(): received = lax.all_to_all(blocks, 'tp', 0, 0, tiled=True)]
    all_to_all x0 -> x1, waiting for transfers between devices: none -> 13.7 us  [exchange_gather(): received = lax.all_to_all(copies, 'tp', 0, 0, tiled=True)]
    ppermute x9 -> x3, waiting for transfers between devices: 25.1 us -> 13 us  [scatter_sum(): values = keep + lax.ppermute(send, 'tp', partner_pairs(count, bit))]
    all_to_all x0 -> x1, starting transfers between devices: none -> 10.5 us  [exchange_gather(): received = lax.all_to_all(copies, 'tp', 0, 0, tiled=True)]
    ppermute x12 -> x6, waiting for transfers between devices: 20.3 us -> 9.86 us  [gather_cols(): other = lax.ppermute(values, 'tp', partner_pairs(count, bit))]
    unnamed x38 -> x42, local copies, waits for them, and re-layouts: 0.87 us -> 6.78 us
  transfers between devices with their start and end apart: 30 -> 19, of which waited for: 28 -> 18; matrix products, arithmetic and copies ran while one was open for 4% -> 4% of each run, Pallas kernels for 0% -> 0%
where the time goes in v6:
time: 220 us; the launch traced here: 219 us
  starting transfers between devices  85.9 us (39%)
  waiting for transfers between devices  62.2 us (28%)
  local copies, waits for them, and re-layouts  23.9 us (11%)
  blocking collectives  18.4 us (8%)
  other arithmetic  15.6 us (7%)
  matrix products  11.9 us (5%)
    ppermute x6, starting transfers between devices, gather_cols(): other = lax.ppermute(values, 'tp', partner_pairs(count, bit))  31.5 us
    all_to_all x1, blocking collectives, exchange_scatter_sum(): received = lax.all_to_all(blocks, 'tp', 0, 0, tiled=True)  18.4 us
    all_to_all x1, waiting for transfers between devices, exchange_gather(): received = lax.all_to_all(copies, 'tp', 0, 0, tiled=True)  13.7 us
    ppermute x3, waiting for transfers between devices, scatter_sum(): values = keep + lax.ppermute(send, 'tp', partner_pairs(count, bit))  13 us
    ppermute x3, waiting for transfers between devices, exchange_sum(): values = values + lax.ppermute(values, 'tp', partner_pairs(count, bit))  12.8 us
    ppermute x3, starting transfers between devices, scatter_sum(): values = keep + lax.ppermute(send, 'tp', partner_pairs(count, bit))  12.6 us
    ppermute x3, starting transfers between devices, exchange_merge(): rows = merge_rows(rows, lax.ppermute(rows, 'tp', partner_pairs(count, bit)))  12.2 us
    all_to_all x1, starting transfers between devices, exchange_gather(): received = lax.all_to_all(copies, 'tp', 0, 0, tiled=True)  10.5 us
  transfers between devices with their start and end apart: 19, of which 18 were waited for; matrix products, arithmetic and copies ran while one was open for 4% of the time, Pallas kernels for 0%

profile of v6, /device:TPU:1, one launch (start us, length us, event | category | flops | bytes accessed | tf_op | source)
XLA Modules:
  0.0 218.9 jit_solution(4263407045298364269)
XLA Ops:
  2.3 2.0 reshape.285
  5.5 8.8 %collective-permute-start = (f32[32,3488]{1,0:T(8,128)S(1)}, f32[32,3488]{1,0:T(8,128)S(1)}, u32[]{:S(2)}, u32[]{:S(2)}) collective-permute-start(f32[32,3488]{1,0:T(8,128)S(1)} %constant_dynamic-slice_fusion.3), channel_id=1, source_target_pairs={{0,1},{1,0},{2,3},{3,2},{4,5},{5,4},{6,7},{7,6},{8,9},{9,8},{10,11... | collective-permute-start | bytes 1339400 | tf_op jit(solution)/shard_map/ppermute | solution.py:57
  18.1 6.7 %collective-permute-done.1 = f32[32,1744]{1,0:T(8,128)S(1)} collective-permute-done((f32[32,1744]{1,0:T(8,128)S(1)}, f32[32,1744]{1,0:T(8,128)S(1)}, u32[]{:S(2)}, u32[]{:S(2)}) %collective-permute-start.1) | collective-permute-done | bytes 223264 | tf_op jit(solution)/shard_map/ppermute | solution.py:57
  25.0 1.9 collective-permute-start.2
  27.1 4.9 %collective-permute-done.2 = f32[32,872]{1,0:T(8,128)S(1)} collective-permute-done((f32[32,872]{1,0:T(8,128)S(1)}, f32[32,872]{1,0:T(8,128)S(1)}, u32[]{:S(2)}, u32[]{:S(2)}) %collective-permute-start.2) | collective-permute-done | bytes 111648 | tf_op jit(solution)/shard_map/ppermute | solution.py:57
  34.1 3.6 %collective-permute-done.3 = f32[32,872]{1,0:T(8,128)S(1)} collective-permute-done((f32[32,872]{1,0:T(8,128)S(1)}, f32[32,872]{1,0:T(8,128)S(1)}, u32[]{:S(2)}, u32[]{:S(2)}) %collective-permute-start.3) | collective-permute-done | bytes 111648 | tf_op jit(solution)/shard_map/ppermute | solution.py:87
  37.7 1.9 collective-permute-start.4
  39.7 5.4 %collective-permute-done.4 = f32[32,872]{1,0:T(8,128)S(1)} collective-permute-done((f32[32,872]{1,0:T(8,128)S(1)}, f32[32,872]{1,0:T(8,128)S(1)}, u32[]{:S(2)}, u32[]{:S(2)}) %collective-permute-start.4) | collective-permute-done | bytes 111648 | tf_op jit(solution)/shard_map/ppermute | solution.py:87
  45.1 5.5 %collective-permute-start.5 = (f32[32,872]{1,0:T(8,128)S(1)}, f32[32,872]{1,0:T(8,128)S(1)}, u32[]{:S(2)}, u32[]{:S(2)}) collective-permute-start(f32[32,872]{1,0:T(8,128)S(1)} %add.227), channel_id=1, source_target_pairs={{0,32},{1,33},{2,34},{3,35},{4,36},{5,37},{6,38},{7,39},{8,40},{9,... | collective-permute-start | bytes 334856 | tf_op jit(solution)/shard_map/ppermute | solution.py:87
  50.8 3.7 %collective-permute-done.5 = f32[32,872]{1,0:T(8,128)S(1)} collective-permute-done((f32[32,872]{1,0:T(8,128)S(1)}, f32[32,872]{1,0:T(8,128)S(1)}, u32[]{:S(2)}, u32[]{:S(2)}) %collective-permute-start.5) | collective-permute-done | bytes 111648 | tf_op jit(solution)/shard_map/ppermute | solution.py:87
  55.4 3.0 %collective-permute-start.6 = (bf16[32,864]{1,0:T(8,128)(2,1)S(1)}, bf16[32,864]{1,0:T(8,128)(2,1)S(1)}, u32[]{:S(2)}, u32[]{:S(2)}) collective-permute-start(bf16[32,864]{1,0:T(8,128)(2,1)S(1)} %reshape.288), channel_id=1, source_target_pairs={{0,4},{1,5},{2,6},{3,7},{4,0},{5,1},{6,2},{7,3},{8,12},{9,13},{10,... | collective-permute-start | bytes 165896 | tf_op jit(solution)/shard_map/ppermute | solution.py:67
  58.5 3.4 %collective-permute-done.6 = bf16[32,864]{1,0:T(8,128)(2,1)S(1)} collective-permute-done((bf16[32,864]{1,0:T(8,128)(2,1)S(1)}, bf16[32,864]{1,0:T(8,128)(2,1)S(1)}, u32[]{:S(2)}, u32[]{:S(2)}) %collective-permute-start.6) | collective-permute-done | bytes 55328 | tf_op jit(solution)/shard_map/ppermute | solution.py:67
  62.0 2.3 %collective-permute-start.7 = (bf16[32,1728]{1,0:T(8,128)(2,1)S(1)}, bf16[32,1728]{1,0:T(8,128)(2,1)S(1)}, u32[]{:S(2)}, u32[]{:S(2)}) collective-permute-start(bf16[32,1728]{1,0:T(8,128)(2,1)S(1)} %maximum_select_fusion.4), channel_id=1, source_target_pairs={{0,2},{1,3},{2,0},{3,1},{4,6},{5,7},{6,4},{7,5},{8,10},{9,11},{10,... | collective-permute-start | bytes 331784 | tf_op jit(solution)/shard_map/ppermute | solution.py:67
  70.5 9.2 %collective-permute-start.8 = (bf16[32,3456]{1,0:T(8,128)(2,1)S(1)}, bf16[32,3456]{1,0:T(8,128)(2,1)S(1)}, u32[]{:S(2)}, u32[]{:S(2)}) collective-permute-start(bf16[32,3456]{1,0:T(8,128)(2,1)S(1)} %maximum_select_fusion.2), channel_id=1, source_target_pairs={{0,1},{1,0},{2,3},{3,2},{4,5},{5,4},{6,7},{7,6},{8,9},{9,8},{10,11... | collective-permute-start | bytes 663560 | tf_op jit(solution)/shard_map/ppermute | solution.py:67
  85.0 2.5 %fusion.80 = (f32[8,4,36]{1,2,0:T(8,128)S(1)}, f32[8,4,36,8]{3,1,2,0:T(4,128)}) fusion(bf16[8,8,36,64]{3,2,1,0:T(8,128)(2,1)} %reshape.292, bf16[8,4,36,64]{3,0,1,2:T(8,128)(2,1)S(1)} %pad_maximum_fusion.2, pred[8,8]{1,0:T(8,128)(4,1)S(1)} %broadcast_compare_fusion), kind=kOutput, calls=%fused_computation.178 | convolution fusion | flops 1206144 | bytes 483904 | tf_op jit(solution)/shard_map/rjhd,rphd->rjhp/dot_general | solution.py:216
  95.1 2.4 %collective-permute-start.9 = (f32[576,66]{1,0:T(8,128)S(1)}, f32[576,66]{1,0:T(8,128)S(1)}, u32[]{:S(2)}, u32[]{:S(2)}) collective-permute-start(f32[576,66]{1,0:T(8,128)S(1)} %constant_dynamic-slice_fusion), channel_id=1, source_target_pairs={{0,1},{1,0},{2,3},{3,2},{4,5},{5,4},{6,7},{7,6},{8,9},{9,8},{10,11... | collective-permute-start | bytes 456200 | tf_op jit(solution)/shard_map/ppermute | solution.py:114
  99.5 3.3 %collective-permute-start.10 = (f32[288,66]{1,0:T(8,128)S(1)}, f32[288,66]{1,0:T(8,128)S(1)}, u32[]{:S(2)}, u32[]{:S(2)}) collective-permute-start(f32[288,66]{1,0:T(8,128)S(1)} %get-tuple-element.31), channel_id=1, source_target_pairs={{0,2},{1,3},{2,0},{3,1},{4,6},{5,7},{6,4},{7,5},{8,10},{9,11},{10,... | collective-permute-start | bytes 228104 | tf_op jit(solution)/shard_map/ppermute | solution.py:114
  103.1 3.3 %collective-permute-done.10 = f32[288,66]{1,0:T(8,128)S(1)} collective-permute-done((f32[288,66]{1,0:T(8,128)S(1)}, f32[288,66]{1,0:T(8,128)S(1)}, u32[]{:S(2)}, u32[]{:S(2)}) %collective-permute-start.10) | collective-permute-done | bytes 76064 | tf_op jit(solution)/shard_map/ppermute | solution.py:114
  107.0 4.0 %collective-permute-start.11 = (f32[144,66]{1,0:T(8,128)S(1)}, f32[144,66]{1,0:T(8,128)S(1)}, u32[]{:S(2)}, u32[]{:S(2)}) collective-permute-start(f32[144,66]{1,0:T(8,128)S(1)} %get-tuple-element.35), channel_id=1, source_target_pairs={{0,4},{1,5},{2,6},{3,7},{4,0},{5,1},{6,2},{7,3},{8,12},{9,13},{10,... | collective-permute-start | bytes 114056 | tf_op jit(solution)/shard_map/ppermute | solution.py:114
  116.5 2.6 %collective-permute-done.12 = f32[144,66]{1,0:T(8,128)S(1)} collective-permute-done((f32[144,66]{1,0:T(8,128)S(1)}, f32[144,66]{1,0:T(8,128)S(1)}, u32[]{:S(2)}, u32[]{:S(2)}) %collective-permute-start.12) | collective-permute-done | bytes 38048 | tf_op jit(solution)/shard_map/ppermute | solution.py:94
  119.6 3.7 %collective-permute-start.13 = (f32[144,66]{1,0:T(8,128)S(1)}, f32[144,66]{1,0:T(8,128)S(1)}, u32[]{:S(2)}, u32[]{:S(2)}) collective-permute-start(f32[144,66]{1,0:T(8,128)S(1)} %pad_maximum_fusion.4), channel_id=1, source_target_pairs={{0,16},{1,17},{2,18},{3,19},{4,20},{5,21},{6,22},{7,23},{8,24},{9,... | collective-permute-start | bytes 114056 | tf_op jit(solution)/shard_map/ppermute | solution.py:94
  126.9 6.6 %collective-permute-start.14 = (f32[144,66]{1,0:T(8,128)S(1)}, f32[144,66]{1,0:T(8,128)S(1)}, u32[]{:S(2)}, u32[]{:S(2)}) collective-permute-start(f32[144,66]{1,0:T(8,128)S(1)} %pad_maximum_fusion.5), channel_id=1, source_target_pairs={{0,32},{1,33},{2,34},{3,35},{4,36},{5,37},{6,38},{7,39},{8,40},{9,... | collective-permute-start | bytes 114056 | tf_op jit(solution)/shard_map/ppermute | solution.py:94
  133.5 2.5 %collective-permute-done.14 = f32[144,66]{1,0:T(8,128)S(1)} collective-permute-done((f32[144,66]{1,0:T(8,128)S(1)}, f32[144,66]{1,0:T(8,128)S(1)}, u32[]{:S(2)}, u32[]{:S(2)}) %collective-permute-start.14) | collective-permute-done | bytes 38048 | tf_op jit(solution)/shard_map/ppermute | solution.py:94
  136.8 3.9 %collective-permute-start.15 = (bf16[144,64]{1,0:T(8,128)(2,1)S(1)}, bf16[144,64]{1,0:T(8,128)(2,1)S(1)}, u32[]{:S(2)}, u32[]{:S(2)}) collective-permute-start(bf16[144,64]{1,0:T(8,128)(2,1)S(1)} %fusion.51), channel_id=1, source_target_pairs={{0,4},{1,5},{2,6},{3,7},{4,0},{5,1},{6,2},{7,3},{8,12},{9,13},{10,... | collective-permute-start | bytes 55304 | tf_op jit(solution)/shard_map/ppermute | solution.py:67
  140.7 2.3 %collective-permute-done.15 = bf16[144,64]{1,0:T(8,128)(2,1)S(1)} collective-permute-done((bf16[144,64]{1,0:T(8,128)(2,1)S(1)}, bf16[144,64]{1,0:T(8,128)(2,1)S(1)}, u32[]{:S(2)}, u32[]{:S(2)}) %collective-permute-start.15) | collective-permute-done | bytes 18464 | tf_op jit(solution)/shard_map/ppermute | solution.py:67
  143.0 3.2 %collective-permute-start.16 = (bf16[288,64]{1,0:T(8,128)(2,1)S(1)}, bf16[288,64]{1,0:T(8,128)(2,1)S(1)}, u32[]{:S(2)}, u32[]{:S(2)}) collective-permute-start(bf16[288,64]{1,0:T(8,128)(2,1)S(1)} %maximum_select_fusion.5), channel_id=1, source_target_pairs={{0,2},{1,3},{2,0},{3,1},{4,6},{5,7},{6,4},{7,5},{8,10},{9,11},{10,... | collective-permute-start | bytes 110600 | tf_op jit(solution)/shard_map/ppermute | solution.py:67
  146.2 2.3 %collective-permute-done.16 = bf16[288,64]{1,0:T(8,128)(2,1)S(1)} collective-permute-done((bf16[288,64]{1,0:T(8,128)(2,1)S(1)}, bf16[288,64]{1,0:T(8,128)(2,1)S(1)}, u32[]{:S(2)}, u32[]{:S(2)}) %collective-permute-start.16) | collective-permute-done | bytes 36896 | tf_op jit(solution)/shard_map/ppermute | solution.py:67
  148.6 9.9 %collective-permute-start.17 = (bf16[576,64]{1,0:T(8,128)(2,1)S(1)}, bf16[576,64]{1,0:T(8,128)(2,1)S(1)}, u32[]{:S(2)}, u32[]{:S(2)}) collective-permute-start(bf16[576,64]{1,0:T(8,128)(2,1)S(1)} %maximum_select_fusion.3), channel_id=1, source_target_pairs={{0,1},{1,0},{2,3},{3,2},{4,5},{5,4},{6,7},{7,6},{8,9},{9,8},{10,11... | collective-permute-start | bytes 221192 | tf_op jit(solution)/shard_map/ppermute | solution.py:67
  160.2 2.0 reshape.328
  162.1 10.5 %all-to-all-start = ((f32[64,1,1152]{2,1,0:T(1,128)}), f32[64,1,1152]{2,1,0:T(1,128)S(1)}, u32[]{:S(2)}, u32[]{:S(2)}) async-start(f32[64,1,1152]{2,1,0:T(1,128)} %reshape.328), calls=%async_computation | async-start | bytes 589824 | tf_op jit(solution)/shard_map/all_to_all | solution.py:129
  172.7 13.7 %all-to-all-done = f32[64,1,1152]{2,1,0:T(1,128)S(1)} async-done(((f32[64,1,1152]{2,1,0:T(1,128)}), f32[64,1,1152]{2,1,0:T(1,128)S(1)}, u32[]{:S(2)}, u32[]{:S(2)}) %all-to-all-start) | async-done | bytes 294944 | tf_op jit(solution)/shard_map/all_to_all | solution.py:129
  197.1 18.4 %all_to_all.10 = f32[64,1,1152]{2,1,0:T(1,128)S(1)} all-to-all(f32[64,1,1152]{2,1,0:T(1,128)S(1)} %reshape.330), channel_id=1, replica_groups=mesh['rep'=8,'tp'=64] {'tp'}, dimensions={0} | all-to-all | bytes 589824 | tf_op jit(solution)/shard_map/all_to_all | solution.py:137
  (169 shorter events, 58.3 us)
Async XLA Ops:
  0.0 193.0 %copy-start = (bf16[180,2304]{1,0:T(8,128)(2,1)S(1)}, bf16[180,2304]{1,0:T(8,128)(2,1)}, u32[]{:S(2)}) copy-start(bf16[180,2304]{1,0:T(8,128)(2,1)} %param.30) | copy-start | bytes 2488324
  5.3 21.6 %copy-start.16 = (s32[8]{0:T(128)S(1)}, s32[8]{0:T(128)}, u32[]{:S(2)}) copy-start(s32[8]{0:T(128)} %param.25) | copy-start | bytes 100
  5.5 10.2 %collective-permute-start = (f32[32,3488]{1,0:T(8,128)S(1)}, f32[32,3488]{1,0:T(8,128)S(1)}, u32[]{:S(2)}, u32[]{:S(2)}) collective-permute-start(f32[32,3488]{1,0:T(8,128)S(1)} %constant_dynamic-slice_fusion.3), channel_id=1, source_target_pairs={{0,1},{1,0},{2,3},{3,2},{4,5},{5,4},{6,7},{7,6},{8,9},{9,8},{10,11... | collective-permute-start | bytes 1339400 | tf_op jit(solution)/shard_map/ppermute | solution.py:57
  15.9 48.4 %copy-start.8 = (bf16[3,32,2304]{2,1,0:T(8,128)(2,1)S(1)}, bf16[3,32,2304]{2,1,0:T(8,128)(2,1)}, u32[]{:S(2)}) copy-start(bf16[3,32,2304]{2,1,0:T(8,128)(2,1)} %param.20) | copy-start | bytes 1327108
  16.1 8.7 %collective-permute-start.1 = (f32[32,1744]{1,0:T(8,128)S(1)}, f32[32,1744]{1,0:T(8,128)S(1)}, u32[]{:S(2)}, u32[]{:S(2)}) collective-permute-start(f32[32,1744]{1,0:T(8,128)S(1)} %constant_dynamic-slice_fusion.2), channel_id=1, source_target_pairs={{0,2},{1,3},{2,0},{3,1},{4,6},{5,7},{6,4},{7,5},{8,10},{9,11},{10,... | collective-permute-start | bytes 669704 | tf_op jit(solution)/shard_map/ppermute | solution.py:57
  25.0 7.0 %collective-permute-start.2 = (f32[32,872]{1,0:T(8,128)S(1)}, f32[32,872]{1,0:T(8,128)S(1)}, u32[]{:S(2)}, u32[]{:S(2)}) collective-permute-start(f32[32,872]{1,0:T(8,128)S(1)} %constant_dynamic-slice_fusion.1), channel_id=1, source_target_pairs={{0,4},{1,5},{2,6},{3,7},{4,0},{5,1},{6,2},{7,3},{8,12},{9,13},{10,... | collective-permute-start | bytes 334856 | tf_op jit(solution)/shard_map/ppermute | solution.py:57
  27.1 38.9 %copy-start.10 = (bf16[8,8,2304]{2,1,0:T(8,128)(2,1)S(1)}, bf16[8,8,2304]{2,1,0:T(8,128)(2,1)}, u32[]{:S(2)}) copy-start(bf16[8,8,2304]{2,1,0:T(8,128)(2,1)} %param.22) | copy-start | bytes 884740
  32.2 5.5 %collective-permute-start.3 = (f32[32,872]{1,0:T(8,128)S(1)}, f32[32,872]{1,0:T(8,128)S(1)}, u32[]{:S(2)}, u32[]{:S(2)}) collective-permute-start(f32[32,872]{1,0:T(8,128)S(1)} %dynamic-slice_add_fusion.2), channel_id=1, source_target_pairs={{0,8},{1,9},{2,10},{3,11},{4,12},{5,13},{6,14},{7,15},{8,0},{9,1},... | collective-permute-start | bytes 334856 | tf_op jit(solution)/shard_map/ppermute | solution.py:87
  37.7 7.4 %collective-permute-start.4 = (f32[32,872]{1,0:T(8,128)S(1)}, f32[32,872]{1,0:T(8,128)S(1)}, u32[]{:S(2)}, u32[]{:S(2)}) collective-permute-start(f32[32,872]{1,0:T(8,128)S(1)} %add.226), channel_id=1, source_target_pairs={{0,16},{1,17},{2,18},{3,19},{4,20},{5,21},{6,22},{7,23},{8,24},{9,... | collective-permute-start | bytes 334856 | tf_op jit(solution)/shard_map/ppermute | solution.py:87
  45.1 9.4 %collective-permute-start.5 = (f32[32,872]{1,0:T(8,128)S(1)}, f32[32,872]{1,0:T(8,128)S(1)}, u32[]{:S(2)}, u32[]{:S(2)}) collective-permute-start(f32[32,872]{1,0:T(8,128)S(1)} %add.227), channel_id=1, source_target_pairs={{0,32},{1,33},{2,34},{3,35},{4,36},{5,37},{6,38},{7,39},{8,40},{9,... | collective-permute-start | bytes 334856 | tf_op jit(solution)/shard_map/ppermute | solution.py:87
  50.8 16.5 %copy-start.11 = (bf16[8,8,2304]{2,1,0:T(8,128)(2,1)S(1)}, bf16[8,8,2304]{2,1,0:T(8,128)(2,1)}, u32[]{:S(2)}) copy-start(bf16[8,8,2304]{2,1,0:T(8,128)(2,1)} %param.23) | copy-start | bytes 884740
  55.4 6.4 %collective-permute-start.6 = (bf16[32,864]{1,0:T(8,128)(2,1)S(1)}, bf16[32,864]{1,0:T(8,128)(2,1)S(1)}, u32[]{:S(2)}, u32[]{:S(2)}) collective-permute-start(bf16[32,864]{1,0:T(8,128)(2,1)S(1)} %reshape.288), channel_id=1, source_target_pairs={{0,4},{1,5},{2,6},{3,7},{4,0},{5,1},{6,2},{7,3},{8,12},{9,13},{10,... | collective-permute-start | bytes 165896 | tf_op jit(solution)/shard_map/ppermute | solution.py:67
  58.5 10.2 %copy-start.9 = (bf16[3,32,2304]{2,1,0:T(8,128)(2,1)S(1)}, bf16[3,32,2304]{2,1,0:T(8,128)(2,1)}, u32[]{:S(2)}) copy-start(bf16[3,32,2304]{2,1,0:T(8,128)(2,1)} %param.21) | copy-start | bytes 1327108
  62.0 8.3 %collective-permute-start.7 = (bf16[32,1728]{1,0:T(8,128)(2,1)S(1)}, bf16[32,1728]{1,0:T(8,128)(2,1)S(1)}, u32[]{:S(2)}, u32[]{:S(2)}) collective-permute-start(bf16[32,1728]{1,0:T(8,128)(2,1)S(1)} %maximum_select_fusion.4), channel_id=1, source_target_pairs={{0,2},{1,3},{2,0},{3,1},{4,6},{5,7},{6,4},{7,5},{8,10},{9,11},{10,... | collective-permute-start | bytes 331784 | tf_op jit(solution)/shard_map/ppermute | solution.py:67
  66.1 13.6 %copy-start.18 = (s32[8]{0:T(128)S(1)}, s32[8]{0:T(128)}, u32[]{:S(2)}) copy-start(s32[8]{0:T(128)} %param.24) | copy-start | bytes 100
  70.5 10.1 %collective-permute-start.8 = (bf16[32,3456]{1,0:T(8,128)(2,1)S(1)}, bf16[32,3456]{1,0:T(8,128)(2,1)S(1)}, u32[]{:S(2)}, u32[]{:S(2)}) collective-permute-start(bf16[32,3456]{1,0:T(8,128)(2,1)S(1)} %maximum_select_fusion.2), channel_id=1, source_target_pairs={{0,1},{1,0},{2,3},{3,2},{4,5},{5,4},{6,7},{7,6},{8,9},{9,8},{10,11... | collective-permute-start | bytes 663560 | tf_op jit(solution)/shard_map/ppermute | solution.py:67
  95.0 7.8 %copy-start.3 = (bf16[32,36,32]{2,1,0:T(8,128)(2,1)S(1)}, bf16[32,36,32]{2,1,0:T(8,128)(2,1)}, u32[]{:S(2)}) copy-start(bf16[32,36,32]{2,1,0:T(8,128)(2,1)} %get-tuple-element.38) | copy-start | bytes 221188
  95.1 7.9 %copy-start.2 = (bf16[32,36,32]{2,1,0:T(8,128)(2,1)S(1)}, bf16[32,36,32]{2,1,0:T(8,128)(2,1)}, u32[]{:S(2)}) copy-start(bf16[32,36,32]{2,1,0:T(8,128)(2,1)} %get-tuple-element.37) | copy-start | bytes 221188
  95.1 3.6 %collective-permute-start.9 = (f32[576,66]{1,0:T(8,128)S(1)}, f32[576,66]{1,0:T(8,128)S(1)}, u32[]{:S(2)}, u32[]{:S(2)}) collective-permute-start(f32[576,66]{1,0:T(8,128)S(1)} %constant_dynamic-slice_fusion), channel_id=1, source_target_pairs={{0,1},{1,0},{2,3},{3,2},{4,5},{5,4},{6,7},{7,6},{8,9},{9,8},{10,11... | collective-permute-start | bytes 456200 | tf_op jit(solution)/shard_map/ppermute | solution.py:114
  99.3 11.7 %copy-start.5 = (bf16[8,4,36,64]{3,0,1,2:T(8,128)(2,1)S(1)}, bf16[8,4,36,64]{3,0,1,2:T(8,128)(2,1)}, u32[]{:S(2)}) copy-start(bf16[8,4,36,64]{3,0,1,2:T(8,128)(2,1)} %copy-done.4) | copy-start | bytes 442372
  99.5 7.0 %collective-permute-start.10 = (f32[288,66]{1,0:T(8,128)S(1)}, f32[288,66]{1,0:T(8,128)S(1)}, u32[]{:S(2)}, u32[]{:S(2)}) collective-permute-start(f32[288,66]{1,0:T(8,128)S(1)} %get-tuple-element.31), channel_id=1, source_target_pairs={{0,2},{1,3},{2,0},{3,1},{4,6},{5,7},{6,4},{7,5},{8,10},{9,11},{10,... | collective-permute-start | bytes 228104 | tf_op jit(solution)/shard_map/ppermute | solution.py:114
  107.0 6.6 %collective-permute-start.11 = (f32[144,66]{1,0:T(8,128)S(1)}, f32[144,66]{1,0:T(8,128)S(1)}, u32[]{:S(2)}, u32[]{:S(2)}) collective-permute-start(f32[144,66]{1,0:T(8,128)S(1)} %get-tuple-element.35), channel_id=1, source_target_pairs={{0,4},{1,5},{2,6},{3,7},{4,0},{5,1},{6,2},{7,3},{8,12},{9,13},{10,... | collective-permute-start | bytes 114056 | tf_op jit(solution)/shard_map/ppermute | solution.py:114
  114.1 5.1 %collective-permute-start.12 = (f32[144,66]{1,0:T(8,128)S(1)}, f32[144,66]{1,0:T(8,128)S(1)}, u32[]{:S(2)}, u32[]{:S(2)}) collective-permute-start(f32[144,66]{1,0:T(8,128)S(1)} %pad_maximum_fusion.3), channel_id=1, source_target_pairs={{0,8},{1,9},{2,10},{3,11},{4,12},{5,13},{6,14},{7,15},{8,0},{9,1},... | collective-permute-start | bytes 114056 | tf_op jit(solution)/shard_map/ppermute | solution.py:94
  119.6 6.8 %collective-permute-start.13 = (f32[144,66]{1,0:T(8,128)S(1)}, f32[144,66]{1,0:T(8,128)S(1)}, u32[]{:S(2)}, u32[]{:S(2)}) collective-permute-start(f32[144,66]{1,0:T(8,128)S(1)} %pad_maximum_fusion.4), channel_id=1, source_target_pairs={{0,16},{1,17},{2,18},{3,19},{4,20},{5,21},{6,22},{7,23},{8,24},{9,... | collective-permute-start | bytes 114056 | tf_op jit(solution)/shard_map/ppermute | solution.py:94
  126.8 33.0 %copy-start.12 = (bf16[2304,36]{0,1:T(8,128)(2,1)S(1)}, bf16[2304,36]{0,1:T(8,128)(2,1)}, u32[]{:S(2)}) copy-start(bf16[2304,36]{0,1:T(8,128)(2,1)} %param.19) | copy-start | bytes 497668
  126.9 33.0 %copy-start.13 = (f32[32,36]{1,0:T(8,128)S(1)}, f32[32,36]{1,0:T(8,128)}, u32[]{:S(2)}) copy-start(f32[32,36]{1,0:T(8,128)} %param.16) | copy-start | bytes 13828
  126.9 9.1 %collective-permute-start.14 = (f32[144,66]{1,0:T(8,128)S(1)}, f32[144,66]{1,0:T(8,128)S(1)}, u32[]{:S(2)}, u32[]{:S(2)}) collective-permute-start(f32[144,66]{1,0:T(8,128)S(1)} %pad_maximum_fusion.5), channel_id=1, source_target_pairs={{0,32},{1,33},{2,34},{3,35},{4,36},{5,37},{6,38},{7,39},{8,40},{9,... | collective-permute-start | bytes 114056 | tf_op jit(solution)/shard_map/ppermute | solution.py:94
  136.8 6.2 %collective-permute-start.15 = (bf16[144,64]{1,0:T(8,128)(2,1)S(1)}, bf16[144,64]{1,0:T(8,128)(2,1)S(1)}, u32[]{:S(2)}, u32[]{:S(2)}) collective-permute-start(bf16[144,64]{1,0:T(8,128)(2,1)S(1)} %fusion.51), channel_id=1, source_target_pairs={{0,4},{1,5},{2,6},{3,7},{4,0},{5,1},{6,2},{7,3},{8,12},{9,13},{10,... | collective-permute-start | bytes 55304 | tf_op jit(solution)/shard_map/ppermute | solution.py:67
  143.0 5.5 %collective-permute-start.16 = (bf16[288,64]{1,0:T(8,128)(2,1)S(1)}, bf16[288,64]{1,0:T(8,128)(2,1)S(1)}, u32[]{:S(2)}, u32[]{:S(2)}) collective-permute-start(bf16[288,64]{1,0:T(8,128)(2,1)S(1)} %maximum_select_fusion.5), channel_id=1, source_target_pairs={{0,2},{1,3},{2,0},{3,1},{4,6},{5,7},{6,4},{7,5},{8,10},{9,11},{10,... | collective-permute-start | bytes 110600 | tf_op jit(solution)/shard_map/ppermute | solution.py:67
  148.6 10.9 %collective-permute-start.17 = (bf16[576,64]{1,0:T(8,128)(2,1)S(1)}, bf16[576,64]{1,0:T(8,128)(2,1)S(1)}, u32[]{:S(2)}, u32[]{:S(2)}) collective-permute-start(bf16[576,64]{1,0:T(8,128)(2,1)S(1)} %maximum_select_fusion.3), channel_id=1, source_target_pairs={{0,1},{1,0},{2,3},{3,2},{4,5},{5,4},{6,7},{7,6},{8,9},{9,8},{10,11... | collective-permute-start | bytes 221192 | tf_op jit(solution)/shard_map/ppermute | solution.py:67
  159.8 12.8 %copy-start.15 = (s32[32,2]{0,1:T(2,128)S(1)}, s32[32,2]{0,1:T(2,128)}, u32[]{:S(2)}) copy-start(s32[32,2]{0,1:T(2,128)} %param.31) | copy-start | bytes 772
  162.1 24.2 %all-to-all-start = ((f32[64,1,1152]{2,1,0:T(1,128)}), f32[64,1,1152]{2,1,0:T(1,128)S(1)}, u32[]{:S(2)}, u32[]{:S(2)}) async-start(f32[64,1,1152]{2,1,0:T(1,128)} %reshape.328), calls=%async_computation | async-start | bytes 589824 | tf_op jit(solution)/shard_map/all_to_all | solution.py:129
  (6 other events, 14.4 us)

commit v7 on v6

--- a/solution.py
+++ b/solution.py
@@ -130,12 +130,9 @@
     return jnp.transpose(received, (1, 0, 2)).reshape(values.shape[0], -1)
 
 
-def exchange_scatter_sum(values):
-    count = lax.axis_size("tp")
-    rows = values.shape[0]
-    blocks = jnp.transpose(values.reshape(rows, count, -1), (1, 0, 2))
+def exchange_scatter_sum(blocks):
     received = lax.all_to_all(blocks, "tp", 0, 0, tiled=True)
-    return jnp.sum(received, axis=0)
+    return jnp.sum(received.astype(jnp.float32), axis=0)
 
 
 def reverse_blocks(values, count):
@@ -249,7 +246,7 @@
     attended_rows = (final_rows[:, :HDIM] / final_rows[:, HDIM : HDIM + 1]).astype(jnp.bfloat16)
     attended = gather_cols(attended_rows, axis=0, bits=near_bits).reshape(all_tokens, model_width)
     residual_cols = hidden + jnp.dot(attended, w_out, preferred_element_type=jnp.float32)
-    full_rows = exchange_gather(residual_cols)
+    full_rows = exchange_gather(residual_cols.astype(jnp.bfloat16)).astype(jnp.float32)
     inv_norm = lax.rsqrt(jnp.mean(full_rows * full_rows, axis=1) + EPSILON)
     normed = (full_rows * inv_norm[:, None] * moe_gain[None, :]).astype(jnp.bfloat16)
     logits = jnp.dot(normed, router, preferred_element_type=jnp.float32)
@@ -267,8 +264,13 @@
     gate_out = jnp.dot(normed, w_gate, preferred_element_type=jnp.float32)
     up_out = jnp.dot(normed, w_up, preferred_element_type=jnp.float32)
     inner_act = (jax.nn.silu(gate_out) * up_out * mix_coef[:, None]).astype(jnp.bfloat16)
-    expert_term = jnp.dot(inner_act, w_down, preferred_element_type=jnp.float32)
-    return residual_cols + exchange_scatter_sum(expert_term)
+    expert_blocks = jnp.einsum(
+        "tf,fbc->btc",
+        inner_act,
+        w_down.reshape(w_down.shape[0], tp_count, -1),
+        preferred_element_type=jnp.float32,
+    )
+    return residual_cols + exchange_scatter_sum(expert_blocks.astype(jnp.bfloat16))
 
 
 def solution(mesh):

time: 220 us -> 211 us (0.959)
  waiting for transfers between devices: 62.2 us -> 58.2 us
  blocking collectives: 18.4 us -> 15.6 us
  other arithmetic: 15.6 us -> 13.2 us
    all_to_all x1, waiting for transfers between devices: 13.7 us -> 9.75 us  [exchange_gather(): received = lax.all_to_all(copies, 'tp', 0, 0, tiled=True)]
    all_to_all x1, blocking collectives: 18.4 us -> 15.6 us  [exchange_scatter_sum(): received = lax.all_to_all(blocks, 'tp', 0, 0, tiled=True)]
    all_to_all x2 -> x0, other arithmetic: 2.74 us -> none  [the longest x1 1.37 us: exchange_scatter_sum(): received = lax.all_to_all(blocks, 'tp', 0, 0, tiled=True)]
    convert_element_type x0 -> x3, local copies, waits for them, and re-layouts: none -> 2.21 us  [the longest x2 1.23 us: on_device(): exchange_gather(residual_cols.astype(jnp.bfloat16)).astype(jnp.float32)]
    unnamed x42 -> x39, local copies, waits for them, and re-layouts: 6.78 us -> 6.09 us
  transfers between devices with their start and end apart: 19 -> 19, of which waited for: 18 -> 18; matrix products, arithmetic and copies ran while one was open for 4% -> 5% of each run, Pallas kernels for 0% -> 0%
where the time goes in v7:
time: 211 us; the launch traced here: 210 us
  starting transfers between devices  85.9 us (41%)
  waiting for transfers between devices  58.2 us (28%)
  local copies, waits for them, and re-layouts  22.9 us (11%)
  blocking collectives  15.6 us (7%)
  other arithmetic  13.2 us (6%)
  matrix products  13.1 us (6%)
    ppermute x6, starting transfers between devices, gather_cols(): other = lax.ppermute(values, 'tp', partner_pairs(count, bit))  31.5 us
    all_to_all x1, blocking collectives, exchange_scatter_sum(): received = lax.all_to_all(blocks, 'tp', 0, 0, tiled=True)  15.6 us
    ppermute x3, waiting for transfers between devices, scatter_sum(): values = keep + lax.ppermute(send, 'tp', partner_pairs(count, bit))  13 us
    ppermute x3, waiting for transfers between devices, exchange_sum(): values = values + lax.ppermute(values, 'tp', partner_pairs(count, bit))  12.8 us
    ppermute x3, starting transfers between devices, scatter_sum(): values = keep + lax.ppermute(send, 'tp', partner_pairs(count, bit))  12.6 us
    ppermute x3, starting transfers between devices, exchange_merge(): rows = merge_rows(rows, lax.ppermute(rows, 'tp', partner_pairs(count, bit)))  12.2 us
    all_to_all x1, starting transfers between devices, exchange_gather(): received = lax.all_to_all(copies, 'tp', 0, 0, tiled=True)  10.5 us
    ppermute x6, waiting for transfers between devices, gather_cols(): other = lax.ppermute(values, 'tp', partner_pairs(count, bit))  9.86 us
  transfers between devices with their start and end apart: 19, of which 18 were waited for; matrix products, arithmetic and copies ran while one was open for 5% of the time, Pallas kernels for 0%

profile of v7, /device:TPU:1, one launch (start us, length us, event | category | flops | bytes accessed | tf_op | source)
XLA Modules:
  0.0 210.0 jit_solution(13611053953074356790)
XLA Ops:
  2.3 2.0 reshape.285
  5.5 8.8 %collective-permute-start = (f32[32,3488]{1,0:T(8,128)S(1)}, f32[32,3488]{1,0:T(8,128)S(1)}, u32[]{:S(2)}, u32[]{:S(2)}) collective-permute-start(f32[32,3488]{1,0:T(8,128)S(1)} %constant_dynamic-slice_fusion.3), channel_id=1, source_target_pairs={{0,1},{1,0},{2,3},{3,2},{4,5},{5,4},{6,7},{7,6},{8,9},{9,8},{10,11... | collective-permute-start | bytes 1339400 | tf_op jit(solution)/shard_map/ppermute | solution.py:57
  16.1 1.9 collective-permute-start.1
  18.1 6.7 %collective-permute-done.1 = f32[32,1744]{1,0:T(8,128)S(1)} collective-permute-done((f32[32,1744]{1,0:T(8,128)S(1)}, f32[32,1744]{1,0:T(8,128)S(1)}, u32[]{:S(2)}, u32[]{:S(2)}) %collective-permute-start.1) | collective-permute-done | bytes 223264 | tf_op jit(solution)/shard_map/ppermute | solution.py:57
  25.0 1.9 collective-permute-start.2
  27.2 4.9 %collective-permute-done.2 = f32[32,872]{1,0:T(8,128)S(1)} collective-permute-done((f32[32,872]{1,0:T(8,128)S(1)}, f32[32,872]{1,0:T(8,128)S(1)}, u32[]{:S(2)}, u32[]{:S(2)}) %collective-permute-start.2) | collective-permute-done | bytes 111648 | tf_op jit(solution)/shard_map/ppermute | solution.py:57
  32.2 1.9 collective-permute-start.3
  34.1 3.6 %collective-permute-done.3 = f32[32,872]{1,0:T(8,128)S(1)} collective-permute-done((f32[32,872]{1,0:T(8,128)S(1)}, f32[32,872]{1,0:T(8,128)S(1)}, u32[]{:S(2)}, u32[]{:S(2)}) %collective-permute-start.3) | collective-permute-done | bytes 111648 | tf_op jit(solution)/shard_map/ppermute | solution.py:87
  39.7 5.4 %collective-permute-done.4 = f32[32,872]{1,0:T(8,128)S(1)} collective-permute-done((f32[32,872]{1,0:T(8,128)S(1)}, f32[32,872]{1,0:T(8,128)S(1)}, u32[]{:S(2)}, u32[]{:S(2)}) %collective-permute-start.4) | collective-permute-done | bytes 111648 | tf_op jit(solution)/shard_map/ppermute | solution.py:87
  45.2 5.5 %collective-permute-start.5 = (f32[32,872]{1,0:T(8,128)S(1)}, f32[32,872]{1,0:T(8,128)S(1)}, u32[]{:S(2)}, u32[]{:S(2)}) collective-permute-start(f32[32,872]{1,0:T(8,128)S(1)} %add.227), channel_id=1, source_target_pairs={{0,32},{1,33},{2,34},{3,35},{4,36},{5,37},{6,38},{7,39},{8,40},{9,... | collective-permute-start | bytes 334856 | tf_op jit(solution)/shard_map/ppermute | solution.py:87
  50.9 3.7 %collective-permute-done.5 = f32[32,872]{1,0:T(8,128)S(1)} collective-permute-done((f32[32,872]{1,0:T(8,128)S(1)}, f32[32,872]{1,0:T(8,128)S(1)}, u32[]{:S(2)}, u32[]{:S(2)}) %collective-permute-start.5) | collective-permute-done | bytes 111648 | tf_op jit(solution)/shard_map/ppermute | solution.py:87
  55.5 3.0 %collective-permute-start.6 = (bf16[32,864]{1,0:T(8,128)(2,1)S(1)}, bf16[32,864]{1,0:T(8,128)(2,1)S(1)}, u32[]{:S(2)}, u32[]{:S(2)}) collective-permute-start(bf16[32,864]{1,0:T(8,128)(2,1)S(1)} %reshape.288), channel_id=1, source_target_pairs={{0,4},{1,5},{2,6},{3,7},{4,0},{5,1},{6,2},{7,3},{8,12},{9,13},{10,... | collective-permute-start | bytes 165896 | tf_op jit(solution)/shard_map/ppermute | solution.py:67
  58.5 3.4 %collective-permute-done.6 = bf16[32,864]{1,0:T(8,128)(2,1)S(1)} collective-permute-done((bf16[32,864]{1,0:T(8,128)(2,1)S(1)}, bf16[32,864]{1,0:T(8,128)(2,1)S(1)}, u32[]{:S(2)}, u32[]{:S(2)}) %collective-permute-start.6) | collective-permute-done | bytes 55328 | tf_op jit(solution)/shard_map/ppermute | solution.py:67
  62.0 2.3 %collective-permute-start.7 = (bf16[32,1728]{1,0:T(8,128)(2,1)S(1)}, bf16[32,1728]{1,0:T(8,128)(2,1)S(1)}, u32[]{:S(2)}, u32[]{:S(2)}) collective-permute-start(bf16[32,1728]{1,0:T(8,128)(2,1)S(1)} %maximum_select_fusion.4), channel_id=1, source_target_pairs={{0,2},{1,3},{2,0},{3,1},{4,6},{5,7},{6,4},{7,5},{8,10},{9,11},{10,... | collective-permute-start | bytes 331784 | tf_op jit(solution)/shard_map/ppermute | solution.py:67
  70.5 9.2 %collective-permute-start.8 = (bf16[32,3456]{1,0:T(8,128)(2,1)S(1)}, bf16[32,3456]{1,0:T(8,128)(2,1)S(1)}, u32[]{:S(2)}, u32[]{:S(2)}) collective-permute-start(bf16[32,3456]{1,0:T(8,128)(2,1)S(1)} %maximum_select_fusion.2), channel_id=1, source_target_pairs={{0,1},{1,0},{2,3},{3,2},{4,5},{5,4},{6,7},{7,6},{8,9},{9,8},{10,11... | collective-permute-start | bytes 663560 | tf_op jit(solution)/shard_map/ppermute | solution.py:67
  85.1 2.4 %fusion.85 = (f32[8,4,36]{1,2,0:T(8,128)S(1)}, f32[8,4,36,8]{3,1,2,0:T(4,128)}) fusion(bf16[8,8,36,64]{3,2,1,0:T(8,128)(2,1)} %reshape.292, bf16[8,4,36,64]{3,0,1,2:T(8,128)(2,1)S(1)} %pad_maximum_fusion.2, pred[8,8]{1,0:T(8,128)(4,1)S(1)} %broadcast_compare_fusion), kind=kOutput, calls=%fused_computation.184 | convolution fusion | flops 1206144 | bytes 483904 | tf_op jit(solution)/shard_map/rjhd,rphd->rjhp/dot_general | solution.py:213
  95.1 2.4 %collective-permute-start.9 = (f32[576,66]{1,0:T(8,128)S(1)}, f32[576,66]{1,0:T(8,128)S(1)}, u32[]{:S(2)}, u32[]{:S(2)}) collective-permute-start(f32[576,66]{1,0:T(8,128)S(1)} %constant_dynamic-slice_fusion), channel_id=1, source_target_pairs={{0,1},{1,0},{2,3},{3,2},{4,5},{5,4},{6,7},{7,6},{8,9},{9,8},{10,11... | collective-permute-start | bytes 456200 | tf_op jit(solution)/shard_map/ppermute | solution.py:114
  99.5 3.3 %collective-permute-start.10 = (f32[288,66]{1,0:T(8,128)S(1)}, f32[288,66]{1,0:T(8,128)S(1)}, u32[]{:S(2)}, u32[]{:S(2)}) collective-permute-start(f32[288,66]{1,0:T(8,128)S(1)} %get-tuple-element.31), channel_id=1, source_target_pairs={{0,2},{1,3},{2,0},{3,1},{4,6},{5,7},{6,4},{7,5},{8,10},{9,11},{10,... | collective-permute-start | bytes 228104 | tf_op jit(solution)/shard_map/ppermute | solution.py:114
  103.2 3.3 %collective-permute-done.10 = f32[288,66]{1,0:T(8,128)S(1)} collective-permute-done((f32[288,66]{1,0:T(8,128)S(1)}, f32[288,66]{1,0:T(8,128)S(1)}, u32[]{:S(2)}, u32[]{:S(2)}) %collective-permute-start.10) | collective-permute-done | bytes 76064 | tf_op jit(solution)/shard_map/ppermute | solution.py:114
  107.1 4.0 %collective-permute-start.11 = (f32[144,66]{1,0:T(8,128)S(1)}, f32[144,66]{1,0:T(8,128)S(1)}, u32[]{:S(2)}, u32[]{:S(2)}) collective-permute-start(f32[144,66]{1,0:T(8,128)S(1)} %get-tuple-element.35), channel_id=1, source_target_pairs={{0,4},{1,5},{2,6},{3,7},{4,0},{5,1},{6,2},{7,3},{8,12},{9,13},{10,... | collective-permute-start | bytes 114056 | tf_op jit(solution)/shard_map/ppermute | solution.py:114
  116.6 2.6 %collective-permute-done.12 = f32[144,66]{1,0:T(8,128)S(1)} collective-permute-done((f32[144,66]{1,0:T(8,128)S(1)}, f32[144,66]{1,0:T(8,128)S(1)}, u32[]{:S(2)}, u32[]{:S(2)}) %collective-permute-start.12) | collective-permute-done | bytes 38048 | tf_op jit(solution)/shard_map/ppermute | solution.py:94
  119.7 3.7 %collective-permute-start.13 = (f32[144,66]{1,0:T(8,128)S(1)}, f32[144,66]{1,0:T(8,128)S(1)}, u32[]{:S(2)}, u32[]{:S(2)}) collective-permute-start(f32[144,66]{1,0:T(8,128)S(1)} %pad_maximum_fusion.4), channel_id=1, source_target_pairs={{0,16},{1,17},{2,18},{3,19},{4,20},{5,21},{6,22},{7,23},{8,24},{9,... | collective-permute-start | bytes 114056 | tf_op jit(solution)/shard_map/ppermute | solution.py:94
  126.9 6.6 %collective-permute-start.14 = (f32[144,66]{1,0:T(8,128)S(1)}, f32[144,66]{1,0:T(8,128)S(1)}, u32[]{:S(2)}, u32[]{:S(2)}) collective-permute-start(f32[144,66]{1,0:T(8,128)S(1)} %pad_maximum_fusion.5), channel_id=1, source_target_pairs={{0,32},{1,33},{2,34},{3,35},{4,36},{5,37},{6,38},{7,39},{8,40},{9,... | collective-permute-start | bytes 114056 | tf_op jit(solution)/shard_map/ppermute | solution.py:94
  133.6 2.5 %collective-permute-done.14 = f32[144,66]{1,0:T(8,128)S(1)} collective-permute-done((f32[144,66]{1,0:T(8,128)S(1)}, f32[144,66]{1,0:T(8,128)S(1)}, u32[]{:S(2)}, u32[]{:S(2)}) %collective-permute-start.14) | collective-permute-done | bytes 38048 | tf_op jit(solution)/shard_map/ppermute | solution.py:94
  136.8 3.9 %collective-permute-start.15 = (bf16[144,64]{1,0:T(8,128)(2,1)S(1)}, bf16[144,64]{1,0:T(8,128)(2,1)S(1)}, u32[]{:S(2)}, u32[]{:S(2)}) collective-permute-start(bf16[144,64]{1,0:T(8,128)(2,1)S(1)} %fusion.56), channel_id=1, source_target_pairs={{0,4},{1,5},{2,6},{3,7},{4,0},{5,1},{6,2},{7,3},{8,12},{9,13},{10,... | collective-permute-start | bytes 55304 | tf_op jit(solution)/shard_map/ppermute | solution.py:67
  140.7 2.3 %collective-permute-done.15 = bf16[144,64]{1,0:T(8,128)(2,1)S(1)} collective-permute-done((bf16[144,64]{1,0:T(8,128)(2,1)S(1)}, bf16[144,64]{1,0:T(8,128)(2,1)S(1)}, u32[]{:S(2)}, u32[]{:S(2)}) %collective-permute-start.15) | collective-permute-done | bytes 18464 | tf_op jit(solution)/shard_map/ppermute | solution.py:67
  143.1 3.1 %collective-permute-start.16 = (bf16[288,64]{1,0:T(8,128)(2,1)S(1)}, bf16[288,64]{1,0:T(8,128)(2,1)S(1)}, u32[]{:S(2)}, u32[]{:S(2)}) collective-permute-start(bf16[288,64]{1,0:T(8,128)(2,1)S(1)} %maximum_select_fusion.5), channel_id=1, source_target_pairs={{0,2},{1,3},{2,0},{3,1},{4,6},{5,7},{6,4},{7,5},{8,10},{9,11},{10,... | collective-permute-start | bytes 110600 | tf_op jit(solution)/shard_map/ppermute | solution.py:67
  146.2 2.3 %collective-permute-done.16 = bf16[288,64]{1,0:T(8,128)(2,1)S(1)} collective-permute-done((bf16[288,64]{1,0:T(8,128)(2,1)S(1)}, bf16[288,64]{1,0:T(8,128)(2,1)S(1)}, u32[]{:S(2)}, u32[]{:S(2)}) %collective-permute-start.16) | collective-permute-done | bytes 36896 | tf_op jit(solution)/shard_map/ppermute | solution.py:67
  148.6 10.0 %collective-permute-start.17 = (bf16[576,64]{1,0:T(8,128)(2,1)S(1)}, bf16[576,64]{1,0:T(8,128)(2,1)S(1)}, u32[]{:S(2)}, u32[]{:S(2)}) collective-permute-start(bf16[576,64]{1,0:T(8,128)(2,1)S(1)} %maximum_select_fusion.3), channel_id=1, source_target_pairs={{0,1},{1,0},{2,3},{3,2},{4,5},{5,4},{6,7},{7,6},{8,9},{9,8},{10,11... | collective-permute-start | bytes 221192 | tf_op jit(solution)/shard_map/ppermute | solution.py:67
  161.6 10.5 %all-to-all-start = ((bf16[64,2,576]{2,1,0:T(2,128)(2,1)}), bf16[64,2,576]{2,1,0:T(2,128)(2,1)S(1)}, u32[]{:S(2)}, u32[]{:S(2)}) async-start(bf16[64,2,576]{2,1,0:T(2,128)(2,1)} %reshape.329), calls=%async_computation | async-start | bytes 327680 | tf_op jit(solution)/shard_map/all_to_all | solution.py:129
  174.0 9.7 %all-to-all-done = bf16[64,2,576]{2,1,0:T(2,128)(2,1)S(1)} async-done(((bf16[64,2,576]{2,1,0:T(2,128)(2,1)}), bf16[64,2,576]{2,1,0:T(2,128)(2,1)S(1)}, u32[]{:S(2)}, u32[]{:S(2)}) %all-to-all-start) | async-done | bytes 147488 | tf_op jit(solution)/shard_map/all_to_all | solution.py:129
  191.8 15.6 %all_to_all.10 = bf16[64,2,576]{2,1,0:T(2,128)(2,1)S(1)} all-to-all(bf16[64,2,576]{2,1,0:T(2,128)(2,1)S(1)} %reshape.331), channel_id=1, replica_groups=mesh['rep'=8,'tp'=64] {'tp'}, dimensions={0} | all-to-all | bytes 294912 | tf_op jit(solution)/shard_map/all_to_all | solution.py:134
  (166 shorter events, 56.2 us)
Async XLA Ops:
  0.0 188.7 %copy-start = (bf16[2304,180]{0,1:T(8,128)(2,1)S(1)}, bf16[2304,180]{0,1:T(8,128)(2,1)}, u32[]{:S(2)}) copy-start(bf16[2304,180]{0,1:T(8,128)(2,1)} %param.29) | copy-start | bytes 2488324
  5.3 21.6 %copy-start.15 = (s32[8]{0:T(128)S(1)}, s32[8]{0:T(128)}, u32[]{:S(2)}) copy-start(s32[8]{0:T(128)} %param.25) | copy-start | bytes 100
  5.5 10.2 %collective-permute-start = (f32[32,3488]{1,0:T(8,128)S(1)}, f32[32,3488]{1,0:T(8,128)S(1)}, u32[]{:S(2)}, u32[]{:S(2)}) collective-permute-start(f32[32,3488]{1,0:T(8,128)S(1)} %constant_dynamic-slice_fusion.3), channel_id=1, source_target_pairs={{0,1},{1,0},{2,3},{3,2},{4,5},{5,4},{6,7},{7,6},{8,9},{9,8},{10,11... | collective-permute-start | bytes 1339400 | tf_op jit(solution)/shard_map/ppermute | solution.py:57
  15.9 48.4 %copy-start.7 = (bf16[3,32,2304]{2,1,0:T(8,128)(2,1)S(1)}, bf16[3,32,2304]{2,1,0:T(8,128)(2,1)}, u32[]{:S(2)}) copy-start(bf16[3,32,2304]{2,1,0:T(8,128)(2,1)} %param.20) | copy-start | bytes 1327108
  16.1 8.7 %collective-permute-start.1 = (f32[32,1744]{1,0:T(8,128)S(1)}, f32[32,1744]{1,0:T(8,128)S(1)}, u32[]{:S(2)}, u32[]{:S(2)}) collective-permute-start(f32[32,1744]{1,0:T(8,128)S(1)} %constant_dynamic-slice_fusion.2), channel_id=1, source_target_pairs={{0,2},{1,3},{2,0},{3,1},{4,6},{5,7},{6,4},{7,5},{8,10},{9,11},{10,... | collective-permute-start | bytes 669704 | tf_op jit(solution)/shard_map/ppermute | solution.py:57
  25.0 7.0 %collective-permute-start.2 = (f32[32,872]{1,0:T(8,128)S(1)}, f32[32,872]{1,0:T(8,128)S(1)}, u32[]{:S(2)}, u32[]{:S(2)}) collective-permute-start(f32[32,872]{1,0:T(8,128)S(1)} %constant_dynamic-slice_fusion.1), channel_id=1, source_target_pairs={{0,4},{1,5},{2,6},{3,7},{4,0},{5,1},{6,2},{7,3},{8,12},{9,13},{10,... | collective-permute-start | bytes 334856 | tf_op jit(solution)/shard_map/ppermute | solution.py:57
  27.2 38.9 %copy-start.9 = (bf16[8,8,2304]{2,1,0:T(8,128)(2,1)S(1)}, bf16[8,8,2304]{2,1,0:T(8,128)(2,1)}, u32[]{:S(2)}) copy-start(bf16[8,8,2304]{2,1,0:T(8,128)(2,1)} %param.22) | copy-start | bytes 884740
  32.2 5.5 %collective-permute-start.3 = (f32[32,872]{1,0:T(8,128)S(1)}, f32[32,872]{1,0:T(8,128)S(1)}, u32[]{:S(2)}, u32[]{:S(2)}) collective-permute-start(f32[32,872]{1,0:T(8,128)S(1)} %dynamic-slice_add_fusion.2), channel_id=1, source_target_pairs={{0,8},{1,9},{2,10},{3,11},{4,12},{5,13},{6,14},{7,15},{8,0},{9,1},... | collective-permute-start | bytes 334856 | tf_op jit(solution)/shard_map/ppermute | solution.py:87
  37.7 7.4 %collective-permute-start.4 = (f32[32,872]{1,0:T(8,128)S(1)}, f32[32,872]{1,0:T(8,128)S(1)}, u32[]{:S(2)}, u32[]{:S(2)}) collective-permute-start(f32[32,872]{1,0:T(8,128)S(1)} %add.226), channel_id=1, source_target_pairs={{0,16},{1,17},{2,18},{3,19},{4,20},{5,21},{6,22},{7,23},{8,24},{9,... | collective-permute-start | bytes 334856 | tf_op jit(solution)/shard_map/ppermute | solution.py:87
  45.2 9.4 %collective-permute-start.5 = (f32[32,872]{1,0:T(8,128)S(1)}, f32[32,872]{1,0:T(8,128)S(1)}, u32[]{:S(2)}, u32[]{:S(2)}) collective-permute-start(f32[32,872]{1,0:T(8,128)S(1)} %add.227), channel_id=1, source_target_pairs={{0,32},{1,33},{2,34},{3,35},{4,36},{5,37},{6,38},{7,39},{8,40},{9,... | collective-permute-start | bytes 334856 | tf_op jit(solution)/shard_map/ppermute | solution.py:87
  50.8 16.5 %copy-start.10 = (bf16[8,8,2304]{2,1,0:T(8,128)(2,1)S(1)}, bf16[8,8,2304]{2,1,0:T(8,128)(2,1)}, u32[]{:S(2)}) copy-start(bf16[8,8,2304]{2,1,0:T(8,128)(2,1)} %param.23) | copy-start | bytes 884740
  55.5 6.4 %collective-permute-start.6 = (bf16[32,864]{1,0:T(8,128)(2,1)S(1)}, bf16[32,864]{1,0:T(8,128)(2,1)S(1)}, u32[]{:S(2)}, u32[]{:S(2)}) collective-permute-start(bf16[32,864]{1,0:T(8,128)(2,1)S(1)} %reshape.288), channel_id=1, source_target_pairs={{0,4},{1,5},{2,6},{3,7},{4,0},{5,1},{6,2},{7,3},{8,12},{9,13},{10,... | collective-permute-start | bytes 165896 | tf_op jit(solution)/shard_map/ppermute | solution.py:67
  58.5 10.2 %copy-start.8 = (bf16[3,32,2304]{2,1,0:T(8,128)(2,1)S(1)}, bf16[3,32,2304]{2,1,0:T(8,128)(2,1)}, u32[]{:S(2)}) copy-start(bf16[3,32,2304]{2,1,0:T(8,128)(2,1)} %param.21) | copy-start | bytes 1327108
  62.0 8.3 %collective-permute-start.7 = (bf16[32,1728]{1,0:T(8,128)(2,1)S(1)}, bf16[32,1728]{1,0:T(8,128)(2,1)S(1)}, u32[]{:S(2)}, u32[]{:S(2)}) collective-permute-start(bf16[32,1728]{1,0:T(8,128)(2,1)S(1)} %maximum_select_fusion.4), channel_id=1, source_target_pairs={{0,2},{1,3},{2,0},{3,1},{4,6},{5,7},{6,4},{7,5},{8,10},{9,11},{10,... | collective-permute-start | bytes 331784 | tf_op jit(solution)/shard_map/ppermute | solution.py:67
  66.1 13.6 %copy-start.16 = (s32[8]{0:T(128)S(1)}, s32[8]{0:T(128)}, u32[]{:S(2)}) copy-start(s32[8]{0:T(128)} %param.24) | copy-start | bytes 100
  70.5 10.1 %collective-permute-start.8 = (bf16[32,3456]{1,0:T(8,128)(2,1)S(1)}, bf16[32,3456]{1,0:T(8,128)(2,1)S(1)}, u32[]{:S(2)}, u32[]{:S(2)}) collective-permute-start(bf16[32,3456]{1,0:T(8,128)(2,1)S(1)} %maximum_select_fusion.2), channel_id=1, source_target_pairs={{0,1},{1,0},{2,3},{3,2},{4,5},{5,4},{6,7},{7,6},{8,9},{9,8},{10,11... | collective-permute-start | bytes 663560 | tf_op jit(solution)/shard_map/ppermute | solution.py:67
  83.0 4.6 %copy-start.4 = (bf16[8,4,36,64]{3,0,1,2:T(8,128)(2,1)}, bf16[8,4,36,64]{3,0,1,2:T(8,128)(2,1)S(1)}, u32[]{:S(2)}) copy-start(bf16[8,4,36,64]{3,0,1,2:T(8,128)(2,1)S(1)} %pad_maximum_fusion.2) | copy-start | bytes 442372
  95.1 7.8 %copy-start.3 = (bf16[32,36,32]{2,1,0:T(8,128)(2,1)S(1)}, bf16[32,36,32]{2,1,0:T(8,128)(2,1)}, u32[]{:S(2)}) copy-start(bf16[32,36,32]{2,1,0:T(8,128)(2,1)} %get-tuple-element.38) | copy-start | bytes 221188
  95.1 7.9 %copy-start.2 = (bf16[32,36,32]{2,1,0:T(8,128)(2,1)S(1)}, bf16[32,36,32]{2,1,0:T(8,128)(2,1)}, u32[]{:S(2)}) copy-start(bf16[32,36,32]{2,1,0:T(8,128)(2,1)} %get-tuple-element.37) | copy-start | bytes 221188
  95.1 3.6 %collective-permute-start.9 = (f32[576,66]{1,0:T(8,128)S(1)}, f32[576,66]{1,0:T(8,128)S(1)}, u32[]{:S(2)}, u32[]{:S(2)}) collective-permute-start(f32[576,66]{1,0:T(8,128)S(1)} %constant_dynamic-slice_fusion), channel_id=1, source_target_pairs={{0,1},{1,0},{2,3},{3,2},{4,5},{5,4},{6,7},{7,6},{8,9},{9,8},{10,11... | collective-permute-start | bytes 456200 | tf_op jit(solution)/shard_map/ppermute | solution.py:114
  99.4 11.7 %copy-start.5 = (bf16[8,4,36,64]{3,0,1,2:T(8,128)(2,1)S(1)}, bf16[8,4,36,64]{3,0,1,2:T(8,128)(2,1)}, u32[]{:S(2)}) copy-start(bf16[8,4,36,64]{3,0,1,2:T(8,128)(2,1)} %copy-done.4) | copy-start | bytes 442372
  99.5 7.0 %collective-permute-start.10 = (f32[288,66]{1,0:T(8,128)S(1)}, f32[288,66]{1,0:T(8,128)S(1)}, u32[]{:S(2)}, u32[]{:S(2)}) collective-permute-start(f32[288,66]{1,0:T(8,128)S(1)} %get-tuple-element.31), channel_id=1, source_target_pairs={{0,2},{1,3},{2,0},{3,1},{4,6},{5,7},{6,4},{7,5},{8,10},{9,11},{10,... | collective-permute-start | bytes 228104 | tf_op jit(solution)/shard_map/ppermute | solution.py:114
  107.1 6.6 %collective-permute-start.11 = (f32[144,66]{1,0:T(8,128)S(1)}, f32[144,66]{1,0:T(8,128)S(1)}, u32[]{:S(2)}, u32[]{:S(2)}) collective-permute-start(f32[144,66]{1,0:T(8,128)S(1)} %get-tuple-element.35), channel_id=1, source_target_pairs={{0,4},{1,5},{2,6},{3,7},{4,0},{5,1},{6,2},{7,3},{8,12},{9,13},{10,... | collective-permute-start | bytes 114056 | tf_op jit(solution)/shard_map/ppermute | solution.py:114
  114.1 5.1 %collective-permute-start.12 = (f32[144,66]{1,0:T(8,128)S(1)}, f32[144,66]{1,0:T(8,128)S(1)}, u32[]{:S(2)}, u32[]{:S(2)}) collective-permute-start(f32[144,66]{1,0:T(8,128)S(1)} %pad_maximum_fusion.3), channel_id=1, source_target_pairs={{0,8},{1,9},{2,10},{3,11},{4,12},{5,13},{6,14},{7,15},{8,0},{9,1},... | collective-permute-start | bytes 114056 | tf_op jit(solution)/shard_map/ppermute | solution.py:94
  119.7 6.8 %collective-permute-start.13 = (f32[144,66]{1,0:T(8,128)S(1)}, f32[144,66]{1,0:T(8,128)S(1)}, u32[]{:S(2)}, u32[]{:S(2)}) collective-permute-start(f32[144,66]{1,0:T(8,128)S(1)} %pad_maximum_fusion.4), channel_id=1, source_target_pairs={{0,16},{1,17},{2,18},{3,19},{4,20},{5,21},{6,22},{7,23},{8,24},{9,... | collective-permute-start | bytes 114056 | tf_op jit(solution)/shard_map/ppermute | solution.py:94
  126.9 33.0 %copy-start.11 = (bf16[2304,36]{0,1:T(8,128)(2,1)S(1)}, bf16[2304,36]{0,1:T(8,128)(2,1)}, u32[]{:S(2)}) copy-start(bf16[2304,36]{0,1:T(8,128)(2,1)} %param.19) | copy-start | bytes 497668
  126.9 33.0 %copy-start.12 = (f32[32,36]{1,0:T(8,128)S(1)}, f32[32,36]{1,0:T(8,128)}, u32[]{:S(2)}) copy-start(f32[32,36]{1,0:T(8,128)} %param.16) | copy-start | bytes 13828
  126.9 9.1 %collective-permute-start.14 = (f32[144,66]{1,0:T(8,128)S(1)}, f32[144,66]{1,0:T(8,128)S(1)}, u32[]{:S(2)}, u32[]{:S(2)}) collective-permute-start(f32[144,66]{1,0:T(8,128)S(1)} %pad_maximum_fusion.5), channel_id=1, source_target_pairs={{0,32},{1,33},{2,34},{3,35},{4,36},{5,37},{6,38},{7,39},{8,40},{9,... | collective-permute-start | bytes 114056 | tf_op jit(solution)/shard_map/ppermute | solution.py:94
  136.8 6.2 %collective-permute-start.15 = (bf16[144,64]{1,0:T(8,128)(2,1)S(1)}, bf16[144,64]{1,0:T(8,128)(2,1)S(1)}, u32[]{:S(2)}, u32[]{:S(2)}) collective-permute-start(bf16[144,64]{1,0:T(8,128)(2,1)S(1)} %fusion.56), channel_id=1, source_target_pairs={{0,4},{1,5},{2,6},{3,7},{4,0},{5,1},{6,2},{7,3},{8,12},{9,13},{10,... | collective-permute-start | bytes 55304 | tf_op jit(solution)/shard_map/ppermute | solution.py:67
  143.1 5.5 %collective-permute-start.16 = (bf16[288,64]{1,0:T(8,128)(2,1)S(1)}, bf16[288,64]{1,0:T(8,128)(2,1)S(1)}, u32[]{:S(2)}, u32[]{:S(2)}) collective-permute-start(bf16[288,64]{1,0:T(8,128)(2,1)S(1)} %maximum_select_fusion.5), channel_id=1, source_target_pairs={{0,2},{1,3},{2,0},{3,1},{4,6},{5,7},{6,4},{7,5},{8,10},{9,11},{10,... | collective-permute-start | bytes 110600 | tf_op jit(solution)/shard_map/ppermute | solution.py:67
  148.6 10.9 %collective-permute-start.17 = (bf16[576,64]{1,0:T(8,128)(2,1)S(1)}, bf16[576,64]{1,0:T(8,128)(2,1)S(1)}, u32[]{:S(2)}, u32[]{:S(2)}) collective-permute-start(bf16[576,64]{1,0:T(8,128)(2,1)S(1)} %maximum_select_fusion.3), channel_id=1, source_target_pairs={{0,1},{1,0},{2,3},{3,2},{4,5},{5,4},{6,7},{7,6},{8,9},{9,8},{10,11... | collective-permute-start | bytes 221192 | tf_op jit(solution)/shard_map/ppermute | solution.py:67
  161.6 22.2 %all-to-all-start = ((bf16[64,2,576]{2,1,0:T(2,128)(2,1)}), bf16[64,2,576]{2,1,0:T(2,128)(2,1)S(1)}, u32[]{:S(2)}, u32[]{:S(2)}) async-start(bf16[64,2,576]{2,1,0:T(2,128)(2,1)} %reshape.329), calls=%async_computation | async-start | bytes 327680 | tf_op jit(solution)/shard_map/all_to_all | solution.py:129
  (4 other events, 7.4 us)

commit v8 on v7

--- a/solution.py
+++ b/solution.py
@@ -133,6 +133,24 @@
 def exchange_scatter_sum(blocks):
     received = lax.all_to_all(blocks, "tp", 0, 0, tiled=True)
     return jnp.sum(received.astype(jnp.float32), axis=0)
+
+
+def spread_requests(values, bits):
+    count, _ = tp_bits()
+    own_rank = lax.axis_index("tp")
+    for step, bit in enumerate(reversed(bits)):
+        side = (own_rank // bit) % 2
+        held, tokens, width = values.shape
+        split = values.reshape(held // 2, 2, tokens, width)
+        keep = lax.dynamic_index_in_dim(split, side, axis=1, keepdims=False)
+        send = lax.dynamic_index_in_dim(split, 1 - side, axis=1, keepdims=False)
+        other = lax.ppermute(send, "tp", partner_pairs(count, bit))
+        values = jnp.where(
+            side == 0,
+            jnp.concatenate([keep, other], axis=2),
+            jnp.concatenate([other, keep], axis=2),
+        )
+    return values
 
 
 def reverse_blocks(values, count):
@@ -172,12 +190,14 @@
     scaled = (hidden * attn_gain[None, :]).astype(jnp.bfloat16)
     partial_qkv = jnp.dot(scaled, w_qkv, preferred_element_type=jnp.float32)
     own_squares = jnp.sum(hidden * hidden, axis=1)
-    qkv_width = partial_qkv.shape[1]
     tp_count = lax.axis_size("tp")
-    block = qkv_width // tp_count
+    query_block = model_width // tp_count
+    kv_block = 2 * model_width // tp_count
+    block = query_block + kv_block
     packed = jnp.concatenate(
         [
-            partial_qkv.reshape(all_tokens, tp_count, block),
+            partial_qkv[:, :model_width].reshape(all_tokens, tp_count, query_block),
+            partial_qkv[:, model_width:].reshape(all_tokens, tp_count, kv_block),
             jnp.broadcast_to(own_squares[:, None, None], (all_tokens, tp_count, 1)),
         ],
         axis=2,
@@ -185,11 +205,15 @@
     _, all_bits = tp_bits()
     near_bits = all_bits[: len(all_bits) // 2]
     far_bits = all_bits[len(all_bits) // 2 :]
+    assert 2 ** len(near_bits) == requests
     own_block = exchange_sum(scatter_sum(packed, near_bits), far_bits)
     own_block = own_block.reshape(all_tokens, -1, block + 1)
     inv_attn = lax.rsqrt(own_block[:, 0, block] / model_width + EPSILON)
     own_qkv = (inv_attn[:, None, None] * own_block[:, :, :block]).astype(jnp.bfloat16)
-    qkv = gather_cols(own_qkv.reshape(all_tokens, -1), bits=near_bits)
+    query_cols = gather_cols(own_qkv[:, :, :query_block].reshape(all_tokens, -1), bits=near_bits)
+    own_kv = own_qkv[:, :, query_block:].reshape(requests, NEW, -1)
+    own_request = kept_position(near_bits)
+    request_kv = spread_requests(own_kv, near_bits).reshape(NEW, 2 * model_width)
     own_lengths = jnp.broadcast_to(private_lengths[:, None], (requests, NEW)).reshape(all_tokens)
     places = (
         prefix_block * lax.axis_size("tp")
@@ -197,13 +221,14 @@
         + jnp.arange(all_tokens, dtype=jnp.int32) % NEW
     )
     queries = rotate_heads(
-        qkv[:, :model_width].astype(jnp.float32).reshape(all_tokens, HEADS, HDIM), places
+        query_cols.astype(jnp.float32).reshape(all_tokens, HEADS, HDIM), places
     ).astype(jnp.bfloat16)
+    request_places = lax.dynamic_slice_in_dim(places, own_request * NEW, NEW)
     fresh_keys = rotate_heads(
-        qkv[:, model_width : 2 * model_width].astype(jnp.float32).reshape(all_tokens, HEADS, HDIM),
-        places,
+        request_kv[:, :model_width].astype(jnp.float32).reshape(NEW, HEADS, HDIM),
+        request_places,
     ).astype(jnp.bfloat16)
-    fresh_values = qkv[:, 2 * model_width :].astype(jnp.float32).reshape(requests, NEW, HEADS, HDIM)
+    fresh_values = request_kv[:, model_width:].astype(jnp.float32).reshape(NEW, HEADS, HDIM)
     query_f = queries.astype(jnp.float32).reshape(requests, NEW, HEADS, HDIM)
     pre_keys = prefix_keys.astype(jnp.float32).reshape(group_count, prefix_block, HEADS, HDIM)
     pre_scores = jnp.einsum("rjhd,gphd->rjhgp", query_f, pre_keys) * score_scale
@@ -228,20 +253,16 @@
     local_weighted = local_weighted.reshape(all_tokens, model_width)
     cache_rows = scatter_merge(state_rows(local_peak, local_total, local_weighted), near_bits)
     cache_rows = exchange_merge(cache_rows, far_bits)
-    key_f = fresh_keys.astype(jnp.float32).reshape(requests, NEW, HEADS, HDIM)
-    new_scores = jnp.einsum("rjhd,rihd->rjhi", query_f, key_f) * score_scale
+    request_query = lax.dynamic_index_in_dim(query_f, own_request, axis=0, keepdims=False)
+    key_f = fresh_keys.astype(jnp.float32)
+    new_scores = jnp.einsum("jhd,ihd->jhi", request_query, key_f) * score_scale
     causal = jnp.arange(NEW)[:, None] >= jnp.arange(NEW)[None, :]
-    new_scores = jnp.where(causal[None, :, None, :], new_scores, BLOCKED)
-    new_peak = jnp.max(new_scores, axis=3)
+    new_scores = jnp.where(causal[:, None, :], new_scores, BLOCKED)
+    new_peak = jnp.max(new_scores, axis=2)
     new_weights = jnp.exp(new_scores - new_peak[..., None])
-    new_total = jnp.sum(new_weights, axis=3).reshape(all_tokens, HEADS)
-    new_weighted = jnp.einsum("rjhi,rihd->rjhd", new_weights, fresh_values).reshape(
-        all_tokens, model_width
-    )
-    new_peak = new_peak.reshape(all_tokens, HEADS)
+    new_total = jnp.sum(new_weights, axis=2)
+    new_weighted = jnp.einsum("jhi,ihd->jhd", new_weights, fresh_values)
     new_rows = state_rows(new_peak, new_total, new_weighted)
-    own_count = cache_rows.shape[0]
-    new_rows = lax.dynamic_slice_in_dim(new_rows, kept_position(near_bits) * own_count, own_count, axis=0)
     final_rows = merge_rows(cache_rows, new_rows)
     attended_rows = (final_rows[:, :HDIM] / final_rows[:, HDIM : HDIM + 1]).astype(jnp.bfloat16)
     attended = gather_cols(attended_rows, axis=0, bits=near_bits).reshape(all_tokens, model_width)

time: 211 us -> 232 us (1.100)
  starting transfers between devices: 85.9 us -> 99.7 us
  local copies, waits for them, and re-layouts: 22.9 us -> 29.4 us
  other arithmetic: 13.2 us -> 15.6 us
    ppermute x0 -> x3, starting transfers between devices: none -> 14.9 us  [spread_requests(): other = lax.ppermute(send, 'tp', partner_pairs(count, bit))]
    ppermute x6, waiting for transfers between devices: 9.86 us -> 5.96 us  [gather_cols(): other = lax.ppermute(values, 'tp', partner_pairs(count, bit))]
    ppermute x0 -> x3, waiting for transfers between devices: none -> 2.94 us  [spread_requests(): other = lax.ppermute(send, 'tp', partner_pairs(count, bit))]
    ppermute x6, starting transfers between devices: 31.5 us -> 28.7 us  [gather_cols(): other = lax.ppermute(values, 'tp', partner_pairs(count, bit))]
    reshape x6 -> x9, local copies, waits for them, and re-layouts: 3.28 us -> 5.34 us  [the longest x1 1.82 us: on_device(): packed = jnp.concatenate([partial_qkv[:, :model_width].reshape(all_tokens...]
    unnamed x39 -> x49, local copies, waits for them, and re-layouts: 6.09 us -> 6.66 us
  transfers between devices with their start and end apart: 19 -> 22, of which waited for: 18 -> 19; matrix products, arithmetic and copies ran while one was open for 5% -> 6% of each run, Pallas kernels for 0% -> 0%
where the time goes in v8:
time: 232 us; the launch traced here: 231 us
  starting transfers between devices  99.7 us (43%)
  waiting for transfers between devices  56.1 us (24%)
  local copies, waits for them, and re-layouts  29.4 us (13%)
  other arithmetic  15.6 us (7%)
  blocking collectives  15.6 us (7%)
  matrix products  13.6 us (6%)
    ppermute x6, starting transfers between devices, gather_cols(): other = lax.ppermute(values, 'tp', partner_pairs(count, bit))  28.7 us
    all_to_all x1, blocking collectives, exchange_scatter_sum(): received = lax.all_to_all(blocks, 'tp', 0, 0, tiled=True)  15.6 us
    ppermute x3, starting transfers between devices, spread_requests(): other = lax.ppermute(send, 'tp', partner_pairs(count, bit))  14.9 us
    ppermute x3, starting transfers between devices, exchange_merge(): rows = merge_rows(rows, lax.ppermute(rows, 'tp', partner_pairs(count, bit)))  13.6 us
    ppermute x3, waiting for transfers between devices, scatter_sum(): values = keep + lax.ppermute(send, 'tp', partner_pairs(count, bit))  12.8 us
    ppermute x3, starting transfers between devices, scatter_sum(): values = keep + lax.ppermute(send, 'tp', partner_pairs(count, bit))  12.8 us
    ppermute x3, waiting for transfers between devices, exchange_sum(): values = values + lax.ppermute(values, 'tp', partner_pairs(count, bit))  12.2 us
    all_to_all x1, starting transfers between devices, exchange_gather(): received = lax.all_to_all(copies, 'tp', 0, 0, tiled=True)  10.3 us
  transfers between devices with their start and end apart: 22, of which 19 were waited for; matrix products, arithmetic and copies ran while one was open for 6% of the time, Pallas kernels for 0%

profile of v8, /device:TPU:1, one launch (start us, length us, event | category | flops | bytes accessed | tf_op | source)
XLA Modules:
  0.0 231.2 jit_solution(3155449681677294404)
XLA Ops:
  8.8 8.8 %collective-permute-start = (f32[32,3488]{1,0:T(8,128)S(1)}, f32[32,3488]{1,0:T(8,128)S(1)}, u32[]{:S(2)}, u32[]{:S(2)}) collective-permute-start(f32[32,3488]{1,0:T(8,128)S(1)} %constant_dynamic-slice_fusion.5), channel_id=1, source_target_pairs={{0,1},{1,0},{2,3},{3,2},{4,5},{5,4},{6,7},{7,6},{8,9},{9,8},{10,11... | collective-permute-start | bytes 1339400 | tf_op jit(solution)/shard_map/ppermute | solution.py:57
  19.4 2.1 collective-permute-start.1
  21.6 6.6 %collective-permute-done.1 = f32[32,1744]{1,0:T(8,128)S(1)} collective-permute-done((f32[32,1744]{1,0:T(8,128)S(1)}, f32[32,1744]{1,0:T(8,128)S(1)}, u32[]{:S(2)}, u32[]{:S(2)}) %collective-permute-start.1) | collective-permute-done | bytes 223264 | tf_op jit(solution)/shard_map/ppermute | solution.py:57
  30.5 5.0 %collective-permute-done.2 = f32[32,872]{1,0:T(8,128)S(1)} collective-permute-done((f32[32,872]{1,0:T(8,128)S(1)}, f32[32,872]{1,0:T(8,128)S(1)}, u32[]{:S(2)}, u32[]{:S(2)}) %collective-permute-start.2) | collective-permute-done | bytes 111648 | tf_op jit(solution)/shard_map/ppermute | solution.py:57
  35.6 2.1 collective-permute-start.3
  38.3 2.9 %collective-permute-done.3 = f32[32,872]{1,0:T(8,128)S(1)} collective-permute-done((f32[32,872]{1,0:T(8,128)S(1)}, f32[32,872]{1,0:T(8,128)S(1)}, u32[]{:S(2)}, u32[]{:S(2)}) %collective-permute-start.3) | collective-permute-done | bytes 111648 | tf_op jit(solution)/shard_map/ppermute | solution.py:87
  43.2 5.5 %collective-permute-done.4 = f32[32,872]{1,0:T(8,128)S(1)} collective-permute-done((f32[32,872]{1,0:T(8,128)S(1)}, f32[32,872]{1,0:T(8,128)S(1)}, u32[]{:S(2)}, u32[]{:S(2)}) %collective-permute-start.4) | collective-permute-done | bytes 111648 | tf_op jit(solution)/shard_map/ppermute | solution.py:87
  48.7 5.5 %collective-permute-start.5 = (f32[32,872]{1,0:T(8,128)S(1)}, f32[32,872]{1,0:T(8,128)S(1)}, u32[]{:S(2)}, u32[]{:S(2)}) collective-permute-start(f32[32,872]{1,0:T(8,128)S(1)} %add.258), channel_id=1, source_target_pairs={{0,32},{1,33},{2,34},{3,35},{4,36},{5,37},{6,38},{7,39},{8,40},{9,... | collective-permute-start | bytes 334856 | tf_op jit(solution)/shard_map/ppermute | solution.py:87
  54.3 3.8 %collective-permute-done.5 = f32[32,872]{1,0:T(8,128)S(1)} collective-permute-done((f32[32,872]{1,0:T(8,128)S(1)}, f32[32,872]{1,0:T(8,128)S(1)}, u32[]{:S(2)}, u32[]{:S(2)}) %collective-permute-start.5) | collective-permute-done | bytes 111648 | tf_op jit(solution)/shard_map/ppermute | solution.py:87
  59.1 3.0 %collective-permute-start.15 = (bf16[4,4,576]{2,1,0:T(4,128)(2,1)S(1)}, bf16[4,4,576]{2,1,0:T(4,128)(2,1)S(1)}, u32[]{:S(2)}, u32[]{:S(2)}) collective-permute-start(bf16[4,4,576]{2,1,0:T(4,128)(2,1)S(1)} %get-tuple-element.39), channel_id=1, source_target_pairs={{0,4},{1,5},{2,6},{3,7},{4,0},{5,1},{6,2},{7,3},{8,12},{9,13},{10,... | collective-permute-start | bytes 55304 | tf_op jit(solution)/shard_map/ppermute | solution.py:147
  62.2 2.9 %collective-permute-done.15 = bf16[4,4,576]{2,1,0:T(4,128)(2,1)S(1)} collective-permute-done((bf16[4,4,576]{2,1,0:T(4,128)(2,1)S(1)}, bf16[4,4,576]{2,1,0:T(4,128)(2,1)S(1)}, u32[]{:S(2)}, u32[]{:S(2)}) %collective-permute-start.15) | collective-permute-done | bytes 18464 | tf_op jit(solution)/shard_map/ppermute | solution.py:147
  65.3 2.3 %collective-permute-start.16 = (bf16[2,4,1152]{2,1,0:T(4,128)(2,1)S(1)}, bf16[2,4,1152]{2,1,0:T(4,128)(2,1)S(1)}, u32[]{:S(2)}, u32[]{:S(2)}) collective-permute-start(bf16[2,4,1152]{2,1,0:T(4,128)(2,1)S(1)} %get-tuple-element.45), channel_id=1, source_target_pairs={{0,2},{1,3},{2,0},{3,1},{4,6},{5,7},{6,4},{7,5},{8,10},{9,11},{10,... | collective-permute-start | bytes 55304 | tf_op jit(solution)/shard_map/ppermute | solution.py:147
  74.2 3.5 %collective-permute-start.6 = (bf16[32,288]{1,0:T(8,128)(2,1)S(1)}, bf16[32,288]{1,0:T(8,128)(2,1)S(1)}, u32[]{:S(2)}, u32[]{:S(2)}) collective-permute-start(bf16[32,288]{1,0:T(8,128)(2,1)S(1)} %reshape.381), channel_id=1, source_target_pairs={{0,4},{1,5},{2,6},{3,7},{4,0},{5,1},{6,2},{7,3},{8,12},{9,13},{10,... | collective-permute-start | bytes 55304 | tf_op jit(solution)/shard_map/ppermute | solution.py:67
  77.8 9.6 %collective-permute-start.17 = (bf16[1,4,2304]{2,1,0:T(4,128)(2,1)S(1)}, bf16[1,4,2304]{2,1,0:T(4,128)(2,1)S(1)}, u32[]{:S(2)}, u32[]{:S(2)}) collective-permute-start(bf16[1,4,2304]{2,1,0:T(4,128)(2,1)S(1)} %get-tuple-element.43), channel_id=1, source_target_pairs={{0,1},{1,0},{2,3},{3,2},{4,5},{5,4},{6,7},{7,6},{8,9},{9,8},{10,11... | collective-permute-start | bytes 55304 | tf_op jit(solution)/shard_map/ppermute | solution.py:147
  92.3 3.8 %collective-permute-start.8 = (bf16[32,1152]{1,0:T(8,128)(2,1)S(1)}, bf16[32,1152]{1,0:T(8,128)(2,1)S(1)}, u32[]{:S(2)}, u32[]{:S(2)}) collective-permute-start(bf16[32,1152]{1,0:T(8,128)(2,1)S(1)} %maximum_select_fusion.4), channel_id=1, source_target_pairs={{0,1},{1,0},{2,3},{3,2},{4,5},{5,4},{6,7},{7,6},{8,9},{9,8},{10,11... | collective-permute-start | bytes 221192 | tf_op jit(solution)/shard_map/ppermute | solution.py:67
  101.3 3.1 %fusion.87 = (f32[8,4,36]{1,2,0:T(8,128)}, f32[8,4,36,8]{3,1,2,0:T(4,128)}) fusion(bf16[8,8,36,64]{3,2,1,0:T(8,128)(2,1)} %reshape.383, bf16[8,4,36,64]{3,0,1,2:T(8,128)(2,1)S(1)} %pad_maximum_fusion.2, pred[8,8]{1,0:T(8,128)(4,1)S(1)} %broadcast_compare_fusion), kind=kOutput, calls=%fused_computation.196 | convolution fusion | flops 1206144 | bytes 483904 | tf_op jit(solution)/shard_map/rjhd,rphd->rjhp/dot_general | solution.py:238
  116.1 2.3 collective-permute-start.9
  120.4 3.3 %collective-permute-start.10 = (f32[288,66]{1,0:T(8,128)S(1)}, f32[288,66]{1,0:T(8,128)S(1)}, u32[]{:S(2)}, u32[]{:S(2)}) collective-permute-start(f32[288,66]{1,0:T(8,128)S(1)} %get-tuple-element.31), channel_id=1, source_target_pairs={{0,2},{1,3},{2,0},{3,1},{4,6},{5,7},{6,4},{7,5},{8,10},{9,11},{10,... | collective-permute-start | bytes 228104 | tf_op jit(solution)/shard_map/ppermute | solution.py:114
  123.9 3.4 %collective-permute-done.10 = f32[288,66]{1,0:T(8,128)S(1)} collective-permute-done((f32[288,66]{1,0:T(8,128)S(1)}, f32[288,66]{1,0:T(8,128)S(1)}, u32[]{:S(2)}, u32[]{:S(2)}) %collective-permute-start.10) | collective-permute-done | bytes 76064 | tf_op jit(solution)/shard_map/ppermute | solution.py:114
  127.9 4.3 %collective-permute-start.11 = (f32[144,66]{1,0:T(8,128)S(1)}, f32[144,66]{1,0:T(8,128)S(1)}, u32[]{:S(2)}, u32[]{:S(2)}) collective-permute-start(f32[144,66]{1,0:T(8,128)S(1)} %get-tuple-element.32), channel_id=1, source_target_pairs={{0,4},{1,5},{2,6},{3,7},{4,0},{5,1},{6,2},{7,3},{8,12},{9,13},{10,... | collective-permute-start | bytes 114056 | tf_op jit(solution)/shard_map/ppermute | solution.py:114
  132.5 2.0 collective-permute-done.11
  135.0 2.3 collective-permute-start.12
  137.5 2.5 %collective-permute-done.12 = f32[144,66]{1,0:T(8,128)S(1)} collective-permute-done((f32[144,66]{1,0:T(8,128)S(1)}, f32[144,66]{1,0:T(8,128)S(1)}, u32[]{:S(2)}, u32[]{:S(2)}) %collective-permute-start.12) | collective-permute-done | bytes 38048 | tf_op jit(solution)/shard_map/ppermute | solution.py:94
  140.5 4.0 %collective-permute-start.13 = (f32[144,66]{1,0:T(8,128)S(1)}, f32[144,66]{1,0:T(8,128)S(1)}, u32[]{:S(2)}, u32[]{:S(2)}) collective-permute-start(f32[144,66]{1,0:T(8,128)S(1)} %pad_maximum_fusion.4), channel_id=1, source_target_pairs={{0,16},{1,17},{2,18},{3,19},{4,20},{5,21},{6,22},{7,23},{8,24},{9,... | collective-permute-start | bytes 114056 | tf_op jit(solution)/shard_map/ppermute | solution.py:94
  146.9 7.3 %collective-permute-start.14 = (f32[144,66]{1,0:T(8,128)S(1)}, f32[144,66]{1,0:T(8,128)S(1)}, u32[]{:S(2)}, u32[]{:S(2)}) collective-permute-start(f32[144,66]{1,0:T(8,128)S(1)} %pad_maximum_fusion.5), channel_id=1, source_target_pairs={{0,32},{1,33},{2,34},{3,35},{4,36},{5,37},{6,38},{7,39},{8,40},{9,... | collective-permute-start | bytes 114056 | tf_op jit(solution)/shard_map/ppermute | solution.py:94
  157.2 4.9 %collective-permute-start.18 = (bf16[144,64]{1,0:T(8,128)(2,1)S(1)}, bf16[144,64]{1,0:T(8,128)(2,1)S(1)}, u32[]{:S(2)}, u32[]{:S(2)}) collective-permute-start(bf16[144,64]{1,0:T(8,128)(2,1)S(1)} %fusion.49), channel_id=1, source_target_pairs={{0,4},{1,5},{2,6},{3,7},{4,0},{5,1},{6,2},{7,3},{8,12},{9,13},{10,... | collective-permute-start | bytes 55304 | tf_op jit(solution)/shard_map/ppermute | solution.py:67
  163.4 3.6 %collective-permute-start.19 = (bf16[288,64]{1,0:T(8,128)(2,1)S(1)}, bf16[288,64]{1,0:T(8,128)(2,1)S(1)}, u32[]{:S(2)}, u32[]{:S(2)}) collective-permute-start(bf16[288,64]{1,0:T(8,128)(2,1)S(1)} %maximum_select_fusion.5), channel_id=1, source_target_pairs={{0,2},{1,3},{2,0},{3,1},{4,6},{5,7},{6,4},{7,5},{8,10},{9,11},{10,... | collective-permute-start | bytes 110600 | tf_op jit(solution)/shard_map/ppermute | solution.py:67
  167.1 2.1 collective-permute-done.19
  169.2 10.9 %collective-permute-start.20 = (bf16[576,64]{1,0:T(8,128)(2,1)S(1)}, bf16[576,64]{1,0:T(8,128)(2,1)S(1)}, u32[]{:S(2)}, u32[]{:S(2)}) collective-permute-start(bf16[576,64]{1,0:T(8,128)(2,1)S(1)} %maximum_select_fusion.3), channel_id=1, source_target_pairs={{0,1},{1,0},{2,3},{3,2},{4,5},{5,4},{6,7},{7,6},{8,9},{9,8},{10,11... | collective-permute-start | bytes 221192 | tf_op jit(solution)/shard_map/ppermute | solution.py:67
  182.9 10.3 %all-to-all-start = ((bf16[64,2,576]{2,1,0:T(2,128)(2,1)}), bf16[64,2,576]{2,1,0:T(2,128)(2,1)S(1)}, u32[]{:S(2)}, u32[]{:S(2)}) async-start(bf16[64,2,576]{2,1,0:T(2,128)(2,1)} %reshape.422), calls=%async_computation | async-start | bytes 327680 | tf_op jit(solution)/shard_map/all_to_all | solution.py:129
  195.2 9.7 %all-to-all-done = bf16[64,2,576]{2,1,0:T(2,128)(2,1)S(1)} async-done(((bf16[64,2,576]{2,1,0:T(2,128)(2,1)}), bf16[64,2,576]{2,1,0:T(2,128)(2,1)S(1)}, u32[]{:S(2)}, u32[]{:S(2)}) %all-to-all-start) | async-done | bytes 147488 | tf_op jit(solution)/shard_map/all_to_all | solution.py:129
  213.0 15.6 %all_to_all.10 = bf16[64,2,576]{2,1,0:T(2,128)(2,1)S(1)} all-to-all(bf16[64,2,576]{2,1,0:T(2,128)(2,1)S(1)} %reshape.424), channel_id=1, replica_groups=mesh['rep'=8,'tp'=64] {'tp'}, dimensions={0} | all-to-all | bytes 294912 | tf_op jit(solution)/shard_map/all_to_all | solution.py:134
  (199 shorter events, 70.7 us)
Async XLA Ops:
  0.0 209.9 %copy-start = (bf16[2304,180]{0,1:T(8,128)(2,1)S(1)}, bf16[2304,180]{0,1:T(8,128)(2,1)}, u32[]{:S(2)}) copy-start(bf16[2304,180]{0,1:T(8,128)(2,1)} %param.29) | copy-start | bytes 2488324
  6.8 10.8 %copy-start.19 = (s32[8]{0:T(128)S(1)}, s32[8]{0:T(128)}, u32[]{:S(2)}) copy-start(s32[8]{0:T(128)} %param.25) | copy-start | bytes 100
  8.8 10.2 %collective-permute-start = (f32[32,3488]{1,0:T(8,128)S(1)}, f32[32,3488]{1,0:T(8,128)S(1)}, u32[]{:S(2)}, u32[]{:S(2)}) collective-permute-start(f32[32,3488]{1,0:T(8,128)S(1)} %constant_dynamic-slice_fusion.5), channel_id=1, source_target_pairs={{0,1},{1,0},{2,3},{3,2},{4,5},{5,4},{6,7},{7,6},{8,9},{9,8},{10,11... | collective-permute-start | bytes 1339400 | tf_op jit(solution)/shard_map/ppermute | solution.py:57
  19.2 43.0 %copy-start.20 = (s32[8]{0:T(128)S(1)}, s32[8]{0:T(128)}, u32[]{:S(2)}) copy-start(s32[8]{0:T(128)} %param.24) | copy-start | bytes 100
  19.3 48.8 %copy-start.5 = (bf16[3,32,2304]{2,1,0:T(8,128)(2,1)S(1)}, bf16[3,32,2304]{2,1,0:T(8,128)(2,1)}, u32[]{:S(2)}) copy-start(bf16[3,32,2304]{2,1,0:T(8,128)(2,1)} %param.20) | copy-start | bytes 1327108
  19.4 8.8 %collective-permute-start.1 = (f32[32,1744]{1,0:T(8,128)S(1)}, f32[32,1744]{1,0:T(8,128)S(1)}, u32[]{:S(2)}, u32[]{:S(2)}) collective-permute-start(f32[32,1744]{1,0:T(8,128)S(1)} %constant_dynamic-slice_fusion.4), channel_id=1, source_target_pairs={{0,2},{1,3},{2,0},{3,1},{4,6},{5,7},{6,4},{7,5},{8,10},{9,11},{10,... | collective-permute-start | bytes 669704 | tf_op jit(solution)/shard_map/ppermute | solution.py:57
  28.4 7.0 %collective-permute-start.2 = (f32[32,872]{1,0:T(8,128)S(1)}, f32[32,872]{1,0:T(8,128)S(1)}, u32[]{:S(2)}, u32[]{:S(2)}) collective-permute-start(f32[32,872]{1,0:T(8,128)S(1)} %constant_dynamic-slice_fusion.3), channel_id=1, source_target_pairs={{0,4},{1,5},{2,6},{3,7},{4,0},{5,1},{6,2},{7,3},{8,12},{9,13},{10,... | collective-permute-start | bytes 334856 | tf_op jit(solution)/shard_map/ppermute | solution.py:57
  35.6 34.2 %copy-start.8 = (bf16[8,8,2304]{2,1,0:T(8,128)(2,1)S(1)}, bf16[8,8,2304]{2,1,0:T(8,128)(2,1)}, u32[]{:S(2)}) copy-start(bf16[8,8,2304]{2,1,0:T(8,128)(2,1)} %param.22) | copy-start | bytes 884740
  35.6 5.7 %collective-permute-start.3 = (f32[32,872]{1,0:T(8,128)S(1)}, f32[32,872]{1,0:T(8,128)S(1)}, u32[]{:S(2)}, u32[]{:S(2)}) collective-permute-start(f32[32,872]{1,0:T(8,128)S(1)} %dynamic-slice_add_fusion.2), channel_id=1, source_target_pairs={{0,8},{1,9},{2,10},{3,11},{4,12},{5,13},{6,14},{7,15},{8,0},{9,1},... | collective-permute-start | bytes 334856 | tf_op jit(solution)/shard_map/ppermute | solution.py:87
  41.3 7.4 %collective-permute-start.4 = (f32[32,872]{1,0:T(8,128)S(1)}, f32[32,872]{1,0:T(8,128)S(1)}, u32[]{:S(2)}, u32[]{:S(2)}) collective-permute-start(f32[32,872]{1,0:T(8,128)S(1)} %add.257), channel_id=1, source_target_pairs={{0,16},{1,17},{2,18},{3,19},{4,20},{5,21},{6,22},{7,23},{8,24},{9,... | collective-permute-start | bytes 334856 | tf_op jit(solution)/shard_map/ppermute | solution.py:87
  48.7 9.4 %collective-permute-start.5 = (f32[32,872]{1,0:T(8,128)S(1)}, f32[32,872]{1,0:T(8,128)S(1)}, u32[]{:S(2)}, u32[]{:S(2)}) collective-permute-start(f32[32,872]{1,0:T(8,128)S(1)} %add.258), channel_id=1, source_target_pairs={{0,32},{1,33},{2,34},{3,35},{4,36},{5,37},{6,38},{7,39},{8,40},{9,... | collective-permute-start | bytes 334856 | tf_op jit(solution)/shard_map/ppermute | solution.py:87
  58.2 13.0 %copy-start.9 = (bf16[8,8,2304]{2,1,0:T(8,128)(2,1)S(1)}, bf16[8,8,2304]{2,1,0:T(8,128)(2,1)}, u32[]{:S(2)}) copy-start(bf16[8,8,2304]{2,1,0:T(8,128)(2,1)} %param.23) | copy-start | bytes 884740
  59.1 6.0 %collective-permute-start.15 = (bf16[4,4,576]{2,1,0:T(4,128)(2,1)S(1)}, bf16[4,4,576]{2,1,0:T(4,128)(2,1)S(1)}, u32[]{:S(2)}, u32[]{:S(2)}) collective-permute-start(bf16[4,4,576]{2,1,0:T(4,128)(2,1)S(1)} %get-tuple-element.39), channel_id=1, source_target_pairs={{0,4},{1,5},{2,6},{3,7},{4,0},{5,1},{6,2},{7,3},{8,12},{9,13},{10,... | collective-permute-start | bytes 55304 | tf_op jit(solution)/shard_map/ppermute | solution.py:147
  62.2 35.8 %copy-start.17 = (pred[8,3]{0,1:T(4,128)(4,1)}, pred[8,3]{0,1:T(4,128)(4,1)S(1)}, u32[]{:S(2)}) copy-start(pred[8,3]{0,1:T(4,128)(4,1)S(1)} %iota_compare_fusion.3) | copy-start | bytes 76
  62.2 10.2 %copy-start.6 = (bf16[3,32,2304]{2,1,0:T(8,128)(2,1)S(1)}, bf16[3,32,2304]{2,1,0:T(8,128)(2,1)}, u32[]{:S(2)}) copy-start(bf16[3,32,2304]{2,1,0:T(8,128)(2,1)} %param.21) | copy-start | bytes 1327108
  65.3 12.4 %collective-permute-start.16 = (bf16[2,4,1152]{2,1,0:T(4,128)(2,1)S(1)}, bf16[2,4,1152]{2,1,0:T(4,128)(2,1)S(1)}, u32[]{:S(2)}, u32[]{:S(2)}) collective-permute-start(bf16[2,4,1152]{2,1,0:T(4,128)(2,1)S(1)} %get-tuple-element.45), channel_id=1, source_target_pairs={{0,2},{1,3},{2,0},{3,1},{4,6},{5,7},{6,4},{7,5},{8,10},{9,11},{10,... | collective-permute-start | bytes 55304 | tf_op jit(solution)/shard_map/ppermute | solution.py:147
  74.2 13.2 %collective-permute-start.6 = (bf16[32,288]{1,0:T(8,128)(2,1)S(1)}, bf16[32,288]{1,0:T(8,128)(2,1)S(1)}, u32[]{:S(2)}, u32[]{:S(2)}) collective-permute-start(bf16[32,288]{1,0:T(8,128)(2,1)S(1)} %reshape.381), channel_id=1, source_target_pairs={{0,4},{1,5},{2,6},{3,7},{4,0},{5,1},{6,2},{7,3},{8,12},{9,13},{10,... | collective-permute-start | bytes 55304 | tf_op jit(solution)/shard_map/ppermute | solution.py:67
  77.8 11.7 %collective-permute-start.17 = (bf16[1,4,2304]{2,1,0:T(4,128)(2,1)S(1)}, bf16[1,4,2304]{2,1,0:T(4,128)(2,1)S(1)}, u32[]{:S(2)}, u32[]{:S(2)}) collective-permute-start(bf16[1,4,2304]{2,1,0:T(4,128)(2,1)S(1)} %get-tuple-element.43), channel_id=1, source_target_pairs={{0,1},{1,0},{2,3},{3,2},{4,5},{5,4},{6,7},{7,6},{8,9},{9,8},{10,11... | collective-permute-start | bytes 55304 | tf_op jit(solution)/shard_map/ppermute | solution.py:147
  87.5 4.7 %collective-permute-start.7 = (bf16[32,576]{1,0:T(8,128)(2,1)S(1)}, bf16[32,576]{1,0:T(8,128)(2,1)S(1)}, u32[]{:S(2)}, u32[]{:S(2)}) collective-permute-start(bf16[32,576]{1,0:T(8,128)(2,1)S(1)} %maximum_select_fusion.6), channel_id=1, source_target_pairs={{0,2},{1,3},{2,0},{3,1},{4,6},{5,7},{6,4},{7,5},{8,10},{9,11},{10,... | collective-permute-start | bytes 110600 | tf_op jit(solution)/shard_map/ppermute | solution.py:67
  92.3 4.6 %collective-permute-start.8 = (bf16[32,1152]{1,0:T(8,128)(2,1)S(1)}, bf16[32,1152]{1,0:T(8,128)(2,1)S(1)}, u32[]{:S(2)}, u32[]{:S(2)}) collective-permute-start(bf16[32,1152]{1,0:T(8,128)(2,1)S(1)} %maximum_select_fusion.4), channel_id=1, source_target_pairs={{0,1},{1,0},{2,3},{3,2},{4,5},{5,4},{6,7},{7,6},{8,9},{9,8},{10,11... | collective-permute-start | bytes 221192 | tf_op jit(solution)/shard_map/ppermute | solution.py:67
  116.1 3.5 %collective-permute-start.9 = (f32[576,66]{1,0:T(8,128)S(1)}, f32[576,66]{1,0:T(8,128)S(1)}, u32[]{:S(2)}, u32[]{:S(2)}) collective-permute-start(f32[576,66]{1,0:T(8,128)S(1)} %constant_dynamic-slice_fusion.2), channel_id=1, source_target_pairs={{0,1},{1,0},{2,3},{3,2},{4,5},{5,4},{6,7},{7,6},{8,9},{9,8},{10,11... | collective-permute-start | bytes 456200 | tf_op jit(solution)/shard_map/ppermute | solution.py:114
  120.2 17.1 %copy-start.21 = (pred[4,4]{0,1:T(4,128)(4,1)S(1)}, pred[4,4]{0,1:T(4,128)(4,1)}, u32[]{:S(2)}) copy-start(pred[4,4]{0,1:T(4,128)(4,1)} %iota_compare_fusion.2) | copy-start | bytes 52
  120.4 7.0 %collective-permute-start.10 = (f32[288,66]{1,0:T(8,128)S(1)}, f32[288,66]{1,0:T(8,128)S(1)}, u32[]{:S(2)}, u32[]{:S(2)}) collective-permute-start(f32[288,66]{1,0:T(8,128)S(1)} %get-tuple-element.31), channel_id=1, source_target_pairs={{0,2},{1,3},{2,0},{3,1},{4,6},{5,7},{6,4},{7,5},{8,10},{9,11},{10,... | collective-permute-start | bytes 228104 | tf_op jit(solution)/shard_map/ppermute | solution.py:114
  127.9 6.6 %collective-permute-start.11 = (f32[144,66]{1,0:T(8,128)S(1)}, f32[144,66]{1,0:T(8,128)S(1)}, u32[]{:S(2)}, u32[]{:S(2)}) collective-permute-start(f32[144,66]{1,0:T(8,128)S(1)} %get-tuple-element.32), channel_id=1, source_target_pairs={{0,4},{1,5},{2,6},{3,7},{4,0},{5,1},{6,2},{7,3},{8,12},{9,13},{10,... | collective-permute-start | bytes 114056 | tf_op jit(solution)/shard_map/ppermute | solution.py:114
  135.0 5.1 %collective-permute-start.12 = (f32[144,66]{1,0:T(8,128)S(1)}, f32[144,66]{1,0:T(8,128)S(1)}, u32[]{:S(2)}, u32[]{:S(2)}) collective-permute-start(f32[144,66]{1,0:T(8,128)S(1)} %pad_maximum_fusion.3), channel_id=1, source_target_pairs={{0,8},{1,9},{2,10},{3,11},{4,12},{5,13},{6,14},{7,15},{8,0},{9,1},... | collective-permute-start | bytes 114056 | tf_op jit(solution)/shard_map/ppermute | solution.py:94
  140.5 6.0 %collective-permute-start.13 = (f32[144,66]{1,0:T(8,128)S(1)}, f32[144,66]{1,0:T(8,128)S(1)}, u32[]{:S(2)}, u32[]{:S(2)}) collective-permute-start(f32[144,66]{1,0:T(8,128)S(1)} %pad_maximum_fusion.4), channel_id=1, source_target_pairs={{0,16},{1,17},{2,18},{3,19},{4,20},{5,21},{6,22},{7,23},{8,24},{9,... | collective-permute-start | bytes 114056 | tf_op jit(solution)/shard_map/ppermute | solution.py:94
  144.7 36.5 %copy-start.10 = (bf16[2304,36]{0,1:T(8,128)(2,1)S(1)}, bf16[2304,36]{0,1:T(8,128)(2,1)}, u32[]{:S(2)}) copy-start(bf16[2304,36]{0,1:T(8,128)(2,1)} %param.19) | copy-start | bytes 497668
  146.9 9.4 %collective-permute-start.14 = (f32[144,66]{1,0:T(8,128)S(1)}, f32[144,66]{1,0:T(8,128)S(1)}, u32[]{:S(2)}, u32[]{:S(2)}) collective-permute-start(f32[144,66]{1,0:T(8,128)S(1)} %pad_maximum_fusion.5), channel_id=1, source_target_pairs={{0,32},{1,33},{2,34},{3,35},{4,36},{5,37},{6,38},{7,39},{8,40},{9,... | collective-permute-start | bytes 114056 | tf_op jit(solution)/shard_map/ppermute | solution.py:94
  157.2 6.3 %collective-permute-start.18 = (bf16[144,64]{1,0:T(8,128)(2,1)S(1)}, bf16[144,64]{1,0:T(8,128)(2,1)S(1)}, u32[]{:S(2)}, u32[]{:S(2)}) collective-permute-start(bf16[144,64]{1,0:T(8,128)(2,1)S(1)} %fusion.49), channel_id=1, source_target_pairs={{0,4},{1,5},{2,6},{3,7},{4,0},{5,1},{6,2},{7,3},{8,12},{9,13},{10,... | collective-permute-start | bytes 55304 | tf_op jit(solution)/shard_map/ppermute | solution.py:67
  163.4 5.7 %collective-permute-start.19 = (bf16[288,64]{1,0:T(8,128)(2,1)S(1)}, bf16[288,64]{1,0:T(8,128)(2,1)S(1)}, u32[]{:S(2)}, u32[]{:S(2)}) collective-permute-start(bf16[288,64]{1,0:T(8,128)(2,1)S(1)} %maximum_select_fusion.5), channel_id=1, source_target_pairs={{0,2},{1,3},{2,0},{3,1},{4,6},{5,7},{6,4},{7,5},{8,10},{9,11},{10,... | collective-permute-start | bytes 110600 | tf_op jit(solution)/shard_map/ppermute | solution.py:67
  169.2 11.6 %collective-permute-start.20 = (bf16[576,64]{1,0:T(8,128)(2,1)S(1)}, bf16[576,64]{1,0:T(8,128)(2,1)S(1)}, u32[]{:S(2)}, u32[]{:S(2)}) collective-permute-start(bf16[576,64]{1,0:T(8,128)(2,1)S(1)} %maximum_select_fusion.3), channel_id=1, source_target_pairs={{0,1},{1,0},{2,3},{3,2},{4,5},{5,4},{6,7},{7,6},{8,9},{9,8},{10,11... | collective-permute-start | bytes 221192 | tf_op jit(solution)/shard_map/ppermute | solution.py:67
  182.9 22.0 %all-to-all-start = ((bf16[64,2,576]{2,1,0:T(2,128)(2,1)}), bf16[64,2,576]{2,1,0:T(2,128)(2,1)S(1)}, u32[]{:S(2)}, u32[]{:S(2)}) async-start(bf16[64,2,576]{2,1,0:T(2,128)(2,1)} %reshape.422), calls=%async_computation | async-start | bytes 327680 | tf_op jit(solution)/shard_map/all_to_all | solution.py:129
  (13 other events, 41.7 us)

commit v9 on v8

--- a/solution.py
+++ b/solution.py
@@ -135,22 +135,32 @@
     return jnp.sum(received.astype(jnp.float32), axis=0)
 
 
-def spread_requests(values, bits):
+def gather_and_spread(queries, kv, bits):
     count, _ = tp_bits()
     own_rank = lax.axis_index("tp")
-    for step, bit in enumerate(reversed(bits)):
+    query_rows, _ = queries.shape
+    for bit in reversed(bits):
         side = (own_rank // bit) % 2
-        held, tokens, width = values.shape
-        split = values.reshape(held // 2, 2, tokens, width)
+        held, tokens, width = kv.shape
+        split = kv.reshape(held // 2, 2, tokens, width)
         keep = lax.dynamic_index_in_dim(split, side, axis=1, keepdims=False)
         send = lax.dynamic_index_in_dim(split, 1 - side, axis=1, keepdims=False)
-        other = lax.ppermute(send, "tp", partner_pairs(count, bit))
-        values = jnp.where(
+        query_width = queries.shape[1]
+        payload = jnp.concatenate([queries, send.reshape(query_rows, -1)], axis=1)
+        other = lax.ppermute(payload, "tp", partner_pairs(count, bit))
+        other_queries = other[:, :query_width]
+        other_kv = other[:, query_width:].reshape(send.shape)
+        queries = jnp.where(
             side == 0,
-            jnp.concatenate([keep, other], axis=2),
-            jnp.concatenate([other, keep], axis=2),
+            jnp.concatenate([queries, other_queries], axis=1),
+            jnp.concatenate([other_queries, queries], axis=1),
         )
-    return values
+        kv = jnp.where(
+            side == 0,
+            jnp.concatenate([keep, other_kv], axis=2),
+            jnp.concatenate([other_kv, keep], axis=2),
+        )
+    return queries, kv
 
 
 def reverse_blocks(values, count):
@@ -210,10 +220,12 @@
     own_block = own_block.reshape(all_tokens, -1, block + 1)
     inv_attn = lax.rsqrt(own_block[:, 0, block] / model_width + EPSILON)
     own_qkv = (inv_attn[:, None, None] * own_block[:, :, :block]).astype(jnp.bfloat16)
-    query_cols = gather_cols(own_qkv[:, :, :query_block].reshape(all_tokens, -1), bits=near_bits)
     own_kv = own_qkv[:, :, query_block:].reshape(requests, NEW, -1)
     own_request = kept_position(near_bits)
-    request_kv = spread_requests(own_kv, near_bits).reshape(NEW, 2 * model_width)
+    query_cols, request_kv = gather_and_spread(
+        own_qkv[:, :, :query_block].reshape(all_tokens, -1), own_kv, near_bits
+    )
+    request_kv = request_kv.reshape(NEW, 2 * model_width)
     own_lengths = jnp.broadcast_to(private_lengths[:, None], (requests, NEW)).reshape(all_tokens)
     places = (
         prefix_block * lax.axis_size("tp")

time: 232 us -> 225 us (0.970)
  starting transfers between devices: 99.7 us -> 85.9 us
  waiting for transfers between devices: 56.1 us -> 59.4 us
    ppermute x6 -> x3, starting transfers between devices: 28.7 us -> 17.6 us  [gather_cols(): other = lax.ppermute(values, 'tp', partner_pairs(count, bit))]
    ppermute x6 -> x3, waiting for transfers between devices: 5.96 us -> 5.24 us  [gather_cols(): other = lax.ppermute(values, 'tp', partner_pairs(count, bit))]
    unnamed x49 -> x43, local copies, waits for them, and re-layouts: 6.66 us -> 7.13 us
  transfers between devices with their start and end apart: 22 -> 19, of which waited for: 19 -> 18; matrix products, arithmetic and copies ran while one was open for 6% -> 5% of each run, Pallas kernels for 0% -> 0%
where the time goes in v9:
time: 225 us; the launch traced here: 224 us
  starting transfers between devices  85.9 us (38%)
  waiting for transfers between devices  59.4 us (26%)
  local copies, waits for them, and re-layouts  31.5 us (14%)
  other arithmetic  16.7 us (7%)
  blocking collectives  15.6 us (7%)
  matrix products  13.5 us (6%)
    ppermute x3, starting transfers between devices, gather_cols(): other = lax.ppermute(values, 'tp', partner_pairs(count, bit))  17.6 us
    all_to_all x1, blocking collectives, exchange_scatter_sum(): received = lax.all_to_all(blocks, 'tp', 0, 0, tiled=True)  15.6 us
    ppermute x3, starting transfers between devices, gather_and_spread(): other = lax.ppermute(payload, 'tp', partner_pairs(count, bit))  14.5 us
    ppermute x3, waiting for transfers between devices, scatter_sum(): values = keep + lax.ppermute(send, 'tp', partner_pairs(count, bit))  12.8 us
    ppermute x3, waiting for transfers between devices, exchange_sum(): values = values + lax.ppermute(values, 'tp', partner_pairs(count, bit))  12.8 us
    ppermute x3, starting transfers between devices, scatter_sum(): values = keep + lax.ppermute(send, 'tp', partner_pairs(count, bit))  12.8 us
    ppermute x3, starting transfers between devices, exchange_merge(): rows = merge_rows(rows, lax.ppermute(rows, 'tp', partner_pairs(count, bit)))  11.8 us
    all_to_all x1, starting transfers between devices, exchange_gather(): received = lax.all_to_all(copies, 'tp', 0, 0, tiled=True)  10.3 us
  transfers between devices with their start and end apart: 19, of which 18 were waited for; matrix products, arithmetic and copies ran while one was open for 5% of the time, Pallas kernels for 0%

profile of v9, /device:TPU:1, one launch (start us, length us, event | category | flops | bytes accessed | tf_op | source)
XLA Modules:
  0.0 223.8 jit_solution(9831336678628294311)
XLA Ops:
  8.8 8.8 %collective-permute-start = (f32[32,3488]{1,0:T(8,128)S(1)}, f32[32,3488]{1,0:T(8,128)S(1)}, u32[]{:S(2)}, u32[]{:S(2)}) collective-permute-start(f32[32,3488]{1,0:T(8,128)S(1)} %constant_dynamic-slice_fusion.7), channel_id=1, source_target_pairs={{0,1},{1,0},{2,3},{3,2},{4,5},{5,4},{6,7},{7,6},{8,9},{9,8},{10,11... | collective-permute-start | bytes 1339400 | tf_op jit(solution)/shard_map/ppermute | solution.py:57
  21.4 6.6 %collective-permute-done.1 = f32[32,1744]{1,0:T(8,128)S(1)} collective-permute-done((f32[32,1744]{1,0:T(8,128)S(1)}, f32[32,1744]{1,0:T(8,128)S(1)}, u32[]{:S(2)}, u32[]{:S(2)}) %collective-permute-start.1) | collective-permute-done | bytes 223264 | tf_op jit(solution)/shard_map/ppermute | solution.py:57
  28.3 2.1 collective-permute-start.2
  30.5 5.0 %collective-permute-done.2 = f32[32,872]{1,0:T(8,128)S(1)} collective-permute-done((f32[32,872]{1,0:T(8,128)S(1)}, f32[32,872]{1,0:T(8,128)S(1)}, u32[]{:S(2)}, u32[]{:S(2)}) %collective-permute-start.2) | collective-permute-done | bytes 111648 | tf_op jit(solution)/shard_map/ppermute | solution.py:57
  37.6 3.5 %collective-permute-done.3 = f32[32,872]{1,0:T(8,128)S(1)} collective-permute-done((f32[32,872]{1,0:T(8,128)S(1)}, f32[32,872]{1,0:T(8,128)S(1)}, u32[]{:S(2)}, u32[]{:S(2)}) %collective-permute-start.3) | collective-permute-done | bytes 111648 | tf_op jit(solution)/shard_map/ppermute | solution.py:87
  43.1 5.5 %collective-permute-done.4 = f32[32,872]{1,0:T(8,128)S(1)} collective-permute-done((f32[32,872]{1,0:T(8,128)S(1)}, f32[32,872]{1,0:T(8,128)S(1)}, u32[]{:S(2)}, u32[]{:S(2)}) %collective-permute-start.4) | collective-permute-done | bytes 111648 | tf_op jit(solution)/shard_map/ppermute | solution.py:87
  48.6 5.7 %collective-permute-start.5 = (f32[32,872]{1,0:T(8,128)S(1)}, f32[32,872]{1,0:T(8,128)S(1)}, u32[]{:S(2)}, u32[]{:S(2)}) collective-permute-start(f32[32,872]{1,0:T(8,128)S(1)} %add.255), channel_id=1, source_target_pairs={{0,32},{1,33},{2,34},{3,35},{4,36},{5,37},{6,38},{7,39},{8,40},{9,... | collective-permute-start | bytes 334856 | tf_op jit(solution)/shard_map/ppermute | solution.py:87
  54.3 3.8 %collective-permute-done.5 = f32[32,872]{1,0:T(8,128)S(1)} collective-permute-done((f32[32,872]{1,0:T(8,128)S(1)}, f32[32,872]{1,0:T(8,128)S(1)}, u32[]{:S(2)}, u32[]{:S(2)}) %collective-permute-start.5) | collective-permute-done | bytes 111648 | tf_op jit(solution)/shard_map/ppermute | solution.py:87
  59.4 3.1 %collective-permute-start.6 = (bf16[32,576]{1,0:T(8,128)(2,1)S(1)}, bf16[32,576]{1,0:T(8,128)(2,1)S(1)}, u32[]{:S(2)}, u32[]{:S(2)}) collective-permute-start(bf16[32,576]{1,0:T(8,128)(2,1)S(1)} %pad_maximum_fusion.8), channel_id=1, source_target_pairs={{0,4},{1,5},{2,6},{3,7},{4,0},{5,1},{6,2},{7,3},{8,12},{9,13},{10,... | collective-permute-start | bytes 110600 | tf_op jit(solution)/shard_map/ppermute | solution.py:150
  62.6 3.1 %collective-permute-done.6 = bf16[32,576]{1,0:T(8,128)(2,1)S(1)} collective-permute-done((bf16[32,576]{1,0:T(8,128)(2,1)S(1)}, bf16[32,576]{1,0:T(8,128)(2,1)S(1)}, u32[]{:S(2)}, u32[]{:S(2)}) %collective-permute-start.6) | collective-permute-done | bytes 36896 | tf_op jit(solution)/shard_map/ppermute | solution.py:150
  66.3 2.2 collective-permute-start.7
  76.3 9.2 %collective-permute-start.8 = (bf16[32,1440]{1,0:T(8,128)(2,1)S(1)}, bf16[32,1440]{1,0:T(8,128)(2,1)S(1)}, u32[]{:S(2)}, u32[]{:S(2)}) collective-permute-start(bf16[32,1440]{1,0:T(8,128)(2,1)S(1)} %pad_maximum_fusion.3), channel_id=1, source_target_pairs={{0,1},{1,0},{2,3},{3,2},{4,5},{5,4},{6,7},{7,6},{8,9},{9,8},{10,11... | collective-permute-start | bytes 276488 | tf_op jit(solution)/shard_map/ppermute | solution.py:150
  90.6 3.1 %fusion.89 = (f32[8,4,36]{1,2,0:T(8,128)}, f32[8,4,36,8]{3,1,2,0:T(4,128)}) fusion(bf16[8,8,36,64]{3,2,1,0:T(8,128)(2,1)} %reshape.408, bf16[8,4,36,64]{3,0,1,2:T(8,128)(2,1)S(1)} %pad_maximum_fusion.2, pred[8,8]{1,0:T(8,128)(4,1)S(1)} %broadcast_compare_fusion), kind=kOutput, calls=%fused_computation.201 | convolution fusion | flops 1206144 | bytes 483904 | tf_op jit(solution)/shard_map/rjhd,rphd->rjhp/dot_general | solution.py:250
  98.9 2.4 %fusion.32 = f32[8,4,36]{1,2,0:T(8,128)} fusion(f32[8,4,36,8]{3,1,2,0:T(4,128)} %get-tuple-element.57, f32[8,4,36]{1,2,0:T(8,128)S(1)} %copy.163), kind=kLoop, calls=%fused_computation.43 | loop fusion | flops 17280 | bytes 46080 | tf_op jit(solution)/shard_map/reduce_sum | solution.py:257
  109.1 2.3 %collective-permute-start.9 = (f32[576,66]{1,0:T(8,128)S(1)}, f32[576,66]{1,0:T(8,128)S(1)}, u32[]{:S(2)}, u32[]{:S(2)}) collective-permute-start(f32[576,66]{1,0:T(8,128)S(1)} %constant_dynamic-slice_fusion), channel_id=1, source_target_pairs={{0,1},{1,0},{2,3},{3,2},{4,5},{5,4},{6,7},{7,6},{8,9},{9,8},{10,11... | collective-permute-start | bytes 456200 | tf_op jit(solution)/shard_map/ppermute | solution.py:114
  113.4 3.3 %collective-permute-start.10 = (f32[288,66]{1,0:T(8,128)S(1)}, f32[288,66]{1,0:T(8,128)S(1)}, u32[]{:S(2)}, u32[]{:S(2)}) collective-permute-start(f32[288,66]{1,0:T(8,128)S(1)} %get-tuple-element.31), channel_id=1, source_target_pairs={{0,2},{1,3},{2,0},{3,1},{4,6},{5,7},{6,4},{7,5},{8,10},{9,11},{10,... | collective-permute-start | bytes 228104 | tf_op jit(solution)/shard_map/ppermute | solution.py:114
  116.8 3.6 %collective-permute-done.10 = f32[288,66]{1,0:T(8,128)S(1)} collective-permute-done((f32[288,66]{1,0:T(8,128)S(1)}, f32[288,66]{1,0:T(8,128)S(1)}, u32[]{:S(2)}, u32[]{:S(2)}) %collective-permute-start.10) | collective-permute-done | bytes 76064 | tf_op jit(solution)/shard_map/ppermute | solution.py:114
  120.9 3.7 %collective-permute-start.11 = (f32[144,66]{1,0:T(8,128)S(1)}, f32[144,66]{1,0:T(8,128)S(1)}, u32[]{:S(2)}, u32[]{:S(2)}) collective-permute-start(f32[144,66]{1,0:T(8,128)S(1)} %get-tuple-element.32), channel_id=1, source_target_pairs={{0,4},{1,5},{2,6},{3,7},{4,0},{5,1},{6,2},{7,3},{8,12},{9,13},{10,... | collective-permute-start | bytes 114056 | tf_op jit(solution)/shard_map/ppermute | solution.py:114
  124.9 2.6 %collective-permute-done.11 = f32[144,66]{1,0:T(8,128)S(1)} collective-permute-done((f32[144,66]{1,0:T(8,128)S(1)}, f32[144,66]{1,0:T(8,128)S(1)}, u32[]{:S(2)}, u32[]{:S(2)}) %collective-permute-start.11) | collective-permute-done | bytes 38048 | tf_op jit(solution)/shard_map/ppermute | solution.py:114
  130.3 2.8 %collective-permute-done.12 = f32[144,66]{1,0:T(8,128)S(1)} collective-permute-done((f32[144,66]{1,0:T(8,128)S(1)}, f32[144,66]{1,0:T(8,128)S(1)}, u32[]{:S(2)}, u32[]{:S(2)}) %collective-permute-start.12) | collective-permute-done | bytes 38048 | tf_op jit(solution)/shard_map/ppermute | solution.py:94
  133.5 3.6 %collective-permute-start.13 = (f32[144,66]{1,0:T(8,128)S(1)}, f32[144,66]{1,0:T(8,128)S(1)}, u32[]{:S(2)}, u32[]{:S(2)}) collective-permute-start(f32[144,66]{1,0:T(8,128)S(1)} %pad_maximum_fusion.5), channel_id=1, source_target_pairs={{0,16},{1,17},{2,18},{3,19},{4,20},{5,21},{6,22},{7,23},{8,24},{9,... | collective-permute-start | bytes 114056 | tf_op jit(solution)/shard_map/ppermute | solution.py:94
  137.3 3.0 %collective-permute-done.13 = f32[144,66]{1,0:T(8,128)S(1)} collective-permute-done((f32[144,66]{1,0:T(8,128)S(1)}, f32[144,66]{1,0:T(8,128)S(1)}, u32[]{:S(2)}, u32[]{:S(2)}) %collective-permute-start.13) | collective-permute-done | bytes 38048 | tf_op jit(solution)/shard_map/ppermute | solution.py:94
  140.7 6.3 %collective-permute-start.14 = (f32[144,66]{1,0:T(8,128)S(1)}, f32[144,66]{1,0:T(8,128)S(1)}, u32[]{:S(2)}, u32[]{:S(2)}) collective-permute-start(f32[144,66]{1,0:T(8,128)S(1)} %pad_maximum_fusion.6), channel_id=1, source_target_pairs={{0,32},{1,33},{2,34},{3,35},{4,36},{5,37},{6,38},{7,39},{8,40},{9,... | collective-permute-start | bytes 114056 | tf_op jit(solution)/shard_map/ppermute | solution.py:94
  147.6 2.2 collective-permute-done.14
  150.5 4.1 %collective-permute-start.15 = (bf16[144,64]{1,0:T(8,128)(2,1)S(1)}, bf16[144,64]{1,0:T(8,128)(2,1)S(1)}, u32[]{:S(2)}, u32[]{:S(2)}) collective-permute-start(bf16[144,64]{1,0:T(8,128)(2,1)S(1)} %fusion.49), channel_id=1, source_target_pairs={{0,4},{1,5},{2,6},{3,7},{4,0},{5,1},{6,2},{7,3},{8,12},{9,13},{10,... | collective-permute-start | bytes 55304 | tf_op jit(solution)/shard_map/ppermute | solution.py:67
  154.6 2.1 collective-permute-done.15
  156.7 3.1 %collective-permute-start.16 = (bf16[288,64]{1,0:T(8,128)(2,1)S(1)}, bf16[288,64]{1,0:T(8,128)(2,1)S(1)}, u32[]{:S(2)}, u32[]{:S(2)}) collective-permute-start(bf16[288,64]{1,0:T(8,128)(2,1)S(1)} %maximum_select_fusion.5), channel_id=1, source_target_pairs={{0,2},{1,3},{2,0},{3,1},{4,6},{5,7},{6,4},{7,5},{8,10},{9,11},{10,... | collective-permute-start | bytes 110600 | tf_op jit(solution)/shard_map/ppermute | solution.py:67
  159.8 2.4 %collective-permute-done.16 = bf16[288,64]{1,0:T(8,128)(2,1)S(1)} collective-permute-done((bf16[288,64]{1,0:T(8,128)(2,1)S(1)}, bf16[288,64]{1,0:T(8,128)(2,1)S(1)}, u32[]{:S(2)}, u32[]{:S(2)}) %collective-permute-start.16) | collective-permute-done | bytes 36896 | tf_op jit(solution)/shard_map/ppermute | solution.py:67
  162.3 10.4 %collective-permute-start.17 = (bf16[576,64]{1,0:T(8,128)(2,1)S(1)}, bf16[576,64]{1,0:T(8,128)(2,1)S(1)}, u32[]{:S(2)}, u32[]{:S(2)}) collective-permute-start(bf16[576,64]{1,0:T(8,128)(2,1)S(1)} %maximum_select_fusion.3), channel_id=1, source_target_pairs={{0,1},{1,0},{2,3},{3,2},{4,5},{5,4},{6,7},{7,6},{8,9},{9,8},{10,11... | collective-permute-start | bytes 221192 | tf_op jit(solution)/shard_map/ppermute | solution.py:67
  175.5 10.3 %all-to-all-start = ((bf16[64,2,576]{2,1,0:T(2,128)(2,1)}), bf16[64,2,576]{2,1,0:T(2,128)(2,1)S(1)}, u32[]{:S(2)}, u32[]{:S(2)}) async-start(bf16[64,2,576]{2,1,0:T(2,128)(2,1)} %reshape.447), calls=%async_computation | async-start | bytes 327680 | tf_op jit(solution)/shard_map/all_to_all | solution.py:129
  187.8 9.7 %all-to-all-done = bf16[64,2,576]{2,1,0:T(2,128)(2,1)S(1)} async-done(((bf16[64,2,576]{2,1,0:T(2,128)(2,1)}), bf16[64,2,576]{2,1,0:T(2,128)(2,1)S(1)}, u32[]{:S(2)}, u32[]{:S(2)}) %all-to-all-start) | async-done | bytes 147488 | tf_op jit(solution)/shard_map/all_to_all | solution.py:129
  205.6 15.6 %all_to_all.10 = bf16[64,2,576]{2,1,0:T(2,128)(2,1)S(1)} all-to-all(bf16[64,2,576]{2,1,0:T(2,128)(2,1)S(1)} %reshape.449), channel_id=1, replica_groups=mesh['rep'=8,'tp'=64] {'tp'}, dimensions={0} | all-to-all | bytes 294912 | tf_op jit(solution)/shard_map/all_to_all | solution.py:134
  (201 shorter events, 67.5 us)
Async XLA Ops:
  0.0 202.5 %copy-start = (bf16[2304,180]{0,1:T(8,128)(2,1)S(1)}, bf16[2304,180]{0,1:T(8,128)(2,1)}, u32[]{:S(2)}) copy-start(bf16[2304,180]{0,1:T(8,128)(2,1)} %param.29) | copy-start | bytes 2488324
  0.0 2.4 %copy-start.10 = (f32[32,36]{1,0:T(8,128)S(1)}, f32[32,36]{1,0:T(8,128)}, u32[]{:S(2)}) copy-start(f32[32,36]{1,0:T(8,128)} %param.16) | copy-start | bytes 13828
  6.8 10.8 %copy-start.16 = (s32[8]{0:T(128)S(1)}, s32[8]{0:T(128)}, u32[]{:S(2)}) copy-start(s32[8]{0:T(128)} %param.25) | copy-start | bytes 100
  8.8 10.2 %collective-permute-start = (f32[32,3488]{1,0:T(8,128)S(1)}, f32[32,3488]{1,0:T(8,128)S(1)}, u32[]{:S(2)}, u32[]{:S(2)}) collective-permute-start(f32[32,3488]{1,0:T(8,128)S(1)} %constant_dynamic-slice_fusion.7), channel_id=1, source_target_pairs={{0,1},{1,0},{2,3},{3,2},{4,5},{5,4},{6,7},{7,6},{8,9},{9,8},{10,11... | collective-permute-start | bytes 1339400 | tf_op jit(solution)/shard_map/ppermute | solution.py:57
  19.3 43.2 %copy-start.17 = (s32[8]{0:T(128)S(1)}, s32[8]{0:T(128)}, u32[]{:S(2)}) copy-start(s32[8]{0:T(128)} %param.24) | copy-start | bytes 100
  19.3 8.7 %collective-permute-start.1 = (f32[32,1744]{1,0:T(8,128)S(1)}, f32[32,1744]{1,0:T(8,128)S(1)}, u32[]{:S(2)}, u32[]{:S(2)}) collective-permute-start(f32[32,1744]{1,0:T(8,128)S(1)} %constant_dynamic-slice_fusion.6), channel_id=1, source_target_pairs={{0,2},{1,3},{2,0},{3,1},{4,6},{5,7},{6,4},{7,5},{8,10},{9,11},{10,... | collective-permute-start | bytes 669704 | tf_op jit(solution)/shard_map/ppermute | solution.py:57
  28.2 40.8 %copy-start.5 = (bf16[3,32,2304]{2,1,0:T(8,128)(2,1)S(1)}, bf16[3,32,2304]{2,1,0:T(8,128)(2,1)}, u32[]{:S(2)}) copy-start(bf16[3,32,2304]{2,1,0:T(8,128)(2,1)} %param.20) | copy-start | bytes 1327108
  28.3 7.2 %collective-permute-start.2 = (f32[32,872]{1,0:T(8,128)S(1)}, f32[32,872]{1,0:T(8,128)S(1)}, u32[]{:S(2)}, u32[]{:S(2)}) collective-permute-start(f32[32,872]{1,0:T(8,128)S(1)} %constant_dynamic-slice_fusion.5), channel_id=1, source_target_pairs={{0,4},{1,5},{2,6},{3,7},{4,0},{5,1},{6,2},{7,3},{8,12},{9,13},{10,... | collective-permute-start | bytes 334856 | tf_op jit(solution)/shard_map/ppermute | solution.py:57
  35.6 5.5 %collective-permute-start.3 = (f32[32,872]{1,0:T(8,128)S(1)}, f32[32,872]{1,0:T(8,128)S(1)}, u32[]{:S(2)}, u32[]{:S(2)}) collective-permute-start(f32[32,872]{1,0:T(8,128)S(1)} %dynamic-slice_add_fusion.2), channel_id=1, source_target_pairs={{0,8},{1,9},{2,10},{3,11},{4,12},{5,13},{6,14},{7,15},{8,0},{9,1},... | collective-permute-start | bytes 334856 | tf_op jit(solution)/shard_map/ppermute | solution.py:87
  41.1 7.4 %collective-permute-start.4 = (f32[32,872]{1,0:T(8,128)S(1)}, f32[32,872]{1,0:T(8,128)S(1)}, u32[]{:S(2)}, u32[]{:S(2)}) collective-permute-start(f32[32,872]{1,0:T(8,128)S(1)} %add.254), channel_id=1, source_target_pairs={{0,16},{1,17},{2,18},{3,19},{4,20},{5,21},{6,22},{7,23},{8,24},{9,... | collective-permute-start | bytes 334856 | tf_op jit(solution)/shard_map/ppermute | solution.py:87
  48.6 22.2 %copy-start.7 = (bf16[8,8,2304]{2,1,0:T(8,128)(2,1)S(1)}, bf16[8,8,2304]{2,1,0:T(8,128)(2,1)}, u32[]{:S(2)}) copy-start(bf16[8,8,2304]{2,1,0:T(8,128)(2,1)} %param.22) | copy-start | bytes 884740
  48.6 9.6 %collective-permute-start.5 = (f32[32,872]{1,0:T(8,128)S(1)}, f32[32,872]{1,0:T(8,128)S(1)}, u32[]{:S(2)}, u32[]{:S(2)}) collective-permute-start(f32[32,872]{1,0:T(8,128)S(1)} %add.255), channel_id=1, source_target_pairs={{0,32},{1,33},{2,34},{3,35},{4,36},{5,37},{6,38},{7,39},{8,40},{9,... | collective-permute-start | bytes 334856 | tf_op jit(solution)/shard_map/ppermute | solution.py:87
  58.9 13.1 %copy-start.8 = (bf16[8,8,2304]{2,1,0:T(8,128)(2,1)S(1)}, bf16[8,8,2304]{2,1,0:T(8,128)(2,1)}, u32[]{:S(2)}) copy-start(bf16[8,8,2304]{2,1,0:T(8,128)(2,1)} %param.23) | copy-start | bytes 884740
  59.4 6.2 %collective-permute-start.6 = (bf16[32,576]{1,0:T(8,128)(2,1)S(1)}, bf16[32,576]{1,0:T(8,128)(2,1)S(1)}, u32[]{:S(2)}, u32[]{:S(2)}) collective-permute-start(bf16[32,576]{1,0:T(8,128)(2,1)S(1)} %pad_maximum_fusion.8), channel_id=1, source_target_pairs={{0,4},{1,5},{2,6},{3,7},{4,0},{5,1},{6,2},{7,3},{8,12},{9,13},{10,... | collective-permute-start | bytes 110600 | tf_op jit(solution)/shard_map/ppermute | solution.py:150
  66.1 7.3 %copy-start.6 = (bf16[3,32,2304]{2,1,0:T(8,128)(2,1)S(1)}, bf16[3,32,2304]{2,1,0:T(8,128)(2,1)}, u32[]{:S(2)}) copy-start(bf16[3,32,2304]{2,1,0:T(8,128)(2,1)} %param.21) | copy-start | bytes 1327108
  66.3 8.8 %collective-permute-start.7 = (bf16[32,864]{1,0:T(8,128)(2,1)S(1)}, bf16[32,864]{1,0:T(8,128)(2,1)S(1)}, u32[]{:S(2)}, u32[]{:S(2)}) collective-permute-start(bf16[32,864]{1,0:T(8,128)(2,1)S(1)} %pad_maximum_fusion.7), channel_id=1, source_target_pairs={{0,2},{1,3},{2,0},{3,1},{4,6},{5,7},{6,4},{7,5},{8,10},{9,11},{10,... | collective-permute-start | bytes 165896 | tf_op jit(solution)/shard_map/ppermute | solution.py:150
  76.3 9.9 %collective-permute-start.8 = (bf16[32,1440]{1,0:T(8,128)(2,1)S(1)}, bf16[32,1440]{1,0:T(8,128)(2,1)S(1)}, u32[]{:S(2)}, u32[]{:S(2)}) collective-permute-start(bf16[32,1440]{1,0:T(8,128)(2,1)S(1)} %pad_maximum_fusion.3), channel_id=1, source_target_pairs={{0,1},{1,0},{2,3},{3,2},{4,5},{5,4},{6,7},{7,6},{8,9},{9,8},{10,11... | collective-permute-start | bytes 276488 | tf_op jit(solution)/shard_map/ppermute | solution.py:150
  101.3 3.0 %copy-start.3 = (bf16[3,32,36,64]{3,2,1,0:T(8,128)(2,1)S(1)}, bf16[3,32,36,64]{3,2,1,0:T(8,128)(2,1)}, u32[]{:S(2)}) copy-start(bf16[3,32,36,64]{3,2,1,0:T(8,128)(2,1)} %reshape.409) | copy-start | bytes 1327108
  109.1 3.5 %collective-permute-start.9 = (f32[576,66]{1,0:T(8,128)S(1)}, f32[576,66]{1,0:T(8,128)S(1)}, u32[]{:S(2)}, u32[]{:S(2)}) collective-permute-start(f32[576,66]{1,0:T(8,128)S(1)} %constant_dynamic-slice_fusion), channel_id=1, source_target_pairs={{0,1},{1,0},{2,3},{3,2},{4,5},{5,4},{6,7},{7,6},{8,9},{9,8},{10,11... | collective-permute-start | bytes 456200 | tf_op jit(solution)/shard_map/ppermute | solution.py:114
  113.2 16.7 %copy-start.18 = (pred[4,4]{0,1:T(4,128)(4,1)S(1)}, pred[4,4]{0,1:T(4,128)(4,1)}, u32[]{:S(2)}) copy-start(pred[4,4]{0,1:T(4,128)(4,1)} %iota_compare_fusion.2) | copy-start | bytes 52
  113.4 16.8 %copy-start.12 = (bf16[4,2304]{1,0:T(4,128)(2,1)S(1)}, bf16[4,2304]{1,0:T(4,128)(2,1)}, u32[]{:S(2)}) copy-start(bf16[4,2304]{1,0:T(4,128)(2,1)} %get-tuple-element.42) | copy-start | bytes 55300
  113.4 7.0 %collective-permute-start.10 = (f32[288,66]{1,0:T(8,128)S(1)}, f32[288,66]{1,0:T(8,128)S(1)}, u32[]{:S(2)}, u32[]{:S(2)}) collective-permute-start(f32[288,66]{1,0:T(8,128)S(1)} %get-tuple-element.31), channel_id=1, source_target_pairs={{0,2},{1,3},{2,0},{3,1},{4,6},{5,7},{6,4},{7,5},{8,10},{9,11},{10,... | collective-permute-start | bytes 228104 | tf_op jit(solution)/shard_map/ppermute | solution.py:114
  120.9 6.6 %collective-permute-start.11 = (f32[144,66]{1,0:T(8,128)S(1)}, f32[144,66]{1,0:T(8,128)S(1)}, u32[]{:S(2)}, u32[]{:S(2)}) collective-permute-start(f32[144,66]{1,0:T(8,128)S(1)} %get-tuple-element.32), channel_id=1, source_target_pairs={{0,4},{1,5},{2,6},{3,7},{4,0},{5,1},{6,2},{7,3},{8,12},{9,13},{10,... | collective-permute-start | bytes 114056 | tf_op jit(solution)/shard_map/ppermute | solution.py:114
  127.9 5.1 %collective-permute-start.12 = (f32[144,66]{1,0:T(8,128)S(1)}, f32[144,66]{1,0:T(8,128)S(1)}, u32[]{:S(2)}, u32[]{:S(2)}) collective-permute-start(f32[144,66]{1,0:T(8,128)S(1)} %pad_maximum_fusion.4), channel_id=1, source_target_pairs={{0,8},{1,9},{2,10},{3,11},{4,12},{5,13},{6,14},{7,15},{8,0},{9,1},... | collective-permute-start | bytes 114056 | tf_op jit(solution)/shard_map/ppermute | solution.py:94
  133.5 6.8 %collective-permute-start.13 = (f32[144,66]{1,0:T(8,128)S(1)}, f32[144,66]{1,0:T(8,128)S(1)}, u32[]{:S(2)}, u32[]{:S(2)}) collective-permute-start(f32[144,66]{1,0:T(8,128)S(1)} %pad_maximum_fusion.5), channel_id=1, source_target_pairs={{0,16},{1,17},{2,18},{3,19},{4,20},{5,21},{6,22},{7,23},{8,24},{9,... | collective-permute-start | bytes 114056 | tf_op jit(solution)/shard_map/ppermute | solution.py:94
  137.3 36.5 %copy-start.9 = (bf16[2304,36]{0,1:T(8,128)(2,1)S(1)}, bf16[2304,36]{0,1:T(8,128)(2,1)}, u32[]{:S(2)}) copy-start(bf16[2304,36]{0,1:T(8,128)(2,1)} %param.19) | copy-start | bytes 497668
  140.7 9.0 %collective-permute-start.14 = (f32[144,66]{1,0:T(8,128)S(1)}, f32[144,66]{1,0:T(8,128)S(1)}, u32[]{:S(2)}, u32[]{:S(2)}) collective-permute-start(f32[144,66]{1,0:T(8,128)S(1)} %pad_maximum_fusion.6), channel_id=1, source_target_pairs={{0,32},{1,33},{2,34},{3,35},{4,36},{5,37},{6,38},{7,39},{8,40},{9,... | collective-permute-start | bytes 114056 | tf_op jit(solution)/shard_map/ppermute | solution.py:94
  150.5 6.2 %collective-permute-start.15 = (bf16[144,64]{1,0:T(8,128)(2,1)S(1)}, bf16[144,64]{1,0:T(8,128)(2,1)S(1)}, u32[]{:S(2)}, u32[]{:S(2)}) collective-permute-start(bf16[144,64]{1,0:T(8,128)(2,1)S(1)} %fusion.49), channel_id=1, source_target_pairs={{0,4},{1,5},{2,6},{3,7},{4,0},{5,1},{6,2},{7,3},{8,12},{9,13},{10,... | collective-permute-start | bytes 55304 | tf_op jit(solution)/shard_map/ppermute | solution.py:67
  156.7 5.5 %collective-permute-start.16 = (bf16[288,64]{1,0:T(8,128)(2,1)S(1)}, bf16[288,64]{1,0:T(8,128)(2,1)S(1)}, u32[]{:S(2)}, u32[]{:S(2)}) collective-permute-start(bf16[288,64]{1,0:T(8,128)(2,1)S(1)} %maximum_select_fusion.5), channel_id=1, source_target_pairs={{0,2},{1,3},{2,0},{3,1},{4,6},{5,7},{6,4},{7,5},{8,10},{9,11},{10,... | collective-permute-start | bytes 110600 | tf_op jit(solution)/shard_map/ppermute | solution.py:67
  162.3 11.2 %collective-permute-start.17 = (bf16[576,64]{1,0:T(8,128)(2,1)S(1)}, bf16[576,64]{1,0:T(8,128)(2,1)S(1)}, u32[]{:S(2)}, u32[]{:S(2)}) collective-permute-start(bf16[576,64]{1,0:T(8,128)(2,1)S(1)} %maximum_select_fusion.3), channel_id=1, source_target_pairs={{0,1},{1,0},{2,3},{3,2},{4,5},{5,4},{6,7},{7,6},{8,9},{9,8},{10,11... | collective-permute-start | bytes 221192 | tf_op jit(solution)/shard_map/ppermute | solution.py:67
  175.5 22.0 %all-to-all-start = ((bf16[64,2,576]{2,1,0:T(2,128)(2,1)}), bf16[64,2,576]{2,1,0:T(2,128)(2,1)S(1)}, u32[]{:S(2)}, u32[]{:S(2)}) async-start(bf16[64,2,576]{2,1,0:T(2,128)(2,1)} %reshape.447), calls=%async_computation | async-start | bytes 327680 | tf_op jit(solution)/shard_map/all_to_all | solution.py:129
  185.8 1.9 copy-start.15
  (7 other events, 7.7 us)

commit v10 on v7

--- a/solution.py
+++ b/solution.py
@@ -244,7 +244,8 @@
     new_rows = lax.dynamic_slice_in_dim(new_rows, kept_position(near_bits) * own_count, own_count, axis=0)
     final_rows = merge_rows(cache_rows, new_rows)
     attended_rows = (final_rows[:, :HDIM] / final_rows[:, HDIM : HDIM + 1]).astype(jnp.bfloat16)
-    attended = gather_cols(attended_rows, axis=0, bits=near_bits).reshape(all_tokens, model_width)
+    attended_lines = attended_rows.reshape(attended_rows.shape[0] // 2, 2 * HDIM)
+    attended = gather_cols(attended_lines, axis=0, bits=near_bits).reshape(all_tokens, model_width)
     residual_cols = hidden + jnp.dot(attended, w_out, preferred_element_type=jnp.float32)
     full_rows = exchange_gather(residual_cols.astype(jnp.bfloat16)).astype(jnp.float32)
     inv_norm = lax.rsqrt(jnp.mean(full_rows * full_rows, axis=1) + EPSILON)

time: 211 us -> 210 us (level)
  no operation moved by 1% of the time
where the time goes in v10:
time: 210 us; the launch traced here: 209 us
  starting transfers between devices  86.1 us (41%)
  waiting for transfers between devices  57.3 us (27%)
  local copies, waits for them, and re-layouts  23 us (11%)
  blocking collectives  15.6 us (7%)
  matrix products  13.1 us (6%)
  other arithmetic  13 us (6%)
    ppermute x6, starting transfers between devices, gather_cols(): other = lax.ppermute(values, 'tp', partner_pairs(count, bit))  31.7 us
    all_to_all x1, blocking collectives, exchange_scatter_sum(): received = lax.all_to_all(blocks, 'tp', 0, 0, tiled=True)  15.6 us
    ppermute x3, waiting for transfers between devices, scatter_sum(): values = keep + lax.ppermute(send, 'tp', partner_pairs(count, bit))  13 us
    ppermute x3, waiting for transfers between devices, exchange_sum(): values = values + lax.ppermute(values, 'tp', partner_pairs(count, bit))  12.8 us
    ppermute x3, starting transfers between devices, scatter_sum(): values = keep + lax.ppermute(send, 'tp', partner_pairs(count, bit))  12.6 us
    ppermute x3, starting transfers between devices, exchange_merge(): rows = merge_rows(rows, lax.ppermute(rows, 'tp', partner_pairs(count, bit)))  12.2 us
    all_to_all x1, starting transfers between devices, exchange_gather(): received = lax.all_to_all(copies, 'tp', 0, 0, tiled=True)  10.6 us
    all_to_all x1, waiting for transfers between devices, exchange_gather(): received = lax.all_to_all(copies, 'tp', 0, 0, tiled=True)  9.75 us
  transfers between devices with their start and end apart: 19, of which 18 were waited for; matrix products, arithmetic and copies ran while one was open for 5% of the time, Pallas kernels for 0%

profile of v10, /device:TPU:1, one launch (start us, length us, event | category | flops | bytes accessed | tf_op | source)
XLA Modules:
  0.0 209.3 jit_solution(4415162073675196923)
XLA Ops:
  2.3 2.0 reshape.288
  5.5 8.8 %collective-permute-start = (f32[32,3488]{1,0:T(8,128)S(1)}, f32[32,3488]{1,0:T(8,128)S(1)}, u32[]{:S(2)}, u32[]{:S(2)}) collective-permute-start(f32[32,3488]{1,0:T(8,128)S(1)} %constant_dynamic-slice_fusion.3), channel_id=1, source_target_pairs={{0,1},{1,0},{2,3},{3,2},{4,5},{5,4},{6,7},{7,6},{8,9},{9,8},{10,11... | collective-permute-start | bytes 1339400 | tf_op jit(solution)/shard_map/ppermute | solution.py:57
  16.1 1.9 collective-permute-start.1
  18.1 6.7 %collective-permute-done.1 = f32[32,1744]{1,0:T(8,128)S(1)} collective-permute-done((f32[32,1744]{1,0:T(8,128)S(1)}, f32[32,1744]{1,0:T(8,128)S(1)}, u32[]{:S(2)}, u32[]{:S(2)}) %collective-permute-start.1) | collective-permute-done | bytes 223264 | tf_op jit(solution)/shard_map/ppermute | solution.py:57
  25.0 1.9 collective-permute-start.2
  27.2 4.9 %collective-permute-done.2 = f32[32,872]{1,0:T(8,128)S(1)} collective-permute-done((f32[32,872]{1,0:T(8,128)S(1)}, f32[32,872]{1,0:T(8,128)S(1)}, u32[]{:S(2)}, u32[]{:S(2)}) %collective-permute-start.2) | collective-permute-done | bytes 111648 | tf_op jit(solution)/shard_map/ppermute | solution.py:57
  32.2 1.9 collective-permute-start.3
  34.1 3.6 %collective-permute-done.3 = f32[32,872]{1,0:T(8,128)S(1)} collective-permute-done((f32[32,872]{1,0:T(8,128)S(1)}, f32[32,872]{1,0:T(8,128)S(1)}, u32[]{:S(2)}, u32[]{:S(2)}) %collective-permute-start.3) | collective-permute-done | bytes 111648 | tf_op jit(solution)/shard_map/ppermute | solution.py:87
  37.7 1.9 collective-permute-start.4
  39.7 5.4 %collective-permute-done.4 = f32[32,872]{1,0:T(8,128)S(1)} collective-permute-done((f32[32,872]{1,0:T(8,128)S(1)}, f32[32,872]{1,0:T(8,128)S(1)}, u32[]{:S(2)}, u32[]{:S(2)}) %collective-permute-start.4) | collective-permute-done | bytes 111648 | tf_op jit(solution)/shard_map/ppermute | solution.py:87
  45.2 5.5 %collective-permute-start.5 = (f32[32,872]{1,0:T(8,128)S(1)}, f32[32,872]{1,0:T(8,128)S(1)}, u32[]{:S(2)}, u32[]{:S(2)}) collective-permute-start(f32[32,872]{1,0:T(8,128)S(1)} %add.227), channel_id=1, source_target_pairs={{0,32},{1,33},{2,34},{3,35},{4,36},{5,37},{6,38},{7,39},{8,40},{9,... | collective-permute-start | bytes 334856 | tf_op jit(solution)/shard_map/ppermute | solution.py:87
  50.9 3.7 %collective-permute-done.5 = f32[32,872]{1,0:T(8,128)S(1)} collective-permute-done((f32[32,872]{1,0:T(8,128)S(1)}, f32[32,872]{1,0:T(8,128)S(1)}, u32[]{:S(2)}, u32[]{:S(2)}) %collective-permute-start.5) | collective-permute-done | bytes 111648 | tf_op jit(solution)/shard_map/ppermute | solution.py:87
  55.5 3.0 %collective-permute-start.6 = (bf16[32,864]{1,0:T(8,128)(2,1)S(1)}, bf16[32,864]{1,0:T(8,128)(2,1)S(1)}, u32[]{:S(2)}, u32[]{:S(2)}) collective-permute-start(bf16[32,864]{1,0:T(8,128)(2,1)S(1)} %reshape.291), channel_id=1, source_target_pairs={{0,4},{1,5},{2,6},{3,7},{4,0},{5,1},{6,2},{7,3},{8,12},{9,13},{10,... | collective-permute-start | bytes 165896 | tf_op jit(solution)/shard_map/ppermute | solution.py:67
  58.5 3.4 %collective-permute-done.6 = bf16[32,864]{1,0:T(8,128)(2,1)S(1)} collective-permute-done((bf16[32,864]{1,0:T(8,128)(2,1)S(1)}, bf16[32,864]{1,0:T(8,128)(2,1)S(1)}, u32[]{:S(2)}, u32[]{:S(2)}) %collective-permute-start.6) | collective-permute-done | bytes 55328 | tf_op jit(solution)/shard_map/ppermute | solution.py:67
  62.0 2.3 %collective-permute-start.7 = (bf16[32,1728]{1,0:T(8,128)(2,1)S(1)}, bf16[32,1728]{1,0:T(8,128)(2,1)S(1)}, u32[]{:S(2)}, u32[]{:S(2)}) collective-permute-start(bf16[32,1728]{1,0:T(8,128)(2,1)S(1)} %maximum_select_fusion.3), channel_id=1, source_target_pairs={{0,2},{1,3},{2,0},{3,1},{4,6},{5,7},{6,4},{7,5},{8,10},{9,11},{10,... | collective-permute-start | bytes 331784 | tf_op jit(solution)/shard_map/ppermute | solution.py:67
  70.5 9.2 %collective-permute-start.8 = (bf16[32,3456]{1,0:T(8,128)(2,1)S(1)}, bf16[32,3456]{1,0:T(8,128)(2,1)S(1)}, u32[]{:S(2)}, u32[]{:S(2)}) collective-permute-start(bf16[32,3456]{1,0:T(8,128)(2,1)S(1)} %maximum_select_fusion.1), channel_id=1, source_target_pairs={{0,1},{1,0},{2,3},{3,2},{4,5},{5,4},{6,7},{7,6},{8,9},{9,8},{10,11... | collective-permute-start | bytes 663560 | tf_op jit(solution)/shard_map/ppermute | solution.py:67
  85.1 2.4 %fusion.85 = (f32[8,4,36]{1,2,0:T(8,128)S(1)}, f32[8,4,36,8]{3,1,2,0:T(4,128)}) fusion(bf16[8,8,36,64]{3,2,1,0:T(8,128)(2,1)} %reshape.295, bf16[8,4,36,64]{3,0,1,2:T(8,128)(2,1)S(1)} %pad_maximum_fusion.2, pred[8,8]{1,0:T(8,128)(4,1)S(1)} %broadcast_compare_fusion), kind=kOutput, calls=%fused_computation.184 | convolution fusion | flops 1206144 | bytes 483904 | tf_op jit(solution)/shard_map/rjhd,rphd->rjhp/dot_general | solution.py:213
  95.1 2.4 %collective-permute-start.9 = (f32[576,66]{1,0:T(8,128)S(1)}, f32[576,66]{1,0:T(8,128)S(1)}, u32[]{:S(2)}, u32[]{:S(2)}) collective-permute-start(f32[576,66]{1,0:T(8,128)S(1)} %constant_dynamic-slice_fusion), channel_id=1, source_target_pairs={{0,1},{1,0},{2,3},{3,2},{4,5},{5,4},{6,7},{7,6},{8,9},{9,8},{10,11... | collective-permute-start | bytes 456200 | tf_op jit(solution)/shard_map/ppermute | solution.py:114
  99.5 3.3 %collective-permute-start.10 = (f32[288,66]{1,0:T(8,128)S(1)}, f32[288,66]{1,0:T(8,128)S(1)}, u32[]{:S(2)}, u32[]{:S(2)}) collective-permute-start(f32[288,66]{1,0:T(8,128)S(1)} %get-tuple-element.31), channel_id=1, source_target_pairs={{0,2},{1,3},{2,0},{3,1},{4,6},{5,7},{6,4},{7,5},{8,10},{9,11},{10,... | collective-permute-start | bytes 228104 | tf_op jit(solution)/shard_map/ppermute | solution.py:114
  103.2 3.3 %collective-permute-done.10 = f32[288,66]{1,0:T(8,128)S(1)} collective-permute-done((f32[288,66]{1,0:T(8,128)S(1)}, f32[288,66]{1,0:T(8,128)S(1)}, u32[]{:S(2)}, u32[]{:S(2)}) %collective-permute-start.10) | collective-permute-done | bytes 76064 | tf_op jit(solution)/shard_map/ppermute | solution.py:114
  107.1 4.0 %collective-permute-start.11 = (f32[144,66]{1,0:T(8,128)S(1)}, f32[144,66]{1,0:T(8,128)S(1)}, u32[]{:S(2)}, u32[]{:S(2)}) collective-permute-start(f32[144,66]{1,0:T(8,128)S(1)} %get-tuple-element.35), channel_id=1, source_target_pairs={{0,4},{1,5},{2,6},{3,7},{4,0},{5,1},{6,2},{7,3},{8,12},{9,13},{10,... | collective-permute-start | bytes 114056 | tf_op jit(solution)/shard_map/ppermute | solution.py:114
  116.6 2.6 %collective-permute-done.12 = f32[144,66]{1,0:T(8,128)S(1)} collective-permute-done((f32[144,66]{1,0:T(8,128)S(1)}, f32[144,66]{1,0:T(8,128)S(1)}, u32[]{:S(2)}, u32[]{:S(2)}) %collective-permute-start.12) | collective-permute-done | bytes 38048 | tf_op jit(solution)/shard_map/ppermute | solution.py:94
  119.7 3.7 %collective-permute-start.13 = (f32[144,66]{1,0:T(8,128)S(1)}, f32[144,66]{1,0:T(8,128)S(1)}, u32[]{:S(2)}, u32[]{:S(2)}) collective-permute-start(f32[144,66]{1,0:T(8,128)S(1)} %pad_maximum_fusion.4), channel_id=1, source_target_pairs={{0,16},{1,17},{2,18},{3,19},{4,20},{5,21},{6,22},{7,23},{8,24},{9,... | collective-permute-start | bytes 114056 | tf_op jit(solution)/shard_map/ppermute | solution.py:94
  126.9 6.6 %collective-permute-start.14 = (f32[144,66]{1,0:T(8,128)S(1)}, f32[144,66]{1,0:T(8,128)S(1)}, u32[]{:S(2)}, u32[]{:S(2)}) collective-permute-start(f32[144,66]{1,0:T(8,128)S(1)} %pad_maximum_fusion.5), channel_id=1, source_target_pairs={{0,32},{1,33},{2,34},{3,35},{4,36},{5,37},{6,38},{7,39},{8,40},{9,... | collective-permute-start | bytes 114056 | tf_op jit(solution)/shard_map/ppermute | solution.py:94
  133.6 2.5 %collective-permute-done.14 = f32[144,66]{1,0:T(8,128)S(1)} collective-permute-done((f32[144,66]{1,0:T(8,128)S(1)}, f32[144,66]{1,0:T(8,128)S(1)}, u32[]{:S(2)}, u32[]{:S(2)}) %collective-permute-start.14) | collective-permute-done | bytes 38048 | tf_op jit(solution)/shard_map/ppermute | solution.py:94
  136.9 3.9 %collective-permute-start.15 = (bf16[72,128]{1,0:T(8,128)(2,1)S(1)}, bf16[72,128]{1,0:T(8,128)(2,1)S(1)}, u32[]{:S(2)}, u32[]{:S(2)}) collective-permute-start(bf16[72,128]{1,0:T(8,128)(2,1)S(1)} %reshape.301), channel_id=1, source_target_pairs={{0,4},{1,5},{2,6},{3,7},{4,0},{5,1},{6,2},{7,3},{8,12},{9,13},{10,... | collective-permute-start | bytes 55304 | tf_op jit(solution)/shard_map/ppermute | solution.py:67
  140.8 2.1 %collective-permute-done.15 = bf16[72,128]{1,0:T(8,128)(2,1)S(1)} collective-permute-done((bf16[72,128]{1,0:T(8,128)(2,1)S(1)}, bf16[72,128]{1,0:T(8,128)(2,1)S(1)}, u32[]{:S(2)}, u32[]{:S(2)}) %collective-permute-start.15) | collective-permute-done | bytes 18464 | tf_op jit(solution)/shard_map/ppermute | solution.py:67
  142.9 3.1 %collective-permute-start.16 = (bf16[144,128]{1,0:T(8,128)(2,1)S(1)}, bf16[144,128]{1,0:T(8,128)(2,1)S(1)}, u32[]{:S(2)}, u32[]{:S(2)}) collective-permute-start(bf16[144,128]{1,0:T(8,128)(2,1)S(1)} %maximum_select_fusion.5), channel_id=1, source_target_pairs={{0,2},{1,3},{2,0},{3,1},{4,6},{5,7},{6,4},{7,5},{8,10},{9,11},{10,... | collective-permute-start | bytes 110600 | tf_op jit(solution)/shard_map/ppermute | solution.py:67
  147.8 10.1 %collective-permute-start.17 = (bf16[288,128]{1,0:T(8,128)(2,1)S(1)}, bf16[288,128]{1,0:T(8,128)(2,1)S(1)}, u32[]{:S(2)}, u32[]{:S(2)}) collective-permute-start(bf16[288,128]{1,0:T(8,128)(2,1)S(1)} %maximum_select_fusion.4), channel_id=1, source_target_pairs={{0,1},{1,0},{2,3},{3,2},{4,5},{5,4},{6,7},{7,6},{8,9},{9,8},{10,11... | collective-permute-start | bytes 221192 | tf_op jit(solution)/shard_map/ppermute | solution.py:67
  160.8 10.6 %all-to-all-start = ((bf16[64,2,576]{2,1,0:T(2,128)(2,1)}), bf16[64,2,576]{2,1,0:T(2,128)(2,1)S(1)}, u32[]{:S(2)}, u32[]{:S(2)}) async-start(bf16[64,2,576]{2,1,0:T(2,128)(2,1)} %reshape.333), calls=%async_computation | async-start | bytes 327680 | tf_op jit(solution)/shard_map/all_to_all | solution.py:129
  173.3 9.7 %all-to-all-done = bf16[64,2,576]{2,1,0:T(2,128)(2,1)S(1)} async-done(((bf16[64,2,576]{2,1,0:T(2,128)(2,1)}), bf16[64,2,576]{2,1,0:T(2,128)(2,1)S(1)}, u32[]{:S(2)}, u32[]{:S(2)}) %all-to-all-start) | async-done | bytes 147488 | tf_op jit(solution)/shard_map/all_to_all | solution.py:129
  191.1 15.6 %all_to_all.10 = bf16[64,2,576]{2,1,0:T(2,128)(2,1)S(1)} all-to-all(bf16[64,2,576]{2,1,0:T(2,128)(2,1)S(1)} %reshape.335), channel_id=1, replica_groups=mesh['rep'=8,'tp'=64] {'tp'}, dimensions={0} | all-to-all | bytes 294912 | tf_op jit(solution)/shard_map/all_to_all | solution.py:134
  (167 shorter events, 55.9 us)
Async XLA Ops:
  0.0 188.0 %copy-start = (bf16[2304,180]{0,1:T(8,128)(2,1)S(1)}, bf16[2304,180]{0,1:T(8,128)(2,1)}, u32[]{:S(2)}) copy-start(bf16[2304,180]{0,1:T(8,128)(2,1)} %param.29) | copy-start | bytes 2488324
  5.3 21.6 %copy-start.15 = (s32[8]{0:T(128)S(1)}, s32[8]{0:T(128)}, u32[]{:S(2)}) copy-start(s32[8]{0:T(128)} %param.25) | copy-start | bytes 100
  5.5 10.2 %collective-permute-start = (f32[32,3488]{1,0:T(8,128)S(1)}, f32[32,3488]{1,0:T(8,128)S(1)}, u32[]{:S(2)}, u32[]{:S(2)}) collective-permute-start(f32[32,3488]{1,0:T(8,128)S(1)} %constant_dynamic-slice_fusion.3), channel_id=1, source_target_pairs={{0,1},{1,0},{2,3},{3,2},{4,5},{5,4},{6,7},{7,6},{8,9},{9,8},{10,11... | collective-permute-start | bytes 1339400 | tf_op jit(solution)/shard_map/ppermute | solution.py:57
  15.9 48.4 %copy-start.7 = (bf16[3,32,2304]{2,1,0:T(8,128)(2,1)S(1)}, bf16[3,32,2304]{2,1,0:T(8,128)(2,1)}, u32[]{:S(2)}) copy-start(bf16[3,32,2304]{2,1,0:T(8,128)(2,1)} %param.20) | copy-start | bytes 1327108
  16.1 8.7 %collective-permute-start.1 = (f32[32,1744]{1,0:T(8,128)S(1)}, f32[32,1744]{1,0:T(8,128)S(1)}, u32[]{:S(2)}, u32[]{:S(2)}) collective-permute-start(f32[32,1744]{1,0:T(8,128)S(1)} %constant_dynamic-slice_fusion.2), channel_id=1, source_target_pairs={{0,2},{1,3},{2,0},{3,1},{4,6},{5,7},{6,4},{7,5},{8,10},{9,11},{10,... | collective-permute-start | bytes 669704 | tf_op jit(solution)/shard_map/ppermute | solution.py:57
  25.0 7.0 %collective-permute-start.2 = (f32[32,872]{1,0:T(8,128)S(1)}, f32[32,872]{1,0:T(8,128)S(1)}, u32[]{:S(2)}, u32[]{:S(2)}) collective-permute-start(f32[32,872]{1,0:T(8,128)S(1)} %constant_dynamic-slice_fusion.1), channel_id=1, source_target_pairs={{0,4},{1,5},{2,6},{3,7},{4,0},{5,1},{6,2},{7,3},{8,12},{9,13},{10,... | collective-permute-start | bytes 334856 | tf_op jit(solution)/shard_map/ppermute | solution.py:57
  27.2 38.9 %copy-start.9 = (bf16[8,8,2304]{2,1,0:T(8,128)(2,1)S(1)}, bf16[8,8,2304]{2,1,0:T(8,128)(2,1)}, u32[]{:S(2)}) copy-start(bf16[8,8,2304]{2,1,0:T(8,128)(2,1)} %param.22) | copy-start | bytes 884740
  32.2 5.5 %collective-permute-start.3 = (f32[32,872]{1,0:T(8,128)S(1)}, f32[32,872]{1,0:T(8,128)S(1)}, u32[]{:S(2)}, u32[]{:S(2)}) collective-permute-start(f32[32,872]{1,0:T(8,128)S(1)} %dynamic-slice_add_fusion.2), channel_id=1, source_target_pairs={{0,8},{1,9},{2,10},{3,11},{4,12},{5,13},{6,14},{7,15},{8,0},{9,1},... | collective-permute-start | bytes 334856 | tf_op jit(solution)/shard_map/ppermute | solution.py:87
  37.7 7.4 %collective-permute-start.4 = (f32[32,872]{1,0:T(8,128)S(1)}, f32[32,872]{1,0:T(8,128)S(1)}, u32[]{:S(2)}, u32[]{:S(2)}) collective-permute-start(f32[32,872]{1,0:T(8,128)S(1)} %add.226), channel_id=1, source_target_pairs={{0,16},{1,17},{2,18},{3,19},{4,20},{5,21},{6,22},{7,23},{8,24},{9,... | collective-permute-start | bytes 334856 | tf_op jit(solution)/shard_map/ppermute | solution.py:87
  45.2 9.4 %collective-permute-start.5 = (f32[32,872]{1,0:T(8,128)S(1)}, f32[32,872]{1,0:T(8,128)S(1)}, u32[]{:S(2)}, u32[]{:S(2)}) collective-permute-start(f32[32,872]{1,0:T(8,128)S(1)} %add.227), channel_id=1, source_target_pairs={{0,32},{1,33},{2,34},{3,35},{4,36},{5,37},{6,38},{7,39},{8,40},{9,... | collective-permute-start | bytes 334856 | tf_op jit(solution)/shard_map/ppermute | solution.py:87
  50.8 16.5 %copy-start.10 = (bf16[8,8,2304]{2,1,0:T(8,128)(2,1)S(1)}, bf16[8,8,2304]{2,1,0:T(8,128)(2,1)}, u32[]{:S(2)}) copy-start(bf16[8,8,2304]{2,1,0:T(8,128)(2,1)} %param.23) | copy-start | bytes 884740
  55.5 6.4 %collective-permute-start.6 = (bf16[32,864]{1,0:T(8,128)(2,1)S(1)}, bf16[32,864]{1,0:T(8,128)(2,1)S(1)}, u32[]{:S(2)}, u32[]{:S(2)}) collective-permute-start(bf16[32,864]{1,0:T(8,128)(2,1)S(1)} %reshape.291), channel_id=1, source_target_pairs={{0,4},{1,5},{2,6},{3,7},{4,0},{5,1},{6,2},{7,3},{8,12},{9,13},{10,... | collective-permute-start | bytes 165896 | tf_op jit(solution)/shard_map/ppermute | solution.py:67
  58.5 10.2 %copy-start.8 = (bf16[3,32,2304]{2,1,0:T(8,128)(2,1)S(1)}, bf16[3,32,2304]{2,1,0:T(8,128)(2,1)}, u32[]{:S(2)}) copy-start(bf16[3,32,2304]{2,1,0:T(8,128)(2,1)} %param.21) | copy-start | bytes 1327108
  62.0 8.3 %collective-permute-start.7 = (bf16[32,1728]{1,0:T(8,128)(2,1)S(1)}, bf16[32,1728]{1,0:T(8,128)(2,1)S(1)}, u32[]{:S(2)}, u32[]{:S(2)}) collective-permute-start(bf16[32,1728]{1,0:T(8,128)(2,1)S(1)} %maximum_select_fusion.3), channel_id=1, source_target_pairs={{0,2},{1,3},{2,0},{3,1},{4,6},{5,7},{6,4},{7,5},{8,10},{9,11},{10,... | collective-permute-start | bytes 331784 | tf_op jit(solution)/shard_map/ppermute | solution.py:67
  66.1 13.6 %copy-start.16 = (s32[8]{0:T(128)S(1)}, s32[8]{0:T(128)}, u32[]{:S(2)}) copy-start(s32[8]{0:T(128)} %param.24) | copy-start | bytes 100
  70.5 10.1 %collective-permute-start.8 = (bf16[32,3456]{1,0:T(8,128)(2,1)S(1)}, bf16[32,3456]{1,0:T(8,128)(2,1)S(1)}, u32[]{:S(2)}, u32[]{:S(2)}) collective-permute-start(bf16[32,3456]{1,0:T(8,128)(2,1)S(1)} %maximum_select_fusion.1), channel_id=1, source_target_pairs={{0,1},{1,0},{2,3},{3,2},{4,5},{5,4},{6,7},{7,6},{8,9},{9,8},{10,11... | collective-permute-start | bytes 663560 | tf_op jit(solution)/shard_map/ppermute | solution.py:67
  83.0 4.6 %copy-start.4 = (bf16[8,4,36,64]{3,0,1,2:T(8,128)(2,1)}, bf16[8,4,36,64]{3,0,1,2:T(8,128)(2,1)S(1)}, u32[]{:S(2)}) copy-start(bf16[8,4,36,64]{3,0,1,2:T(8,128)(2,1)S(1)} %pad_maximum_fusion.2) | copy-start | bytes 442372
  95.1 7.8 %copy-start.3 = (bf16[32,36,32]{2,1,0:T(8,128)(2,1)S(1)}, bf16[32,36,32]{2,1,0:T(8,128)(2,1)}, u32[]{:S(2)}) copy-start(bf16[32,36,32]{2,1,0:T(8,128)(2,1)} %get-tuple-element.38) | copy-start | bytes 221188
  95.1 7.9 %copy-start.2 = (bf16[32,36,32]{2,1,0:T(8,128)(2,1)S(1)}, bf16[32,36,32]{2,1,0:T(8,128)(2,1)}, u32[]{:S(2)}) copy-start(bf16[32,36,32]{2,1,0:T(8,128)(2,1)} %get-tuple-element.37) | copy-start | bytes 221188
  95.1 3.6 %collective-permute-start.9 = (f32[576,66]{1,0:T(8,128)S(1)}, f32[576,66]{1,0:T(8,128)S(1)}, u32[]{:S(2)}, u32[]{:S(2)}) collective-permute-start(f32[576,66]{1,0:T(8,128)S(1)} %constant_dynamic-slice_fusion), channel_id=1, source_target_pairs={{0,1},{1,0},{2,3},{3,2},{4,5},{5,4},{6,7},{7,6},{8,9},{9,8},{10,11... | collective-permute-start | bytes 456200 | tf_op jit(solution)/shard_map/ppermute | solution.py:114
  99.4 11.7 %copy-start.5 = (bf16[8,4,36,64]{3,0,1,2:T(8,128)(2,1)S(1)}, bf16[8,4,36,64]{3,0,1,2:T(8,128)(2,1)}, u32[]{:S(2)}) copy-start(bf16[8,4,36,64]{3,0,1,2:T(8,128)(2,1)} %copy-done.4) | copy-start | bytes 442372
  99.5 7.0 %collective-permute-start.10 = (f32[288,66]{1,0:T(8,128)S(1)}, f32[288,66]{1,0:T(8,128)S(1)}, u32[]{:S(2)}, u32[]{:S(2)}) collective-permute-start(f32[288,66]{1,0:T(8,128)S(1)} %get-tuple-element.31), channel_id=1, source_target_pairs={{0,2},{1,3},{2,0},{3,1},{4,6},{5,7},{6,4},{7,5},{8,10},{9,11},{10,... | collective-permute-start | bytes 228104 | tf_op jit(solution)/shard_map/ppermute | solution.py:114
  107.1 6.6 %collective-permute-start.11 = (f32[144,66]{1,0:T(8,128)S(1)}, f32[144,66]{1,0:T(8,128)S(1)}, u32[]{:S(2)}, u32[]{:S(2)}) collective-permute-start(f32[144,66]{1,0:T(8,128)S(1)} %get-tuple-element.35), channel_id=1, source_target_pairs={{0,4},{1,5},{2,6},{3,7},{4,0},{5,1},{6,2},{7,3},{8,12},{9,13},{10,... | collective-permute-start | bytes 114056 | tf_op jit(solution)/shard_map/ppermute | solution.py:114
  114.1 5.1 %collective-permute-start.12 = (f32[144,66]{1,0:T(8,128)S(1)}, f32[144,66]{1,0:T(8,128)S(1)}, u32[]{:S(2)}, u32[]{:S(2)}) collective-permute-start(f32[144,66]{1,0:T(8,128)S(1)} %pad_maximum_fusion.3), channel_id=1, source_target_pairs={{0,8},{1,9},{2,10},{3,11},{4,12},{5,13},{6,14},{7,15},{8,0},{9,1},... | collective-permute-start | bytes 114056 | tf_op jit(solution)/shard_map/ppermute | solution.py:94
  119.7 6.8 %collective-permute-start.13 = (f32[144,66]{1,0:T(8,128)S(1)}, f32[144,66]{1,0:T(8,128)S(1)}, u32[]{:S(2)}, u32[]{:S(2)}) collective-permute-start(f32[144,66]{1,0:T(8,128)S(1)} %pad_maximum_fusion.4), channel_id=1, source_target_pairs={{0,16},{1,17},{2,18},{3,19},{4,20},{5,21},{6,22},{7,23},{8,24},{9,... | collective-permute-start | bytes 114056 | tf_op jit(solution)/shard_map/ppermute | solution.py:94
  126.9 32.2 %copy-start.11 = (bf16[2304,36]{0,1:T(8,128)(2,1)S(1)}, bf16[2304,36]{0,1:T(8,128)(2,1)}, u32[]{:S(2)}) copy-start(bf16[2304,36]{0,1:T(8,128)(2,1)} %param.19) | copy-start | bytes 497668
  126.9 32.2 %copy-start.12 = (f32[32,36]{1,0:T(8,128)S(1)}, f32[32,36]{1,0:T(8,128)}, u32[]{:S(2)}) copy-start(f32[32,36]{1,0:T(8,128)} %param.16) | copy-start | bytes 13828
  126.9 9.1 %collective-permute-start.14 = (f32[144,66]{1,0:T(8,128)S(1)}, f32[144,66]{1,0:T(8,128)S(1)}, u32[]{:S(2)}, u32[]{:S(2)}) collective-permute-start(f32[144,66]{1,0:T(8,128)S(1)} %pad_maximum_fusion.5), channel_id=1, source_target_pairs={{0,32},{1,33},{2,34},{3,35},{4,36},{5,37},{6,38},{7,39},{8,40},{9,... | collective-permute-start | bytes 114056 | tf_op jit(solution)/shard_map/ppermute | solution.py:94
  136.9 6.0 %collective-permute-start.15 = (bf16[72,128]{1,0:T(8,128)(2,1)S(1)}, bf16[72,128]{1,0:T(8,128)(2,1)S(1)}, u32[]{:S(2)}, u32[]{:S(2)}) collective-permute-start(bf16[72,128]{1,0:T(8,128)(2,1)S(1)} %reshape.301), channel_id=1, source_target_pairs={{0,4},{1,5},{2,6},{3,7},{4,0},{5,1},{6,2},{7,3},{8,12},{9,13},{10,... | collective-permute-start | bytes 55304 | tf_op jit(solution)/shard_map/ppermute | solution.py:67
  142.9 4.9 %collective-permute-start.16 = (bf16[144,128]{1,0:T(8,128)(2,1)S(1)}, bf16[144,128]{1,0:T(8,128)(2,1)S(1)}, u32[]{:S(2)}, u32[]{:S(2)}) collective-permute-start(bf16[144,128]{1,0:T(8,128)(2,1)S(1)} %maximum_select_fusion.5), channel_id=1, source_target_pairs={{0,2},{1,3},{2,0},{3,1},{4,6},{5,7},{6,4},{7,5},{8,10},{9,11},{10,... | collective-permute-start | bytes 110600 | tf_op jit(solution)/shard_map/ppermute | solution.py:67
  147.8 11.0 %collective-permute-start.17 = (bf16[288,128]{1,0:T(8,128)(2,1)S(1)}, bf16[288,128]{1,0:T(8,128)(2,1)S(1)}, u32[]{:S(2)}, u32[]{:S(2)}) collective-permute-start(bf16[288,128]{1,0:T(8,128)(2,1)S(1)} %maximum_select_fusion.4), channel_id=1, source_target_pairs={{0,1},{1,0},{2,3},{3,2},{4,5},{5,4},{6,7},{7,6},{8,9},{9,8},{10,11... | collective-permute-start | bytes 221192 | tf_op jit(solution)/shard_map/ppermute | solution.py:67
  160.8 22.3 %all-to-all-start = ((bf16[64,2,576]{2,1,0:T(2,128)(2,1)}), bf16[64,2,576]{2,1,0:T(2,128)(2,1)S(1)}, u32[]{:S(2)}, u32[]{:S(2)}) async-start(bf16[64,2,576]{2,1,0:T(2,128)(2,1)} %reshape.333), calls=%async_computation | async-start | bytes 327680 | tf_op jit(solution)/shard_map/all_to_all | solution.py:129
  (4 other events, 7.4 us)

commit v11 on v10

--- a/solution.py
+++ b/solution.py
@@ -205,12 +205,19 @@
     ).astype(jnp.bfloat16)
     fresh_values = qkv[:, 2 * model_width :].astype(jnp.float32).reshape(requests, NEW, HEADS, HDIM)
     query_f = queries.astype(jnp.float32).reshape(requests, NEW, HEADS, HDIM)
-    pre_keys = prefix_keys.astype(jnp.float32).reshape(group_count, prefix_block, HEADS, HDIM)
-    pre_scores = jnp.einsum("rjhd,gphd->rjhgp", query_f, pre_keys) * score_scale
+    query_b = queries.reshape(requests, NEW, HEADS, HDIM)
+    pre_keys = prefix_keys.reshape(group_count, prefix_block, HEADS, HDIM)
+    pre_scores = (
+        jnp.einsum("rjhd,gphd->rjhgp", query_b, pre_keys, preferred_element_type=jnp.float32)
+        * score_scale
+    )
     member = group_ids[:, None] == jnp.arange(group_count, dtype=jnp.int32)[None, :]
     pre_scores = jnp.where(member[:, None, None, :, None], pre_scores, BLOCKED)
-    priv_keys = private_keys.astype(jnp.float32).reshape(requests, private_block, HEADS, HDIM)
-    priv_scores = jnp.einsum("rjhd,rphd->rjhp", query_f, priv_keys) * score_scale
+    priv_keys = private_keys.reshape(requests, private_block, HEADS, HDIM)
+    priv_scores = (
+        jnp.einsum("rjhd,rphd->rjhp", query_b, priv_keys, preferred_element_type=jnp.float32)
+        * score_scale
+    )
     slots = own_rank * private_block + jnp.arange(private_block, dtype=jnp.int32)
     live = slots[None, :] < private_lengths[:, None]
     priv_scores = jnp.where(live[:, None, None, :], priv_scores, BLOCKED)

time: 210 us -> 210 us (level)
  no operation moved by 1% of the time
where the time goes in v11:
time: 210 us; the launch traced here: 209 us
  starting transfers between devices  86.1 us (41%)
  waiting for transfers between devices  57.3 us (27%)
  local copies, waits for them, and re-layouts  23 us (11%)
  blocking collectives  15.6 us (7%)
  matrix products  13.1 us (6%)
  other arithmetic  13 us (6%)
    ppermute x6, starting transfers between devices, gather_cols(): other = lax.ppermute(values, 'tp', partner_pairs(count, bit))  31.7 us
    all_to_all x1, blocking collectives, exchange_scatter_sum(): received = lax.all_to_all(blocks, 'tp', 0, 0, tiled=True)  15.6 us
    ppermute x3, waiting for transfers between devices, scatter_sum(): values = keep + lax.ppermute(send, 'tp', partner_pairs(count, bit))  13 us
    ppermute x3, waiting for transfers between devices, exchange_sum(): values = values + lax.ppermute(values, 'tp', partner_pairs(count, bit))  12.8 us
    ppermute x3, starting transfers between devices, scatter_sum(): values = keep + lax.ppermute(send, 'tp', partner_pairs(count, bit))  12.6 us
    ppermute x3, starting transfers between devices, exchange_merge(): rows = merge_rows(rows, lax.ppermute(rows, 'tp', partner_pairs(count, bit)))  12.2 us
    all_to_all x1, starting transfers between devices, exchange_gather(): received = lax.all_to_all(copies, 'tp', 0, 0, tiled=True)  10.6 us
    all_to_all x1, waiting for transfers between devices, exchange_gather(): received = lax.all_to_all(copies, 'tp', 0, 0, tiled=True)  9.75 us
  transfers between devices with their start and end apart: 19, of which 18 were waited for; matrix products, arithmetic and copies ran while one was open for 5% of the time, Pallas kernels for 0%

profile of v11, /device:TPU:1, one launch (start us, length us, event | category | flops | bytes accessed | tf_op | source)
XLA Modules:
  0.0 209.3 jit_solution(4415162073675196923)
XLA Ops:
  2.3 2.0 reshape.289
  5.5 8.8 %collective-permute-start = (f32[32,3488]{1,0:T(8,128)S(1)}, f32[32,3488]{1,0:T(8,128)S(1)}, u32[]{:S(2)}, u32[]{:S(2)}) collective-permute-start(f32[32,3488]{1,0:T(8,128)S(1)} %constant_dynamic-slice_fusion.3), channel_id=1, source_target_pairs={{0,1},{1,0},{2,3},{3,2},{4,5},{5,4},{6,7},{7,6},{8,9},{9,8},{10,11... | collective-permute-start | bytes 1339400 | tf_op jit(solution)/shard_map/ppermute | solution.py:57
  16.1 1.9 collective-permute-start.1
  18.1 6.7 %collective-permute-done.1 = f32[32,1744]{1,0:T(8,128)S(1)} collective-permute-done((f32[32,1744]{1,0:T(8,128)S(1)}, f32[32,1744]{1,0:T(8,128)S(1)}, u32[]{:S(2)}, u32[]{:S(2)}) %collective-permute-start.1) | collective-permute-done | bytes 223264 | tf_op jit(solution)/shard_map/ppermute | solution.py:57
  25.0 1.9 collective-permute-start.2
  27.2 4.9 %collective-permute-done.2 = f32[32,872]{1,0:T(8,128)S(1)} collective-permute-done((f32[32,872]{1,0:T(8,128)S(1)}, f32[32,872]{1,0:T(8,128)S(1)}, u32[]{:S(2)}, u32[]{:S(2)}) %collective-permute-start.2) | collective-permute-done | bytes 111648 | tf_op jit(solution)/shard_map/ppermute | solution.py:57
  32.2 1.9 collective-permute-start.3
  34.1 3.6 %collective-permute-done.3 = f32[32,872]{1,0:T(8,128)S(1)} collective-permute-done((f32[32,872]{1,0:T(8,128)S(1)}, f32[32,872]{1,0:T(8,128)S(1)}, u32[]{:S(2)}, u32[]{:S(2)}) %collective-permute-start.3) | collective-permute-done | bytes 111648 | tf_op jit(solution)/shard_map/ppermute | solution.py:87
  37.7 1.9 collective-permute-start.4
  39.7 5.4 %collective-permute-done.4 = f32[32,872]{1,0:T(8,128)S(1)} collective-permute-done((f32[32,872]{1,0:T(8,128)S(1)}, f32[32,872]{1,0:T(8,128)S(1)}, u32[]{:S(2)}, u32[]{:S(2)}) %collective-permute-start.4) | collective-permute-done | bytes 111648 | tf_op jit(solution)/shard_map/ppermute | solution.py:87
  45.2 5.5 %collective-permute-start.5 = (f32[32,872]{1,0:T(8,128)S(1)}, f32[32,872]{1,0:T(8,128)S(1)}, u32[]{:S(2)}, u32[]{:S(2)}) collective-permute-start(f32[32,872]{1,0:T(8,128)S(1)} %add.227), channel_id=1, source_target_pairs={{0,32},{1,33},{2,34},{3,35},{4,36},{5,37},{6,38},{7,39},{8,40},{9,... | collective-permute-start | bytes 334856 | tf_op jit(solution)/shard_map/ppermute | solution.py:87
  50.9 3.7 %collective-permute-done.5 = f32[32,872]{1,0:T(8,128)S(1)} collective-permute-done((f32[32,872]{1,0:T(8,128)S(1)}, f32[32,872]{1,0:T(8,128)S(1)}, u32[]{:S(2)}, u32[]{:S(2)}) %collective-permute-start.5) | collective-permute-done | bytes 111648 | tf_op jit(solution)/shard_map/ppermute | solution.py:87
  55.5 3.0 %collective-permute-start.6 = (bf16[32,864]{1,0:T(8,128)(2,1)S(1)}, bf16[32,864]{1,0:T(8,128)(2,1)S(1)}, u32[]{:S(2)}, u32[]{:S(2)}) collective-permute-start(bf16[32,864]{1,0:T(8,128)(2,1)S(1)} %reshape.292), channel_id=1, source_target_pairs={{0,4},{1,5},{2,6},{3,7},{4,0},{5,1},{6,2},{7,3},{8,12},{9,13},{10,... | collective-permute-start | bytes 165896 | tf_op jit(solution)/shard_map/ppermute | solution.py:67
  58.5 3.4 %collective-permute-done.6 = bf16[32,864]{1,0:T(8,128)(2,1)S(1)} collective-permute-done((bf16[32,864]{1,0:T(8,128)(2,1)S(1)}, bf16[32,864]{1,0:T(8,128)(2,1)S(1)}, u32[]{:S(2)}, u32[]{:S(2)}) %collective-permute-start.6) | collective-permute-done | bytes 55328 | tf_op jit(solution)/shard_map/ppermute | solution.py:67
  62.0 2.3 %collective-permute-start.7 = (bf16[32,1728]{1,0:T(8,128)(2,1)S(1)}, bf16[32,1728]{1,0:T(8,128)(2,1)S(1)}, u32[]{:S(2)}, u32[]{:S(2)}) collective-permute-start(bf16[32,1728]{1,0:T(8,128)(2,1)S(1)} %maximum_select_fusion.3), channel_id=1, source_target_pairs={{0,2},{1,3},{2,0},{3,1},{4,6},{5,7},{6,4},{7,5},{8,10},{9,11},{10,... | collective-permute-start | bytes 331784 | tf_op jit(solution)/shard_map/ppermute | solution.py:67
  70.5 9.2 %collective-permute-start.8 = (bf16[32,3456]{1,0:T(8,128)(2,1)S(1)}, bf16[32,3456]{1,0:T(8,128)(2,1)S(1)}, u32[]{:S(2)}, u32[]{:S(2)}) collective-permute-start(bf16[32,3456]{1,0:T(8,128)(2,1)S(1)} %maximum_select_fusion.1), channel_id=1, source_target_pairs={{0,1},{1,0},{2,3},{3,2},{4,5},{5,4},{6,7},{7,6},{8,9},{9,8},{10,11... | collective-permute-start | bytes 663560 | tf_op jit(solution)/shard_map/ppermute | solution.py:67
  85.1 2.4 %fusion.85 = (f32[8,4,36]{1,2,0:T(8,128)S(1)}, f32[8,4,36,8]{3,1,2,0:T(4,128)}) fusion(bf16[8,8,36,64]{3,2,1,0:T(8,128)(2,1)} %reshape.296, bf16[8,4,36,64]{3,0,1,2:T(8,128)(2,1)S(1)} %pad_maximum_fusion.2, pred[8,8]{1,0:T(8,128)(4,1)S(1)} %broadcast_compare_fusion), kind=kOutput, calls=%fused_computation.184 | convolution fusion | flops 1206144 | bytes 483904 | tf_op jit(solution)/shard_map/rjhd,rphd->rjhp/dot_general | solution.py:218
  95.1 2.4 %collective-permute-start.9 = (f32[576,66]{1,0:T(8,128)S(1)}, f32[576,66]{1,0:T(8,128)S(1)}, u32[]{:S(2)}, u32[]{:S(2)}) collective-permute-start(f32[576,66]{1,0:T(8,128)S(1)} %constant_dynamic-slice_fusion), channel_id=1, source_target_pairs={{0,1},{1,0},{2,3},{3,2},{4,5},{5,4},{6,7},{7,6},{8,9},{9,8},{10,11... | collective-permute-start | bytes 456200 | tf_op jit(solution)/shard_map/ppermute | solution.py:114
  99.5 3.3 %collective-permute-start.10 = (f32[288,66]{1,0:T(8,128)S(1)}, f32[288,66]{1,0:T(8,128)S(1)}, u32[]{:S(2)}, u32[]{:S(2)}) collective-permute-start(f32[288,66]{1,0:T(8,128)S(1)} %get-tuple-element.31), channel_id=1, source_target_pairs={{0,2},{1,3},{2,0},{3,1},{4,6},{5,7},{6,4},{7,5},{8,10},{9,11},{10,... | collective-permute-start | bytes 228104 | tf_op jit(solution)/shard_map/ppermute | solution.py:114
  103.2 3.3 %collective-permute-done.10 = f32[288,66]{1,0:T(8,128)S(1)} collective-permute-done((f32[288,66]{1,0:T(8,128)S(1)}, f32[288,66]{1,0:T(8,128)S(1)}, u32[]{:S(2)}, u32[]{:S(2)}) %collective-permute-start.10) | collective-permute-done | bytes 76064 | tf_op jit(solution)/shard_map/ppermute | solution.py:114
  107.1 4.0 %collective-permute-start.11 = (f32[144,66]{1,0:T(8,128)S(1)}, f32[144,66]{1,0:T(8,128)S(1)}, u32[]{:S(2)}, u32[]{:S(2)}) collective-permute-start(f32[144,66]{1,0:T(8,128)S(1)} %get-tuple-element.35), channel_id=1, source_target_pairs={{0,4},{1,5},{2,6},{3,7},{4,0},{5,1},{6,2},{7,3},{8,12},{9,13},{10,... | collective-permute-start | bytes 114056 | tf_op jit(solution)/shard_map/ppermute | solution.py:114
  116.6 2.6 %collective-permute-done.12 = f32[144,66]{1,0:T(8,128)S(1)} collective-permute-done((f32[144,66]{1,0:T(8,128)S(1)}, f32[144,66]{1,0:T(8,128)S(1)}, u32[]{:S(2)}, u32[]{:S(2)}) %collective-permute-start.12) | collective-permute-done | bytes 38048 | tf_op jit(solution)/shard_map/ppermute | solution.py:94
  119.7 3.7 %collective-permute-start.13 = (f32[144,66]{1,0:T(8,128)S(1)}, f32[144,66]{1,0:T(8,128)S(1)}, u32[]{:S(2)}, u32[]{:S(2)}) collective-permute-start(f32[144,66]{1,0:T(8,128)S(1)} %pad_maximum_fusion.4), channel_id=1, source_target_pairs={{0,16},{1,17},{2,18},{3,19},{4,20},{5,21},{6,22},{7,23},{8,24},{9,... | collective-permute-start | bytes 114056 | tf_op jit(solution)/shard_map/ppermute | solution.py:94
  126.9 6.6 %collective-permute-start.14 = (f32[144,66]{1,0:T(8,128)S(1)}, f32[144,66]{1,0:T(8,128)S(1)}, u32[]{:S(2)}, u32[]{:S(2)}) collective-permute-start(f32[144,66]{1,0:T(8,128)S(1)} %pad_maximum_fusion.5), channel_id=1, source_target_pairs={{0,32},{1,33},{2,34},{3,35},{4,36},{5,37},{6,38},{7,39},{8,40},{9,... | collective-permute-start | bytes 114056 | tf_op jit(solution)/shard_map/ppermute | solution.py:94
  133.6 2.5 %collective-permute-done.14 = f32[144,66]{1,0:T(8,128)S(1)} collective-permute-done((f32[144,66]{1,0:T(8,128)S(1)}, f32[144,66]{1,0:T(8,128)S(1)}, u32[]{:S(2)}, u32[]{:S(2)}) %collective-permute-start.14) | collective-permute-done | bytes 38048 | tf_op jit(solution)/shard_map/ppermute | solution.py:94
  136.9 3.9 %collective-permute-start.15 = (bf16[72,128]{1,0:T(8,128)(2,1)S(1)}, bf16[72,128]{1,0:T(8,128)(2,1)S(1)}, u32[]{:S(2)}, u32[]{:S(2)}) collective-permute-start(bf16[72,128]{1,0:T(8,128)(2,1)S(1)} %reshape.302), channel_id=1, source_target_pairs={{0,4},{1,5},{2,6},{3,7},{4,0},{5,1},{6,2},{7,3},{8,12},{9,13},{10,... | collective-permute-start | bytes 55304 | tf_op jit(solution)/shard_map/ppermute | solution.py:67
  140.8 2.1 %collective-permute-done.15 = bf16[72,128]{1,0:T(8,128)(2,1)S(1)} collective-permute-done((bf16[72,128]{1,0:T(8,128)(2,1)S(1)}, bf16[72,128]{1,0:T(8,128)(2,1)S(1)}, u32[]{:S(2)}, u32[]{:S(2)}) %collective-permute-start.15) | collective-permute-done | bytes 18464 | tf_op jit(solution)/shard_map/ppermute | solution.py:67
  142.9 3.1 %collective-permute-start.16 = (bf16[144,128]{1,0:T(8,128)(2,1)S(1)}, bf16[144,128]{1,0:T(8,128)(2,1)S(1)}, u32[]{:S(2)}, u32[]{:S(2)}) collective-permute-start(bf16[144,128]{1,0:T(8,128)(2,1)S(1)} %maximum_select_fusion.5), channel_id=1, source_target_pairs={{0,2},{1,3},{2,0},{3,1},{4,6},{5,7},{6,4},{7,5},{8,10},{9,11},{10,... | collective-permute-start | bytes 110600 | tf_op jit(solution)/shard_map/ppermute | solution.py:67
  147.8 10.1 %collective-permute-start.17 = (bf16[288,128]{1,0:T(8,128)(2,1)S(1)}, bf16[288,128]{1,0:T(8,128)(2,1)S(1)}, u32[]{:S(2)}, u32[]{:S(2)}) collective-permute-start(bf16[288,128]{1,0:T(8,128)(2,1)S(1)} %maximum_select_fusion.4), channel_id=1, source_target_pairs={{0,1},{1,0},{2,3},{3,2},{4,5},{5,4},{6,7},{7,6},{8,9},{9,8},{10,11... | collective-permute-start | bytes 221192 | tf_op jit(solution)/shard_map/ppermute | solution.py:67
  160.8 10.6 %all-to-all-start = ((bf16[64,2,576]{2,1,0:T(2,128)(2,1)}), bf16[64,2,576]{2,1,0:T(2,128)(2,1)S(1)}, u32[]{:S(2)}, u32[]{:S(2)}) async-start(bf16[64,2,576]{2,1,0:T(2,128)(2,1)} %reshape.334), calls=%async_computation | async-start | bytes 327680 | tf_op jit(solution)/shard_map/all_to_all | solution.py:129
  173.3 9.7 %all-to-all-done = bf16[64,2,576]{2,1,0:T(2,128)(2,1)S(1)} async-done(((bf16[64,2,576]{2,1,0:T(2,128)(2,1)}), bf16[64,2,576]{2,1,0:T(2,128)(2,1)S(1)}, u32[]{:S(2)}, u32[]{:S(2)}) %all-to-all-start) | async-done | bytes 147488 | tf_op jit(solution)/shard_map/all_to_all | solution.py:129
  191.1 15.6 %all_to_all.10 = bf16[64,2,576]{2,1,0:T(2,128)(2,1)S(1)} all-to-all(bf16[64,2,576]{2,1,0:T(2,128)(2,1)S(1)} %reshape.336), channel_id=1, replica_groups=mesh['rep'=8,'tp'=64] {'tp'}, dimensions={0} | all-to-all | bytes 294912 | tf_op jit(solution)/shard_map/all_to_all | solution.py:134
  (167 shorter events, 55.9 us)
Async XLA Ops:
  0.0 188.0 %copy-start = (bf16[2304,180]{0,1:T(8,128)(2,1)S(1)}, bf16[2304,180]{0,1:T(8,128)(2,1)}, u32[]{:S(2)}) copy-start(bf16[2304,180]{0,1:T(8,128)(2,1)} %param.29) | copy-start | bytes 2488324
  5.3 21.6 %copy-start.15 = (s32[8]{0:T(128)S(1)}, s32[8]{0:T(128)}, u32[]{:S(2)}) copy-start(s32[8]{0:T(128)} %param.25) | copy-start | bytes 100
  5.5 10.2 %collective-permute-start = (f32[32,3488]{1,0:T(8,128)S(1)}, f32[32,3488]{1,0:T(8,128)S(1)}, u32[]{:S(2)}, u32[]{:S(2)}) collective-permute-start(f32[32,3488]{1,0:T(8,128)S(1)} %constant_dynamic-slice_fusion.3), channel_id=1, source_target_pairs={{0,1},{1,0},{2,3},{3,2},{4,5},{5,4},{6,7},{7,6},{8,9},{9,8},{10,11... | collective-permute-start | bytes 1339400 | tf_op jit(solution)/shard_map/ppermute | solution.py:57
  15.9 48.4 %copy-start.7 = (bf16[3,32,2304]{2,1,0:T(8,128)(2,1)S(1)}, bf16[3,32,2304]{2,1,0:T(8,128)(2,1)}, u32[]{:S(2)}) copy-start(bf16[3,32,2304]{2,1,0:T(8,128)(2,1)} %param.20) | copy-start | bytes 1327108
  16.1 8.7 %collective-permute-start.1 = (f32[32,1744]{1,0:T(8,128)S(1)}, f32[32,1744]{1,0:T(8,128)S(1)}, u32[]{:S(2)}, u32[]{:S(2)}) collective-permute-start(f32[32,1744]{1,0:T(8,128)S(1)} %constant_dynamic-slice_fusion.2), channel_id=1, source_target_pairs={{0,2},{1,3},{2,0},{3,1},{4,6},{5,7},{6,4},{7,5},{8,10},{9,11},{10,... | collective-permute-start | bytes 669704 | tf_op jit(solution)/shard_map/ppermute | solution.py:57
  25.0 7.0 %collective-permute-start.2 = (f32[32,872]{1,0:T(8,128)S(1)}, f32[32,872]{1,0:T(8,128)S(1)}, u32[]{:S(2)}, u32[]{:S(2)}) collective-permute-start(f32[32,872]{1,0:T(8,128)S(1)} %constant_dynamic-slice_fusion.1), channel_id=1, source_target_pairs={{0,4},{1,5},{2,6},{3,7},{4,0},{5,1},{6,2},{7,3},{8,12},{9,13},{10,... | collective-permute-start | bytes 334856 | tf_op jit(solution)/shard_map/ppermute | solution.py:57
  27.2 38.9 %copy-start.9 = (bf16[8,8,2304]{2,1,0:T(8,128)(2,1)S(1)}, bf16[8,8,2304]{2,1,0:T(8,128)(2,1)}, u32[]{:S(2)}) copy-start(bf16[8,8,2304]{2,1,0:T(8,128)(2,1)} %param.22) | copy-start | bytes 884740
  32.2 5.5 %collective-permute-start.3 = (f32[32,872]{1,0:T(8,128)S(1)}, f32[32,872]{1,0:T(8,128)S(1)}, u32[]{:S(2)}, u32[]{:S(2)}) collective-permute-start(f32[32,872]{1,0:T(8,128)S(1)} %dynamic-slice_add_fusion.2), channel_id=1, source_target_pairs={{0,8},{1,9},{2,10},{3,11},{4,12},{5,13},{6,14},{7,15},{8,0},{9,1},... | collective-permute-start | bytes 334856 | tf_op jit(solution)/shard_map/ppermute | solution.py:87
  37.7 7.4 %collective-permute-start.4 = (f32[32,872]{1,0:T(8,128)S(1)}, f32[32,872]{1,0:T(8,128)S(1)}, u32[]{:S(2)}, u32[]{:S(2)}) collective-permute-start(f32[32,872]{1,0:T(8,128)S(1)} %add.226), channel_id=1, source_target_pairs={{0,16},{1,17},{2,18},{3,19},{4,20},{5,21},{6,22},{7,23},{8,24},{9,... | collective-permute-start | bytes 334856 | tf_op jit(solution)/shard_map/ppermute | solution.py:87
  45.2 9.4 %collective-permute-start.5 = (f32[32,872]{1,0:T(8,128)S(1)}, f32[32,872]{1,0:T(8,128)S(1)}, u32[]{:S(2)}, u32[]{:S(2)}) collective-permute-start(f32[32,872]{1,0:T(8,128)S(1)} %add.227), channel_id=1, source_target_pairs={{0,32},{1,33},{2,34},{3,35},{4,36},{5,37},{6,38},{7,39},{8,40},{9,... | collective-permute-start | bytes 334856 | tf_op jit(solution)/shard_map/ppermute | solution.py:87
  50.8 16.5 %copy-start.10 = (bf16[8,8,2304]{2,1,0:T(8,128)(2,1)S(1)}, bf16[8,8,2304]{2,1,0:T(8,128)(2,1)}, u32[]{:S(2)}) copy-start(bf16[8,8,2304]{2,1,0:T(8,128)(2,1)} %param.23) | copy-start | bytes 884740
  55.5 6.4 %collective-permute-start.6 = (bf16[32,864]{1,0:T(8,128)(2,1)S(1)}, bf16[32,864]{1,0:T(8,128)(2,1)S(1)}, u32[]{:S(2)}, u32[]{:S(2)}) collective-permute-start(bf16[32,864]{1,0:T(8,128)(2,1)S(1)} %reshape.292), channel_id=1, source_target_pairs={{0,4},{1,5},{2,6},{3,7},{4,0},{5,1},{6,2},{7,3},{8,12},{9,13},{10,... | collective-permute-start | bytes 165896 | tf_op jit(solution)/shard_map/ppermute | solution.py:67
  58.5 10.2 %copy-start.8 = (bf16[3,32,2304]{2,1,0:T(8,128)(2,1)S(1)}, bf16[3,32,2304]{2,1,0:T(8,128)(2,1)}, u32[]{:S(2)}) copy-start(bf16[3,32,2304]{2,1,0:T(8,128)(2,1)} %param.21) | copy-start | bytes 1327108
  62.0 8.3 %collective-permute-start.7 = (bf16[32,1728]{1,0:T(8,128)(2,1)S(1)}, bf16[32,1728]{1,0:T(8,128)(2,1)S(1)}, u32[]{:S(2)}, u32[]{:S(2)}) collective-permute-start(bf16[32,1728]{1,0:T(8,128)(2,1)S(1)} %maximum_select_fusion.3), channel_id=1, source_target_pairs={{0,2},{1,3},{2,0},{3,1},{4,6},{5,7},{6,4},{7,5},{8,10},{9,11},{10,... | collective-permute-start | bytes 331784 | tf_op jit(solution)/shard_map/ppermute | solution.py:67
  66.1 13.6 %copy-start.16 = (s32[8]{0:T(128)S(1)}, s32[8]{0:T(128)}, u32[]{:S(2)}) copy-start(s32[8]{0:T(128)} %param.24) | copy-start | bytes 100
  70.5 10.1 %collective-permute-start.8 = (bf16[32,3456]{1,0:T(8,128)(2,1)S(1)}, bf16[32,3456]{1,0:T(8,128)(2,1)S(1)}, u32[]{:S(2)}, u32[]{:S(2)}) collective-permute-start(bf16[32,3456]{1,0:T(8,128)(2,1)S(1)} %maximum_select_fusion.1), channel_id=1, source_target_pairs={{0,1},{1,0},{2,3},{3,2},{4,5},{5,4},{6,7},{7,6},{8,9},{9,8},{10,11... | collective-permute-start | bytes 663560 | tf_op jit(solution)/shard_map/ppermute | solution.py:67
  83.0 4.6 %copy-start.4 = (bf16[8,4,36,64]{3,0,1,2:T(8,128)(2,1)}, bf16[8,4,36,64]{3,0,1,2:T(8,128)(2,1)S(1)}, u32[]{:S(2)}) copy-start(bf16[8,4,36,64]{3,0,1,2:T(8,128)(2,1)S(1)} %pad_maximum_fusion.2) | copy-start | bytes 442372
  95.1 7.8 %copy-start.3 = (bf16[32,36,32]{2,1,0:T(8,128)(2,1)S(1)}, bf16[32,36,32]{2,1,0:T(8,128)(2,1)}, u32[]{:S(2)}) copy-start(bf16[32,36,32]{2,1,0:T(8,128)(2,1)} %get-tuple-element.38) | copy-start | bytes 221188
  95.1 7.9 %copy-start.2 = (bf16[32,36,32]{2,1,0:T(8,128)(2,1)S(1)}, bf16[32,36,32]{2,1,0:T(8,128)(2,1)}, u32[]{:S(2)}) copy-start(bf16[32,36,32]{2,1,0:T(8,128)(2,1)} %get-tuple-element.37) | copy-start | bytes 221188
  95.1 3.6 %collective-permute-start.9 = (f32[576,66]{1,0:T(8,128)S(1)}, f32[576,66]{1,0:T(8,128)S(1)}, u32[]{:S(2)}, u32[]{:S(2)}) collective-permute-start(f32[576,66]{1,0:T(8,128)S(1)} %constant_dynamic-slice_fusion), channel_id=1, source_target_pairs={{0,1},{1,0},{2,3},{3,2},{4,5},{5,4},{6,7},{7,6},{8,9},{9,8},{10,11... | collective-permute-start | bytes 456200 | tf_op jit(solution)/shard_map/ppermute | solution.py:114
  99.4 11.7 %copy-start.5 = (bf16[8,4,36,64]{3,0,1,2:T(8,128)(2,1)S(1)}, bf16[8,4,36,64]{3,0,1,2:T(8,128)(2,1)}, u32[]{:S(2)}) copy-start(bf16[8,4,36,64]{3,0,1,2:T(8,128)(2,1)} %copy-done.4) | copy-start | bytes 442372
  99.5 7.0 %collective-permute-start.10 = (f32[288,66]{1,0:T(8,128)S(1)}, f32[288,66]{1,0:T(8,128)S(1)}, u32[]{:S(2)}, u32[]{:S(2)}) collective-permute-start(f32[288,66]{1,0:T(8,128)S(1)} %get-tuple-element.31), channel_id=1, source_target_pairs={{0,2},{1,3},{2,0},{3,1},{4,6},{5,7},{6,4},{7,5},{8,10},{9,11},{10,... | collective-permute-start | bytes 228104 | tf_op jit(solution)/shard_map/ppermute | solution.py:114
  107.1 6.6 %collective-permute-start.11 = (f32[144,66]{1,0:T(8,128)S(1)}, f32[144,66]{1,0:T(8,128)S(1)}, u32[]{:S(2)}, u32[]{:S(2)}) collective-permute-start(f32[144,66]{1,0:T(8,128)S(1)} %get-tuple-element.35), channel_id=1, source_target_pairs={{0,4},{1,5},{2,6},{3,7},{4,0},{5,1},{6,2},{7,3},{8,12},{9,13},{10,... | collective-permute-start | bytes 114056 | tf_op jit(solution)/shard_map/ppermute | solution.py:114
  114.1 5.1 %collective-permute-start.12 = (f32[144,66]{1,0:T(8,128)S(1)}, f32[144,66]{1,0:T(8,128)S(1)}, u32[]{:S(2)}, u32[]{:S(2)}) collective-permute-start(f32[144,66]{1,0:T(8,128)S(1)} %pad_maximum_fusion.3), channel_id=1, source_target_pairs={{0,8},{1,9},{2,10},{3,11},{4,12},{5,13},{6,14},{7,15},{8,0},{9,1},... | collective-permute-start | bytes 114056 | tf_op jit(solution)/shard_map/ppermute | solution.py:94
  119.7 6.8 %collective-permute-start.13 = (f32[144,66]{1,0:T(8,128)S(1)}, f32[144,66]{1,0:T(8,128)S(1)}, u32[]{:S(2)}, u32[]{:S(2)}) collective-permute-start(f32[144,66]{1,0:T(8,128)S(1)} %pad_maximum_fusion.4), channel_id=1, source_target_pairs={{0,16},{1,17},{2,18},{3,19},{4,20},{5,21},{6,22},{7,23},{8,24},{9,... | collective-permute-start | bytes 114056 | tf_op jit(solution)/shard_map/ppermute | solution.py:94
  126.9 32.2 %copy-start.11 = (bf16[2304,36]{0,1:T(8,128)(2,1)S(1)}, bf16[2304,36]{0,1:T(8,128)(2,1)}, u32[]{:S(2)}) copy-start(bf16[2304,36]{0,1:T(8,128)(2,1)} %param.19) | copy-start | bytes 497668
  126.9 32.2 %copy-start.12 = (f32[32,36]{1,0:T(8,128)S(1)}, f32[32,36]{1,0:T(8,128)}, u32[]{:S(2)}) copy-start(f32[32,36]{1,0:T(8,128)} %param.16) | copy-start | bytes 13828
  126.9 9.1 %collective-permute-start.14 = (f32[144,66]{1,0:T(8,128)S(1)}, f32[144,66]{1,0:T(8,128)S(1)}, u32[]{:S(2)}, u32[]{:S(2)}) collective-permute-start(f32[144,66]{1,0:T(8,128)S(1)} %pad_maximum_fusion.5), channel_id=1, source_target_pairs={{0,32},{1,33},{2,34},{3,35},{4,36},{5,37},{6,38},{7,39},{8,40},{9,... | collective-permute-start | bytes 114056 | tf_op jit(solution)/shard_map/ppermute | solution.py:94
  136.9 6.0 %collective-permute-start.15 = (bf16[72,128]{1,0:T(8,128)(2,1)S(1)}, bf16[72,128]{1,0:T(8,128)(2,1)S(1)}, u32[]{:S(2)}, u32[]{:S(2)}) collective-permute-start(bf16[72,128]{1,0:T(8,128)(2,1)S(1)} %reshape.302), channel_id=1, source_target_pairs={{0,4},{1,5},{2,6},{3,7},{4,0},{5,1},{6,2},{7,3},{8,12},{9,13},{10,... | collective-permute-start | bytes 55304 | tf_op jit(solution)/shard_map/ppermute | solution.py:67
  142.9 4.9 %collective-permute-start.16 = (bf16[144,128]{1,0:T(8,128)(2,1)S(1)}, bf16[144,128]{1,0:T(8,128)(2,1)S(1)}, u32[]{:S(2)}, u32[]{:S(2)}) collective-permute-start(bf16[144,128]{1,0:T(8,128)(2,1)S(1)} %maximum_select_fusion.5), channel_id=1, source_target_pairs={{0,2},{1,3},{2,0},{3,1},{4,6},{5,7},{6,4},{7,5},{8,10},{9,11},{10,... | collective-permute-start | bytes 110600 | tf_op jit(solution)/shard_map/ppermute | solution.py:67
  147.8 11.0 %collective-permute-start.17 = (bf16[288,128]{1,0:T(8,128)(2,1)S(1)}, bf16[288,128]{1,0:T(8,128)(2,1)S(1)}, u32[]{:S(2)}, u32[]{:S(2)}) collective-permute-start(bf16[288,128]{1,0:T(8,128)(2,1)S(1)} %maximum_select_fusion.4), channel_id=1, source_target_pairs={{0,1},{1,0},{2,3},{3,2},{4,5},{5,4},{6,7},{7,6},{8,9},{9,8},{10,11... | collective-permute-start | bytes 221192 | tf_op jit(solution)/shard_map/ppermute | solution.py:67
  160.8 22.3 %all-to-all-start = ((bf16[64,2,576]{2,1,0:T(2,128)(2,1)}), bf16[64,2,576]{2,1,0:T(2,128)(2,1)S(1)}, u32[]{:S(2)}, u32[]{:S(2)}) async-start(bf16[64,2,576]{2,1,0:T(2,128)(2,1)} %reshape.334), calls=%async_computation | async-start | bytes 327680 | tf_op jit(solution)/shard_map/all_to_all | solution.py:129
  (4 other events, 7.4 us)

commit v12 on v11

--- a/solution.py
+++ b/solution.py
@@ -133,6 +133,35 @@
 def exchange_scatter_sum(blocks):
     received = lax.all_to_all(blocks, "tp", 0, 0, tiled=True)
     return jnp.sum(received.astype(jnp.float32), axis=0)
+
+
+def merge_states(first, second, heads):
+    width = first.shape[1] - 2 * heads
+    joint = jnp.maximum(first[:, width + heads :], second[:, width + heads :])
+    first_factor = jnp.exp(first[:, width + heads :] - joint)
+    second_factor = jnp.exp(second[:, width + heads :] - joint)
+    total = first[:, width : width + heads] * first_factor + second[:, width : width + heads] * second_factor
+    weighted = scale_rows(first[:, :width], first_factor) + scale_rows(second[:, :width], second_factor)
+    return jnp.concatenate([weighted, total, joint], axis=1)
+
+
+def scatter_states(states, bits, heads):
+    count, _ = tp_bits()
+    own_rank = lax.axis_index("tp")
+    for bit in bits:
+        half = states.shape[0] // 2
+        side = (own_rank // bit) % 2
+        keep = lax.dynamic_slice_in_dim(states, side * half, half, axis=0)
+        send = lax.dynamic_slice_in_dim(states, (1 - side) * half, half, axis=0)
+        states = merge_states(keep, lax.ppermute(send, "tp", partner_pairs(count, bit)), heads)
+    return states
+
+
+def exchange_states(states, bits, heads):
+    count, _ = tp_bits()
+    for bit in bits:
+        states = merge_states(states, lax.ppermute(states, "tp", partner_pairs(count, bit)), heads)
+    return states
 
 
 def reverse_blocks(values, count):
@@ -233,8 +262,10 @@
     local_peak = local_peak.reshape(all_tokens, HEADS)
     local_total = local_total.reshape(all_tokens, HEADS)
     local_weighted = local_weighted.reshape(all_tokens, model_width)
-    cache_rows = scatter_merge(state_rows(local_peak, local_total, local_weighted), near_bits)
-    cache_rows = exchange_merge(cache_rows, far_bits)
+    cache_state = scatter_states(
+        jnp.concatenate([local_weighted, local_total, local_peak], axis=1), near_bits, HEADS
+    )
+    cache_state = exchange_states(cache_state, far_bits, HEADS)
     key_f = fresh_keys.astype(jnp.float32).reshape(requests, NEW, HEADS, HDIM)
     new_scores = jnp.einsum("rjhd,rihd->rjhi", query_f, key_f) * score_scale
     causal = jnp.arange(NEW)[:, None] >= jnp.arange(NEW)[None, :]
@@ -246,12 +277,14 @@
         all_tokens, model_width
     )
     new_peak = new_peak.reshape(all_tokens, HEADS)
-    new_rows = state_rows(new_peak, new_total, new_weighted)
-    own_count = cache_rows.shape[0]
-    new_rows = lax.dynamic_slice_in_dim(new_rows, kept_position(near_bits) * own_count, own_count, axis=0)
-    final_rows = merge_rows(cache_rows, new_rows)
-    attended_rows = (final_rows[:, :HDIM] / final_rows[:, HDIM : HDIM + 1]).astype(jnp.bfloat16)
-    attended_lines = attended_rows.reshape(attended_rows.shape[0] // 2, 2 * HDIM)
+    new_state = jnp.concatenate([new_weighted, new_total, new_peak], axis=1)
+    own_count = cache_state.shape[0]
+    new_state = lax.dynamic_slice_in_dim(new_state, kept_position(near_bits) * own_count, own_count, axis=0)
+    final_state = merge_states(cache_state, new_state, HEADS)
+    final_weighted = final_state[:, :model_width].reshape(own_count, HEADS, HDIM)
+    final_total = final_state[:, model_width : model_width + HEADS]
+    attended_own = (final_weighted / final_total[..., None]).astype(jnp.bfloat16)
+    attended_lines = attended_own.reshape(own_count * HEADS // 2, 2 * HDIM)
     attended = gather_cols(attended_lines, axis=0, bits=near_bits).reshape(all_tokens, model_width)
     residual_cols = hidden + jnp.dot(attended, w_out, preferred_element_type=jnp.float32)
     full_rows = exchange_gather(residual_cols.astype(jnp.bfloat16)).astype(jnp.float32)

time: 210 us -> 211 us (level)
  local copies, waits for them, and re-layouts: 23 us -> 28 us
  waiting for transfers between devices: 57.3 us -> 52.4 us
    ppermute x6, waiting for transfers between devices: 12.8 us -> 8.77 us  [the longest x3 5.04 us: scatter_states(): lax.ppermute(send, 'tp', partner_pairs(count, bit))]
    mul x0 -> x28, local copies, waits for them, and re-layouts: none -> 2.63 us  [scale_rows(): values.reshape(row_count, head_count, -1) * factor[..., None]]
    unnamed x39 -> x37, local copies, waits for them, and re-layouts: 6.09 us -> 6.09 us
where the time goes in v12:
time: 211 us; the launch traced here: 210 us
  starting transfers between devices  87.6 us (42%)
  waiting for transfers between devices  52.4 us (25%)
  local copies, waits for them, and re-layouts  28 us (13%)
  blocking collectives  15.6 us (7%)
  matrix products  13.1 us (6%)
  other arithmetic  11.9 us (6%)
    ppermute x6, starting transfers between devices, gather_cols(): other = lax.ppermute(values, 'tp', partner_pairs(count, bit))  33 us
    all_to_all x1, blocking collectives, exchange_scatter_sum(): received = lax.all_to_all(blocks, 'tp', 0, 0, tiled=True)  15.6 us
    ppermute x3, waiting for transfers between devices, scatter_sum(): values = keep + lax.ppermute(send, 'tp', partner_pairs(count, bit))  13 us
    ppermute x3, waiting for transfers between devices, exchange_sum(): values = values + lax.ppermute(values, 'tp', partner_pairs(count, bit))  12.8 us
    ppermute x3, starting transfers between devices, scatter_sum(): values = keep + lax.ppermute(send, 'tp', partner_pairs(count, bit))  12.6 us
    ppermute x3, starting transfers between devices, exchange_states(): lax.ppermute(states, 'tp', partner_pairs(count, bit))  12.6 us
    all_to_all x1, starting transfers between devices, exchange_gather(): received = lax.all_to_all(copies, 'tp', 0, 0, tiled=True)  10.3 us
    all_to_all x1, waiting for transfers between devices, exchange_gather(): received = lax.all_to_all(copies, 'tp', 0, 0, tiled=True)  9.75 us
  transfers between devices with their start and end apart: 19, of which 18 were waited for; matrix products, arithmetic and copies ran while one was open for 5% of the time, Pallas kernels for 0%

profile of v12, /device:TPU:1, one launch (start us, length us, event | category | flops | bytes accessed | tf_op | source)
XLA Modules:
  0.0 209.7 jit_solution(18409809776323791158)
XLA Ops:
  2.3 2.0 reshape.333
  5.5 8.8 %collective-permute-start = (f32[32,3488]{1,0:T(8,128)S(1)}, f32[32,3488]{1,0:T(8,128)S(1)}, u32[]{:S(2)}, u32[]{:S(2)}) collective-permute-start(f32[32,3488]{1,0:T(8,128)S(1)} %constant_dynamic-slice_fusion.5), channel_id=1, source_target_pairs={{0,1},{1,0},{2,3},{3,2},{4,5},{5,4},{6,7},{7,6},{8,9},{9,8},{10,11... | collective-permute-start | bytes 1339400 | tf_op jit(solution)/shard_map/ppermute | solution.py:57
  16.1 1.9 collective-permute-start.1
  18.1 6.7 %collective-permute-done.1 = f32[32,1744]{1,0:T(8,128)S(1)} collective-permute-done((f32[32,1744]{1,0:T(8,128)S(1)}, f32[32,1744]{1,0:T(8,128)S(1)}, u32[]{:S(2)}, u32[]{:S(2)}) %collective-permute-start.1) | collective-permute-done | bytes 223264 | tf_op jit(solution)/shard_map/ppermute | solution.py:57
  25.0 1.9 collective-permute-start.2
  27.1 4.9 %collective-permute-done.2 = f32[32,872]{1,0:T(8,128)S(1)} collective-permute-done((f32[32,872]{1,0:T(8,128)S(1)}, f32[32,872]{1,0:T(8,128)S(1)}, u32[]{:S(2)}, u32[]{:S(2)}) %collective-permute-start.2) | collective-permute-done | bytes 111648 | tf_op jit(solution)/shard_map/ppermute | solution.py:57
  32.2 1.9 collective-permute-start.3
  34.1 3.6 %collective-permute-done.3 = f32[32,872]{1,0:T(8,128)S(1)} collective-permute-done((f32[32,872]{1,0:T(8,128)S(1)}, f32[32,872]{1,0:T(8,128)S(1)}, u32[]{:S(2)}, u32[]{:S(2)}) %collective-permute-start.3) | collective-permute-done | bytes 111648 | tf_op jit(solution)/shard_map/ppermute | solution.py:87
  37.7 1.9 collective-permute-start.4
  39.7 5.4 %collective-permute-done.4 = f32[32,872]{1,0:T(8,128)S(1)} collective-permute-done((f32[32,872]{1,0:T(8,128)S(1)}, f32[32,872]{1,0:T(8,128)S(1)}, u32[]{:S(2)}, u32[]{:S(2)}) %collective-permute-start.4) | collective-permute-done | bytes 111648 | tf_op jit(solution)/shard_map/ppermute | solution.py:87
  45.1 5.5 %collective-permute-start.5 = (f32[32,872]{1,0:T(8,128)S(1)}, f32[32,872]{1,0:T(8,128)S(1)}, u32[]{:S(2)}, u32[]{:S(2)}) collective-permute-start(f32[32,872]{1,0:T(8,128)S(1)} %add.242), channel_id=1, source_target_pairs={{0,32},{1,33},{2,34},{3,35},{4,36},{5,37},{6,38},{7,39},{8,40},{9,... | collective-permute-start | bytes 334856 | tf_op jit(solution)/shard_map/ppermute | solution.py:87
  50.8 3.7 %collective-permute-done.5 = f32[32,872]{1,0:T(8,128)S(1)} collective-permute-done((f32[32,872]{1,0:T(8,128)S(1)}, f32[32,872]{1,0:T(8,128)S(1)}, u32[]{:S(2)}, u32[]{:S(2)}) %collective-permute-start.5) | collective-permute-done | bytes 111648 | tf_op jit(solution)/shard_map/ppermute | solution.py:87
  55.4 3.0 %collective-permute-start.6 = (bf16[32,864]{1,0:T(8,128)(2,1)S(1)}, bf16[32,864]{1,0:T(8,128)(2,1)S(1)}, u32[]{:S(2)}, u32[]{:S(2)}) collective-permute-start(bf16[32,864]{1,0:T(8,128)(2,1)S(1)} %reshape.336), channel_id=1, source_target_pairs={{0,4},{1,5},{2,6},{3,7},{4,0},{5,1},{6,2},{7,3},{8,12},{9,13},{10,... | collective-permute-start | bytes 165896 | tf_op jit(solution)/shard_map/ppermute | solution.py:67
  58.5 3.4 %collective-permute-done.6 = bf16[32,864]{1,0:T(8,128)(2,1)S(1)} collective-permute-done((bf16[32,864]{1,0:T(8,128)(2,1)S(1)}, bf16[32,864]{1,0:T(8,128)(2,1)S(1)}, u32[]{:S(2)}, u32[]{:S(2)}) %collective-permute-start.6) | collective-permute-done | bytes 55328 | tf_op jit(solution)/shard_map/ppermute | solution.py:67
  62.0 2.3 %collective-permute-start.7 = (bf16[32,1728]{1,0:T(8,128)(2,1)S(1)}, bf16[32,1728]{1,0:T(8,128)(2,1)S(1)}, u32[]{:S(2)}, u32[]{:S(2)}) collective-permute-start(bf16[32,1728]{1,0:T(8,128)(2,1)S(1)} %maximum_select_fusion.3), channel_id=1, source_target_pairs={{0,2},{1,3},{2,0},{3,1},{4,6},{5,7},{6,4},{7,5},{8,10},{9,11},{10,... | collective-permute-start | bytes 331784 | tf_op jit(solution)/shard_map/ppermute | solution.py:67
  70.5 9.2 %collective-permute-start.8 = (bf16[32,3456]{1,0:T(8,128)(2,1)S(1)}, bf16[32,3456]{1,0:T(8,128)(2,1)S(1)}, u32[]{:S(2)}, u32[]{:S(2)}) collective-permute-start(bf16[32,3456]{1,0:T(8,128)(2,1)S(1)} %maximum_select_fusion.1), channel_id=1, source_target_pairs={{0,1},{1,0},{2,3},{3,2},{4,5},{5,4},{6,7},{7,6},{8,9},{9,8},{10,11... | collective-permute-start | bytes 663560 | tf_op jit(solution)/shard_map/ppermute | solution.py:67
  84.9 2.5 %fusion.86 = (f32[8,4,36]{1,2,0:T(8,128)S(1)}, f32[8,4,36,8]{3,1,2,0:T(4,128)}) fusion(bf16[8,8,36,64]{3,2,1,0:T(8,128)(2,1)} %reshape.340, bf16[8,4,36,64]{3,0,1,2:T(8,128)(2,1)} %copy-done.2, pred[8,8]{1,0:T(8,128)(4,1)S(1)} %broadcast_compare_fusion), kind=kOutput, calls=%fused_computation.179 | convolution fusion | flops 1206144 | bytes 483904 | tf_op jit(solution)/shard_map/rjhd,rphd->rjhp/dot_general | solution.py:247
  87.8 2.5 %fusion.32 = f32[8,4,36]{1,2,0:T(8,128)} fusion(f32[8,4,36,8]{3,1,2,0:T(4,128)} %get-tuple-element.50, f32[8,4,36]{1,2,0:T(8,128)S(1)} %copy.182), kind=kLoop, calls=%fused_computation.45 | loop fusion | flops 17280 | bytes 46080 | tf_op jit(solution)/shard_map/reduce_sum | solution.py:256
  98.7 2.3 %collective-permute-start.9 = (f32[16,2376]{1,0:T(8,128)S(1)}, f32[16,2376]{1,0:T(8,128)S(1)}, u32[]{:S(2)}, u32[]{:S(2)}) collective-permute-start(f32[16,2376]{1,0:T(8,128)S(1)} %constant_dynamic-slice_fusion.2), channel_id=1, source_target_pairs={{0,1},{1,0},{2,3},{3,2},{4,5},{5,4},{6,7},{7,6},{8,9},{9,8},{10,11... | collective-permute-start | bytes 456200 | tf_op jit(solution)/shard_map/ppermute | solution.py:156
  102.8 3.5 %collective-permute-start.10 = (f32[8,2376]{1,0:T(8,128)S(1)}, f32[8,2376]{1,0:T(8,128)S(1)}, u32[]{:S(2)}, u32[]{:S(2)}) collective-permute-start(f32[8,2376]{1,0:T(8,128)S(1)} %constant_dynamic-slice_fusion.1), channel_id=1, source_target_pairs={{0,2},{1,3},{2,0},{3,1},{4,6},{5,7},{6,4},{7,5},{8,10},{9,11},{10,... | collective-permute-start | bytes 228104 | tf_op jit(solution)/shard_map/ppermute | solution.py:156
  106.3 2.1 %collective-permute-done.10 = f32[8,2376]{1,0:T(8,128)S(1)} collective-permute-done((f32[8,2376]{1,0:T(8,128)S(1)}, f32[8,2376]{1,0:T(8,128)S(1)}, u32[]{:S(2)}, u32[]{:S(2)}) %collective-permute-start.10) | collective-permute-done | bytes 76064 | tf_op jit(solution)/shard_map/ppermute | solution.py:156
  109.0 4.0 %collective-permute-start.11 = (f32[4,2376]{1,0:T(4,128)S(1)}, f32[4,2376]{1,0:T(4,128)S(1)}, u32[]{:S(2)}, u32[]{:S(2)}) collective-permute-start(f32[4,2376]{1,0:T(4,128)S(1)} %constant_dynamic-slice_fusion), channel_id=1, source_target_pairs={{0,4},{1,5},{2,6},{3,7},{4,0},{5,1},{6,2},{7,3},{8,12},{9,13},{10,... | collective-permute-start | bytes 114056 | tf_op jit(solution)/shard_map/ppermute | solution.py:156
  113.3 2.0 collective-permute-done.11
  115.8 1.9 collective-permute-start.12
  121.1 3.5 %collective-permute-start.13 = (f32[4,2376]{1,0:T(4,128)S(1)}, f32[4,2376]{1,0:T(4,128)S(1)}, u32[]{:S(2)}, u32[]{:S(2)}) collective-permute-start(f32[4,2376]{1,0:T(4,128)S(1)} %concatenate.92), channel_id=1, source_target_pairs={{0,16},{1,17},{2,18},{3,19},{4,20},{5,21},{6,22},{7,23},{8,24},{9,... | collective-permute-start | bytes 114056 | tf_op jit(solution)/shard_map/ppermute | solution.py:163
  127.3 7.2 %collective-permute-start.14 = (f32[4,2376]{1,0:T(4,128)S(1)}, f32[4,2376]{1,0:T(4,128)S(1)}, u32[]{:S(2)}, u32[]{:S(2)}) collective-permute-start(f32[4,2376]{1,0:T(4,128)S(1)} %concatenate.93), channel_id=1, source_target_pairs={{0,32},{1,33},{2,34},{3,35},{4,36},{5,37},{6,38},{7,39},{8,40},{9,... | collective-permute-start | bytes 114056 | tf_op jit(solution)/shard_map/ppermute | solution.py:163
  137.2 4.5 %collective-permute-start.15 = (bf16[72,128]{1,0:T(8,128)(2,1)S(1)}, bf16[72,128]{1,0:T(8,128)(2,1)S(1)}, u32[]{:S(2)}, u32[]{:S(2)}) collective-permute-start(bf16[72,128]{1,0:T(8,128)(2,1)S(1)} %divide_convert_fusion), channel_id=1, source_target_pairs={{0,4},{1,5},{2,6},{3,7},{4,0},{5,1},{6,2},{7,3},{8,12},{9,13},{10,... | collective-permute-start | bytes 55304 | tf_op jit(solution)/shard_map/ppermute | solution.py:67
  143.2 3.3 %collective-permute-start.16 = (bf16[144,128]{1,0:T(8,128)(2,1)S(1)}, bf16[144,128]{1,0:T(8,128)(2,1)S(1)}, u32[]{:S(2)}, u32[]{:S(2)}) collective-permute-start(bf16[144,128]{1,0:T(8,128)(2,1)S(1)} %maximum_select_fusion.5), channel_id=1, source_target_pairs={{0,2},{1,3},{2,0},{3,1},{4,6},{5,7},{6,4},{7,5},{8,10},{9,11},{10,... | collective-permute-start | bytes 110600 | tf_op jit(solution)/shard_map/ppermute | solution.py:67
  147.9 10.6 %collective-permute-start.17 = (bf16[288,128]{1,0:T(8,128)(2,1)S(1)}, bf16[288,128]{1,0:T(8,128)(2,1)S(1)}, u32[]{:S(2)}, u32[]{:S(2)}) collective-permute-start(bf16[288,128]{1,0:T(8,128)(2,1)S(1)} %maximum_select_fusion.4), channel_id=1, source_target_pairs={{0,1},{1,0},{2,3},{3,2},{4,5},{5,4},{6,7},{7,6},{8,9},{9,8},{10,11... | collective-permute-start | bytes 221192 | tf_op jit(solution)/shard_map/ppermute | solution.py:67
  161.4 10.3 %all-to-all-start = ((bf16[64,2,576]{2,1,0:T(2,128)(2,1)}), bf16[64,2,576]{2,1,0:T(2,128)(2,1)S(1)}, u32[]{:S(2)}, u32[]{:S(2)}) async-start(bf16[64,2,576]{2,1,0:T(2,128)(2,1)} %reshape.367), calls=%async_computation | async-start | bytes 327680 | tf_op jit(solution)/shard_map/all_to_all | solution.py:129
  173.7 9.7 %all-to-all-done = bf16[64,2,576]{2,1,0:T(2,128)(2,1)S(1)} async-done(((bf16[64,2,576]{2,1,0:T(2,128)(2,1)}), bf16[64,2,576]{2,1,0:T(2,128)(2,1)S(1)}, u32[]{:S(2)}, u32[]{:S(2)}) %all-to-all-start) | async-done | bytes 147488 | tf_op jit(solution)/shard_map/all_to_all | solution.py:129
  191.5 15.6 %all_to_all.10 = bf16[64,2,576]{2,1,0:T(2,128)(2,1)S(1)} all-to-all(bf16[64,2,576]{2,1,0:T(2,128)(2,1)S(1)} %reshape.369), channel_id=1, replica_groups=mesh['rep'=8,'tp'=64] {'tp'}, dimensions={0} | all-to-all | bytes 294912 | tf_op jit(solution)/shard_map/all_to_all | solution.py:134
  (192 shorter events, 56.8 us)
Async XLA Ops:
  0.0 188.4 %copy-start = (bf16[2304,180]{0,1:T(8,128)(2,1)S(1)}, bf16[2304,180]{0,1:T(8,128)(2,1)}, u32[]{:S(2)}) copy-start(bf16[2304,180]{0,1:T(8,128)(2,1)} %param.29) | copy-start | bytes 2488324
  5.3 21.6 %copy-start.14 = (s32[8]{0:T(128)S(1)}, s32[8]{0:T(128)}, u32[]{:S(2)}) copy-start(s32[8]{0:T(128)} %param.25) | copy-start | bytes 100
  5.5 10.2 %collective-permute-start = (f32[32,3488]{1,0:T(8,128)S(1)}, f32[32,3488]{1,0:T(8,128)S(1)}, u32[]{:S(2)}, u32[]{:S(2)}) collective-permute-start(f32[32,3488]{1,0:T(8,128)S(1)} %constant_dynamic-slice_fusion.5), channel_id=1, source_target_pairs={{0,1},{1,0},{2,3},{3,2},{4,5},{5,4},{6,7},{7,6},{8,9},{9,8},{10,11... | collective-permute-start | bytes 1339400 | tf_op jit(solution)/shard_map/ppermute | solution.py:57
  15.9 48.4 %copy-start.6 = (bf16[3,32,2304]{2,1,0:T(8,128)(2,1)S(1)}, bf16[3,32,2304]{2,1,0:T(8,128)(2,1)}, u32[]{:S(2)}) copy-start(bf16[3,32,2304]{2,1,0:T(8,128)(2,1)} %param.20) | copy-start | bytes 1327108
  16.1 8.7 %collective-permute-start.1 = (f32[32,1744]{1,0:T(8,128)S(1)}, f32[32,1744]{1,0:T(8,128)S(1)}, u32[]{:S(2)}, u32[]{:S(2)}) collective-permute-start(f32[32,1744]{1,0:T(8,128)S(1)} %constant_dynamic-slice_fusion.4), channel_id=1, source_target_pairs={{0,2},{1,3},{2,0},{3,1},{4,6},{5,7},{6,4},{7,5},{8,10},{9,11},{10,... | collective-permute-start | bytes 669704 | tf_op jit(solution)/shard_map/ppermute | solution.py:57
  25.0 7.0 %collective-permute-start.2 = (f32[32,872]{1,0:T(8,128)S(1)}, f32[32,872]{1,0:T(8,128)S(1)}, u32[]{:S(2)}, u32[]{:S(2)}) collective-permute-start(f32[32,872]{1,0:T(8,128)S(1)} %constant_dynamic-slice_fusion.3), channel_id=1, source_target_pairs={{0,4},{1,5},{2,6},{3,7},{4,0},{5,1},{6,2},{7,3},{8,12},{9,13},{10,... | collective-permute-start | bytes 334856 | tf_op jit(solution)/shard_map/ppermute | solution.py:57
  27.1 38.9 %copy-start.8 = (bf16[8,8,2304]{2,1,0:T(8,128)(2,1)S(1)}, bf16[8,8,2304]{2,1,0:T(8,128)(2,1)}, u32[]{:S(2)}) copy-start(bf16[8,8,2304]{2,1,0:T(8,128)(2,1)} %param.22) | copy-start | bytes 884740
  32.2 5.5 %collective-permute-start.3 = (f32[32,872]{1,0:T(8,128)S(1)}, f32[32,872]{1,0:T(8,128)S(1)}, u32[]{:S(2)}, u32[]{:S(2)}) collective-permute-start(f32[32,872]{1,0:T(8,128)S(1)} %dynamic-slice_add_fusion.2), channel_id=1, source_target_pairs={{0,8},{1,9},{2,10},{3,11},{4,12},{5,13},{6,14},{7,15},{8,0},{9,1},... | collective-permute-start | bytes 334856 | tf_op jit(solution)/shard_map/ppermute | solution.py:87
  37.7 7.4 %collective-permute-start.4 = (f32[32,872]{1,0:T(8,128)S(1)}, f32[32,872]{1,0:T(8,128)S(1)}, u32[]{:S(2)}, u32[]{:S(2)}) collective-permute-start(f32[32,872]{1,0:T(8,128)S(1)} %add.241), channel_id=1, source_target_pairs={{0,16},{1,17},{2,18},{3,19},{4,20},{5,21},{6,22},{7,23},{8,24},{9,... | collective-permute-start | bytes 334856 | tf_op jit(solution)/shard_map/ppermute | solution.py:87
  45.1 9.4 %collective-permute-start.5 = (f32[32,872]{1,0:T(8,128)S(1)}, f32[32,872]{1,0:T(8,128)S(1)}, u32[]{:S(2)}, u32[]{:S(2)}) collective-permute-start(f32[32,872]{1,0:T(8,128)S(1)} %add.242), channel_id=1, source_target_pairs={{0,32},{1,33},{2,34},{3,35},{4,36},{5,37},{6,38},{7,39},{8,40},{9,... | collective-permute-start | bytes 334856 | tf_op jit(solution)/shard_map/ppermute | solution.py:87
  50.8 16.6 %copy-start.9 = (bf16[8,8,2304]{2,1,0:T(8,128)(2,1)S(1)}, bf16[8,8,2304]{2,1,0:T(8,128)(2,1)}, u32[]{:S(2)}) copy-start(bf16[8,8,2304]{2,1,0:T(8,128)(2,1)} %param.23) | copy-start | bytes 884740
  55.4 6.4 %collective-permute-start.6 = (bf16[32,864]{1,0:T(8,128)(2,1)S(1)}, bf16[32,864]{1,0:T(8,128)(2,1)S(1)}, u32[]{:S(2)}, u32[]{:S(2)}) collective-permute-start(bf16[32,864]{1,0:T(8,128)(2,1)S(1)} %reshape.336), channel_id=1, source_target_pairs={{0,4},{1,5},{2,6},{3,7},{4,0},{5,1},{6,2},{7,3},{8,12},{9,13},{10,... | collective-permute-start | bytes 165896 | tf_op jit(solution)/shard_map/ppermute | solution.py:67
  58.5 10.2 %copy-start.7 = (bf16[3,32,2304]{2,1,0:T(8,128)(2,1)S(1)}, bf16[3,32,2304]{2,1,0:T(8,128)(2,1)}, u32[]{:S(2)}) copy-start(bf16[3,32,2304]{2,1,0:T(8,128)(2,1)} %param.21) | copy-start | bytes 1327108
  62.0 8.4 %collective-permute-start.7 = (bf16[32,1728]{1,0:T(8,128)(2,1)S(1)}, bf16[32,1728]{1,0:T(8,128)(2,1)S(1)}, u32[]{:S(2)}, u32[]{:S(2)}) collective-permute-start(bf16[32,1728]{1,0:T(8,128)(2,1)S(1)} %maximum_select_fusion.3), channel_id=1, source_target_pairs={{0,2},{1,3},{2,0},{3,1},{4,6},{5,7},{6,4},{7,5},{8,10},{9,11},{10,... | collective-permute-start | bytes 331784 | tf_op jit(solution)/shard_map/ppermute | solution.py:67
  66.1 13.6 %copy-start.15 = (s32[8]{0:T(128)S(1)}, s32[8]{0:T(128)}, u32[]{:S(2)}) copy-start(s32[8]{0:T(128)} %param.24) | copy-start | bytes 100
  70.5 10.1 %collective-permute-start.8 = (bf16[32,3456]{1,0:T(8,128)(2,1)S(1)}, bf16[32,3456]{1,0:T(8,128)(2,1)S(1)}, u32[]{:S(2)}, u32[]{:S(2)}) collective-permute-start(bf16[32,3456]{1,0:T(8,128)(2,1)S(1)} %maximum_select_fusion.1), channel_id=1, source_target_pairs={{0,1},{1,0},{2,3},{3,2},{4,5},{5,4},{6,7},{7,6},{8,9},{9,8},{10,11... | collective-permute-start | bytes 663560 | tf_op jit(solution)/shard_map/ppermute | solution.py:67
  82.8 2.0 copy-start.2
  94.6 2.7 %copy-start.4 = (bf16[3,32,36,64]{3,2,1,0:T(8,128)(2,1)S(1)}, bf16[3,32,36,64]{3,2,1,0:T(8,128)(2,1)}, u32[]{:S(2)}) copy-start(bf16[3,32,36,64]{3,2,1,0:T(8,128)(2,1)} %reshape.341) | copy-start | bytes 1327108
  98.7 3.3 %collective-permute-start.9 = (f32[16,2376]{1,0:T(8,128)S(1)}, f32[16,2376]{1,0:T(8,128)S(1)}, u32[]{:S(2)}, u32[]{:S(2)}) collective-permute-start(f32[16,2376]{1,0:T(8,128)S(1)} %constant_dynamic-slice_fusion.2), channel_id=1, source_target_pairs={{0,1},{1,0},{2,3},{3,2},{4,5},{5,4},{6,7},{7,6},{8,9},{9,8},{10,11... | collective-permute-start | bytes 456200 | tf_op jit(solution)/shard_map/ppermute | solution.py:156
  102.8 15.0 %copy-start.3 = (bf16[8,4,36,64]{3,0,1,2:T(8,128)(2,1)S(1)}, bf16[8,4,36,64]{3,0,1,2:T(8,128)(2,1)}, u32[]{:S(2)}) copy-start(bf16[8,4,36,64]{3,0,1,2:T(8,128)(2,1)} %copy-done.2) | copy-start | bytes 442372
  102.8 5.6 %collective-permute-start.10 = (f32[8,2376]{1,0:T(8,128)S(1)}, f32[8,2376]{1,0:T(8,128)S(1)}, u32[]{:S(2)}, u32[]{:S(2)}) collective-permute-start(f32[8,2376]{1,0:T(8,128)S(1)} %constant_dynamic-slice_fusion.1), channel_id=1, source_target_pairs={{0,2},{1,3},{2,0},{3,1},{4,6},{5,7},{6,4},{7,5},{8,10},{9,11},{10,... | collective-permute-start | bytes 228104 | tf_op jit(solution)/shard_map/ppermute | solution.py:156
  109.0 6.2 %collective-permute-start.11 = (f32[4,2376]{1,0:T(4,128)S(1)}, f32[4,2376]{1,0:T(4,128)S(1)}, u32[]{:S(2)}, u32[]{:S(2)}) collective-permute-start(f32[4,2376]{1,0:T(4,128)S(1)} %constant_dynamic-slice_fusion), channel_id=1, source_target_pairs={{0,4},{1,5},{2,6},{3,7},{4,0},{5,1},{6,2},{7,3},{8,12},{9,13},{10,... | collective-permute-start | bytes 114056 | tf_op jit(solution)/shard_map/ppermute | solution.py:156
  113.3 5.3 %copy-start.5 = (bf16[32,2304]{1,0:T(8,128)(2,1)S(1)}, bf16[32,2304]{1,0:T(8,128)(2,1)}, u32[]{:S(2)}) copy-start(bf16[32,2304]{1,0:T(8,128)(2,1)} %get-tuple-element.36) | copy-start | bytes 442372
  115.8 4.7 %collective-permute-start.12 = (f32[4,2376]{1,0:T(4,128)S(1)}, f32[4,2376]{1,0:T(4,128)S(1)}, u32[]{:S(2)}, u32[]{:S(2)}) collective-permute-start(f32[4,2376]{1,0:T(4,128)S(1)} %concatenate.91), channel_id=1, source_target_pairs={{0,8},{1,9},{2,10},{3,11},{4,12},{5,13},{6,14},{7,15},{8,0},{9,1},... | collective-permute-start | bytes 114056 | tf_op jit(solution)/shard_map/ppermute | solution.py:163
  121.1 5.6 %collective-permute-start.13 = (f32[4,2376]{1,0:T(4,128)S(1)}, f32[4,2376]{1,0:T(4,128)S(1)}, u32[]{:S(2)}, u32[]{:S(2)}) collective-permute-start(f32[4,2376]{1,0:T(4,128)S(1)} %concatenate.92), channel_id=1, source_target_pairs={{0,16},{1,17},{2,18},{3,19},{4,20},{5,21},{6,22},{7,23},{8,24},{9,... | collective-permute-start | bytes 114056 | tf_op jit(solution)/shard_map/ppermute | solution.py:163
  127.3 8.8 %collective-permute-start.14 = (f32[4,2376]{1,0:T(4,128)S(1)}, f32[4,2376]{1,0:T(4,128)S(1)}, u32[]{:S(2)}, u32[]{:S(2)}) collective-permute-start(f32[4,2376]{1,0:T(4,128)S(1)} %concatenate.93), channel_id=1, source_target_pairs={{0,32},{1,33},{2,34},{3,35},{4,36},{5,37},{6,38},{7,39},{8,40},{9,... | collective-permute-start | bytes 114056 | tf_op jit(solution)/shard_map/ppermute | solution.py:163
  135.4 24.3 %copy-start.10 = (bf16[2304,36]{0,1:T(8,128)(2,1)S(1)}, bf16[2304,36]{0,1:T(8,128)(2,1)}, u32[]{:S(2)}) copy-start(bf16[2304,36]{0,1:T(8,128)(2,1)} %param.19) | copy-start | bytes 497668
  135.4 24.3 %copy-start.11 = (f32[32,36]{1,0:T(8,128)S(1)}, f32[32,36]{1,0:T(8,128)}, u32[]{:S(2)}) copy-start(f32[32,36]{1,0:T(8,128)} %param.16) | copy-start | bytes 13828
  137.2 6.0 %collective-permute-start.15 = (bf16[72,128]{1,0:T(8,128)(2,1)S(1)}, bf16[72,128]{1,0:T(8,128)(2,1)S(1)}, u32[]{:S(2)}, u32[]{:S(2)}) collective-permute-start(bf16[72,128]{1,0:T(8,128)(2,1)S(1)} %divide_convert_fusion), channel_id=1, source_target_pairs={{0,4},{1,5},{2,6},{3,7},{4,0},{5,1},{6,2},{7,3},{8,12},{9,13},{10,... | collective-permute-start | bytes 55304 | tf_op jit(solution)/shard_map/ppermute | solution.py:67
  143.2 4.7 %collective-permute-start.16 = (bf16[144,128]{1,0:T(8,128)(2,1)S(1)}, bf16[144,128]{1,0:T(8,128)(2,1)S(1)}, u32[]{:S(2)}, u32[]{:S(2)}) collective-permute-start(bf16[144,128]{1,0:T(8,128)(2,1)S(1)} %maximum_select_fusion.5), channel_id=1, source_target_pairs={{0,2},{1,3},{2,0},{3,1},{4,6},{5,7},{6,4},{7,5},{8,10},{9,11},{10,... | collective-permute-start | bytes 110600 | tf_op jit(solution)/shard_map/ppermute | solution.py:67
  147.9 11.5 %collective-permute-start.17 = (bf16[288,128]{1,0:T(8,128)(2,1)S(1)}, bf16[288,128]{1,0:T(8,128)(2,1)S(1)}, u32[]{:S(2)}, u32[]{:S(2)}) collective-permute-start(bf16[288,128]{1,0:T(8,128)(2,1)S(1)} %maximum_select_fusion.4), channel_id=1, source_target_pairs={{0,1},{1,0},{2,3},{3,2},{4,5},{5,4},{6,7},{7,6},{8,9},{9,8},{10,11... | collective-permute-start | bytes 221192 | tf_op jit(solution)/shard_map/ppermute | solution.py:67
  161.4 22.0 %all-to-all-start = ((bf16[64,2,576]{2,1,0:T(2,128)(2,1)}), bf16[64,2,576]{2,1,0:T(2,128)(2,1)S(1)}, u32[]{:S(2)}, u32[]{:S(2)}) async-start(bf16[64,2,576]{2,1,0:T(2,128)(2,1)} %reshape.367), calls=%async_computation | async-start | bytes 327680 | tf_op jit(solution)/shard_map/all_to_all | solution.py:129
  (3 other events, 4.4 us)

commit v13 on v11

--- a/solution.py
+++ b/solution.py
@@ -183,8 +183,8 @@
         axis=2,
     ).reshape(all_tokens, tp_count * (block + 1))
     _, all_bits = tp_bits()
-    near_bits = all_bits[: len(all_bits) // 2]
-    far_bits = all_bits[len(all_bits) // 2 :]
+    near_bits = [all_bits[0], all_bits[1], all_bits[3]]
+    far_bits = [all_bits[2], all_bits[4], all_bits[5]]
     own_block = exchange_sum(scatter_sum(packed, near_bits), far_bits)
     own_block = own_block.reshape(all_tokens, -1, block + 1)
     inv_attn = lax.rsqrt(own_block[:, 0, block] / model_width + EPSILON)

time: 210 us -> 208 us (level)
    ppermute x3, starting transfers between devices: 12.2 us -> 16.1 us  [exchange_merge(): rows = merge_rows(rows, lax.ppermute(rows, 'tp', partner_pairs(count, bit)))]
    ppermute x3, waiting for transfers between devices: 6.82 us -> 4.21 us  [exchange_merge(): rows = merge_rows(rows, lax.ppermute(rows, 'tp', partner_pairs(count, bit)))]
    ppermute x6, starting transfers between devices: 31.7 us -> 29.2 us  [gather_cols(): other = lax.ppermute(values, 'tp', partner_pairs(count, bit))]
    ppermute x3, starting transfers between devices: 9.73 us -> 7.51 us  [scatter_merge(): rows = merge_rows(keep, lax.ppermute(send, 'tp', partner_pairs(count, bit)))]
  transfers between devices with their start and end apart: 19 -> 19, of which waited for: 18 -> 18; matrix products, arithmetic and copies ran while one was open for 5% -> 6% of each run, Pallas kernels for 0% -> 0%
where the time goes in v13:
time: 208 us; the launch traced here: 207 us
  starting transfers between devices  85.7 us (41%)
  waiting for transfers between devices  55.3 us (27%)
  local copies, waits for them, and re-layouts  23 us (11%)
  blocking collectives  15.6 us (8%)
  matrix products  13.1 us (6%)
  other arithmetic  13 us (6%)
    ppermute x6, starting transfers between devices, gather_cols(): other = lax.ppermute(values, 'tp', partner_pairs(count, bit))  29.2 us
    ppermute x3, starting transfers between devices, exchange_merge(): rows = merge_rows(rows, lax.ppermute(rows, 'tp', partner_pairs(count, bit)))  16.1 us
    all_to_all x1, blocking collectives, exchange_scatter_sum(): received = lax.all_to_all(blocks, 'tp', 0, 0, tiled=True)  15.6 us
    ppermute x3, waiting for transfers between devices, exchange_sum(): values = values + lax.ppermute(values, 'tp', partner_pairs(count, bit))  14.3 us
    ppermute x3, starting transfers between devices, scatter_sum(): values = keep + lax.ppermute(send, 'tp', partner_pairs(count, bit))  12.6 us
    ppermute x3, waiting for transfers between devices, scatter_sum(): values = keep + lax.ppermute(send, 'tp', partner_pairs(count, bit))  11.5 us
    all_to_all x1, starting transfers between devices, exchange_gather(): received = lax.all_to_all(copies, 'tp', 0, 0, tiled=True)  11 us
    all_to_all x1, waiting for transfers between devices, exchange_gather(): received = lax.all_to_all(copies, 'tp', 0, 0, tiled=True)  9.75 us
  transfers between devices with their start and end apart: 19, of which 18 were waited for; matrix products, arithmetic and copies ran while one was open for 6% of the time, Pallas kernels for 0%

profile of v13, /device:TPU:1, one launch (start us, length us, event | category | flops | bytes accessed | tf_op | source)
XLA Modules:
  0.0 206.9 jit_solution(14078428152583781260)
XLA Ops:
  2.3 2.0 reshape.289
  5.5 8.8 %collective-permute-start = (f32[32,3488]{1,0:T(8,128)S(1)}, f32[32,3488]{1,0:T(8,128)S(1)}, u32[]{:S(2)}, u32[]{:S(2)}) collective-permute-start(f32[32,3488]{1,0:T(8,128)S(1)} %constant_dynamic-slice_fusion.3), channel_id=1, source_target_pairs={{0,1},{1,0},{2,3},{3,2},{4,5},{5,4},{6,7},{7,6},{8,9},{9,8},{10,11... | collective-permute-start | bytes 1339400 | tf_op jit(solution)/shard_map/ppermute | solution.py:57
  16.1 1.9 collective-permute-start.1
  18.1 6.7 %collective-permute-done.1 = f32[32,1744]{1,0:T(8,128)S(1)} collective-permute-done((f32[32,1744]{1,0:T(8,128)S(1)}, f32[32,1744]{1,0:T(8,128)S(1)}, u32[]{:S(2)}, u32[]{:S(2)}) %collective-permute-start.1) | collective-permute-done | bytes 223264 | tf_op jit(solution)/shard_map/ppermute | solution.py:57
  25.0 1.9 collective-permute-start.2
  27.2 3.4 %collective-permute-done.2 = f32[32,872]{1,0:T(8,128)S(1)} collective-permute-done((f32[32,872]{1,0:T(8,128)S(1)}, f32[32,872]{1,0:T(8,128)S(1)}, u32[]{:S(2)}, u32[]{:S(2)}) %collective-permute-start.2) | collective-permute-done | bytes 111648 | tf_op jit(solution)/shard_map/ppermute | solution.py:57
  30.7 1.9 collective-permute-start.3
  32.6 5.1 %collective-permute-done.3 = f32[32,872]{1,0:T(8,128)S(1)} collective-permute-done((f32[32,872]{1,0:T(8,128)S(1)}, f32[32,872]{1,0:T(8,128)S(1)}, u32[]{:S(2)}, u32[]{:S(2)}) %collective-permute-start.3) | collective-permute-done | bytes 111648 | tf_op jit(solution)/shard_map/ppermute | solution.py:87
  37.7 1.9 collective-permute-start.4
  39.7 5.5 %collective-permute-done.4 = f32[32,872]{1,0:T(8,128)S(1)} collective-permute-done((f32[32,872]{1,0:T(8,128)S(1)}, f32[32,872]{1,0:T(8,128)S(1)}, u32[]{:S(2)}, u32[]{:S(2)}) %collective-permute-start.4) | collective-permute-done | bytes 111648 | tf_op jit(solution)/shard_map/ppermute | solution.py:87
  45.2 5.5 %collective-permute-start.5 = (f32[32,872]{1,0:T(8,128)S(1)}, f32[32,872]{1,0:T(8,128)S(1)}, u32[]{:S(2)}, u32[]{:S(2)}) collective-permute-start(f32[32,872]{1,0:T(8,128)S(1)} %add.227), channel_id=1, source_target_pairs={{0,32},{1,33},{2,34},{3,35},{4,36},{5,37},{6,38},{7,39},{8,40},{9,... | collective-permute-start | bytes 334856 | tf_op jit(solution)/shard_map/ppermute | solution.py:87
  50.9 3.7 %collective-permute-done.5 = f32[32,872]{1,0:T(8,128)S(1)} collective-permute-done((f32[32,872]{1,0:T(8,128)S(1)}, f32[32,872]{1,0:T(8,128)S(1)}, u32[]{:S(2)}, u32[]{:S(2)}) %collective-permute-start.5) | collective-permute-done | bytes 111648 | tf_op jit(solution)/shard_map/ppermute | solution.py:87
  55.5 1.9 collective-permute-start.6
  57.4 3.8 %collective-permute-done.6 = bf16[32,864]{1,0:T(8,128)(2,1)S(1)} collective-permute-done((bf16[32,864]{1,0:T(8,128)(2,1)S(1)}, bf16[32,864]{1,0:T(8,128)(2,1)S(1)}, u32[]{:S(2)}, u32[]{:S(2)}) %collective-permute-start.6) | collective-permute-done | bytes 55328 | tf_op jit(solution)/shard_map/ppermute | solution.py:67
  61.4 1.9 collective-permute-start.7
  69.5 8.3 %collective-permute-start.8 = (bf16[32,3456]{1,0:T(8,128)(2,1)S(1)}, bf16[32,3456]{1,0:T(8,128)(2,1)S(1)}, u32[]{:S(2)}, u32[]{:S(2)}) collective-permute-start(bf16[32,3456]{1,0:T(8,128)(2,1)S(1)} %maximum_select_fusion.1), channel_id=1, source_target_pairs={{0,1},{1,0},{2,3},{3,2},{4,5},{5,4},{6,7},{7,6},{8,9},{9,8},{10,11... | collective-permute-start | bytes 663560 | tf_op jit(solution)/shard_map/ppermute | solution.py:67
  83.2 2.5 %fusion.85 = (f32[8,4,36]{1,2,0:T(8,128)S(1)}, f32[8,4,36,8]{3,1,2,0:T(4,128)}) fusion(bf16[8,8,36,64]{3,2,1,0:T(8,128)(2,1)} %reshape.296, bf16[8,4,36,64]{3,0,1,2:T(8,128)(2,1)S(1)} %pad_maximum_fusion.2, pred[8,8]{1,0:T(8,128)(4,1)S(1)} %broadcast_compare_fusion), kind=kOutput, calls=%fused_computation.184 | convolution fusion | flops 1206144 | bytes 483904 | tf_op jit(solution)/shard_map/rjhd,rphd->rjhp/dot_general | solution.py:218
  93.3 2.4 %collective-permute-start.9 = (f32[576,66]{1,0:T(8,128)S(1)}, f32[576,66]{1,0:T(8,128)S(1)}, u32[]{:S(2)}, u32[]{:S(2)}) collective-permute-start(f32[576,66]{1,0:T(8,128)S(1)} %constant_dynamic-slice_fusion), channel_id=1, source_target_pairs={{0,1},{1,0},{2,3},{3,2},{4,5},{5,4},{6,7},{7,6},{8,9},{9,8},{10,11... | collective-permute-start | bytes 456200 | tf_op jit(solution)/shard_map/ppermute | solution.py:114
  97.7 3.2 %collective-permute-start.10 = (f32[288,66]{1,0:T(8,128)S(1)}, f32[288,66]{1,0:T(8,128)S(1)}, u32[]{:S(2)}, u32[]{:S(2)}) collective-permute-start(f32[288,66]{1,0:T(8,128)S(1)} %get-tuple-element.31), channel_id=1, source_target_pairs={{0,2},{1,3},{2,0},{3,1},{4,6},{5,7},{6,4},{7,5},{8,10},{9,11},{10,... | collective-permute-start | bytes 228104 | tf_op jit(solution)/shard_map/ppermute | solution.py:114
  101.1 3.5 %collective-permute-done.10 = f32[288,66]{1,0:T(8,128)S(1)} collective-permute-done((f32[288,66]{1,0:T(8,128)S(1)}, f32[288,66]{1,0:T(8,128)S(1)}, u32[]{:S(2)}, u32[]{:S(2)}) %collective-permute-start.10) | collective-permute-done | bytes 76064 | tf_op jit(solution)/shard_map/ppermute | solution.py:114
  105.2 1.9 collective-permute-start.11
  108.3 2.0 collective-permute-done.11
  110.7 4.0 %collective-permute-start.12 = (f32[144,66]{1,0:T(8,128)S(1)}, f32[144,66]{1,0:T(8,128)S(1)}, u32[]{:S(2)}, u32[]{:S(2)}) collective-permute-start(f32[144,66]{1,0:T(8,128)S(1)} %pad_maximum_fusion.3), channel_id=1, source_target_pairs={{0,4},{1,5},{2,6},{3,7},{4,0},{5,1},{6,2},{7,3},{8,12},{9,13},{10,... | collective-permute-start | bytes 114056 | tf_op jit(solution)/shard_map/ppermute | solution.py:94
  115.3 2.1 %collective-permute-done.12 = f32[144,66]{1,0:T(8,128)S(1)} collective-permute-done((f32[144,66]{1,0:T(8,128)S(1)}, f32[144,66]{1,0:T(8,128)S(1)}, u32[]{:S(2)}, u32[]{:S(2)}) %collective-permute-start.12) | collective-permute-done | bytes 38048 | tf_op jit(solution)/shard_map/ppermute | solution.py:94
  117.8 4.2 %collective-permute-start.13 = (f32[144,66]{1,0:T(8,128)S(1)}, f32[144,66]{1,0:T(8,128)S(1)}, u32[]{:S(2)}, u32[]{:S(2)}) collective-permute-start(f32[144,66]{1,0:T(8,128)S(1)} %pad_maximum_fusion.4), channel_id=1, source_target_pairs={{0,16},{1,17},{2,18},{3,19},{4,20},{5,21},{6,22},{7,23},{8,24},{9,... | collective-permute-start | bytes 114056 | tf_op jit(solution)/shard_map/ppermute | solution.py:94
  124.2 7.9 %collective-permute-start.14 = (f32[144,66]{1,0:T(8,128)S(1)}, f32[144,66]{1,0:T(8,128)S(1)}, u32[]{:S(2)}, u32[]{:S(2)}) collective-permute-start(f32[144,66]{1,0:T(8,128)S(1)} %pad_maximum_fusion.5), channel_id=1, source_target_pairs={{0,32},{1,33},{2,34},{3,35},{4,36},{5,37},{6,38},{7,39},{8,40},{9,... | collective-permute-start | bytes 114056 | tf_op jit(solution)/shard_map/ppermute | solution.py:94
  134.8 3.3 %collective-permute-start.15 = (bf16[72,128]{1,0:T(8,128)(2,1)S(1)}, bf16[72,128]{1,0:T(8,128)(2,1)S(1)}, u32[]{:S(2)}, u32[]{:S(2)}) collective-permute-start(bf16[72,128]{1,0:T(8,128)(2,1)S(1)} %reshape.302), channel_id=1, source_target_pairs={{0,8},{1,9},{2,10},{3,11},{4,12},{5,13},{6,14},{7,15},{8,0},{9,1},... | collective-permute-start | bytes 55304 | tf_op jit(solution)/shard_map/ppermute | solution.py:67
  139.6 2.9 %collective-permute-start.16 = (bf16[144,128]{1,0:T(8,128)(2,1)S(1)}, bf16[144,128]{1,0:T(8,128)(2,1)S(1)}, u32[]{:S(2)}, u32[]{:S(2)}) collective-permute-start(bf16[144,128]{1,0:T(8,128)(2,1)S(1)} %maximum_select_fusion.5), channel_id=1, source_target_pairs={{0,2},{1,3},{2,0},{3,1},{4,6},{5,7},{6,4},{7,5},{8,10},{9,11},{10,... | collective-permute-start | bytes 110600 | tf_op jit(solution)/shard_map/ppermute | solution.py:67
  144.4 10.7 %collective-permute-start.17 = (bf16[288,128]{1,0:T(8,128)(2,1)S(1)}, bf16[288,128]{1,0:T(8,128)(2,1)S(1)}, u32[]{:S(2)}, u32[]{:S(2)}) collective-permute-start(bf16[288,128]{1,0:T(8,128)(2,1)S(1)} %maximum_select_fusion.4), channel_id=1, source_target_pairs={{0,1},{1,0},{2,3},{3,2},{4,5},{5,4},{6,7},{7,6},{8,9},{9,8},{10,11... | collective-permute-start | bytes 221192 | tf_op jit(solution)/shard_map/ppermute | solution.py:67
  157.9 11.0 %all-to-all-start = ((bf16[64,2,576]{2,1,0:T(2,128)(2,1)}), bf16[64,2,576]{2,1,0:T(2,128)(2,1)S(1)}, u32[]{:S(2)}, u32[]{:S(2)}) async-start(bf16[64,2,576]{2,1,0:T(2,128)(2,1)} %reshape.334), calls=%async_computation | async-start | bytes 327680 | tf_op jit(solution)/shard_map/all_to_all | solution.py:129
  170.9 9.7 %all-to-all-done = bf16[64,2,576]{2,1,0:T(2,128)(2,1)S(1)} async-done(((bf16[64,2,576]{2,1,0:T(2,128)(2,1)}), bf16[64,2,576]{2,1,0:T(2,128)(2,1)S(1)}, u32[]{:S(2)}, u32[]{:S(2)}) %all-to-all-start) | async-done | bytes 147488 | tf_op jit(solution)/shard_map/all_to_all | solution.py:129
  188.7 15.6 %all_to_all.10 = bf16[64,2,576]{2,1,0:T(2,128)(2,1)S(1)} all-to-all(bf16[64,2,576]{2,1,0:T(2,128)(2,1)S(1)} %reshape.336), channel_id=1, replica_groups=mesh['rep'=8,'tp'=64] {'tp'}, dimensions={0} | all-to-all | bytes 294912 | tf_op jit(solution)/shard_map/all_to_all | solution.py:134
  (167 shorter events, 54.4 us)
Async XLA Ops:
  0.0 185.6 %copy-start = (bf16[2304,180]{0,1:T(8,128)(2,1)S(1)}, bf16[2304,180]{0,1:T(8,128)(2,1)}, u32[]{:S(2)}) copy-start(bf16[2304,180]{0,1:T(8,128)(2,1)} %param.29) | copy-start | bytes 2488324
  5.3 21.6 %copy-start.15 = (s32[8]{0:T(128)S(1)}, s32[8]{0:T(128)}, u32[]{:S(2)}) copy-start(s32[8]{0:T(128)} %param.25) | copy-start | bytes 100
  5.5 10.2 %collective-permute-start = (f32[32,3488]{1,0:T(8,128)S(1)}, f32[32,3488]{1,0:T(8,128)S(1)}, u32[]{:S(2)}, u32[]{:S(2)}) collective-permute-start(f32[32,3488]{1,0:T(8,128)S(1)} %constant_dynamic-slice_fusion.3), channel_id=1, source_target_pairs={{0,1},{1,0},{2,3},{3,2},{4,5},{5,4},{6,7},{7,6},{8,9},{9,8},{10,11... | collective-permute-start | bytes 1339400 | tf_op jit(solution)/shard_map/ppermute | solution.py:57
  15.9 47.4 %copy-start.7 = (bf16[3,32,2304]{2,1,0:T(8,128)(2,1)S(1)}, bf16[3,32,2304]{2,1,0:T(8,128)(2,1)}, u32[]{:S(2)}) copy-start(bf16[3,32,2304]{2,1,0:T(8,128)(2,1)} %param.20) | copy-start | bytes 1327108
  16.1 8.7 %collective-permute-start.1 = (f32[32,1744]{1,0:T(8,128)S(1)}, f32[32,1744]{1,0:T(8,128)S(1)}, u32[]{:S(2)}, u32[]{:S(2)}) collective-permute-start(f32[32,1744]{1,0:T(8,128)S(1)} %constant_dynamic-slice_fusion.2), channel_id=1, source_target_pairs={{0,2},{1,3},{2,0},{3,1},{4,6},{5,7},{6,4},{7,5},{8,10},{9,11},{10,... | collective-permute-start | bytes 669704 | tf_op jit(solution)/shard_map/ppermute | solution.py:57
  25.0 5.5 %collective-permute-start.2 = (f32[32,872]{1,0:T(8,128)S(1)}, f32[32,872]{1,0:T(8,128)S(1)}, u32[]{:S(2)}, u32[]{:S(2)}) collective-permute-start(f32[32,872]{1,0:T(8,128)S(1)} %constant_dynamic-slice_fusion.1), channel_id=1, source_target_pairs={{0,8},{1,9},{2,10},{3,11},{4,12},{5,13},{6,14},{7,15},{8,0},{9,1},... | collective-permute-start | bytes 334856 | tf_op jit(solution)/shard_map/ppermute | solution.py:57
  27.2 37.9 %copy-start.9 = (bf16[8,8,2304]{2,1,0:T(8,128)(2,1)S(1)}, bf16[8,8,2304]{2,1,0:T(8,128)(2,1)}, u32[]{:S(2)}) copy-start(bf16[8,8,2304]{2,1,0:T(8,128)(2,1)} %param.22) | copy-start | bytes 884740
  30.7 7.0 %collective-permute-start.3 = (f32[32,872]{1,0:T(8,128)S(1)}, f32[32,872]{1,0:T(8,128)S(1)}, u32[]{:S(2)}, u32[]{:S(2)}) collective-permute-start(f32[32,872]{1,0:T(8,128)S(1)} %dynamic-slice_add_fusion.2), channel_id=1, source_target_pairs={{0,4},{1,5},{2,6},{3,7},{4,0},{5,1},{6,2},{7,3},{8,12},{9,13},{10,... | collective-permute-start | bytes 334856 | tf_op jit(solution)/shard_map/ppermute | solution.py:87
  37.7 7.4 %collective-permute-start.4 = (f32[32,872]{1,0:T(8,128)S(1)}, f32[32,872]{1,0:T(8,128)S(1)}, u32[]{:S(2)}, u32[]{:S(2)}) collective-permute-start(f32[32,872]{1,0:T(8,128)S(1)} %add.226), channel_id=1, source_target_pairs={{0,16},{1,17},{2,18},{3,19},{4,20},{5,21},{6,22},{7,23},{8,24},{9,... | collective-permute-start | bytes 334856 | tf_op jit(solution)/shard_map/ppermute | solution.py:87
  45.2 9.4 %collective-permute-start.5 = (f32[32,872]{1,0:T(8,128)S(1)}, f32[32,872]{1,0:T(8,128)S(1)}, u32[]{:S(2)}, u32[]{:S(2)}) collective-permute-start(f32[32,872]{1,0:T(8,128)S(1)} %add.227), channel_id=1, source_target_pairs={{0,32},{1,33},{2,34},{3,35},{4,36},{5,37},{6,38},{7,39},{8,40},{9,... | collective-permute-start | bytes 334856 | tf_op jit(solution)/shard_map/ppermute | solution.py:87
  50.8 15.5 %copy-start.10 = (bf16[8,8,2304]{2,1,0:T(8,128)(2,1)S(1)}, bf16[8,8,2304]{2,1,0:T(8,128)(2,1)}, u32[]{:S(2)}) copy-start(bf16[8,8,2304]{2,1,0:T(8,128)(2,1)} %param.23) | copy-start | bytes 884740
  55.5 5.8 %collective-permute-start.6 = (bf16[32,864]{1,0:T(8,128)(2,1)S(1)}, bf16[32,864]{1,0:T(8,128)(2,1)S(1)}, u32[]{:S(2)}, u32[]{:S(2)}) collective-permute-start(bf16[32,864]{1,0:T(8,128)(2,1)S(1)} %reshape.292), channel_id=1, source_target_pairs={{0,8},{1,9},{2,10},{3,11},{4,12},{5,13},{6,14},{7,15},{8,0},{9,1},... | collective-permute-start | bytes 165896 | tf_op jit(solution)/shard_map/ppermute | solution.py:67
  57.4 10.3 %copy-start.8 = (bf16[3,32,2304]{2,1,0:T(8,128)(2,1)S(1)}, bf16[3,32,2304]{2,1,0:T(8,128)(2,1)}, u32[]{:S(2)}) copy-start(bf16[3,32,2304]{2,1,0:T(8,128)(2,1)} %param.21) | copy-start | bytes 1327108
  61.4 8.0 %collective-permute-start.7 = (bf16[32,1728]{1,0:T(8,128)(2,1)S(1)}, bf16[32,1728]{1,0:T(8,128)(2,1)S(1)}, u32[]{:S(2)}, u32[]{:S(2)}) collective-permute-start(bf16[32,1728]{1,0:T(8,128)(2,1)S(1)} %maximum_select_fusion.3), channel_id=1, source_target_pairs={{0,2},{1,3},{2,0},{3,1},{4,6},{5,7},{6,4},{7,5},{8,10},{9,11},{10,... | collective-permute-start | bytes 331784 | tf_op jit(solution)/shard_map/ppermute | solution.py:67
  65.1 12.7 %copy-start.16 = (s32[8]{0:T(128)S(1)}, s32[8]{0:T(128)}, u32[]{:S(2)}) copy-start(s32[8]{0:T(128)} %param.24) | copy-start | bytes 100
  69.5 9.2 %collective-permute-start.8 = (bf16[32,3456]{1,0:T(8,128)(2,1)S(1)}, bf16[32,3456]{1,0:T(8,128)(2,1)S(1)}, u32[]{:S(2)}, u32[]{:S(2)}) collective-permute-start(bf16[32,3456]{1,0:T(8,128)(2,1)S(1)} %maximum_select_fusion.1), channel_id=1, source_target_pairs={{0,1},{1,0},{2,3},{3,2},{4,5},{5,4},{6,7},{7,6},{8,9},{9,8},{10,11... | collective-permute-start | bytes 663560 | tf_op jit(solution)/shard_map/ppermute | solution.py:67
  81.1 4.6 %copy-start.4 = (bf16[8,4,36,64]{3,0,1,2:T(8,128)(2,1)}, bf16[8,4,36,64]{3,0,1,2:T(8,128)(2,1)S(1)}, u32[]{:S(2)}) copy-start(bf16[8,4,36,64]{3,0,1,2:T(8,128)(2,1)S(1)} %pad_maximum_fusion.2) | copy-start | bytes 442372
  93.2 7.7 %copy-start.3 = (bf16[32,36,32]{2,1,0:T(8,128)(2,1)S(1)}, bf16[32,36,32]{2,1,0:T(8,128)(2,1)}, u32[]{:S(2)}) copy-start(bf16[32,36,32]{2,1,0:T(8,128)(2,1)} %get-tuple-element.38) | copy-start | bytes 221188
  93.2 7.8 %copy-start.2 = (bf16[32,36,32]{2,1,0:T(8,128)(2,1)S(1)}, bf16[32,36,32]{2,1,0:T(8,128)(2,1)}, u32[]{:S(2)}) copy-start(bf16[32,36,32]{2,1,0:T(8,128)(2,1)} %get-tuple-element.37) | copy-start | bytes 221188
  93.3 3.6 %collective-permute-start.9 = (f32[576,66]{1,0:T(8,128)S(1)}, f32[576,66]{1,0:T(8,128)S(1)}, u32[]{:S(2)}, u32[]{:S(2)}) collective-permute-start(f32[576,66]{1,0:T(8,128)S(1)} %constant_dynamic-slice_fusion), channel_id=1, source_target_pairs={{0,1},{1,0},{2,3},{3,2},{4,5},{5,4},{6,7},{7,6},{8,9},{9,8},{10,11... | collective-permute-start | bytes 456200 | tf_op jit(solution)/shard_map/ppermute | solution.py:114
  97.5 9.6 %copy-start.5 = (bf16[8,4,36,64]{3,0,1,2:T(8,128)(2,1)S(1)}, bf16[8,4,36,64]{3,0,1,2:T(8,128)(2,1)}, u32[]{:S(2)}) copy-start(bf16[8,4,36,64]{3,0,1,2:T(8,128)(2,1)} %copy-done.4) | copy-start | bytes 442372
  97.7 7.0 %collective-permute-start.10 = (f32[288,66]{1,0:T(8,128)S(1)}, f32[288,66]{1,0:T(8,128)S(1)}, u32[]{:S(2)}, u32[]{:S(2)}) collective-permute-start(f32[288,66]{1,0:T(8,128)S(1)} %get-tuple-element.31), channel_id=1, source_target_pairs={{0,2},{1,3},{2,0},{3,1},{4,6},{5,7},{6,4},{7,5},{8,10},{9,11},{10,... | collective-permute-start | bytes 228104 | tf_op jit(solution)/shard_map/ppermute | solution.py:114
  105.2 5.1 %collective-permute-start.11 = (f32[144,66]{1,0:T(8,128)S(1)}, f32[144,66]{1,0:T(8,128)S(1)}, u32[]{:S(2)}, u32[]{:S(2)}) collective-permute-start(f32[144,66]{1,0:T(8,128)S(1)} %get-tuple-element.35), channel_id=1, source_target_pairs={{0,8},{1,9},{2,10},{3,11},{4,12},{5,13},{6,14},{7,15},{8,0},{9,1},... | collective-permute-start | bytes 114056 | tf_op jit(solution)/shard_map/ppermute | solution.py:114
  110.7 6.6 %collective-permute-start.12 = (f32[144,66]{1,0:T(8,128)S(1)}, f32[144,66]{1,0:T(8,128)S(1)}, u32[]{:S(2)}, u32[]{:S(2)}) collective-permute-start(f32[144,66]{1,0:T(8,128)S(1)} %pad_maximum_fusion.3), channel_id=1, source_target_pairs={{0,4},{1,5},{2,6},{3,7},{4,0},{5,1},{6,2},{7,3},{8,12},{9,13},{10,... | collective-permute-start | bytes 114056 | tf_op jit(solution)/shard_map/ppermute | solution.py:94
  117.8 6.0 %collective-permute-start.13 = (f32[144,66]{1,0:T(8,128)S(1)}, f32[144,66]{1,0:T(8,128)S(1)}, u32[]{:S(2)}, u32[]{:S(2)}) collective-permute-start(f32[144,66]{1,0:T(8,128)S(1)} %pad_maximum_fusion.4), channel_id=1, source_target_pairs={{0,16},{1,17},{2,18},{3,19},{4,20},{5,21},{6,22},{7,23},{8,24},{9,... | collective-permute-start | bytes 114056 | tf_op jit(solution)/shard_map/ppermute | solution.py:94
  124.2 32.0 %copy-start.11 = (bf16[2304,36]{0,1:T(8,128)(2,1)S(1)}, bf16[2304,36]{0,1:T(8,128)(2,1)}, u32[]{:S(2)}) copy-start(bf16[2304,36]{0,1:T(8,128)(2,1)} %param.19) | copy-start | bytes 497668
  124.2 32.0 %copy-start.12 = (f32[32,36]{1,0:T(8,128)S(1)}, f32[32,36]{1,0:T(8,128)}, u32[]{:S(2)}) copy-start(f32[32,36]{1,0:T(8,128)} %param.16) | copy-start | bytes 13828
  124.2 9.7 %collective-permute-start.14 = (f32[144,66]{1,0:T(8,128)S(1)}, f32[144,66]{1,0:T(8,128)S(1)}, u32[]{:S(2)}, u32[]{:S(2)}) collective-permute-start(f32[144,66]{1,0:T(8,128)S(1)} %pad_maximum_fusion.5), channel_id=1, source_target_pairs={{0,32},{1,33},{2,34},{3,35},{4,36},{5,37},{6,38},{7,39},{8,40},{9,... | collective-permute-start | bytes 114056 | tf_op jit(solution)/shard_map/ppermute | solution.py:94
  134.8 4.8 %collective-permute-start.15 = (bf16[72,128]{1,0:T(8,128)(2,1)S(1)}, bf16[72,128]{1,0:T(8,128)(2,1)S(1)}, u32[]{:S(2)}, u32[]{:S(2)}) collective-permute-start(bf16[72,128]{1,0:T(8,128)(2,1)S(1)} %reshape.302), channel_id=1, source_target_pairs={{0,8},{1,9},{2,10},{3,11},{4,12},{5,13},{6,14},{7,15},{8,0},{9,1},... | collective-permute-start | bytes 55304 | tf_op jit(solution)/shard_map/ppermute | solution.py:67
  139.6 4.7 %collective-permute-start.16 = (bf16[144,128]{1,0:T(8,128)(2,1)S(1)}, bf16[144,128]{1,0:T(8,128)(2,1)S(1)}, u32[]{:S(2)}, u32[]{:S(2)}) collective-permute-start(bf16[144,128]{1,0:T(8,128)(2,1)S(1)} %maximum_select_fusion.5), channel_id=1, source_target_pairs={{0,2},{1,3},{2,0},{3,1},{4,6},{5,7},{6,4},{7,5},{8,10},{9,11},{10,... | collective-permute-start | bytes 110600 | tf_op jit(solution)/shard_map/ppermute | solution.py:67
  144.4 11.6 %collective-permute-start.17 = (bf16[288,128]{1,0:T(8,128)(2,1)S(1)}, bf16[288,128]{1,0:T(8,128)(2,1)S(1)}, u32[]{:S(2)}, u32[]{:S(2)}) collective-permute-start(bf16[288,128]{1,0:T(8,128)(2,1)S(1)} %maximum_select_fusion.4), channel_id=1, source_target_pairs={{0,1},{1,0},{2,3},{3,2},{4,5},{5,4},{6,7},{7,6},{8,9},{9,8},{10,11... | collective-permute-start | bytes 221192 | tf_op jit(solution)/shard_map/ppermute | solution.py:67
  157.9 22.7 %all-to-all-start = ((bf16[64,2,576]{2,1,0:T(2,128)(2,1)}), bf16[64,2,576]{2,1,0:T(2,128)(2,1)S(1)}, u32[]{:S(2)}, u32[]{:S(2)}) async-start(bf16[64,2,576]{2,1,0:T(2,128)(2,1)} %reshape.334), calls=%async_computation | async-start | bytes 327680 | tf_op jit(solution)/shard_map/all_to_all | solution.py:129
  (4 other events, 7.4 us)

commit v14 on v13

--- a/solution.py
+++ b/solution.py
@@ -183,7 +183,7 @@
         axis=2,
     ).reshape(all_tokens, tp_count * (block + 1))
     _, all_bits = tp_bits()
-    near_bits = [all_bits[0], all_bits[1], all_bits[3]]
+    near_bits = [all_bits[0], all_bits[3], all_bits[1]]
     far_bits = [all_bits[2], all_bits[4], all_bits[5]]
     own_block = exchange_sum(scatter_sum(packed, near_bits), far_bits)
     own_block = own_block.reshape(all_tokens, -1, block + 1)

time: 208 us -> 207 us (level)
    ppermute x6, starting transfers between devices: 29.2 us -> 27 us  [gather_cols(): other = lax.ppermute(values, 'tp', partner_pairs(count, bit))]
where the time goes in v14:
time: 207 us; the launch traced here: 206 us
  starting transfers between devices  83.9 us (41%)
  waiting for transfers between devices  56.5 us (27%)
  local copies, waits for them, and re-layouts  23 us (11%)
  blocking collectives  15.6 us (8%)
  matrix products  13.1 us (6%)
  other arithmetic  13 us (6%)
    ppermute x6, starting transfers between devices, gather_cols(): other = lax.ppermute(values, 'tp', partner_pairs(count, bit))  27 us
    ppermute x3, starting transfers between devices, exchange_merge(): rows = merge_rows(rows, lax.ppermute(rows, 'tp', partner_pairs(count, bit)))  16.1 us
    all_to_all x1, blocking collectives, exchange_scatter_sum(): received = lax.all_to_all(blocks, 'tp', 0, 0, tiled=True)  15.6 us
    ppermute x3, waiting for transfers between devices, exchange_sum(): values = values + lax.ppermute(values, 'tp', partner_pairs(count, bit))  14.8 us
    ppermute x3, starting transfers between devices, scatter_sum(): values = keep + lax.ppermute(send, 'tp', partner_pairs(count, bit))  12.6 us
    ppermute x3, waiting for transfers between devices, scatter_sum(): values = keep + lax.ppermute(send, 'tp', partner_pairs(count, bit))  11.5 us
    all_to_all x1, starting transfers between devices, exchange_gather(): received = lax.all_to_all(copies, 'tp', 0, 0, tiled=True)  11.1 us
    all_to_all x1, waiting for transfers between devices, exchange_gather(): received = lax.all_to_all(copies, 'tp', 0, 0, tiled=True)  9.75 us
  transfers between devices with their start and end apart: 19, of which 18 were waited for; matrix products, arithmetic and copies ran while one was open for 6% of the time, Pallas kernels for 0%

profile of v14, /device:TPU:1, one launch (start us, length us, event | category | flops | bytes accessed | tf_op | source)
XLA Modules:
  0.0 206.3 jit_solution(6509721543462123136)
XLA Ops:
  2.3 2.0 reshape.289
  5.5 8.8 %collective-permute-start = (f32[32,3488]{1,0:T(8,128)S(1)}, f32[32,3488]{1,0:T(8,128)S(1)}, u32[]{:S(2)}, u32[]{:S(2)}) collective-permute-start(f32[32,3488]{1,0:T(8,128)S(1)} %constant_dynamic-slice_fusion.3), channel_id=1, source_target_pairs={{0,1},{1,0},{2,3},{3,2},{4,5},{5,4},{6,7},{7,6},{8,9},{9,8},{10,11... | collective-permute-start | bytes 1339400 | tf_op jit(solution)/shard_map/ppermute | solution.py:57
  16.1 1.9 collective-permute-start.1
  18.1 6.7 %collective-permute-done.1 = f32[32,1744]{1,0:T(8,128)S(1)} collective-permute-done((f32[32,1744]{1,0:T(8,128)S(1)}, f32[32,1744]{1,0:T(8,128)S(1)}, u32[]{:S(2)}, u32[]{:S(2)}) %collective-permute-start.1) | collective-permute-done | bytes 223264 | tf_op jit(solution)/shard_map/ppermute | solution.py:57
  25.0 1.9 collective-permute-start.2
  27.2 3.4 %collective-permute-done.2 = f32[32,872]{1,0:T(8,128)S(1)} collective-permute-done((f32[32,872]{1,0:T(8,128)S(1)}, f32[32,872]{1,0:T(8,128)S(1)}, u32[]{:S(2)}, u32[]{:S(2)}) %collective-permute-start.2) | collective-permute-done | bytes 111648 | tf_op jit(solution)/shard_map/ppermute | solution.py:57
  30.7 1.9 collective-permute-start.3
  32.6 5.1 %collective-permute-done.3 = f32[32,872]{1,0:T(8,128)S(1)} collective-permute-done((f32[32,872]{1,0:T(8,128)S(1)}, f32[32,872]{1,0:T(8,128)S(1)}, u32[]{:S(2)}, u32[]{:S(2)}) %collective-permute-start.3) | collective-permute-done | bytes 111648 | tf_op jit(solution)/shard_map/ppermute | solution.py:87
  39.7 5.7 %collective-permute-done.4 = f32[32,872]{1,0:T(8,128)S(1)} collective-permute-done((f32[32,872]{1,0:T(8,128)S(1)}, f32[32,872]{1,0:T(8,128)S(1)}, u32[]{:S(2)}, u32[]{:S(2)}) %collective-permute-start.4) | collective-permute-done | bytes 111648 | tf_op jit(solution)/shard_map/ppermute | solution.py:87
  45.4 5.3 %collective-permute-start.5 = (f32[32,872]{1,0:T(8,128)S(1)}, f32[32,872]{1,0:T(8,128)S(1)}, u32[]{:S(2)}, u32[]{:S(2)}) collective-permute-start(f32[32,872]{1,0:T(8,128)S(1)} %add.227), channel_id=1, source_target_pairs={{0,32},{1,33},{2,34},{3,35},{4,36},{5,37},{6,38},{7,39},{8,40},{9,... | collective-permute-start | bytes 334856 | tf_op jit(solution)/shard_map/ppermute | solution.py:87
  50.9 4.0 %collective-permute-done.5 = f32[32,872]{1,0:T(8,128)S(1)} collective-permute-done((f32[32,872]{1,0:T(8,128)S(1)}, f32[32,872]{1,0:T(8,128)S(1)}, u32[]{:S(2)}, u32[]{:S(2)}) %collective-permute-start.5) | collective-permute-done | bytes 111648 | tf_op jit(solution)/shard_map/ppermute | solution.py:87
  55.7 2.0 collective-permute-start.6
  57.8 2.8 %collective-permute-done.6 = bf16[32,864]{1,0:T(8,128)(2,1)S(1)} collective-permute-done((bf16[32,864]{1,0:T(8,128)(2,1)S(1)}, bf16[32,864]{1,0:T(8,128)(2,1)S(1)}, u32[]{:S(2)}, u32[]{:S(2)}) %collective-permute-start.6) | collective-permute-done | bytes 55328 | tf_op jit(solution)/shard_map/ppermute | solution.py:67
  68.8 8.8 %collective-permute-start.8 = (bf16[32,3456]{1,0:T(8,128)(2,1)S(1)}, bf16[32,3456]{1,0:T(8,128)(2,1)S(1)}, u32[]{:S(2)}, u32[]{:S(2)}) collective-permute-start(bf16[32,3456]{1,0:T(8,128)(2,1)S(1)} %maximum_select_fusion.1), channel_id=1, source_target_pairs={{0,1},{1,0},{2,3},{3,2},{4,5},{5,4},{6,7},{7,6},{8,9},{9,8},{10,11... | collective-permute-start | bytes 663560 | tf_op jit(solution)/shard_map/ppermute | solution.py:67
  83.0 2.5 %fusion.85 = (f32[8,4,36]{1,2,0:T(8,128)S(1)}, f32[8,4,36,8]{3,1,2,0:T(4,128)}) fusion(bf16[8,8,36,64]{3,2,1,0:T(8,128)(2,1)} %reshape.296, bf16[8,4,36,64]{3,0,1,2:T(8,128)(2,1)S(1)} %pad_maximum_fusion.2, pred[8,8]{1,0:T(8,128)(4,1)S(1)} %broadcast_compare_fusion), kind=kOutput, calls=%fused_computation.184 | convolution fusion | flops 1206144 | bytes 483904 | tf_op jit(solution)/shard_map/rjhd,rphd->rjhp/dot_general | solution.py:218
  93.1 2.4 %collective-permute-start.9 = (f32[576,66]{1,0:T(8,128)S(1)}, f32[576,66]{1,0:T(8,128)S(1)}, u32[]{:S(2)}, u32[]{:S(2)}) collective-permute-start(f32[576,66]{1,0:T(8,128)S(1)} %constant_dynamic-slice_fusion), channel_id=1, source_target_pairs={{0,1},{1,0},{2,3},{3,2},{4,5},{5,4},{6,7},{7,6},{8,9},{9,8},{10,11... | collective-permute-start | bytes 456200 | tf_op jit(solution)/shard_map/ppermute | solution.py:114
  97.5 3.6 %collective-permute-start.10 = (f32[288,66]{1,0:T(8,128)S(1)}, f32[288,66]{1,0:T(8,128)S(1)}, u32[]{:S(2)}, u32[]{:S(2)}) collective-permute-start(f32[288,66]{1,0:T(8,128)S(1)} %get-tuple-element.31), channel_id=1, source_target_pairs={{0,8},{1,9},{2,10},{3,11},{4,12},{5,13},{6,14},{7,15},{8,0},{9,1},... | collective-permute-start | bytes 228104 | tf_op jit(solution)/shard_map/ppermute | solution.py:114
  101.4 3.6 %collective-permute-done.10 = f32[288,66]{1,0:T(8,128)S(1)} collective-permute-done((f32[288,66]{1,0:T(8,128)S(1)}, f32[288,66]{1,0:T(8,128)S(1)}, u32[]{:S(2)}, u32[]{:S(2)}) %collective-permute-start.10) | collective-permute-done | bytes 76064 | tf_op jit(solution)/shard_map/ppermute | solution.py:114
  105.6 1.9 collective-permute-start.11
  108.7 2.0 collective-permute-done.11
  111.2 3.8 %collective-permute-start.12 = (f32[144,66]{1,0:T(8,128)S(1)}, f32[144,66]{1,0:T(8,128)S(1)}, u32[]{:S(2)}, u32[]{:S(2)}) collective-permute-start(f32[144,66]{1,0:T(8,128)S(1)} %pad_maximum_fusion.3), channel_id=1, source_target_pairs={{0,4},{1,5},{2,6},{3,7},{4,0},{5,1},{6,2},{7,3},{8,12},{9,13},{10,... | collective-permute-start | bytes 114056 | tf_op jit(solution)/shard_map/ppermute | solution.py:94
  115.5 2.3 %collective-permute-done.12 = f32[144,66]{1,0:T(8,128)S(1)} collective-permute-done((f32[144,66]{1,0:T(8,128)S(1)}, f32[144,66]{1,0:T(8,128)S(1)}, u32[]{:S(2)}, u32[]{:S(2)}) %collective-permute-start.12) | collective-permute-done | bytes 38048 | tf_op jit(solution)/shard_map/ppermute | solution.py:94
  118.2 4.2 %collective-permute-start.13 = (f32[144,66]{1,0:T(8,128)S(1)}, f32[144,66]{1,0:T(8,128)S(1)}, u32[]{:S(2)}, u32[]{:S(2)}) collective-permute-start(f32[144,66]{1,0:T(8,128)S(1)} %pad_maximum_fusion.4), channel_id=1, source_target_pairs={{0,16},{1,17},{2,18},{3,19},{4,20},{5,21},{6,22},{7,23},{8,24},{9,... | collective-permute-start | bytes 114056 | tf_op jit(solution)/shard_map/ppermute | solution.py:94
  124.7 8.2 %collective-permute-start.14 = (f32[144,66]{1,0:T(8,128)S(1)}, f32[144,66]{1,0:T(8,128)S(1)}, u32[]{:S(2)}, u32[]{:S(2)}) collective-permute-start(f32[144,66]{1,0:T(8,128)S(1)} %pad_maximum_fusion.5), channel_id=1, source_target_pairs={{0,32},{1,33},{2,34},{3,35},{4,36},{5,37},{6,38},{7,39},{8,40},{9,... | collective-permute-start | bytes 114056 | tf_op jit(solution)/shard_map/ppermute | solution.py:94
  135.5 2.2 %collective-permute-start.15 = (bf16[72,128]{1,0:T(8,128)(2,1)S(1)}, bf16[72,128]{1,0:T(8,128)(2,1)S(1)}, u32[]{:S(2)}, u32[]{:S(2)}) collective-permute-start(bf16[72,128]{1,0:T(8,128)(2,1)S(1)} %reshape.302), channel_id=1, source_target_pairs={{0,2},{1,3},{2,0},{3,1},{4,6},{5,7},{6,4},{7,5},{8,10},{9,11},{10,... | collective-permute-start | bytes 55304 | tf_op jit(solution)/shard_map/ppermute | solution.py:67
  137.8 2.3 %collective-permute-done.15 = bf16[72,128]{1,0:T(8,128)(2,1)S(1)} collective-permute-done((bf16[72,128]{1,0:T(8,128)(2,1)S(1)}, bf16[72,128]{1,0:T(8,128)(2,1)S(1)}, u32[]{:S(2)}, u32[]{:S(2)}) %collective-permute-start.15) | collective-permute-done | bytes 18464 | tf_op jit(solution)/shard_map/ppermute | solution.py:67
  140.1 2.5 %collective-permute-start.16 = (bf16[144,128]{1,0:T(8,128)(2,1)S(1)}, bf16[144,128]{1,0:T(8,128)(2,1)S(1)}, u32[]{:S(2)}, u32[]{:S(2)}) collective-permute-start(bf16[144,128]{1,0:T(8,128)(2,1)S(1)} %maximum_select_fusion.5), channel_id=1, source_target_pairs={{0,8},{1,9},{2,10},{3,11},{4,12},{5,13},{6,14},{7,15},{8,0},{9,1},... | collective-permute-start | bytes 110600 | tf_op jit(solution)/shard_map/ppermute | solution.py:67
  142.5 2.2 %collective-permute-done.16 = bf16[144,128]{1,0:T(8,128)(2,1)S(1)} collective-permute-done((bf16[144,128]{1,0:T(8,128)(2,1)S(1)}, bf16[144,128]{1,0:T(8,128)(2,1)S(1)}, u32[]{:S(2)}, u32[]{:S(2)}) %collective-permute-start.16) | collective-permute-done | bytes 36896 | tf_op jit(solution)/shard_map/ppermute | solution.py:67
  144.8 9.6 %collective-permute-start.17 = (bf16[288,128]{1,0:T(8,128)(2,1)S(1)}, bf16[288,128]{1,0:T(8,128)(2,1)S(1)}, u32[]{:S(2)}, u32[]{:S(2)}) collective-permute-start(bf16[288,128]{1,0:T(8,128)(2,1)S(1)} %maximum_select_fusion.4), channel_id=1, source_target_pairs={{0,1},{1,0},{2,3},{3,2},{4,5},{5,4},{6,7},{7,6},{8,9},{9,8},{10,11... | collective-permute-start | bytes 221192 | tf_op jit(solution)/shard_map/ppermute | solution.py:67
  157.2 11.1 %all-to-all-start = ((bf16[64,2,576]{2,1,0:T(2,128)(2,1)}), bf16[64,2,576]{2,1,0:T(2,128)(2,1)S(1)}, u32[]{:S(2)}, u32[]{:S(2)}) async-start(bf16[64,2,576]{2,1,0:T(2,128)(2,1)} %reshape.334), calls=%async_computation | async-start | bytes 327680 | tf_op jit(solution)/shard_map/all_to_all | solution.py:129
  170.3 9.7 %all-to-all-done = bf16[64,2,576]{2,1,0:T(2,128)(2,1)S(1)} async-done(((bf16[64,2,576]{2,1,0:T(2,128)(2,1)}), bf16[64,2,576]{2,1,0:T(2,128)(2,1)S(1)}, u32[]{:S(2)}, u32[]{:S(2)}) %all-to-all-start) | async-done | bytes 147488 | tf_op jit(solution)/shard_map/all_to_all | solution.py:129
  188.1 15.6 %all_to_all.10 = bf16[64,2,576]{2,1,0:T(2,128)(2,1)S(1)} all-to-all(bf16[64,2,576]{2,1,0:T(2,128)(2,1)S(1)} %reshape.336), channel_id=1, replica_groups=mesh['rep'=8,'tp'=64] {'tp'}, dimensions={0} | all-to-all | bytes 294912 | tf_op jit(solution)/shard_map/all_to_all | solution.py:134
  (167 shorter events, 55.0 us)
Async XLA Ops:
  0.0 185.0 %copy-start = (bf16[2304,180]{0,1:T(8,128)(2,1)S(1)}, bf16[2304,180]{0,1:T(8,128)(2,1)}, u32[]{:S(2)}) copy-start(bf16[2304,180]{0,1:T(8,128)(2,1)} %param.29) | copy-start | bytes 2488324
  5.3 21.6 %copy-start.15 = (s32[8]{0:T(128)S(1)}, s32[8]{0:T(128)}, u32[]{:S(2)}) copy-start(s32[8]{0:T(128)} %param.25) | copy-start | bytes 100
  5.5 10.2 %collective-permute-start = (f32[32,3488]{1,0:T(8,128)S(1)}, f32[32,3488]{1,0:T(8,128)S(1)}, u32[]{:S(2)}, u32[]{:S(2)}) collective-permute-start(f32[32,3488]{1,0:T(8,128)S(1)} %constant_dynamic-slice_fusion.3), channel_id=1, source_target_pairs={{0,1},{1,0},{2,3},{3,2},{4,5},{5,4},{6,7},{7,6},{8,9},{9,8},{10,11... | collective-permute-start | bytes 1339400 | tf_op jit(solution)/shard_map/ppermute | solution.py:57
  15.9 46.8 %copy-start.7 = (bf16[3,32,2304]{2,1,0:T(8,128)(2,1)S(1)}, bf16[3,32,2304]{2,1,0:T(8,128)(2,1)}, u32[]{:S(2)}) copy-start(bf16[3,32,2304]{2,1,0:T(8,128)(2,1)} %param.20) | copy-start | bytes 1327108
  16.1 8.7 %collective-permute-start.1 = (f32[32,1744]{1,0:T(8,128)S(1)}, f32[32,1744]{1,0:T(8,128)S(1)}, u32[]{:S(2)}, u32[]{:S(2)}) collective-permute-start(f32[32,1744]{1,0:T(8,128)S(1)} %constant_dynamic-slice_fusion.2), channel_id=1, source_target_pairs={{0,8},{1,9},{2,10},{3,11},{4,12},{5,13},{6,14},{7,15},{8,0},{9,1},... | collective-permute-start | bytes 669704 | tf_op jit(solution)/shard_map/ppermute | solution.py:57
  25.0 5.5 %collective-permute-start.2 = (f32[32,872]{1,0:T(8,128)S(1)}, f32[32,872]{1,0:T(8,128)S(1)}, u32[]{:S(2)}, u32[]{:S(2)}) collective-permute-start(f32[32,872]{1,0:T(8,128)S(1)} %constant_dynamic-slice_fusion.1), channel_id=1, source_target_pairs={{0,2},{1,3},{2,0},{3,1},{4,6},{5,7},{6,4},{7,5},{8,10},{9,11},{10,... | collective-permute-start | bytes 334856 | tf_op jit(solution)/shard_map/ppermute | solution.py:57
  27.2 37.3 %copy-start.9 = (bf16[8,8,2304]{2,1,0:T(8,128)(2,1)S(1)}, bf16[8,8,2304]{2,1,0:T(8,128)(2,1)}, u32[]{:S(2)}) copy-start(bf16[8,8,2304]{2,1,0:T(8,128)(2,1)} %param.22) | copy-start | bytes 884740
  30.7 7.0 %collective-permute-start.3 = (f32[32,872]{1,0:T(8,128)S(1)}, f32[32,872]{1,0:T(8,128)S(1)}, u32[]{:S(2)}, u32[]{:S(2)}) collective-permute-start(f32[32,872]{1,0:T(8,128)S(1)} %dynamic-slice_add_fusion.2), channel_id=1, source_target_pairs={{0,4},{1,5},{2,6},{3,7},{4,0},{5,1},{6,2},{7,3},{8,12},{9,13},{10,... | collective-permute-start | bytes 334856 | tf_op jit(solution)/shard_map/ppermute | solution.py:87
  37.7 7.7 %collective-permute-start.4 = (f32[32,872]{1,0:T(8,128)S(1)}, f32[32,872]{1,0:T(8,128)S(1)}, u32[]{:S(2)}, u32[]{:S(2)}) collective-permute-start(f32[32,872]{1,0:T(8,128)S(1)} %add.226), channel_id=1, source_target_pairs={{0,16},{1,17},{2,18},{3,19},{4,20},{5,21},{6,22},{7,23},{8,24},{9,... | collective-permute-start | bytes 334856 | tf_op jit(solution)/shard_map/ppermute | solution.py:87
  45.4 9.4 %collective-permute-start.5 = (f32[32,872]{1,0:T(8,128)S(1)}, f32[32,872]{1,0:T(8,128)S(1)}, u32[]{:S(2)}, u32[]{:S(2)}) collective-permute-start(f32[32,872]{1,0:T(8,128)S(1)} %add.227), channel_id=1, source_target_pairs={{0,32},{1,33},{2,34},{3,35},{4,36},{5,37},{6,38},{7,39},{8,40},{9,... | collective-permute-start | bytes 334856 | tf_op jit(solution)/shard_map/ppermute | solution.py:87
  50.8 14.9 %copy-start.10 = (bf16[8,8,2304]{2,1,0:T(8,128)(2,1)S(1)}, bf16[8,8,2304]{2,1,0:T(8,128)(2,1)}, u32[]{:S(2)}) copy-start(bf16[8,8,2304]{2,1,0:T(8,128)(2,1)} %param.23) | copy-start | bytes 884740
  55.7 4.9 %collective-permute-start.6 = (bf16[32,864]{1,0:T(8,128)(2,1)S(1)}, bf16[32,864]{1,0:T(8,128)(2,1)S(1)}, u32[]{:S(2)}, u32[]{:S(2)}) collective-permute-start(bf16[32,864]{1,0:T(8,128)(2,1)S(1)} %reshape.292), channel_id=1, source_target_pairs={{0,2},{1,3},{2,0},{3,1},{4,6},{5,7},{6,4},{7,5},{8,10},{9,11},{10,... | collective-permute-start | bytes 165896 | tf_op jit(solution)/shard_map/ppermute | solution.py:67
  57.8 9.3 %copy-start.8 = (bf16[3,32,2304]{2,1,0:T(8,128)(2,1)S(1)}, bf16[3,32,2304]{2,1,0:T(8,128)(2,1)}, u32[]{:S(2)}) copy-start(bf16[3,32,2304]{2,1,0:T(8,128)(2,1)} %param.21) | copy-start | bytes 1327108
  60.8 8.0 %collective-permute-start.7 = (bf16[32,1728]{1,0:T(8,128)(2,1)S(1)}, bf16[32,1728]{1,0:T(8,128)(2,1)S(1)}, u32[]{:S(2)}, u32[]{:S(2)}) collective-permute-start(bf16[32,1728]{1,0:T(8,128)(2,1)S(1)} %maximum_select_fusion.3), channel_id=1, source_target_pairs={{0,8},{1,9},{2,10},{3,11},{4,12},{5,13},{6,14},{7,15},{8,0},{9,1},... | collective-permute-start | bytes 331784 | tf_op jit(solution)/shard_map/ppermute | solution.py:67
  64.4 13.2 %copy-start.16 = (s32[8]{0:T(128)S(1)}, s32[8]{0:T(128)}, u32[]{:S(2)}) copy-start(s32[8]{0:T(128)} %param.24) | copy-start | bytes 100
  68.8 9.7 %collective-permute-start.8 = (bf16[32,3456]{1,0:T(8,128)(2,1)S(1)}, bf16[32,3456]{1,0:T(8,128)(2,1)S(1)}, u32[]{:S(2)}, u32[]{:S(2)}) collective-permute-start(bf16[32,3456]{1,0:T(8,128)(2,1)S(1)} %maximum_select_fusion.1), channel_id=1, source_target_pairs={{0,1},{1,0},{2,3},{3,2},{4,5},{5,4},{6,7},{7,6},{8,9},{9,8},{10,11... | collective-permute-start | bytes 663560 | tf_op jit(solution)/shard_map/ppermute | solution.py:67
  80.9 4.6 %copy-start.4 = (bf16[8,4,36,64]{3,0,1,2:T(8,128)(2,1)}, bf16[8,4,36,64]{3,0,1,2:T(8,128)(2,1)S(1)}, u32[]{:S(2)}) copy-start(bf16[8,4,36,64]{3,0,1,2:T(8,128)(2,1)S(1)} %pad_maximum_fusion.2) | copy-start | bytes 442372
  93.0 8.1 %copy-start.3 = (bf16[32,36,32]{2,1,0:T(8,128)(2,1)S(1)}, bf16[32,36,32]{2,1,0:T(8,128)(2,1)}, u32[]{:S(2)}) copy-start(bf16[32,36,32]{2,1,0:T(8,128)(2,1)} %get-tuple-element.38) | copy-start | bytes 221188
  93.1 8.2 %copy-start.2 = (bf16[32,36,32]{2,1,0:T(8,128)(2,1)S(1)}, bf16[32,36,32]{2,1,0:T(8,128)(2,1)}, u32[]{:S(2)}) copy-start(bf16[32,36,32]{2,1,0:T(8,128)(2,1)} %get-tuple-element.37) | copy-start | bytes 221188
  93.1 3.6 %collective-permute-start.9 = (f32[576,66]{1,0:T(8,128)S(1)}, f32[576,66]{1,0:T(8,128)S(1)}, u32[]{:S(2)}, u32[]{:S(2)}) collective-permute-start(f32[576,66]{1,0:T(8,128)S(1)} %constant_dynamic-slice_fusion), channel_id=1, source_target_pairs={{0,1},{1,0},{2,3},{3,2},{4,5},{5,4},{6,7},{7,6},{8,9},{9,8},{10,11... | collective-permute-start | bytes 456200 | tf_op jit(solution)/shard_map/ppermute | solution.py:114
  97.3 10.2 %copy-start.5 = (bf16[8,4,36,64]{3,0,1,2:T(8,128)(2,1)S(1)}, bf16[8,4,36,64]{3,0,1,2:T(8,128)(2,1)}, u32[]{:S(2)}) copy-start(bf16[8,4,36,64]{3,0,1,2:T(8,128)(2,1)} %copy-done.4) | copy-start | bytes 442372
  97.5 7.6 %collective-permute-start.10 = (f32[288,66]{1,0:T(8,128)S(1)}, f32[288,66]{1,0:T(8,128)S(1)}, u32[]{:S(2)}, u32[]{:S(2)}) collective-permute-start(f32[288,66]{1,0:T(8,128)S(1)} %get-tuple-element.31), channel_id=1, source_target_pairs={{0,8},{1,9},{2,10},{3,11},{4,12},{5,13},{6,14},{7,15},{8,0},{9,1},... | collective-permute-start | bytes 228104 | tf_op jit(solution)/shard_map/ppermute | solution.py:114
  105.6 5.1 %collective-permute-start.11 = (f32[144,66]{1,0:T(8,128)S(1)}, f32[144,66]{1,0:T(8,128)S(1)}, u32[]{:S(2)}, u32[]{:S(2)}) collective-permute-start(f32[144,66]{1,0:T(8,128)S(1)} %get-tuple-element.35), channel_id=1, source_target_pairs={{0,2},{1,3},{2,0},{3,1},{4,6},{5,7},{6,4},{7,5},{8,10},{9,11},{10,... | collective-permute-start | bytes 114056 | tf_op jit(solution)/shard_map/ppermute | solution.py:114
  111.2 6.6 %collective-permute-start.12 = (f32[144,66]{1,0:T(8,128)S(1)}, f32[144,66]{1,0:T(8,128)S(1)}, u32[]{:S(2)}, u32[]{:S(2)}) collective-permute-start(f32[144,66]{1,0:T(8,128)S(1)} %pad_maximum_fusion.3), channel_id=1, source_target_pairs={{0,4},{1,5},{2,6},{3,7},{4,0},{5,1},{6,2},{7,3},{8,12},{9,13},{10,... | collective-permute-start | bytes 114056 | tf_op jit(solution)/shard_map/ppermute | solution.py:94
  118.2 6.0 %collective-permute-start.13 = (f32[144,66]{1,0:T(8,128)S(1)}, f32[144,66]{1,0:T(8,128)S(1)}, u32[]{:S(2)}, u32[]{:S(2)}) collective-permute-start(f32[144,66]{1,0:T(8,128)S(1)} %pad_maximum_fusion.4), channel_id=1, source_target_pairs={{0,16},{1,17},{2,18},{3,19},{4,20},{5,21},{6,22},{7,23},{8,24},{9,... | collective-permute-start | bytes 114056 | tf_op jit(solution)/shard_map/ppermute | solution.py:94
  124.6 30.9 %copy-start.11 = (bf16[2304,36]{0,1:T(8,128)(2,1)S(1)}, bf16[2304,36]{0,1:T(8,128)(2,1)}, u32[]{:S(2)}) copy-start(bf16[2304,36]{0,1:T(8,128)(2,1)} %param.19) | copy-start | bytes 497668
  124.6 30.9 %copy-start.12 = (f32[32,36]{1,0:T(8,128)S(1)}, f32[32,36]{1,0:T(8,128)}, u32[]{:S(2)}) copy-start(f32[32,36]{1,0:T(8,128)} %param.16) | copy-start | bytes 13828
  124.7 10.0 %collective-permute-start.14 = (f32[144,66]{1,0:T(8,128)S(1)}, f32[144,66]{1,0:T(8,128)S(1)}, u32[]{:S(2)}, u32[]{:S(2)}) collective-permute-start(f32[144,66]{1,0:T(8,128)S(1)} %pad_maximum_fusion.5), channel_id=1, source_target_pairs={{0,32},{1,33},{2,34},{3,35},{4,36},{5,37},{6,38},{7,39},{8,40},{9,... | collective-permute-start | bytes 114056 | tf_op jit(solution)/shard_map/ppermute | solution.py:94
  135.5 4.5 %collective-permute-start.15 = (bf16[72,128]{1,0:T(8,128)(2,1)S(1)}, bf16[72,128]{1,0:T(8,128)(2,1)S(1)}, u32[]{:S(2)}, u32[]{:S(2)}) collective-permute-start(bf16[72,128]{1,0:T(8,128)(2,1)S(1)} %reshape.302), channel_id=1, source_target_pairs={{0,2},{1,3},{2,0},{3,1},{4,6},{5,7},{6,4},{7,5},{8,10},{9,11},{10,... | collective-permute-start | bytes 55304 | tf_op jit(solution)/shard_map/ppermute | solution.py:67
  140.1 4.7 %collective-permute-start.16 = (bf16[144,128]{1,0:T(8,128)(2,1)S(1)}, bf16[144,128]{1,0:T(8,128)(2,1)S(1)}, u32[]{:S(2)}, u32[]{:S(2)}) collective-permute-start(bf16[144,128]{1,0:T(8,128)(2,1)S(1)} %maximum_select_fusion.5), channel_id=1, source_target_pairs={{0,8},{1,9},{2,10},{3,11},{4,12},{5,13},{6,14},{7,15},{8,0},{9,1},... | collective-permute-start | bytes 110600 | tf_op jit(solution)/shard_map/ppermute | solution.py:67
  144.8 10.5 %collective-permute-start.17 = (bf16[288,128]{1,0:T(8,128)(2,1)S(1)}, bf16[288,128]{1,0:T(8,128)(2,1)S(1)}, u32[]{:S(2)}, u32[]{:S(2)}) collective-permute-start(bf16[288,128]{1,0:T(8,128)(2,1)S(1)} %maximum_select_fusion.4), channel_id=1, source_target_pairs={{0,1},{1,0},{2,3},{3,2},{4,5},{5,4},{6,7},{7,6},{8,9},{9,8},{10,11... | collective-permute-start | bytes 221192 | tf_op jit(solution)/shard_map/ppermute | solution.py:67
  157.2 22.8 %all-to-all-start = ((bf16[64,2,576]{2,1,0:T(2,128)(2,1)}), bf16[64,2,576]{2,1,0:T(2,128)(2,1)S(1)}, u32[]{:S(2)}, u32[]{:S(2)}) async-start(bf16[64,2,576]{2,1,0:T(2,128)(2,1)} %reshape.334), calls=%async_computation | async-start | bytes 327680 | tf_op jit(solution)/shard_map/all_to_all | solution.py:129
  (4 other events, 7.4 us)
